TPU v7x, 32 devices: a whole 2x2x4 slice. The times are simulated.
32 devices in a mesh: gx: 4 (over x, core), gy: 2 (over y), gz: 4 (over z).
Axes of the slice: x: 2, y: 2, z: 4, core: 2. Of those that a mesh axis runs over, the one named last changes fastest.
Arguments:
- latent: bfloat16 [4096, 512], P(('gx', 'gy', 'gz')), may hold values from -6 to 6
- positions: int32 [3, 4096], P(None, ('gx', 'gy', 'gz')), may hold values from 0 to 1279, as said below
- species: int32 [4096], P(('gx', 'gy', 'gz')), may hold values from 0 to 4
- send_list: int32 [32, 192], P(('gx', 'gy', 'gz')), may hold values from 0 to 287, as said below
- neighbour: int32 [32768], P(('gx', 'gy', 'gz')), may hold values from 0 to 319, as said below
- atom_count: int32 [32], P(('gx', 'gy', 'gz')), may hold values from 64 to 128, as said below
- centre_proj: bfloat16 [512, 512], replicated, may hold values from -0.25 to 0.25
- neigh_proj: bfloat16 [512, 512], replicated, may hold values from -0.25 to 0.25
- centre_table: float32 [5, 512], replicated, may hold values from -3 to 3
- neigh_table: float32 [5, 512], replicated, may hold values from -3 to 3
- basis_proj: bfloat16 [8, 512], replicated, may hold values from -2 to 2
- split_proj: bfloat16 [512, 384], replicated, may hold values from -0.25 to 0.25
- update_proj: bfloat16 [512, 512], replicated, may hold values from -0.25 to 0.25
- tensor_proj: bfloat16 [192, 512], replicated, may hold values from -0.4375 to 0.4375
- energy_proj: float32 [512], replicated, may hold values from -0.25 to 0.25
- species_shift: float32 [5], replicated, may hold values from -4 to 4
Outputs:
- energies: float32 [4096], P(('gx', 'gy', 'gz'))
- forces: float32 [3, 4096], P(None, ('gx', 'gy', 'gz'))
- latent_grad: float32 [4096, 512], P(('gx', 'gy', 'gz'))
Inputs may be any that keep to these rules, and one draw needn't show every extreme that they name: `positions`: coordinates from the domain's lower corner in units of 1/64 angstrom: row one below 1024, row two below 512, row three below 1280. `send_list`: entries of a segment are distinct live rows of the sending domain's table: x segments name own atoms, y segments own atoms or x ghost rows (below 160), z segments own, x or y ghost rows; the rows nearest its low-x, high-x, low-y, high-y, low-z and high-z faces in that order of segments. `neighbour`: the 8 entries of an atom are distinct live table rows other than the atom itself, among its nearest ones. `atom_count`: the live atoms are a domain's first slots; some domain in every draw has all 128 live.
All inputs are finite; a program needn't handle non-finite values.
Results may differ from a plain program's by a relative error of at most 0.015.
Values may be sent and summed in bfloat16 or wider, within the bound.
No kernel may reach another device: no remote copies, remote signals or barrier semaphores. Data moves between devices by JAX's collectives and lax.ppermute only.
A program may use at most 128 MiB of HBM per device.

v0:
```python
import math

import jax
import jax.numpy as jnp
from jax import lax
from jax.sharding import PartitionSpec as P

K = 8
CH = 64
NB = 8
NSPEC = 5
LX_FIX = 1024
LY_FIX = 512
LZ_FIX = 1280


CUTOFF = 6.0
SOFTEN = 0.25


def shortened(shard):
    return jax.tree.map(lambda a: a.astype(jnp.bfloat16) if a.dtype == jnp.float32 else a, shard)


def passed_along(block, axis, distance):
    devices = range(lax.axis_size(axis))
    route = [((i - distance) % len(devices), i) for i in devices]
    return lax.ppermute(block, axis, route)


def by_order(values):
    count = values.shape[1]
    pairs = values.shape[2]
    return jnp.concatenate(
        [
            values[0:1],
            jnp.broadcast_to(values[1:2], (3, count, pairs)),
            jnp.broadcast_to(values[2:3], (5, count, pairs)),
        ],
        axis=0,
    )


def pair_energy(
    delta,
    neigh_rows,
    centre_rows,
    valid_pair,
    basis_proj,
    split_proj,
    update_proj,
    tensor_proj,
    energy_proj,
):
    atoms = centre_rows.shape[0]
    pairs = delta.shape[1]
    radius = jnp.sqrt(jnp.sum(delta * delta, axis=0) + SOFTEN)
    unit = delta / radius
    ratio = radius / CUTOFF
    envelope = jnp.where(ratio < 1.0, (1.0 - ratio * ratio) ** 2, 0.0) * valid_pair
    orders = jnp.arange(1, NB + 1).astype(jnp.float32)
    basis = (
        jnp.sin(orders[:, None] * (math.pi / CUTOFF) * radius[None, :])
        * (envelope / radius)[None, :]
    )
    radial = jnp.einsum(
        "kp,kh->ph", basis, basis_proj.astype(jnp.float32), precision=lax.Precision.HIGHEST
    )
    hidden = (
        jax.nn.silu(jnp.tile(centre_rows, (K, 1)) + neigh_rows + radial) * envelope[:, None]
    )
    hidden_low = hidden.astype(jnp.bfloat16)
    mixed = jnp.einsum("ph,hq->qp", hidden_low, split_proj, preferred_element_type=jnp.float32)
    amplitude = mixed[: 3 * CH].reshape(3, CH, pairs)
    weights = mixed[3 * CH :].reshape(3, CH, pairs)
    unit_x = unit[0]
    unit_y = unit[1]
    unit_z = unit[2]
    root3 = math.sqrt(3.0)
    root15 = math.sqrt(15.0)
    root5 = math.sqrt(5.0)
    harmonics = jnp.stack(
        [
            jnp.ones_like(unit_x),
            root3 * unit_x,
            root3 * unit_y,
            root3 * unit_z,
            root15 * unit_x * unit_y,
            root15 * unit_y * unit_z,
            0.5 * root5 * (2.0 * unit_z * unit_z - unit_x * unit_x - unit_y * unit_y),
            root15 * unit_x * unit_z,
            0.5 * root15 * (unit_x * unit_x - unit_y * unit_y),
        ],
        axis=0,
    )
    gathered = by_order(weights) * harmonics[:, None, :]
    environment = gathered.reshape(9, CH, K, atoms).sum(axis=2) / math.sqrt(K)
    expanded = jnp.tile(environment, (1, 1, K))
    products = by_order(amplitude) * harmonics[:, None, :] * expanded
    scalars = jnp.stack([products[0], products[1:4].sum(axis=0), products[4:9].sum(axis=0)], axis=0)
    scalars = scalars.reshape(3 * CH, pairs).astype(jnp.bfloat16)
    update = jax.nn.silu(
        jnp.dot(hidden_low, update_proj, preferred_element_type=jnp.float32)
        + jnp.einsum("qp,qh->ph", scalars, tensor_proj, preferred_element_type=jnp.float32)
    )
    energy = envelope * jnp.dot(hidden + update, energy_proj, precision=lax.Precision.HIGHEST)
    return energy.reshape(K, atoms).sum(axis=0)


def shards(
    latent,
    positions,
    species,
    send_list,
    neighbour,
    atom_count,
    centre_proj,
    neigh_proj,
    centre_table,
    neigh_table,
    basis_proj,
    split_proj,
    update_proj,
    tensor_proj,
    energy_proj,
    species_shift,
):
    atoms = latent.shape[0]
    face_x = atoms // 8
    face_y = atoms // 2
    face_z = atoms // 8
    lengths = [face_x, face_x, face_y, face_y, face_z, face_z]
    starts = [
        0,
        face_x,
        2 * face_x,
        2 * face_x + face_y,
        2 * face_x + 2 * face_y,
        2 * face_x + 2 * face_y + face_z,
    ]
    kinds = jnp.arange(NSPEC, dtype=jnp.int32)

    def lookup(codes, table):
        onehot = (codes[:, None] == kinds[None, :]).astype(jnp.float32)
        return jnp.dot(onehot, table, precision=lax.Precision.HIGHEST)

    def project(rows, codes, weight, table):
        return (
            jnp.dot(rows, weight, preferred_element_type=jnp.float32) + lookup(codes, table)
        ).astype(jnp.bfloat16)

    proj_c = project(latent, species, centre_proj, centre_table)
    proj_n = project(latent, species, neigh_proj, neigh_table)
    send_rows = send_list[0]
    coded = jnp.concatenate([positions, species[None, :]], axis=0)
    source_tab = latent
    coded_tab = coded
    offsets = [(0, -LX_FIX), (0, LX_FIX), (1, -LY_FIX), (1, LY_FIX), (2, -LZ_FIX), (2, LZ_FIX)]

    def outgoing(segment, rows_tab, codes_tab):
        picked = send_rows[starts[segment] : starts[segment] + lengths[segment]]
        return (jnp.take(rows_tab, picked, axis=0), jnp.take(codes_tab, picked, axis=1))

    def extend(rows_tab, codes_tab, arrivals, first):
        rows_list = [rows_tab]
        codes_list = [codes_tab]
        for number in range(2):
            rows, codes = arrivals[number]
            coord_axis, offset = offsets[first + number]
            rows_list.append(rows)
            codes_list.append(codes.at[coord_axis].add(offset))
        return (jnp.concatenate(rows_list, axis=0), jnp.concatenate(codes_list, axis=1))

    arrivals = []
    for segment, direction in ((1, 1), (0, -1)):
        arrivals.append(
            passed_along(shortened(outgoing(segment, source_tab, coded_tab)), "gx", direction)
        )
    source_tab, coded_tab = extend(source_tab, coded_tab, arrivals, 0)
    arrivals = []
    for segment, direction in ((3, 1), (2, -1)):
        arrivals.append(
            passed_along(shortened(outgoing(segment, source_tab, coded_tab)), "gy", direction)
        )
    source_tab, coded_tab = extend(source_tab, coded_tab, arrivals, 2)
    arrivals = []
    for segment, direction in ((5, 1), (4, -1)):
        arrivals.append(
            passed_along(shortened(outgoing(segment, source_tab, coded_tab)), "gz", direction)
        )
    source_tab, coded_tab = extend(source_tab, coded_tab, arrivals, 4)
    table = jnp.concatenate(
        [proj_n, project(source_tab[atoms:], coded_tab[3, atoms:], neigh_proj, neigh_table)], axis=0
    )
    coords_all = coded_tab[:3]
    total_rows = table.shape[0]
    neighbour = neighbour.reshape(atoms, K).T.reshape(-1)
    select = neighbour[:, None] == jnp.arange(total_rows, dtype=jnp.int32)[None, :]
    neigh_rows = jnp.dot(select.astype(jnp.bfloat16), table, preferred_element_type=jnp.float32)
    delta = (jnp.take(coords_all, neighbour, axis=1) - jnp.tile(positions, (1, K))).astype(
        jnp.float32
    ) * (1.0 / 64.0)
    live = (jnp.arange(atoms) < atom_count[0]).astype(jnp.float32)
    valid_pair = jnp.tile(live, K)

    def energy_of(delta_in, neigh_in, centre_in):
        return pair_energy(
            delta_in,
            neigh_in,
            centre_in,
            valid_pair,
            basis_proj,
            split_proj,
            update_proj,
            tensor_proj,
            energy_proj,
        )

    sums, pull = jax.vjp(energy_of, delta, neigh_rows, proj_c.astype(jnp.float32))
    grad_delta, grad_neigh, grad_centre = pull(jnp.ones_like(sums))
    spread_map = select.astype(jnp.float32)
    row_table = jnp.einsum("pt,ph->th", spread_map, grad_neigh, precision=lax.Precision.HIGHEST)
    pos_table = jnp.dot(grad_delta, spread_map, precision=lax.Precision.HIGHEST)
    pos_table = pos_table.at[:, :atoms].add(-grad_delta.reshape(3, K, atoms).sum(axis=1))
    back_neigh = neigh_proj.astype(jnp.float32).T
    back_centre = centre_proj.astype(jnp.float32).T

    def returning(block, state):
        begin = atoms + starts[block]
        rows = state[0][begin : begin + lengths[block]]
        return (rows, state[1][:, begin : begin + lengths[block]])

    def settle(state, segment, arrived):
        picked = send_rows[starts[segment] : starts[segment] + lengths[segment]]
        moved_pos = state[1].at[:, picked].add(arrived[1])
        return (state[0].at[picked].add(arrived[0]), moved_pos)

    state = (row_table, pos_table)
    plan = ((1, 1), (0, -1), (3, 1), (2, -1), (5, 1), (4, -1))
    for block in (4, 5):
        segment, direction = plan[block]
        state = settle(state, segment, passed_along(returning(block, state), "gz", -direction))
    for block in (2, 3):
        segment, direction = plan[block]
        state = settle(state, segment, passed_along(returning(block, state), "gy", -direction))
    for block in (0, 1):
        segment, direction = plan[block]
        state = settle(state, segment, passed_along(returning(block, state), "gx", -direction))
    latent_grad = jnp.dot(grad_centre, back_centre, precision=lax.Precision.HIGHEST)
    latent_grad = latent_grad + jnp.dot(
        state[0][:atoms], back_neigh, precision=lax.Precision.HIGHEST
    )
    forces = -state[1][:, :atoms]
    energies = live * (lookup(species, species_shift[:, None])[:, 0] + sums)
    return (energies, forces, latent_grad)


def solution(mesh):
    in_specs = (
        P(("gx", "gy", "gz"), None),
        P(None, ("gx", "gy", "gz")),
        P(("gx", "gy", "gz")),
        P(("gx", "gy", "gz"), None),
        P(("gx", "gy", "gz")),
        P(("gx", "gy", "gz")),
        P(),
        P(),
        P(),
        P(),
        P(),
        P(),
        P(),
        P(),
        P(),
        P(),
    )
    out_specs = (P(("gx", "gy", "gz")), P(None, ("gx", "gy", "gz")), P(("gx", "gy", "gz"), None))
    return jax.shard_map(shards, mesh=mesh, in_specs=in_specs, out_specs=out_specs, check_vma=False)
```

profile of v0, /device:TPU:0, one launch (start us, length us, event | category | flops | bytes accessed | tf_op | source)
XLA Modules:
  0.0 145.6 jit_solution(11896838472755424643)
XLA Ops:
  1.6 1.5 %gather_fusion.8 = bf16[16,512]{1,0:T(8,128)(2,1)S(1)} fusion(bf16[128,512]{1,0:T(8,128)(2,1)} %param.42, s32[1024]{0:T(1024)S(1)} %pad_clamp_fusion.4), kind=kCustom, calls=%fused_computation.9.clone | custom fusion | bytes 32832 | tf_op jit(solution)/shard_map/jit(_take)/gather | solution.py:162
  3.2 2.4 %collective-permute-start.7 = (bf16[16,512]{1,0:T(8,128)(2,1)S(1)}, bf16[16,512]{1,0:T(8,128)(2,1)S(1)}, u32[]{:S(2)}, u32[]{:S(2)}) collective-permute-start(bf16[16,512]{1,0:T(8,128)(2,1)S(1)} %broadcast_select_fusion.4), channel_id=1, source_target_pairs={{8,0},{16,8},{24,16},{0,24},{9,1},{17,9},{25,17},{1,25},{10,2},{18... | collective-permute-start | bytes 49160 | tf_op jit(solution)/shard_map/ppermute | solution.py:28
  5.6 1.5 %gather_fusion.7 = bf16[16,512]{1,0:T(8,128)(2,1)S(1)} fusion(bf16[128,512]{1,0:T(8,128)(2,1)} %param.42, s32[1024]{0:T(1024)S(1)} %pad_clamp_fusion.5), kind=kCustom, calls=%fused_computation.3.clone | custom fusion | bytes 32832 | tf_op jit(solution)/shard_map/jit(_take)/gather | solution.py:162
  22.3 1.6 %collective-permute-start.3 = (s32[4,64]{0,1:T(8,128)S(1)}, s32[4,64]{0,1:T(8,128)S(1)}, u32[]{:S(2)}, u32[]{:S(2)}) collective-permute-start(s32[4,64]{0,1:T(8,128)S(1)} %select_bitcast_fusion), channel_id=1, source_target_pairs={{4,0},{0,4},{5,1},{1,5},{6,2},{2,6},{7,3},{3,7},{12,8},{8,12},{13,... | collective-permute-start | bytes 3080 | tf_op jit(solution)/shard_map/ppermute | solution.py:28
  24.5 3.4 %collective-permute-done.2 = s32[4,64]{0,1:T(8,128)S(1)} collective-permute-done((s32[4,64]{0,1:T(8,128)S(1)}, s32[4,64]{0,1:T(8,128)S(1)}, u32[]{:S(2)}, u32[]{:S(2)}) %collective-permute-start.2) | collective-permute-done | bytes 1056 | tf_op jit(solution)/shard_map/ppermute | solution.py:28
  29.7 3.6 %collective-permute-start.5 = (s32[4,16]{0,1:T(8,128)S(1)}, s32[4,16]{0,1:T(8,128)S(1)}, u32[]{:S(2)}, u32[]{:S(2)}) collective-permute-start(s32[4,16]{0,1:T(8,128)S(1)} %select_bitcast_fusion.2), channel_id=1, source_target_pairs={{1,0},{2,1},{3,2},{0,3},{5,4},{6,5},{7,6},{4,7},{9,8},{10,9},{11,1... | collective-permute-start | bytes 776 | tf_op jit(solution)/shard_map/ppermute | solution.py:28
  35.0 4.1 %collective-permute-done.4 = s32[4,16]{0,1:T(8,128)S(1)} collective-permute-done((s32[4,16]{0,1:T(8,128)S(1)}, s32[4,16]{0,1:T(8,128)S(1)}, u32[]{:S(2)}, u32[]{:S(2)}) %collective-permute-start.4) | collective-permute-done | bytes 288 | tf_op jit(solution)/shard_map/ppermute | solution.py:28
  39.6 2.8 %gather_fusion = s32[1024,3]{1,0:T(8,128)S(1)} fusion(s32[3,320]{0,1:T(8,128)S(1)} %copy.134, s32[1024]{0:T(1024)S(1)} %broadcast_clamp_fusion), kind=kCustom, calls=%fused_computation.12 | custom fusion | bytes 28672 | tf_op jit(solution)/shard_map/jit(_take)/gather | solution.py:200
  46.1 1.6 %collective-permute-start.9 = (bf16[64,512]{1,0:T(8,128)(2,1)S(1)}, bf16[64,512]{1,0:T(8,128)(2,1)S(1)}, u32[]{:S(2)}, u32[]{:S(2)}) collective-permute-start(bf16[64,512]{1,0:T(8,128)(2,1)S(1)} %broadcast_select_fusion), channel_id=1, source_target_pairs={{4,0},{0,4},{5,1},{1,5},{6,2},{2,6},{7,3},{3,7},{12,8},{8,12},{13,... | collective-permute-start | bytes 196616 | tf_op jit(solution)/shard_map/ppermute | solution.py:28
  47.6 2.1 %collective-permute-done.8 = bf16[64,512]{1,0:T(8,128)(2,1)S(1)} collective-permute-done((bf16[64,512]{1,0:T(8,128)(2,1)S(1)}, bf16[64,512]{1,0:T(8,128)(2,1)S(1)}, u32[]{:S(2)}, u32[]{:S(2)}) %collective-permute-start.8) | collective-permute-done | bytes 65568 | tf_op jit(solution)/shard_map/ppermute | solution.py:28
  51.8 3.8 %collective-permute-start.11 = (bf16[16,512]{1,0:T(8,128)(2,1)S(1)}, bf16[16,512]{1,0:T(8,128)(2,1)S(1)}, u32[]{:S(2)}, u32[]{:S(2)}) collective-permute-start(bf16[16,512]{1,0:T(8,128)(2,1)S(1)} %broadcast_select_fusion.2), channel_id=1, source_target_pairs={{1,0},{2,1},{3,2},{0,3},{5,4},{6,5},{7,6},{4,7},{9,8},{10,9},{11,1... | collective-permute-start | bytes 49160 | tf_op jit(solution)/shard_map/ppermute | solution.py:28
  55.6 1.6 %collective-permute-done.10 = bf16[16,512]{1,0:T(8,128)(2,1)S(1)} collective-permute-done((bf16[16,512]{1,0:T(8,128)(2,1)S(1)}, bf16[16,512]{1,0:T(8,128)(2,1)S(1)}, u32[]{:S(2)}, u32[]{:S(2)}) %collective-permute-start.10) | collective-permute-done | bytes 16416 | tf_op jit(solution)/shard_map/ppermute | solution.py:28
  58.4 1.4 fusion.14
  63.6 1.6 %tile.42 = f32[9,64,8,128]{3,2,1,0:T(8,128)} broadcast(f32[9,64,128]{2,1,0:T(8,128)S(1)} %broadcast_multiply_fusion.2), dimensions={0,1,3} | broadcast | bytes 2654208 | tf_op jit(solution)/shard_map/jvp()/tile | solution.py:98
  65.2 2.4 %tile.43 = f32[9,64,1024]{2,1,0:T(8,128)S(1)} reshape(f32[9,64,8,128]{3,2,1,0:T(8,128)} %tile.42) | data formatting | bytes 4718592 | tf_op jit(solution)/shard_map/jvp()/tile | solution.py:98
  74.4 2.1 %convolution_convert_fusion = bf16[1024,512]{1,0:T(8,128)(2,1)} fusion(bf16[512,512]{1,0:T(8,128)(2,1)S(1)} %copy-done, f32[1024,512]{1,0:T(8,128)S(1)} %convolution_add_fusion, f32[512]{0:T(512)S(1)} %copy-done.45, f32[1024]{0:T(1024)S(1)} %copy-done.37), kind=kOutput, calls=%fused_computation.69 | convolution fusion | flops 542638080 | bytes 3676160 | tf_op jit(solution)/shard_map/transpose(jvp())/dot_general | solution.py:103
  80.9 1.6 %broadcast_in_dim.170 = f32[9,64,8,128]{3,2,1,0:T(8,128)} broadcast(f32[9,64,128]{2,1,0:T(8,128)S(1)} %broadcast_multiply_fusion.1), dimensions={0,1,3} | broadcast | bytes 2654208 | tf_op jit(solution)/shard_map/transpose(jvp())/broadcast_in_dim | solution.py:97
  82.5 2.7 %reshape.594 = f32[9,64,1024]{2,1,0:T(8,128)S(1)} reshape(f32[9,64,8,128]{3,2,1,0:T(8,128)} %broadcast_in_dim.170) | data formatting | bytes 4718592 | tf_op jit(solution)/shard_map/transpose(jvp())/reshape | solution.py:97
  86.1 1.6 %fusion.45 = (f32[3,64,1024]{2,1,0:T(8,128)S(1)}, f32[3,64,1024]{2,1,0:T(8,128)S(1)}) fusion(f32[9,64,1024]{2,1,0:T(8,128)S(1)} %broadcast_multiply_fusion, f32[1,64,1024]{2,1,0:T(8,128)S(1)} %bitcast.244, f32[1,64,1024]{2,1,0:T(8,128)S(1)} %bitcast.245, pred[3]{0:T(512)(128)(4,1)S(1)} %copy-done.42, f32[9,64,1024]{2,1,0:T(8,128)} %copy-done.3, ...), kind=kLoop, calls=%fused_computation.98 | loop fusion | flops 1179648 | bytes 4194307 | tf_op jit(solution)/shard_map/transpose(jvp())/add_any | solution.py:36
  88.3 1.8 %multiply_reduce_fusion = (f32[1024]{0:T(1024)S(1)}, f32[1024,512]{1,0:T(8,128)S(1)}) fusion(f32[512]{0:T(512)S(1)} %copy-done.45, f32[1024]{0:T(1024)S(1)} %copy-done.37, f32[1024,512]{1,0:T(8,128)S(1)} %copy-done.11, bf16[1024,512]{1,0:T(8,128)(2,1)S(1)} %copy-done.50, bf16[512,384]{1,0:T(8,128)(2,1)S(1)} %copy-done.44, f32[192,1024]{1,0:T(8,128)S(1)} %bitcast.249, ...), kind=kOutput, calls=%fused_computation.50 | convolution fusion | flops 412482560 | bytes 7219200 | tf_op jit(solution)/shard_map/transpose(jvp(ph,hq->qp))/dot_general | solution.py:73
  91.3 2.0 %fusion.24 = f32[320,512]{1,0:T(8,128)S(1)} fusion(f32[1024,512]{1,0:T(8,128)S(1)} %get-tuple-element.126, s32[1024]{0:T(1024)S(1)} %bitcast.258), kind=kOutput, calls=%fused_computation.65 | convolution fusion | flops 2013593600 | bytes 2756608 | tf_op jit(solution)/shard_map/pt,ph->th/dot_general | solution.py:222
  93.3 2.8 %fusion.15 = f32[1,1024]{1,0:T(1,128)S(1)} fusion(f32[512,1]{0,1:T(1,128)S(1)} %bitcast.268, f32[1024,512]{1,0:T(8,128)S(1)} %copy-done.49, f32[1024]{0:T(1024)S(1)} %copy-done.37, f32[1024,512]{1,0:T(8,128)S(1)} %copy-done.11), kind=kOutput, calls=%fused_computation.51 | convolution fusion | flops 11534336 | bytes 4204544 | tf_op jit(solution)/shard_map/jvp()/dot_general | solution.py:106
  96.3 3.9 %collective-permute-start.18 = (f32[16,512]{1,0:T(8,128)S(1)}, f32[16,512]{1,0:T(8,128)S(1)}, u32[]{:S(2)}, u32[]{:S(2)}) collective-permute-start(f32[16,512]{1,0:T(8,128)S(1)} %slice.400), channel_id=1, source_target_pairs={{1,0},{2,1},{3,2},{0,3},{5,4},{6,5},{7,6},{4,7},{9,8},{10,9},{11,1... | collective-permute-start | bytes 98312 | tf_op jit(solution)/shard_map/ppermute | solution.py:28
  104.9 3.8 %collective-permute-start.12 = (f32[3,16]{1,0:T(4,128)S(1)}, f32[3,16]{1,0:T(4,128)S(1)}, u32[]{:S(2)}, u32[]{:S(2)}) collective-permute-start(f32[3,16]{1,0:T(4,128)S(1)} %slice.393), channel_id=1, source_target_pairs={{1,0},{2,1},{3,2},{0,3},{5,4},{6,5},{7,6},{4,7},{9,8},{10,9},{11,1... | collective-permute-start | bytes 584 | tf_op jit(solution)/shard_map/ppermute | solution.py:28
  111.4 5.2 %collective-permute-done.13 = f32[3,16]{0,1:T(8,128)S(1)} collective-permute-done((f32[3,16]{0,1:T(8,128)S(1)}, f32[3,16]{0,1:T(8,128)S(1)}, u32[]{:S(2)}, u32[]{:S(2)}) %collective-permute-start.13) | collective-permute-done | bytes 224 | tf_op jit(solution)/shard_map/ppermute | solution.py:28
  118.1 1.5 %collective-permute-start.14 = (f32[3,64]{0,1:T(8,128)}, f32[3,64]{0,1:T(8,128)}, u32[]{:S(2)}, u32[]{:S(2)}) collective-permute-start(f32[3,64]{0,1:T(8,128)} %slice.395), channel_id=1, source_target_pairs={{4,0},{0,4},{5,1},{1,5},{6,2},{2,6},{7,3},{3,7},{12,8},{8,12},{13,... | collective-permute-start | bytes 2312 | tf_op jit(solution)/shard_map/ppermute | solution.py:28
  122.7 2.7 %scatter_custom_fusion.2 = f32[3,320]{0,1:T(8,128)} fusion(f32[3,320]{0,1:T(8,128)} %copy-done.14, s32[64]{0:T(128)} %get-tuple-element.167, f32[3,64]{0,1:T(8,128)} %collective-permute-done.14), kind=kCustom, calls=%fused_computation.162 | custom fusion | flops 192 | bytes 36608 | tf_op jit(solution)/shard_map/scatter-add | solution.py:235
  126.3 1.5 %collective-permute-start.15 = (f32[3,64]{0,1:T(8,128)S(1)}, f32[3,64]{0,1:T(8,128)S(1)}, u32[]{:S(2)}, u32[]{:S(2)}) collective-permute-start(f32[3,64]{0,1:T(8,128)S(1)} %slice.396), channel_id=1, source_target_pairs={{4,0},{0,4},{5,1},{1,5},{6,2},{2,6},{7,3},{3,7},{12,8},{8,12},{13,... | collective-permute-start | bytes 2312 | tf_op jit(solution)/shard_map/ppermute | solution.py:28
  127.7 1.6 %scatter_fusion.3 = f32[320,512]{1,0:T(8,128)S(1)} fusion(f32[320,512]{1,0:T(8,128)S(1)} %scatter_fusion.2, s32[64]{0:T(128)} %get-tuple-element.167, f32[64,512]{1,0:T(8,128)} %collective-permute-done.20), kind=kCustom, calls=%fused_computation.21 | custom fusion | flops 32768 | bytes 393472 | tf_op jit(solution)/shard_map/scatter-add | solution.py:236
  133.9 1.5 %collective-permute-start.17 = (f32[3,16]{0,1:T(8,128)S(1)}, f32[3,16]{0,1:T(8,128)S(1)}, u32[]{:S(2)}, u32[]{:S(2)}) collective-permute-start(f32[3,16]{0,1:T(8,128)S(1)} %slice.398), channel_id=1, source_target_pairs={{24,0},{0,8},{8,16},{16,24},{25,1},{1,9},{9,17},{17,25},{26,2},{2,... | collective-permute-start | bytes 584 | tf_op jit(solution)/shard_map/ppermute | solution.py:28
  141.7 1.5 %collective-permute-done.23 = f32[16,512]{1,0:T(8,128)S(1)} collective-permute-done((f32[16,512]{1,0:T(8,128)S(1)}, f32[16,512]{1,0:T(8,128)S(1)}, u32[]{:S(2)}, u32[]{:S(2)}) %collective-permute-start.23) | collective-permute-done | bytes 32800 | tf_op jit(solution)/shard_map/ppermute | solution.py:28
  144.2 1.4 convolution_add_fusion.2
  (306 shorter events, 68.3 us)
Async XLA Ops:
  0.6 71.1 %copy-start = (bf16[512,512]{1,0:T(8,128)(2,1)S(1)}, bf16[512,512]{1,0:T(8,128)(2,1)}, u32[]{:S(2)}) copy-start(bf16[512,512]{1,0:T(8,128)(2,1)} %param.54) | copy-start | bytes 1572868
  0.6 19.1 %copy-start.8 = (bf16[128,512]{1,0:T(8,128)(2,1)S(1)}, bf16[128,512]{1,0:T(8,128)(2,1)}, u32[]{:S(2)}) copy-start(bf16[128,512]{1,0:T(8,128)(2,1)} %param.42) | copy-start | bytes 393220
  3.2 40.7 %collective-permute-start.7 = (bf16[16,512]{1,0:T(8,128)(2,1)S(1)}, bf16[16,512]{1,0:T(8,128)(2,1)S(1)}, u32[]{:S(2)}, u32[]{:S(2)}) collective-permute-start(bf16[16,512]{1,0:T(8,128)(2,1)S(1)} %broadcast_select_fusion.4), channel_id=1, source_target_pairs={{8,0},{16,8},{24,16},{0,24},{9,1},{17,9},{25,17},{1,25},{10,2},{18... | collective-permute-start | bytes 49160 | tf_op jit(solution)/shard_map/ppermute | solution.py:28
  7.2 36.7 %collective-permute-start.6 = (bf16[16,512]{1,0:T(8,128)(2,1)S(1)}, bf16[16,512]{1,0:T(8,128)(2,1)S(1)}, u32[]{:S(2)}, u32[]{:S(2)}) collective-permute-start(bf16[16,512]{1,0:T(8,128)(2,1)S(1)} %broadcast_select_fusion.5), channel_id=1, source_target_pairs={{24,0},{0,8},{8,16},{16,24},{25,1},{1,9},{9,17},{17,25},{26,2},{2,... | collective-permute-start | bytes 49160 | tf_op jit(solution)/shard_map/ppermute | solution.py:28
  8.6 12.1 %collective-permute-start = (s32[4,16]{0,1:T(8,128)S(1)}, s32[4,16]{0,1:T(8,128)S(1)}, u32[]{:S(2)}, u32[]{:S(2)}) collective-permute-start(s32[4,16]{0,1:T(8,128)S(1)} %select_bitcast_fusion.5), channel_id=1, source_target_pairs={{24,0},{0,8},{8,16},{16,24},{25,1},{1,9},{9,17},{17,25},{26,2},{2,... | collective-permute-start | bytes 776 | tf_op jit(solution)/shard_map/ppermute | solution.py:28
  10.0 10.9 %collective-permute-start.1 = (s32[4,16]{0,1:T(8,128)S(1)}, s32[4,16]{0,1:T(8,128)S(1)}, u32[]{:S(2)}, u32[]{:S(2)}) collective-permute-start(s32[4,16]{0,1:T(8,128)S(1)} %select_bitcast_fusion.4), channel_id=1, source_target_pairs={{8,0},{16,8},{24,16},{0,24},{9,1},{17,9},{25,17},{1,25},{10,2},{18... | collective-permute-start | bytes 776 | tf_op jit(solution)/shard_map/ppermute | solution.py:28
  11.0 47.3 %copy-start.38 = (f32[8]{0:T(128)}, f32[8]{0:T(128)S(1)}, u32[]{:S(2)}) copy-start(f32[8]{0:T(128)S(1)} %convert_multiply_fusion) | copy-start | bytes 100
  16.4 41.2 %copy-start.17 = (s32[8,128]{1,0:T(8,128)}, s32[8,128]{1,0:T(8,128)S(1)}, u32[]{:S(2)}) copy-start(s32[8,128]{1,0:T(8,128)S(1)} %copy.133) | copy-start | bytes 12292
  16.4 27.3 %copy-start.29 = (pred[1024]{0:T(1024)(128)(4,1)}, pred[1024]{0:T(1024)(128)(4,1)S(1)}, u32[]{:S(2)}) copy-start(pred[1024]{0:T(1024)(128)(4,1)S(1)} %compare_and_fusion.1) | copy-start | bytes 3076
  18.5 24.1 %copy-start.21 = (f32[5,512]{1,0:T(8,128)S(1)}, f32[5,512]{1,0:T(8,128)}, u32[]{:S(2)}) copy-start(f32[5,512]{1,0:T(8,128)} %param.51) | copy-start | bytes 30724
  20.0 25.3 %copy-start.34 = (f32[128]{0:T(128)}, f32[128]{0:T(128)S(1)}, u32[]{:S(2)}) copy-start(f32[128]{0:T(128)S(1)} %compare_convert_fusion) | copy-start | bytes 1540
  22.3 5.9 %collective-permute-start.3 = (s32[4,64]{0,1:T(8,128)S(1)}, s32[4,64]{0,1:T(8,128)S(1)}, u32[]{:S(2)}, u32[]{:S(2)}) collective-permute-start(s32[4,64]{0,1:T(8,128)S(1)} %select_bitcast_fusion), channel_id=1, source_target_pairs={{4,0},{0,4},{5,1},{1,5},{6,2},{2,6},{7,3},{3,7},{12,8},{8,12},{13,... | collective-permute-start | bytes 3080 | tf_op jit(solution)/shard_map/ppermute | solution.py:28
  24.0 4.0 %collective-permute-start.2 = (s32[4,64]{0,1:T(8,128)S(1)}, s32[4,64]{0,1:T(8,128)S(1)}, u32[]{:S(2)}, u32[]{:S(2)}) collective-permute-start(s32[4,64]{0,1:T(8,128)S(1)} %select_bitcast_fusion.1), channel_id=1, source_target_pairs={{4,0},{0,4},{5,1},{1,5},{6,2},{2,6},{7,3},{3,7},{12,8},{8,12},{13,... | collective-permute-start | bytes 3080 | tf_op jit(solution)/shard_map/ppermute | solution.py:28
  29.7 5.0 %collective-permute-start.5 = (s32[4,16]{0,1:T(8,128)S(1)}, s32[4,16]{0,1:T(8,128)S(1)}, u32[]{:S(2)}, u32[]{:S(2)}) collective-permute-start(s32[4,16]{0,1:T(8,128)S(1)} %select_bitcast_fusion.2), channel_id=1, source_target_pairs={{1,0},{2,1},{3,2},{0,3},{5,4},{6,5},{7,6},{4,7},{9,8},{10,9},{11,1... | collective-permute-start | bytes 776 | tf_op jit(solution)/shard_map/ppermute | solution.py:28
  33.6 5.5 %collective-permute-start.4 = (s32[4,16]{0,1:T(8,128)S(1)}, s32[4,16]{0,1:T(8,128)S(1)}, u32[]{:S(2)}, u32[]{:S(2)}) collective-permute-start(s32[4,16]{0,1:T(8,128)S(1)} %select_bitcast_fusion.3), channel_id=1, source_target_pairs={{3,0},{0,1},{1,2},{2,3},{7,4},{4,5},{5,6},{6,7},{11,8},{8,9},{9,10... | collective-permute-start | bytes 776 | tf_op jit(solution)/shard_map/ppermute | solution.py:28
  45.4 4.3 %collective-permute-start.8 = (bf16[64,512]{1,0:T(8,128)(2,1)S(1)}, bf16[64,512]{1,0:T(8,128)(2,1)S(1)}, u32[]{:S(2)}, u32[]{:S(2)}) collective-permute-start(bf16[64,512]{1,0:T(8,128)(2,1)S(1)} %broadcast_select_fusion.1), channel_id=1, source_target_pairs={{4,0},{0,4},{5,1},{1,5},{6,2},{2,6},{7,3},{3,7},{12,8},{8,12},{13,... | collective-permute-start | bytes 196616 | tf_op jit(solution)/shard_map/ppermute | solution.py:28
  46.1 4.4 %collective-permute-start.9 = (bf16[64,512]{1,0:T(8,128)(2,1)S(1)}, bf16[64,512]{1,0:T(8,128)(2,1)S(1)}, u32[]{:S(2)}, u32[]{:S(2)}) collective-permute-start(bf16[64,512]{1,0:T(8,128)(2,1)S(1)} %broadcast_select_fusion), channel_id=1, source_target_pairs={{4,0},{0,4},{5,1},{1,5},{6,2},{2,6},{7,3},{3,7},{12,8},{8,12},{13,... | collective-permute-start | bytes 196616 | tf_op jit(solution)/shard_map/ppermute | solution.py:28
  51.7 5.5 %collective-permute-start.10 = (bf16[16,512]{1,0:T(8,128)(2,1)S(1)}, bf16[16,512]{1,0:T(8,128)(2,1)S(1)}, u32[]{:S(2)}, u32[]{:S(2)}) collective-permute-start(bf16[16,512]{1,0:T(8,128)(2,1)S(1)} %broadcast_select_fusion.3), channel_id=1, source_target_pairs={{3,0},{0,1},{1,2},{2,3},{7,4},{4,5},{5,6},{6,7},{11,8},{8,9},{9,10... | collective-permute-start | bytes 49160 | tf_op jit(solution)/shard_map/ppermute | solution.py:28
  51.8 5.5 %collective-permute-start.11 = (bf16[16,512]{1,0:T(8,128)(2,1)S(1)}, bf16[16,512]{1,0:T(8,128)(2,1)S(1)}, u32[]{:S(2)}, u32[]{:S(2)}) collective-permute-start(bf16[16,512]{1,0:T(8,128)(2,1)S(1)} %broadcast_select_fusion.2), channel_id=1, source_target_pairs={{1,0},{2,1},{3,2},{0,3},{5,4},{6,5},{7,6},{4,7},{9,8},{10,9},{11,1... | collective-permute-start | bytes 49160 | tf_op jit(solution)/shard_map/ppermute | solution.py:28
  96.2 25.7 %copy-start.26 = (s32[1,192]{1,0:T(1,128)S(1)}, s32[1,192]{1,0:T(1,128)}, u32[]{:S(2)}) copy-start(s32[1,192]{1,0:T(1,128)} %param.45) | copy-start | bytes 2308
  96.3 6.8 %collective-permute-start.18 = (f32[16,512]{1,0:T(8,128)S(1)}, f32[16,512]{1,0:T(8,128)S(1)}, u32[]{:S(2)}, u32[]{:S(2)}) collective-permute-start(f32[16,512]{1,0:T(8,128)S(1)} %slice.400), channel_id=1, source_target_pairs={{1,0},{2,1},{3,2},{0,3},{5,4},{6,5},{7,6},{4,7},{9,8},{10,9},{11,1... | collective-permute-start | bytes 98312 | tf_op jit(solution)/shard_map/ppermute | solution.py:28
  104.1 15.5 %collective-permute-start.19 = (f32[16,512]{1,0:T(8,128)S(1)}, f32[16,512]{1,0:T(8,128)S(1)}, u32[]{:S(2)}, u32[]{:S(2)}) collective-permute-start(f32[16,512]{1,0:T(8,128)S(1)} %slice.401), channel_id=1, source_target_pairs={{3,0},{0,1},{1,2},{2,3},{7,4},{4,5},{5,6},{6,7},{11,8},{8,9},{9,10... | collective-permute-start | bytes 98312 | tf_op jit(solution)/shard_map/ppermute | solution.py:28
  104.9 5.1 %collective-permute-start.12 = (f32[3,16]{1,0:T(4,128)S(1)}, f32[3,16]{1,0:T(4,128)S(1)}, u32[]{:S(2)}, u32[]{:S(2)}) collective-permute-start(f32[3,16]{1,0:T(4,128)S(1)} %slice.393), channel_id=1, source_target_pairs={{1,0},{2,1},{3,2},{0,3},{5,4},{6,5},{7,6},{4,7},{9,8},{10,9},{11,1... | collective-permute-start | bytes 584 | tf_op jit(solution)/shard_map/ppermute | solution.py:28
  110.8 5.8 %collective-permute-start.13 = (f32[3,16]{0,1:T(8,128)S(1)}, f32[3,16]{0,1:T(8,128)S(1)}, u32[]{:S(2)}, u32[]{:S(2)}) collective-permute-start(f32[3,16]{0,1:T(8,128)S(1)} %slice.394), channel_id=1, source_target_pairs={{3,0},{0,1},{1,2},{2,3},{7,4},{4,5},{5,6},{6,7},{11,8},{8,9},{9,10... | collective-permute-start | bytes 584 | tf_op jit(solution)/shard_map/ppermute | solution.py:28
  118.1 4.6 %collective-permute-start.14 = (f32[3,64]{0,1:T(8,128)}, f32[3,64]{0,1:T(8,128)}, u32[]{:S(2)}, u32[]{:S(2)}) collective-permute-start(f32[3,64]{0,1:T(8,128)} %slice.395), channel_id=1, source_target_pairs={{4,0},{0,4},{5,1},{1,5},{6,2},{2,6},{7,3},{3,7},{12,8},{8,12},{13,... | collective-permute-start | bytes 2312 | tf_op jit(solution)/shard_map/ppermute | solution.py:28
  121.3 6.4 %collective-permute-start.20 = (f32[64,512]{1,0:T(8,128)}, f32[64,512]{1,0:T(8,128)}, u32[]{:S(2)}, u32[]{:S(2)}) collective-permute-start(f32[64,512]{1,0:T(8,128)} %slice.402), channel_id=1, source_target_pairs={{4,0},{0,4},{5,1},{1,5},{6,2},{2,6},{7,3},{3,7},{12,8},{8,12},{13,... | collective-permute-start | bytes 393224 | tf_op jit(solution)/shard_map/ppermute | solution.py:28
  126.3 4.4 %collective-permute-start.15 = (f32[3,64]{0,1:T(8,128)S(1)}, f32[3,64]{0,1:T(8,128)S(1)}, u32[]{:S(2)}, u32[]{:S(2)}) collective-permute-start(f32[3,64]{0,1:T(8,128)S(1)} %slice.396), channel_id=1, source_target_pairs={{4,0},{0,4},{5,1},{1,5},{6,2},{2,6},{7,3},{3,7},{12,8},{8,12},{13,... | collective-permute-start | bytes 2312 | tf_op jit(solution)/shard_map/ppermute | solution.py:28
  129.4 6.0 %collective-permute-start.21 = (f32[64,512]{1,0:T(8,128)S(1)}, f32[64,512]{1,0:T(8,128)S(1)}, u32[]{:S(2)}, u32[]{:S(2)}) collective-permute-start(f32[64,512]{1,0:T(8,128)S(1)} %slice.403), channel_id=1, source_target_pairs={{4,0},{0,4},{5,1},{1,5},{6,2},{2,6},{7,3},{3,7},{12,8},{8,12},{13,... | collective-permute-start | bytes 393224 | tf_op jit(solution)/shard_map/ppermute | solution.py:28
  131.7 1.4 collective-permute-start.16
  133.9 4.2 %collective-permute-start.17 = (f32[3,16]{0,1:T(8,128)S(1)}, f32[3,16]{0,1:T(8,128)S(1)}, u32[]{:S(2)}, u32[]{:S(2)}) collective-permute-start(f32[3,16]{0,1:T(8,128)S(1)} %slice.398), channel_id=1, source_target_pairs={{24,0},{0,8},{8,16},{16,24},{25,1},{1,9},{9,17},{17,25},{26,2},{2,... | collective-permute-start | bytes 584 | tf_op jit(solution)/shard_map/ppermute | solution.py:28
  136.6 2.3 %collective-permute-start.22 = (f32[16,512]{1,0:T(8,128)S(1)}, f32[16,512]{1,0:T(8,128)S(1)}, u32[]{:S(2)}, u32[]{:S(2)}) collective-permute-start(f32[16,512]{1,0:T(8,128)S(1)} %slice.404), channel_id=1, source_target_pairs={{8,0},{16,8},{24,16},{0,24},{9,1},{17,9},{25,17},{1,25},{10,2},{18... | collective-permute-start | bytes 98312 | tf_op jit(solution)/shard_map/ppermute | solution.py:28
  139.9 3.4 %collective-permute-start.23 = (f32[16,512]{1,0:T(8,128)S(1)}, f32[16,512]{1,0:T(8,128)S(1)}, u32[]{:S(2)}, u32[]{:S(2)}) collective-permute-start(f32[16,512]{1,0:T(8,128)S(1)} %slice.405), channel_id=1, source_target_pairs={{24,0},{0,8},{8,16},{16,24},{25,1},{1,9},{9,17},{17,25},{26,2},{2,... | collective-permute-start | bytes 98312 | tf_op jit(solution)/shard_map/ppermute | solution.py:28
  (43 other events, 223.2 us)
where the time goes:
time: 146 us
  local copies, waits for them, and re-layouts  37.5 us (26%)
  starting transfers between devices  31.7 us (22%)
  other arithmetic  28.2 us (19%)
  matrix products  23 us (16%)
  waiting for transfers between devices  22.4 us (15%)
  between operations  2.72 us (2%)
    ppermute x24, starting transfers between devices, passed_along(): return lax.ppermute(block, axis, route)  31.7 us
    ppermute x24, waiting for transfers between devices, passed_along(): return lax.ppermute(block, axis, route)  22.4 us
    unnamed x120, local copies, waits for them, and re-layouts  7.57 us
    scatter-add x6, other arithmetic, settle(): moved_pos = state[1].at[:, picked].add(arrived[1])  6.78 us
    scatter-add x6, other arithmetic, settle(): return (state[0].at[picked].add(arrived[0]), moved_pos)  6.76 us
    gather x6, local copies, waits for them, and re-layouts, outgoing(): jnp.take(rows_tab, picked, axis=0)  5.61 us
    another operation x2, local copies, waits for them, and re-layouts, pair_energy(): expanded = jnp.tile(environment, (1, 1, K))  4.02 us
    gather x6, local copies, waits for them, and re-layouts, outgoing(): jnp.take(codes_tab, picked, axis=1)  3.44 us
  transfers between devices with their start and end apart: 24, of which 11 were waited for; matrix products, arithmetic and copies ran while one was open for 28% of the time, Pallas kernels for 0%

commit v1 on v0

--- a/solution.py
+++ b/solution.py
@@ -125,7 +125,8 @@
     energy_proj,
     species_shift,
 ):
-    atoms = latent.shape[0]
+    atoms, width = latent.shape
+    extra = 128
     face_x = atoms // 8
     face_y = atoms // 2
     face_z = atoms // 8
@@ -149,57 +150,53 @@
             jnp.dot(rows, weight, preferred_element_type=jnp.float32) + lookup(codes, table)
         ).astype(jnp.bfloat16)
 
+    def spread(onehot, values):
+        high = values.astype(jnp.bfloat16)
+        low = (values - high.astype(jnp.float32)).astype(jnp.bfloat16)
+        return jnp.einsum(
+            "nr,nw->rw", onehot, high, preferred_element_type=jnp.float32
+        ) + jnp.einsum("nr,nw->rw", onehot, low, preferred_element_type=jnp.float32)
+
     proj_c = project(latent, species, centre_proj, centre_table)
     proj_n = project(latent, species, neigh_proj, neigh_table)
     send_rows = send_list[0]
-    coded = jnp.concatenate([positions, species[None, :]], axis=0)
-    source_tab = latent
-    coded_tab = coded
-    offsets = [(0, -LX_FIX), (0, LX_FIX), (1, -LY_FIX), (1, LY_FIX), (2, -LZ_FIX), (2, LZ_FIX)]
-
-    def outgoing(segment, rows_tab, codes_tab):
-        picked = send_rows[starts[segment] : starts[segment] + lengths[segment]]
-        return (jnp.take(rows_tab, picked, axis=0), jnp.take(codes_tab, picked, axis=1))
-
-    def extend(rows_tab, codes_tab, arrivals, first):
-        rows_list = [rows_tab]
-        codes_list = [codes_tab]
-        for number in range(2):
-            rows, codes = arrivals[number]
-            coord_axis, offset = offsets[first + number]
-            rows_list.append(rows)
-            codes_list.append(codes.at[coord_axis].add(offset))
-        return (jnp.concatenate(rows_list, axis=0), jnp.concatenate(codes_list, axis=1))
-
-    arrivals = []
-    for segment, direction in ((1, 1), (0, -1)):
-        arrivals.append(
-            passed_along(shortened(outgoing(segment, source_tab, coded_tab)), "gx", direction)
-        )
-    source_tab, coded_tab = extend(source_tab, coded_tab, arrivals, 0)
-    arrivals = []
-    for segment, direction in ((3, 1), (2, -1)):
-        arrivals.append(
-            passed_along(shortened(outgoing(segment, source_tab, coded_tab)), "gy", direction)
-        )
-    source_tab, coded_tab = extend(source_tab, coded_tab, arrivals, 2)
-    arrivals = []
-    for segment, direction in ((5, 1), (4, -1)):
-        arrivals.append(
-            passed_along(shortened(outgoing(segment, source_tab, coded_tab)), "gz", direction)
-        )
-    source_tab, coded_tab = extend(source_tab, coded_tab, arrivals, 4)
+    coarse = positions // 16
+    fine = positions - coarse * 16
+    coord_cols = jnp.concatenate([coarse, fine], axis=0).T.astype(jnp.bfloat16)
     table = jnp.concatenate(
-        [proj_n, project(source_tab[atoms:], coded_tab[3, atoms:], neigh_proj, neigh_table)], axis=0
-    )
-    coords_all = coded_tab[:3]
+        [proj_n, coord_cols, jnp.zeros((atoms, extra - 6), jnp.bfloat16)], axis=1
+    )
+    shifts = [(0, -LX_FIX), (0, LX_FIX), (1, -LY_FIX), (1, LY_FIX), (2, -LZ_FIX), (2, LZ_FIX)]
+    sections = (("gx", (1, 0)), ("gy", (3, 2)), ("gz", (5, 4)))
+    pickers = {}
+    base_rows = []
+    for section, (axis, segs) in enumerate(sections):
+        rows_now = table.shape[0]
+        base_rows.append(rows_now)
+        parts = [table]
+        for number, (segment, direction) in enumerate(((segs[0], 1), (segs[1], -1))):
+            picked = send_rows[starts[segment] : starts[segment] + lengths[segment]]
+            onehot = (
+                picked[:, None] == jnp.arange(rows_now, dtype=jnp.int32)[None, :]
+            ).astype(jnp.bfloat16)
+            pickers[segment] = onehot
+            out = jnp.dot(onehot, table, preferred_element_type=jnp.float32).astype(jnp.bfloat16)
+            got = passed_along(out, axis, direction)
+            coord_axis, offset = shifts[2 * section + number]
+            shift = jnp.zeros((1, width + extra), jnp.bfloat16).at[0, width + coord_axis].set(
+                offset // 16
+            )
+            parts.append(got + shift)
+        table = jnp.concatenate(parts, axis=0)
     total_rows = table.shape[0]
     neighbour = neighbour.reshape(atoms, K).T.reshape(-1)
-    select = neighbour[:, None] == jnp.arange(total_rows, dtype=jnp.int32)[None, :]
-    neigh_rows = jnp.dot(select.astype(jnp.bfloat16), table, preferred_element_type=jnp.float32)
-    delta = (jnp.take(coords_all, neighbour, axis=1) - jnp.tile(positions, (1, K))).astype(
-        jnp.float32
-    ) * (1.0 / 64.0)
+    select = (neighbour[:, None] == jnp.arange(total_rows, dtype=jnp.int32)[None, :]).astype(
+        jnp.bfloat16
+    )
+    gathered = jnp.dot(select, table, preferred_element_type=jnp.float32)
+    neigh_rows = gathered[:, :width]
+    coords_n = (gathered[:, width : width + 3] * 16.0 + gathered[:, width + 3 : width + 6]).T
+    delta = (coords_n - jnp.tile(positions.astype(jnp.float32), (1, K))) * (1.0 / 64.0)
     live = (jnp.arange(atoms) < atom_count[0]).astype(jnp.float32)
     valid_pair = jnp.tile(live, K)
 
@@ -216,42 +213,35 @@
             energy_proj,
         )
 
-    sums, pull = jax.vjp(energy_of, delta, neigh_rows, proj_c.astype(jnp.float32))
-    grad_delta, grad_neigh, grad_centre = pull(jnp.ones_like(sums))
-    spread_map = select.astype(jnp.float32)
-    row_table = jnp.einsum("pt,ph->th", spread_map, grad_neigh, precision=lax.Precision.HIGHEST)
-    pos_table = jnp.dot(grad_delta, spread_map, precision=lax.Precision.HIGHEST)
-    pos_table = pos_table.at[:, :atoms].add(-grad_delta.reshape(3, K, atoms).sum(axis=1))
+    atom_energy, pull = jax.vjp(energy_of, delta, neigh_rows, proj_c.astype(jnp.float32))
+    grad_delta, grad_neigh, grad_centre = pull(jnp.ones_like(atom_energy))
+    pairs = grad_neigh.shape[0]
+    grads = jnp.concatenate(
+        [grad_neigh, grad_delta.T, jnp.zeros((pairs, extra - 3), jnp.float32)], axis=1
+    )
+    sums = spread(select, grads)
+    own_pos = grad_delta.reshape(3, K, atoms).sum(axis=1)
+    sums = sums.at[:atoms, width : width + 3].add(-own_pos.T)
+    for section in (2, 1, 0):
+        axis, segs = sections[section]
+        rows_now = base_rows[section]
+        first = atoms + starts[2 * section]
+        second = atoms + starts[2 * section + 1]
+        back_first = passed_along(sums[first : first + lengths[2 * section]], axis, -1)
+        back_second = passed_along(sums[second : second + lengths[2 * section + 1]], axis, 1)
+        sums = (
+            sums[:rows_now]
+            + spread(pickers[segs[0]], back_first)
+            + spread(pickers[segs[1]], back_second)
+        )
     back_neigh = neigh_proj.astype(jnp.float32).T
     back_centre = centre_proj.astype(jnp.float32).T
-
-    def returning(block, state):
-        begin = atoms + starts[block]
-        rows = state[0][begin : begin + lengths[block]]
-        return (rows, state[1][:, begin : begin + lengths[block]])
-
-    def settle(state, segment, arrived):
-        picked = send_rows[starts[segment] : starts[segment] + lengths[segment]]
-        moved_pos = state[1].at[:, picked].add(arrived[1])
-        return (state[0].at[picked].add(arrived[0]), moved_pos)
-
-    state = (row_table, pos_table)
-    plan = ((1, 1), (0, -1), (3, 1), (2, -1), (5, 1), (4, -1))
-    for block in (4, 5):
-        segment, direction = plan[block]
-        state = settle(state, segment, passed_along(returning(block, state), "gz", -direction))
-    for block in (2, 3):
-        segment, direction = plan[block]
-        state = settle(state, segment, passed_along(returning(block, state), "gy", -direction))
-    for block in (0, 1):
-        segment, direction = plan[block]
-        state = settle(state, segment, passed_along(returning(block, state), "gx", -direction))
     latent_grad = jnp.dot(grad_centre, back_centre, precision=lax.Precision.HIGHEST)
     latent_grad = latent_grad + jnp.dot(
-        state[0][:atoms], back_neigh, precision=lax.Precision.HIGHEST
-    )
-    forces = -state[1][:, :atoms]
-    energies = live * (lookup(species, species_shift[:, None])[:, 0] + sums)
+        sums[:, :width], back_neigh, precision=lax.Precision.HIGHEST
+    )
+    forces = -sums[:, width : width + 3].T
+    energies = live * (lookup(species, species_shift[:, None])[:, 0] + atom_energy)
     return (energies, forces, latent_grad)
 
 

time: 146 us -> 135 us (0.925)
  starting transfers between devices: 31.7 us -> 16.6 us
  other arithmetic: 28.2 us -> 14.2 us
  waiting for transfers between devices: 22.4 us -> 35.2 us
  between operations: 2.72 us -> 6.29 us
  matrix products: 23 us -> 26.2 us
  local copies, waits for them, and re-layouts: 37.5 us -> 36 us
    ppermute x24 -> x12, starting transfers between devices: 31.7 us -> 16.6 us  [passed_along(): return lax.ppermute(block, axis, route)]
    scatter-add x13 -> x0, other arithmetic: 14.2 us -> none  [the longest x6 6.78 us: settle(): moved_pos = state[1].at[:, picked].add(arrived[1])]
    ppermute x24 -> x12, waiting for transfers between devices: 22.4 us -> 35.2 us  [passed_along(): return lax.ppermute(block, axis, route)]
    gather x14 -> x0, local copies, waits for them, and re-layouts: 12 us -> none  [the longest x6 5.61 us: outgoing(): jnp.take(rows_tab, picked, axis=0)]
    dot_general x4 -> x22, matrix products: 4.75 us -> 10.2 us  [the longest x7 2.73 us: spread(): jnp.einsum('nr,nw->rw', onehot, high, preferred_element_type=jnp.float32)]
    another operation x1 -> x9, other arithmetic: 0.69 us -> 5.27 us
    scatter x0 -> x6, local copies, waits for them, and re-layouts: none -> 4.52 us  [shards(): jnp.zeros((1, width + extra), jnp.bfloat16).at[0, width + coord_axis]]
    select_n x15 -> x0, other arithmetic: 2.84 us -> none  [the longest x2 1.93 us: settle(): moved_pos = state[1].at[:, picked].add(arrived[1])]
  transfers between devices with their start and end apart: 24 -> 12, of which waited for: 11 -> 8; matrix products, arithmetic and copies ran while one was open for 28% -> 12% of each run, Pallas kernels for 0% -> 0%
where the time goes in v1:
time: 135 us; the launch traced here: 134 us
  local copies, waits for them, and re-layouts  36 us (27%)
  waiting for transfers between devices  35.2 us (26%)
  matrix products  26.2 us (19%)
  starting transfers between devices  16.6 us (12%)
  other arithmetic  14.2 us (11%)
  between operations  6.29 us (5%)
    ppermute x12, waiting for transfers between devices, passed_along(): return lax.ppermute(block, axis, route)  35.2 us
    ppermute x12, starting transfers between devices, passed_along(): return lax.ppermute(block, axis, route)  16.6 us
    unnamed x113, local copies, waits for them, and re-layouts  9.38 us
    another operation x9, other arithmetic  5.27 us
    scatter x6, local copies, waits for them, and re-layouts, shards(): jnp.zeros((1, width + extra), jnp.bfloat16).at[0, width + coord_axis]  4.52 us
    another operation x2, local copies, waits for them, and re-layouts, pair_energy(): expanded = jnp.tile(environment, (1, 1, K))  4.04 us
    scatter-add x1, local copies, waits for them, and re-layouts, shards(): sums = sums.at[:atoms, width:width + 3].add(-own_pos.T)  3.75 us
    dot_general x2, matrix products, pair_energy(): jnp.dot(hidden_low, update_proj, preferred_element_type=jnp.float32)  3.18 us
  transfers between devices with their start and end apart: 12, of which 8 were waited for; matrix products, arithmetic and copies ran while one was open for 12% of the time, Pallas kernels for 0%

profile of v1, /device:TPU:0, one launch (start us, length us, event | category | flops | bytes accessed | tf_op | source)
XLA Modules:
  0.0 134.4 jit_solution(10629523653033511362)
XLA Ops:
  3.6 1.3 %fusion.42 = bf16[128,512]{1,0:T(8,128)(2,1)S(1)} fusion(f32[128,512]{1,0:T(8,128)S(1)} %fusion.80, bf16[128,512]{1,0:T(8,128)(2,1)} %param.30, bf16[512,512]{1,0:T(8,128)(2,1)} %param.37), kind=kOutput, calls=%fused_computation.72 | convolution fusion | flops 67239936 | bytes 1048576 | tf_op jit(solution)/shard_map/dot_general | solution.py:150
  5.8 1.9 %collective-permute-start.1 = (bf16[16,640]{1,0:T(8,128)(2,1)S(1)}, bf16[16,640]{1,0:T(8,128)(2,1)S(1)}, u32[]{:S(2)}, u32[]{:S(2)}) collective-permute-start(bf16[16,640]{1,0:T(8,128)(2,1)S(1)} %convolution_convert_fusion.6), channel_id=1, source_target_pairs={{8,0},{16,8},{24,16},{0,24},{9,1},{17,9},{25,17},{1,25},{10,2},{18... | collective-permute-start | bytes 61448 | tf_op jit(solution)/shard_map/ppermute | solution.py:28
  24.2 2.4 %collective-permute-start.2 = (bf16[64,640]{1,0:T(8,128)(2,1)S(1)}, bf16[64,640]{1,0:T(8,128)(2,1)S(1)}, u32[]{:S(2)}, u32[]{:S(2)}) collective-permute-start(bf16[64,640]{1,0:T(8,128)(2,1)S(1)} %convolution_convert_fusion.3), channel_id=1, source_target_pairs={{4,0},{0,4},{5,1},{1,5},{6,2},{2,6},{7,3},{3,7},{12,8},{8,12},{13,... | collective-permute-start | bytes 245768 | tf_op jit(solution)/shard_map/ppermute | solution.py:28
  26.7 3.2 %collective-permute-done.2 = bf16[64,640]{1,0:T(8,128)(2,1)S(1)} collective-permute-done((bf16[64,640]{1,0:T(8,128)(2,1)S(1)}, bf16[64,640]{1,0:T(8,128)(2,1)S(1)}, u32[]{:S(2)}, u32[]{:S(2)}) %collective-permute-start.2) | collective-permute-done | bytes 81952 | tf_op jit(solution)/shard_map/ppermute | solution.py:28
  29.9 1.2 collective-permute-done.3
  31.3 1.8 %collective-permute-start.4 = (bf16[16,640]{1,0:T(8,128)(2,1)S(1)}, bf16[16,640]{1,0:T(8,128)(2,1)S(1)}, u32[]{:S(2)}, u32[]{:S(2)}) collective-permute-start(bf16[16,640]{1,0:T(8,128)(2,1)S(1)} %convolution_convert_fusion.5), channel_id=1, source_target_pairs={{3,0},{0,1},{1,2},{2,3},{7,4},{4,5},{5,6},{6,7},{11,8},{8,9},{9,10... | collective-permute-start | bytes 61448 | tf_op jit(solution)/shard_map/ppermute | solution.py:28
  33.3 2.1 %collective-permute-start.5 = (bf16[16,640]{1,0:T(8,128)(2,1)S(1)}, bf16[16,640]{1,0:T(8,128)(2,1)S(1)}, u32[]{:S(2)}, u32[]{:S(2)}) collective-permute-start(bf16[16,640]{1,0:T(8,128)(2,1)S(1)} %convolution_convert_fusion.4), channel_id=1, source_target_pairs={{1,0},{2,1},{3,2},{0,3},{5,4},{6,5},{7,6},{4,7},{9,8},{10,9},{11,1... | collective-permute-start | bytes 61448 | tf_op jit(solution)/shard_map/ppermute | solution.py:28
  35.5 1.5 %collective-permute-done.4 = bf16[16,640]{1,0:T(8,128)(2,1)S(1)} collective-permute-done((bf16[16,640]{1,0:T(8,128)(2,1)S(1)}, bf16[16,640]{1,0:T(8,128)(2,1)S(1)}, u32[]{:S(2)}, u32[]{:S(2)}) %collective-permute-start.4) | collective-permute-done | bytes 20512 | tf_op jit(solution)/shard_map/ppermute | solution.py:28
  38.0 2.1 %fusion.27 = f32[1024,640]{0,1:T(8,128)S(1)} fusion(bf16[320,640]{1,0:T(8,128)(2,1)} %copy-done.15, s32[1024]{0:T(1024)S(1)} %bitcast.199), kind=kOutput, calls=%fused_computation.46 | convolution fusion | flops 419758080 | bytes 3035136 | tf_op jit(solution)/shard_map/dot_general | solution.py:196
  42.7 1.4 %fusion.15 = f32[1024,512]{0,1:T(8,128)S(1)} fusion(f32[64,8,8,128]{3,2,1,0:T(8,128)S(1)} %bitcast.174, f32[1024,640]{0,1:T(8,128)S(1)} %fusion.27, bf16[8,512]{1,0:T(8,128)(2,1)S(1)} %copy-done.18, f32[1024]{0:T(1024)S(1)} %get-tuple-element.143, f32[1024]{0:T(1024)S(1)} %get-tuple-element.146, f32[8]{0:T(128)S(1)} %copy-done.40), kind=kOutput, calls=%fused_computation.28 | convolution fusion | flops 51396608 | bytes 6307872 | tf_op jit(solution)/shard_map/jvp(kp,kh->ph)/dot_general | solution.py:66
  48.0 1.6 %tile.42 = f32[9,64,8,128]{3,2,1,0:T(8,128)} broadcast(f32[9,64,128]{2,1,0:T(8,128)S(1)} %broadcast_multiply_fusion.2), dimensions={0,1,3} | broadcast | bytes 2654208 | tf_op jit(solution)/shard_map/jvp()/tile | solution.py:98
  49.6 2.4 %tile.43 = f32[9,64,1024]{2,1,0:T(8,128)S(1)} reshape(f32[9,64,8,128]{3,2,1,0:T(8,128)} %tile.42) | data formatting | bytes 4718592 | tf_op jit(solution)/shard_map/jvp()/tile | solution.py:98
  53.1 1.1 broadcast_in_dim.38
  58.8 2.2 %convolution_convert_fusion = bf16[1024,512]{0,1:T(8,128)(2,1)} fusion(bf16[512,512]{1,0:T(8,128)(2,1)S(1)} %copy-done, f32[1024,512]{0,1:T(8,128)S(1)} %convolution_add_fusion, f32[512]{0:T(512)S(1)} %copy-done.44, f32[1024]{0:T(1024)S(1)} %copy-done.37), kind=kOutput, calls=%fused_computation.48 | convolution fusion | flops 542638080 | bytes 3676160 | tf_op jit(solution)/shard_map/transpose(jvp())/dot_general | solution.py:103
  61.4 1.2 fusion.31
  65.5 1.6 %broadcast_in_dim.45 = f32[9,64,8,128]{3,2,1,0:T(8,128)} broadcast(f32[9,64,128]{2,1,0:T(8,128)S(1)} %broadcast_multiply_fusion.1), dimensions={0,1,3} | broadcast | bytes 2654208 | tf_op jit(solution)/shard_map/transpose(jvp())/broadcast_in_dim | solution.py:97
  67.1 2.7 %reshape.415 = f32[9,64,1024]{2,1,0:T(8,128)S(1)} reshape(f32[9,64,8,128]{3,2,1,0:T(8,128)} %broadcast_in_dim.45) | data formatting | bytes 4718592 | tf_op jit(solution)/shard_map/transpose(jvp())/reshape | solution.py:97
  70.2 1.2 copy-done.49
  72.1 2.1 %fusion.16 = f32[1,1024]{1,0:T(1,128)S(1)} fusion(f32[512,1]{0,1:T(1,128)S(1)} %bitcast.204, f32[1024,512]{0,1:T(8,128)S(1)} %copy-done.49, f32[1024]{0:T(1024)S(1)} %copy-done.37, f32[1024,512]{0,1:T(8,128)S(1)} %copy-done.11), kind=kOutput, calls=%fused_computation.30 | convolution fusion | flops 11534336 | bytes 4204544 | tf_op jit(solution)/shard_map/jvp()/dot_general | solution.py:106
  74.2 1.5 %fusion.50 = (f32[3,64,1024]{2,1,0:T(8,128)S(1)}, f32[3,64,1024]{2,1,0:T(8,128)S(1)}) fusion(f32[9,64,1024]{2,1,0:T(8,128)S(1)} %broadcast_multiply_fusion, f32[1,64,1024]{2,1,0:T(8,128)S(1)} %bitcast.182, f32[1,64,1024]{2,1,0:T(8,128)S(1)} %bitcast.183, pred[3]{0:T(512)(128)(4,1)S(1)} %copy-done.41, f32[9,64,1024]{2,1,0:T(8,128)} %copy-done.4, ...), kind=kLoop, calls=%fused_computation.91 | loop fusion | flops 1179648 | bytes 4194307 | tf_op jit(solution)/shard_map/transpose(jvp())/add_any | solution.py:36
  75.8 1.7 %multiply_reduce_fusion = (f32[1024]{0:T(1024)S(1)}, f32[1024,512]{0,1:T(8,128)S(1)}) fusion(f32[512]{0:T(512)S(1)} %copy-done.45, f32[1024]{0:T(1024)S(1)} %copy-done.37, f32[1024,512]{0,1:T(8,128)S(1)} %copy-done.11, bf16[1024,512]{0,1:T(8,128)(2,1)S(1)} %copy-done.50, bf16[512,384]{1,0:T(8,128)(2,1)S(1)} %copy-done.43, f32[192,1024]{1,0:T(8,128)S(1)} %bitcast.187, ...), kind=kOutput, calls=%fused_computation.29 | convolution fusion | flops 412482560 | bytes 7219200 | tf_op jit(solution)/shard_map/transpose(jvp(ph,hq->qp))/dot_general | solution.py:73
  81.3 1.9 %add_select_fusion = f32[128,3]{0,1:T(4,128)S(1)} fusion(f32[3,128]{1,0:T(4,128)S(1)} %bitcast_reduce_fusion.2, f32[320,640]{0,1:T(8,128)S(1)} %fusion.35, s32[]{:T(128)} %bitcast.41, s32[]{:T(128)} %bitcast.8, pred[]{:T(512)} %and_reduce_fusion), kind=kLoop, calls=%fused_computation.244 | loop fusion | flops 1152 | bytes 4617 | tf_op jit(solution)/shard_map/select.13
  83.2 3.8 %scatter-add.4 = f32[320,640]{0,1:T(8,128)} dynamic-update-slice(f32[320,640]{0,1:T(8,128)} %copy-done.7, f32[128,3]{0,1:T(4,128)S(1)} %add_select_fusion, s32[]{:T(128)} %bitcast.41, s32[]{:T(128)} %bitcast.8) | dynamic-update-slice | bytes 3076 | tf_op jit(solution)/shard_map/scatter-add | solution.py:224
  87.0 1.3 fusion.154
  88.3 3.9 %collective-permute-start.6 = (f32[16,640]{0,1:T(8,128)S(1)}, f32[16,640]{0,1:T(8,128)S(1)}, u32[]{:S(2)}, u32[]{:S(2)}) collective-permute-start(f32[16,640]{0,1:T(8,128)S(1)} %get-tuple-element.120), channel_id=1, source_target_pairs={{1,0},{2,1},{3,2},{0,3},{5,4},{6,5},{7,6},{4,7},{9,8},{10,9},{11,1... | collective-permute-start | bytes 122888 | tf_op jit(solution)/shard_map/ppermute | solution.py:28
  93.2 12.1 %collective-permute-done.7 = f32[16,640]{0,1:T(8,128)S(1)} collective-permute-done((f32[16,640]{0,1:T(8,128)S(1)}, f32[16,640]{0,1:T(8,128)S(1)}, u32[]{:S(2)}, u32[]{:S(2)}) %collective-permute-start.7) | collective-permute-done | bytes 40992 | tf_op jit(solution)/shard_map/ppermute | solution.py:28
  107.4 1.1 collective-permute-start.8
  110.3 7.7 %collective-permute-done.8 = f32[64,640]{0,1:T(8,128)S(1)} collective-permute-done((f32[64,640]{0,1:T(8,128)S(1)}, f32[64,640]{0,1:T(8,128)S(1)}, u32[]{:S(2)}, u32[]{:S(2)}) %collective-permute-start.8) | collective-permute-done | bytes 163872 | tf_op jit(solution)/shard_map/ppermute | solution.py:28
  118.6 2.9 %collective-permute-done.9 = f32[64,640]{0,1:T(8,128)S(1)} collective-permute-done((f32[64,640]{0,1:T(8,128)S(1)}, f32[64,640]{0,1:T(8,128)S(1)}, u32[]{:S(2)}, u32[]{:S(2)}) %collective-permute-start.9) | collective-permute-done | bytes 163872 | tf_op jit(solution)/shard_map/ppermute | solution.py:28
  123.3 1.7 %collective-permute-start.10 = (f32[16,640]{0,1:T(8,128)S(1)}, f32[16,640]{0,1:T(8,128)S(1)}, u32[]{:S(2)}, u32[]{:S(2)}) collective-permute-start(f32[16,640]{0,1:T(8,128)S(1)} %get-tuple-element.126), channel_id=1, source_target_pairs={{8,0},{16,8},{24,16},{0,24},{9,1},{17,9},{25,17},{1,25},{10,2},{18... | collective-permute-start | bytes 122888 | tf_op jit(solution)/shard_map/ppermute | solution.py:28
  124.9 6.5 %collective-permute-done.11 = f32[16,640]{0,1:T(8,128)S(1)} collective-permute-done((f32[16,640]{0,1:T(8,128)S(1)}, f32[16,640]{0,1:T(8,128)S(1)}, u32[]{:S(2)}, u32[]{:S(2)}) %collective-permute-start.11) | collective-permute-done | bytes 40992 | tf_op jit(solution)/shard_map/ppermute | solution.py:28
  133.0 1.4 %convolution_add_fusion.7 = f32[128,512]{1,0:T(8,128)} fusion(f32[128,512]{1,0:T(8,128)S(1)} %fusion.159, bf16[512,512]{1,0:T(8,128)(2,1)S(1)} %copy-done.14, f32[128,640]{0,1:T(8,128)S(1)} %fusion.55), kind=kOutput, calls=%fused_computation.69 | convolution fusion | flops 402718720 | bytes 1310720 | tf_op jit(solution)/shard_map/dot_general | solution.py:240
  (237 shorter events, 45.8 us)
Async XLA Ops:
  0.6 55.5 %copy-start = (bf16[512,512]{1,0:T(8,128)(2,1)S(1)}, bf16[512,512]{1,0:T(8,128)(2,1)}, u32[]{:S(2)}) copy-start(bf16[512,512]{1,0:T(8,128)(2,1)} %param.42) | copy-start | bytes 1572868
  0.6 8.5 %copy-start.47 = (s32[2]{0:T(128)S(1)}, s32[2]{0:T(128)}, u32[]{:S(2)}) copy-start(s32[2]{0:T(128)} %constant.250.clone.1) | copy-start | bytes 28
  0.7 9.7 %copy-start.38 = (s32[128]{0:T(128)S(1)}, s32[128]{0:T(128)}, u32[]{:S(2)}) copy-start(s32[128]{0:T(128)} %param.32) | copy-start | bytes 1540
  0.7 10.0 %copy-start.16 = (bf16[128,512]{1,0:T(8,128)(2,1)S(1)}, bf16[128,512]{1,0:T(8,128)(2,1)}, u32[]{:S(2)}) copy-start(bf16[128,512]{1,0:T(8,128)(2,1)} %param.30) | copy-start | bytes 393220
  0.7 9.7 %copy-start.19 = (f32[5,512]{1,0:T(8,128)S(1)}, f32[5,512]{1,0:T(8,128)}, u32[]{:S(2)}) copy-start(f32[5,512]{1,0:T(8,128)} %param.38) | copy-start | bytes 30724
  0.7 10.0 %copy-start.12 = (bf16[512,512]{1,0:T(8,128)(2,1)S(1)}, bf16[512,512]{1,0:T(8,128)(2,1)}, u32[]{:S(2)}) copy-start(bf16[512,512]{1,0:T(8,128)(2,1)} %param.36) | copy-start | bytes 1572868
  1.6 9.4 %copy-start.29 = (s32[16]{0:T(128)}, s32[16]{0:T(128)S(1)}, u32[]{:S(2)}) copy-start(s32[16]{0:T(128)S(1)} %get-tuple-element.152) | copy-start | bytes 196
  1.6 29.5 %copy-start.21 = (s32[16]{0:T(128)}, s32[16]{0:T(128)S(1)}, u32[]{:S(2)}) copy-start(s32[16]{0:T(128)S(1)} %get-tuple-element.153) | copy-start | bytes 196
  1.6 31.5 %copy-start.23 = (s32[16]{0:T(128)}, s32[16]{0:T(128)S(1)}, u32[]{:S(2)}) copy-start(s32[16]{0:T(128)S(1)} %get-tuple-element.150) | copy-start | bytes 196
  2.5 9.7 %copy-start.35 = (s32[1024]{0:T(1024)S(1)}, s32[1024]{0:T(1024)}, u32[]{:S(2)}) copy-start(s32[1024]{0:T(1024)} %param.34) | copy-start | bytes 12292
  5.2 18.5 %collective-permute-start = (bf16[16,640]{1,0:T(8,128)(2,1)S(1)}, bf16[16,640]{1,0:T(8,128)(2,1)S(1)}, u32[]{:S(2)}, u32[]{:S(2)}) collective-permute-start(bf16[16,640]{1,0:T(8,128)(2,1)S(1)} %convolution_convert_fusion.7), channel_id=1, source_target_pairs={{24,0},{0,8},{8,16},{16,24},{25,1},{1,9},{9,17},{17,25},{26,2},{2,... | collective-permute-start | bytes 61448 | tf_op jit(solution)/shard_map/ppermute | solution.py:28
  5.8 17.8 %collective-permute-start.1 = (bf16[16,640]{1,0:T(8,128)(2,1)S(1)}, bf16[16,640]{1,0:T(8,128)(2,1)S(1)}, u32[]{:S(2)}, u32[]{:S(2)}) collective-permute-start(bf16[16,640]{1,0:T(8,128)(2,1)S(1)} %convolution_convert_fusion.6), channel_id=1, source_target_pairs={{8,0},{16,8},{24,16},{0,24},{9,1},{17,9},{25,17},{1,25},{10,2},{18... | collective-permute-start | bytes 61448 | tf_op jit(solution)/shard_map/ppermute | solution.py:28
  8.4 15.8 %copy-start.25 = (s32[64]{0:T(128)}, s32[64]{0:T(128)S(1)}, u32[]{:S(2)}) copy-start(s32[64]{0:T(128)S(1)} %get-tuple-element.154) | copy-start | bytes 772
  8.4 15.8 %copy-start.27 = (s32[64]{0:T(128)}, s32[64]{0:T(128)S(1)}, u32[]{:S(2)}) copy-start(s32[64]{0:T(128)S(1)} %get-tuple-element.155) | copy-start | bytes 772
  11.0 29.1 %copy-start.31 = (f32[128]{0:T(128)}, f32[128]{0:T(128)S(1)}, u32[]{:S(2)}) copy-start(f32[128]{0:T(128)S(1)} %compare_convert_fusion) | copy-start | bytes 1540
  24.2 5.7 %collective-permute-start.2 = (bf16[64,640]{1,0:T(8,128)(2,1)S(1)}, bf16[64,640]{1,0:T(8,128)(2,1)S(1)}, u32[]{:S(2)}, u32[]{:S(2)}) collective-permute-start(bf16[64,640]{1,0:T(8,128)(2,1)S(1)} %convolution_convert_fusion.3), channel_id=1, source_target_pairs={{4,0},{0,4},{5,1},{1,5},{6,2},{2,6},{7,3},{3,7},{12,8},{8,12},{13,... | collective-permute-start | bytes 245768 | tf_op jit(solution)/shard_map/ppermute | solution.py:28
  26.6 4.5 %collective-permute-start.3 = (bf16[64,640]{1,0:T(8,128)(2,1)S(1)}, bf16[64,640]{1,0:T(8,128)(2,1)S(1)}, u32[]{:S(2)}, u32[]{:S(2)}) collective-permute-start(bf16[64,640]{1,0:T(8,128)(2,1)S(1)} %convolution_convert_fusion.2), channel_id=1, source_target_pairs={{4,0},{0,4},{5,1},{1,5},{6,2},{2,6},{7,3},{3,7},{12,8},{8,12},{13,... | collective-permute-start | bytes 245768 | tf_op jit(solution)/shard_map/ppermute | solution.py:28
  31.3 5.6 %collective-permute-start.4 = (bf16[16,640]{1,0:T(8,128)(2,1)S(1)}, bf16[16,640]{1,0:T(8,128)(2,1)S(1)}, u32[]{:S(2)}, u32[]{:S(2)}) collective-permute-start(bf16[16,640]{1,0:T(8,128)(2,1)S(1)} %convolution_convert_fusion.5), channel_id=1, source_target_pairs={{3,0},{0,1},{1,2},{2,3},{7,4},{4,5},{5,6},{6,7},{11,8},{8,9},{9,10... | collective-permute-start | bytes 61448 | tf_op jit(solution)/shard_map/ppermute | solution.py:28
  33.3 3.8 %collective-permute-start.5 = (bf16[16,640]{1,0:T(8,128)(2,1)S(1)}, bf16[16,640]{1,0:T(8,128)(2,1)S(1)}, u32[]{:S(2)}, u32[]{:S(2)}) collective-permute-start(bf16[16,640]{1,0:T(8,128)(2,1)S(1)} %convolution_convert_fusion.4), channel_id=1, source_target_pairs={{1,0},{2,1},{3,2},{0,3},{5,4},{6,5},{7,6},{4,7},{9,8},{10,9},{11,1... | collective-permute-start | bytes 61448 | tf_op jit(solution)/shard_map/ppermute | solution.py:28
  88.3 17.7 %collective-permute-start.6 = (f32[16,640]{0,1:T(8,128)S(1)}, f32[16,640]{0,1:T(8,128)S(1)}, u32[]{:S(2)}, u32[]{:S(2)}) collective-permute-start(f32[16,640]{0,1:T(8,128)S(1)} %get-tuple-element.120), channel_id=1, source_target_pairs={{1,0},{2,1},{3,2},{0,3},{5,4},{6,5},{7,6},{4,7},{9,8},{10,9},{11,1... | collective-permute-start | bytes 122888 | tf_op jit(solution)/shard_map/ppermute | solution.py:28
  92.2 13.1 %collective-permute-start.7 = (f32[16,640]{0,1:T(8,128)S(1)}, f32[16,640]{0,1:T(8,128)S(1)}, u32[]{:S(2)}, u32[]{:S(2)}) collective-permute-start(f32[16,640]{0,1:T(8,128)S(1)} %get-tuple-element.121), channel_id=1, source_target_pairs={{3,0},{0,1},{1,2},{2,3},{7,4},{4,5},{5,6},{6,7},{11,8},{8,9},{9,10... | collective-permute-start | bytes 122888 | tf_op jit(solution)/shard_map/ppermute | solution.py:28
  92.7 12.6 %copy-start.24 = (s32[16]{0:T(128)S(1)}, s32[16]{0:T(128)}, u32[]{:S(2)}) copy-start(s32[16]{0:T(128)} %copy-done.23) | copy-start | bytes 196
  93.2 12.8 %copy-start.22 = (s32[16]{0:T(128)S(1)}, s32[16]{0:T(128)}, u32[]{:S(2)}) copy-start(s32[16]{0:T(128)} %copy-done.21) | copy-start | bytes 196
  107.2 10.8 %copy-start.28 = (s32[64]{0:T(128)S(1)}, s32[64]{0:T(128)}, u32[]{:S(2)}) copy-start(s32[64]{0:T(128)} %copy-done.27) | copy-start | bytes 772
  107.4 14.1 %copy-start.26 = (s32[64]{0:T(128)S(1)}, s32[64]{0:T(128)}, u32[]{:S(2)}) copy-start(s32[64]{0:T(128)} %copy-done.25) | copy-start | bytes 772
  107.4 10.6 %collective-permute-start.8 = (f32[64,640]{0,1:T(8,128)S(1)}, f32[64,640]{0,1:T(8,128)S(1)}, u32[]{:S(2)}, u32[]{:S(2)}) collective-permute-start(f32[64,640]{0,1:T(8,128)S(1)} %get-tuple-element.119), channel_id=1, source_target_pairs={{4,0},{0,4},{5,1},{1,5},{6,2},{2,6},{7,3},{3,7},{12,8},{8,12},{13,... | collective-permute-start | bytes 491528 | tf_op jit(solution)/shard_map/ppermute | solution.py:28
  109.3 12.2 %collective-permute-start.9 = (f32[64,640]{0,1:T(8,128)S(1)}, f32[64,640]{0,1:T(8,128)S(1)}, u32[]{:S(2)}, u32[]{:S(2)}) collective-permute-start(f32[64,640]{0,1:T(8,128)S(1)} %get-tuple-element.118), channel_id=1, source_target_pairs={{4,0},{0,4},{5,1},{1,5},{6,2},{2,6},{7,3},{3,7},{12,8},{8,12},{13,... | collective-permute-start | bytes 491528 | tf_op jit(solution)/shard_map/ppermute | solution.py:28
  121.8 9.6 %copy-start.34 = (s32[16]{0:T(128)S(1)}, s32[16]{0:T(128)}, u32[]{:S(2)}) copy-start(s32[16]{0:T(128)} %copy-done.33) | copy-start | bytes 196
  121.9 9.8 %copy-start.30 = (s32[16]{0:T(128)S(1)}, s32[16]{0:T(128)}, u32[]{:S(2)}) copy-start(s32[16]{0:T(128)} %copy-done.29) | copy-start | bytes 196
  122.3 10.7 %copy-start.14 = (bf16[512,512]{1,0:T(8,128)(2,1)S(1)}, bf16[512,512]{1,0:T(8,128)(2,1)}, u32[]{:S(2)}) copy-start(bf16[512,512]{1,0:T(8,128)(2,1)} %param.37) | copy-start | bytes 1572868
  122.3 9.1 %collective-permute-start.11 = (f32[16,640]{0,1:T(8,128)S(1)}, f32[16,640]{0,1:T(8,128)S(1)}, u32[]{:S(2)}, u32[]{:S(2)}) collective-permute-start(f32[16,640]{0,1:T(8,128)S(1)} %get-tuple-element.125), channel_id=1, source_target_pairs={{24,0},{0,8},{8,16},{16,24},{25,1},{1,9},{9,17},{17,25},{26,2},{2,... | collective-permute-start | bytes 122888 | tf_op jit(solution)/shard_map/ppermute | solution.py:28
  123.3 8.4 %collective-permute-start.10 = (f32[16,640]{0,1:T(8,128)S(1)}, f32[16,640]{0,1:T(8,128)S(1)}, u32[]{:S(2)}, u32[]{:S(2)}) collective-permute-start(f32[16,640]{0,1:T(8,128)S(1)} %get-tuple-element.126), channel_id=1, source_target_pairs={{8,0},{16,8},{24,16},{0,24},{9,1},{17,9},{25,17},{1,25},{10,2},{18... | collective-permute-start | bytes 122888 | tf_op jit(solution)/shard_map/ppermute | solution.py:28
  (31 other events, 53.6 us)

commit v2 on v1

--- a/solution.py
+++ b/solution.py
@@ -53,58 +53,61 @@
     energy_proj,
 ):
     atoms = centre_rows.shape[0]
-    pairs = delta.shape[1]
+    width = centre_rows.shape[1]
     radius = jnp.sqrt(jnp.sum(delta * delta, axis=0) + SOFTEN)
     unit = delta / radius
     ratio = radius / CUTOFF
     envelope = jnp.where(ratio < 1.0, (1.0 - ratio * ratio) ** 2, 0.0) * valid_pair
     orders = jnp.arange(1, NB + 1).astype(jnp.float32)
     basis = (
-        jnp.sin(orders[:, None] * (math.pi / CUTOFF) * radius[None, :])
-        * (envelope / radius)[None, :]
+        jnp.sin(orders[:, None, None] * (math.pi / CUTOFF) * radius[None])
+        * (envelope / radius)[None]
     )
     radial = jnp.einsum(
-        "kp,kh->ph", basis, basis_proj.astype(jnp.float32), precision=lax.Precision.HIGHEST
+        "nka,nh->kah", basis, basis_proj.astype(jnp.float32), precision=lax.Precision.HIGHEST
     )
     hidden = (
-        jax.nn.silu(jnp.tile(centre_rows, (K, 1)) + neigh_rows + radial) * envelope[:, None]
+        jax.nn.silu(centre_rows[None] + neigh_rows.reshape(K, atoms, width) + radial)
+        * envelope[:, :, None]
     )
     hidden_low = hidden.astype(jnp.bfloat16)
-    mixed = jnp.einsum("ph,hq->qp", hidden_low, split_proj, preferred_element_type=jnp.float32)
-    amplitude = mixed[: 3 * CH].reshape(3, CH, pairs)
-    weights = mixed[3 * CH :].reshape(3, CH, pairs)
+    mixed = jnp.einsum("kah,hq->qka", hidden_low, split_proj, preferred_element_type=jnp.float32)
+    amplitude = mixed[: 3 * CH].reshape(3, CH, K, atoms)
+    weights = mixed[3 * CH :].reshape(3, CH, K, atoms)
     unit_x = unit[0]
     unit_y = unit[1]
     unit_z = unit[2]
     root3 = math.sqrt(3.0)
     root15 = math.sqrt(15.0)
     root5 = math.sqrt(5.0)
-    harmonics = jnp.stack(
+    harmonics = [
+        [jnp.ones_like(unit_x)],
+        [root3 * unit_x, root3 * unit_y, root3 * unit_z],
         [
-            jnp.ones_like(unit_x),
-            root3 * unit_x,
-            root3 * unit_y,
-            root3 * unit_z,
             root15 * unit_x * unit_y,
             root15 * unit_y * unit_z,
             0.5 * root5 * (2.0 * unit_z * unit_z - unit_x * unit_x - unit_y * unit_y),
             root15 * unit_x * unit_z,
             0.5 * root15 * (unit_x * unit_x - unit_y * unit_y),
         ],
-        axis=0,
-    )
-    gathered = by_order(weights) * harmonics[:, None, :]
-    environment = gathered.reshape(9, CH, K, atoms).sum(axis=2) / math.sqrt(K)
-    expanded = jnp.tile(environment, (1, 1, K))
-    products = by_order(amplitude) * harmonics[:, None, :] * expanded
-    scalars = jnp.stack([products[0], products[1:4].sum(axis=0), products[4:9].sum(axis=0)], axis=0)
-    scalars = scalars.reshape(3 * CH, pairs).astype(jnp.bfloat16)
+    ]
+    scalars = []
+    for order in range(3):
+        total = 0.0
+        for harmonic in harmonics[order]:
+            environment = (weights[order] * harmonic[None]).sum(axis=1) / math.sqrt(K)
+            total = total + harmonic[None] * environment[:, None, :]
+        scalars.append(amplitude[order] * total)
+    scalars = jnp.stack(scalars, axis=0).reshape(3 * CH, K * atoms).astype(jnp.bfloat16)
+    flat_low = hidden_low.reshape(K * atoms, width)
     update = jax.nn.silu(
-        jnp.dot(hidden_low, update_proj, preferred_element_type=jnp.float32)
+        jnp.dot(flat_low, update_proj, preferred_element_type=jnp.float32)
         + jnp.einsum("qp,qh->ph", scalars, tensor_proj, preferred_element_type=jnp.float32)
     )
-    energy = envelope * jnp.dot(hidden + update, energy_proj, precision=lax.Precision.HIGHEST)
-    return energy.reshape(K, atoms).sum(axis=0)
+    energy = envelope * jnp.sum(
+        (hidden + update.reshape(K, atoms, width)) * energy_proj, axis=-1
+    )
+    return energy.sum(axis=0)
 
 
 def shards(
@@ -183,9 +186,8 @@
             out = jnp.dot(onehot, table, preferred_element_type=jnp.float32).astype(jnp.bfloat16)
             got = passed_along(out, axis, direction)
             coord_axis, offset = shifts[2 * section + number]
-            shift = jnp.zeros((1, width + extra), jnp.bfloat16).at[0, width + coord_axis].set(
-                offset // 16
-            )
+            columns = jnp.arange(width + extra, dtype=jnp.int32)[None, :]
+            shift = jnp.where(columns == width + coord_axis, offset // 16, 0).astype(jnp.bfloat16)
             parts.append(got + shift)
         table = jnp.concatenate(parts, axis=0)
     total_rows = table.shape[0]
@@ -196,9 +198,11 @@
     gathered = jnp.dot(select, table, preferred_element_type=jnp.float32)
     neigh_rows = gathered[:, :width]
     coords_n = (gathered[:, width : width + 3] * 16.0 + gathered[:, width + 3 : width + 6]).T
-    delta = (coords_n - jnp.tile(positions.astype(jnp.float32), (1, K))) * (1.0 / 64.0)
+    delta = (coords_n.reshape(3, K, atoms) - positions.astype(jnp.float32)[:, None, :]) * (
+        1.0 / 64.0
+    )
     live = (jnp.arange(atoms) < atom_count[0]).astype(jnp.float32)
-    valid_pair = jnp.tile(live, K)
+    valid_pair = live[None, :]
 
     def energy_of(delta_in, neigh_in, centre_in):
         return pair_energy(
@@ -217,11 +221,16 @@
     grad_delta, grad_neigh, grad_centre = pull(jnp.ones_like(atom_energy))
     pairs = grad_neigh.shape[0]
     grads = jnp.concatenate(
-        [grad_neigh, grad_delta.T, jnp.zeros((pairs, extra - 3), jnp.float32)], axis=1
+        [
+            grad_neigh,
+            grad_delta.reshape(3, pairs).T,
+            jnp.zeros((pairs, extra - 3), jnp.float32),
+        ],
+        axis=1,
     )
     sums = spread(select, grads)
-    own_pos = grad_delta.reshape(3, K, atoms).sum(axis=1)
-    sums = sums.at[:atoms, width : width + 3].add(-own_pos.T)
+    own_pos = grad_delta.sum(axis=1)
+    sums = sums - jnp.pad(own_pos.T, ((0, total_rows - atoms), (width, extra - 3)))
     for section in (2, 1, 0):
         axis, segs = sections[section]
         rows_now = base_rows[section]

time: 135 us -> 124 us (0.919)
  waiting for transfers between devices: 35.2 us -> 15.1 us
  other arithmetic: 14.2 us -> 25.6 us
  matrix products: 26.2 us -> 31 us
  local copies, waits for them, and re-layouts: 36 us -> 32.2 us
  between operations: 6.29 us -> 3.04 us
    ppermute x12, waiting for transfers between devices: 35.2 us -> 15.1 us  [passed_along(): return lax.ppermute(block, axis, route)]
    div x0 -> x18, local copies, waits for them, and re-layouts: none -> 14 us  [pair_energy(): environment = (weights[order] * harmonic[None]).sum(axis=1) / math.sqrt(K)]
    reduce_sum x12 -> x5, other arithmetic: 2.51 us -> 8.9 us  [the longest x3 7.28 us: pair_energy(): total = total + harmonic[None] * environment[:, None, :]]
    div x2 -> x14, other arithmetic: 0.06 us -> 6.39 us  [pair_energy(): environment = (weights[order] * harmonic[None]).sum(axis=1) / math.sqrt(K)]
    scatter x6 -> x0, local copies, waits for them, and re-layouts: 4.52 us -> none  [shards(): jnp.zeros((1, width + extra), jnp.bfloat16).at[0, width + coord_axis]]
    broadcast_in_dim x7 -> x1, local copies, waits for them, and re-layouts: 4.07 us -> 0.02 us  [pair_energy(): environment = (weights[order] * harmonic[None]).sum(axis=1) / math.sqrt(K)]
    scatter-add x1 -> x0, local copies, waits for them, and re-layouts: 3.75 us -> none  [shards(): sums = sums.at[:atoms, width:width + 3].add(-own_pos.T)]
    dot_general x7 -> x6, matrix products: 10.1 us -> 13.1 us  [the longest x2 5.7 us: pair_energy(): jnp.einsum('nka,nh->kah', basis, basis_proj.astype(jnp.float32), precisio...]
  transfers between devices with their start and end apart: 12 -> 12, of which waited for: 8 -> 9; matrix products, arithmetic and copies ran while one was open for 12% -> 4% of each run, Pallas kernels for 0% -> 0%
where the time goes in v2:
time: 124 us; the launch traced here: 122 us
  local copies, waits for them, and re-layouts  32.2 us (26%)
  matrix products  31 us (25%)
  other arithmetic  25.6 us (21%)
  starting transfers between devices  15.5 us (12%)
  waiting for transfers between devices  15.1 us (12%)
  between operations  3.04 us (2%)
    ppermute x12, starting transfers between devices, passed_along(): return lax.ppermute(block, axis, route)  15.5 us
    ppermute x12, waiting for transfers between devices, passed_along(): return lax.ppermute(block, axis, route)  15.1 us
    div x18, local copies, waits for them, and re-layouts, pair_energy(): environment = (weights[order] * harmonic[None]).sum(axis=1) / math.sqrt(K)  14 us
    unnamed x221, local copies, waits for them, and re-layouts  7.86 us
    reduce_sum x3, other arithmetic, pair_energy(): total = total + harmonic[None] * environment[:, None, :]  7.28 us
    div x14, other arithmetic, pair_energy(): environment = (weights[order] * harmonic[None]).sum(axis=1) / math.sqrt(K)  6.39 us
    dot_general x2, matrix products, pair_energy(): jnp.einsum('nka,nh->kah', basis, basis_proj.astype(jnp.float32), precisio...  5.7 us
    another operation x5, local copies, waits for them, and re-layouts, pair_energy(): jnp.stack(scalars, axis=0).reshape(3 * CH, K * atoms).astype(jnp.bfloat16)  5.03 us
  transfers between devices with their start and end apart: 12, of which 9 were waited for; matrix products, arithmetic and copies ran while one was open for 4% of the time, Pallas kernels for 0%

profile of v2, /device:TPU:0, one launch (start us, length us, event | category | flops | bytes accessed | tf_op | source)
XLA Modules:
  0.0 122.4 jit_solution(7166896107162443148)
XLA Ops:
  5.8 1.9 %collective-permute-start.1 = (bf16[16,640]{1,0:T(8,128)(2,1)S(1)}, bf16[16,640]{1,0:T(8,128)(2,1)S(1)}, u32[]{:S(2)}, u32[]{:S(2)}) collective-permute-start(bf16[16,640]{1,0:T(8,128)(2,1)S(1)} %convolution_convert_fusion.6), channel_id=1, source_target_pairs={{8,0},{16,8},{24,16},{0,24},{9,1},{17,9},{25,17},{1,25},{10,2},{18... | collective-permute-start | bytes 61448 | tf_op jit(solution)/shard_map/ppermute | solution.py:28
  10.7 2.4 %collective-permute-start.2 = (bf16[64,640]{1,0:T(8,128)(2,1)S(1)}, bf16[64,640]{1,0:T(8,128)(2,1)S(1)}, u32[]{:S(2)}, u32[]{:S(2)}) collective-permute-start(bf16[64,640]{1,0:T(8,128)(2,1)S(1)} %convolution_convert_fusion.3), channel_id=1, source_target_pairs={{4,0},{0,4},{5,1},{1,5},{6,2},{2,6},{7,3},{3,7},{12,8},{8,12},{13,... | collective-permute-start | bytes 245768 | tf_op jit(solution)/shard_map/ppermute | solution.py:28
  13.1 3.0 %collective-permute-done.2 = bf16[64,640]{1,0:T(8,128)(2,1)S(1)} collective-permute-done((bf16[64,640]{1,0:T(8,128)(2,1)S(1)}, bf16[64,640]{1,0:T(8,128)(2,1)S(1)}, u32[]{:S(2)}, u32[]{:S(2)}) %collective-permute-start.2) | collective-permute-done | bytes 81952 | tf_op jit(solution)/shard_map/ppermute | solution.py:28
  16.2 1.9 %collective-permute-done.3 = bf16[64,640]{1,0:T(8,128)(2,1)S(1)} collective-permute-done((bf16[64,640]{1,0:T(8,128)(2,1)S(1)}, bf16[64,640]{1,0:T(8,128)(2,1)S(1)}, u32[]{:S(2)}, u32[]{:S(2)}) %collective-permute-start.3) | collective-permute-done | bytes 81952 | tf_op jit(solution)/shard_map/ppermute | solution.py:28
  18.4 1.8 %collective-permute-start.4 = (bf16[16,640]{1,0:T(8,128)(2,1)S(1)}, bf16[16,640]{1,0:T(8,128)(2,1)S(1)}, u32[]{:S(2)}, u32[]{:S(2)}) collective-permute-start(bf16[16,640]{1,0:T(8,128)(2,1)S(1)} %convolution_convert_fusion.5), channel_id=1, source_target_pairs={{3,0},{0,1},{1,2},{2,3},{7,4},{4,5},{5,6},{6,7},{11,8},{8,9},{9,10... | collective-permute-start | bytes 61448 | tf_op jit(solution)/shard_map/ppermute | solution.py:28
  20.4 2.1 %collective-permute-start.5 = (bf16[16,640]{1,0:T(8,128)(2,1)S(1)}, bf16[16,640]{1,0:T(8,128)(2,1)S(1)}, u32[]{:S(2)}, u32[]{:S(2)}) collective-permute-start(bf16[16,640]{1,0:T(8,128)(2,1)S(1)} %convolution_convert_fusion.4), channel_id=1, source_target_pairs={{1,0},{2,1},{3,2},{0,3},{5,4},{6,5},{7,6},{4,7},{9,8},{10,9},{11,1... | collective-permute-start | bytes 61448 | tf_op jit(solution)/shard_map/ppermute | solution.py:28
  22.5 1.5 %collective-permute-done.4 = bf16[16,640]{1,0:T(8,128)(2,1)S(1)} collective-permute-done((bf16[16,640]{1,0:T(8,128)(2,1)S(1)}, bf16[16,640]{1,0:T(8,128)(2,1)S(1)}, u32[]{:S(2)}, u32[]{:S(2)}) %collective-permute-start.4) | collective-permute-done | bytes 20512 | tf_op jit(solution)/shard_map/ppermute | solution.py:28
  26.9 2.0 %copy.121 = f32[1024,512]{1,0:T(8,128)} copy(f32[1024,512]{0,1:T(8,128)S(1)} %slice.147) | data formatting | bytes 4194304 | tf_op jit(solution)/shard_map/jvp()/reshape | solution.py:70
  29.0 4.6 %multiply_convert_fusion = (bf16[8,128,512]{2,1,0:T(8,128)(2,1)S(1)}, f32[8,128,512]{2,1,0:T(8,128)}) fusion(f32[8,128]{1,0:T(8,128)S(1)} %get-tuple-element.93, bf16[8,512]{1,0:T(8,128)(2,1)S(1)} %copy-done.76, f32[8,128]{1,0:T(8,128)S(1)} %get-tuple-element.92, f32[8,128]{1,0:T(8,128)S(1)} %get-tuple-element.106, f32[8]{0:T(128)S(1)} %convert_multiply_fusion, ...), kind=kOutput, calls=%fused_computation.19 | convolution fusion | flops 54542336 | bytes 5525536 | tf_op jit(solution)/shard_map/jvp(nka,nh->kah)/dot_general | solution.py:66
  34.4 1.6 %slice_reduce_fusion = (f32[64,128]{0,1:T(8,128)S(1)}, f32[64,128]{0,1:T(8,128)S(1)}, f32[64,128]{0,1:T(8,128)S(1)}, f32[64,128]{0,1:T(8,128)S(1)}, f32[64,128]{...) fusion(f32[384,8,128]{0,2,1:T(8,128)S(1)} %convolution_bitcast_, ...), kind=kLoop, calls=%fused_computation.68 | loop fusion | flops 1040384 | bytes 1114112 | tf_op jit(solution)/shard_map/jvp()/reduce_sum | solution.py:98
  38.2 2.0 %fusion.46 = bf16[1,64,8,128]{1,3,2,0:T(8,128)(2,1)} fusion(f32[384,8,128]{0,2,1:T(8,128)S(1)} %convolution_bitcast_fusion, f32[64,128]{0,1:T(8,128)S(1)} %get-tuple-element.125, f32[8,128]{1,0:T(8,128)} %copy-done.43, f32[64,128]{0,1:T(8,128)S(1)} %get-tuple-element.126, f32[8,128]{1,0:T(8,128)} %copy-done.45, f32[64,128]{0,1:T(8,128)S(1)} %get-tuple-element.127, ...), kind=kLoop, calls=%fused_computation.117 | loop fusion | flops 458752 | bytes 503808 | tf_op jit(solution)/shard_map/jvp()/stack | solution.py:101
  46.6 1.6 %fusion.39 = f32[1024,512]{1,0:T(8,128)S(1)} fusion(bf16[192,512]{1,0:T(8,128)(2,1)} %param.29, bf16[24,8,8,128]{3,2,1,0:T(8,128)(2,1)} %bitcast.232), kind=kOutput, calls=%fused_computation.109 | convolution fusion | flops 201326592 | bytes 2686976 | tf_op jit(solution)/shard_map/jvp(qp,qh->ph)/dot_general | solution.py:105
  48.3 2.3 %fusion.4 = (f32[1024,512]{1,0:T(8,128)}, f32[1024,512]{1,0:T(8,128)S(1)}) fusion(f32[1024,512]{1,0:T(8,128)S(1)} %fusion.39, bf16[1024,512]{1,0:T(8,128)(2,1)S(1)} %bitcast.233, bf16[512,512]{1,0:T(8,128)(2,1)S(1)} %copy-done), kind=kOutput, calls=%fused_computation.14 | convolution fusion | flops 539492352 | bytes 7864320 | tf_op jit(solution)/shard_map/jvp()/dot_general | solution.py:104
  51.7 2.1 %convolution_convert_fusion = bf16[1024,512]{1,0:T(8,128)(2,1)} fusion(bf16[512,512]{1,0:T(8,128)(2,1)S(1)} %copy-done, f32[1024,512]{1,0:T(8,128)S(1)} %get-tuple-element.119, f32[512]{0:T(512)S(1)} %copy-done.101, f32[1024]{0:T(1024)S(1)} %copy-done.93), kind=kOutput, calls=%fused_computation.28 | convolution fusion | flops 542638080 | bytes 3676160 | tf_op jit(solution)/shard_map/transpose(jvp())/dot_general | solution.py:104
  56.8 1.7 %copy.127 = f32[8,8,8,128]{3,2,1,0:T(8,128)} copy(f32[8,8,8,128]{3,1,2,0:T(8,128)} %get-tuple-element.68) | data formatting | bytes 524288
  58.5 1.7 %copy.128 = f32[8,8,8,128]{3,2,1,0:T(8,128)} copy(f32[8,8,8,128]{3,1,2,0:T(8,128)} %get-tuple-element.69) | data formatting | bytes 524288
  62.3 1.5 %slice_multiply_fusion.1 = (f32[64,8,128]{0,2,1:T(8,128)S(1)}, f32[64,8,128]{0,2,1:T(8,128)S(1)}) fusion(f32[64,8,128]{0,2,1:T(8,128)} %bitcast.230, f32[384,8,128]{0,2,1:T(8,128)S(1)} %convolution_bitcast_fusion, f32[64,8,128]{0,2,1:T(8,128)} %bitcast.231), kind=kLoop, calls=%fused_computation.106 | loop fusion | flops 131072 | bytes 1572864 | tf_op jit(solution)/shard_map/transpose(jvp())/mul | solution.py:100
  63.9 1.6 %multiply_reduce_fusion.21 = (f32[64,128]{0,1:T(8,128)S(1)}, f32[8,128]{1,0:T(8,128)}, f32[8,128]{1,0:T(8,128)}, f32[8,128]{1,0:T(8,128)}, f32[64,128]{0,1:T(8,128)}, /*index=5*/f32[64,128]{0,1:T(8,128)}) fusion(f32[64,8,128]{0,2,1:T(8,128)S(1)} %get-tuple-element.60, f32[8,128]{1,0:T(8,128)S(1)} %copy-done.44, f32[64,128]{0,1:T(8,128)S(1)} %copy-done.10, ...), kind=kLoop, calls=%fused_computation.88 | loop fusion | flops 758784 | bytes 483328 | tf_op jit(solution)/shard_map/transpose(jvp())/reduce_sum | solution.py:99
  66.1 2.5 %multiply_reduce_fusion.23 = (f32[64,128]{0,1:T(8,128)S(1)}, f32[8,128]{1,0:T(8,128)}, f32[8,128]{1,0:T(8,128)}, f32[8,128]{1,0:T(8,128)}, f32[8,128]{1,0:T(8,12...) fusion(f32[64,8,128]{0,2,1:T(8,128)S(1)} %get-tuple-element.61, ...), kind=kLoop, calls=%fused_computation.90 | loop fusion | flops 1264640 | bytes 630784 | tf_op jit(solution)/shard_map/transpose(jvp())/reduce_sum | solution.py:99
  69.3 1.5 %copy.103 = f32[64,128]{1,0:T(8,128)} copy(f32[64,128]{0,1:T(8,128)} %broadcast_multiply_fusion.11) | data formatting | bytes 65536 | tf_op jit(solution)/shard_map/transpose(jvp())/div | solution.py:98
  78.5 1.5 %broadcast_multiply_fusion.10 = f32[64,128]{0,1:T(8,128)} fusion(f32[64,128]{0,1:T(8,128)} %get-tuple-element.37), kind=kLoop, calls=%fused_computation.166 | loop fusion | flops 8192 | bytes 65536 | tf_op jit(solution)/shard_map/transpose(jvp())/div | solution.py:98
  79.9 1.5 %copy.104 = f32[64,128]{1,0:T(8,128)} copy(f32[64,128]{0,1:T(8,128)} %broadcast_multiply_fusion.10) | data formatting | bytes 65536 | tf_op jit(solution)/shard_map/transpose(jvp())/div | solution.py:98
  81.5 3.2 %multiply_reduce_fusion.18 = (f32[64,128]{0,1:T(8,128)S(1)}, f32[8,128]{1,0:T(8,128)}, f32[8,128]{1,0:T(8,128)}, f32[8,128]{1,0:T(8,128)}, f32[8,128]{1,0:T(8,12...) fusion(f32[64,8,128]{0,2,1:T(8,128)} %bitcast.229, ...), kind=kLoop, calls=%fused_computation.85 | loop fusion | flops 1163264 | bytes 1376256 | tf_op jit(solution)/shard_map/transpose(jvp())/reduce_sum | solution.py:99
  91.2 2.3 %fusion.142 = (f32[128,512]{1,0:T(8,128)S(1)}, f32[8,128,512]{2,1,0:T(8,128)S(1)}, f32[8,128]{1,0:T(8,128)S(1)}, f32[8,128]{1,0:T(8,128)S(1)}) fusion(f32[8,128,512]{2,1,0:T(8,128)S(1)} %copy-done.106, f32[512]{0:T(512)S(1)} %copy-done.102, f32[8,128]{1,0:T(8,128)S(1)} %copy-done.96, f32[8,128,512]{2,1,0:T(8,128)S(1)} %bitcast.249, ...), kind=kOutput, calls=%fused_computation.336 | convolution fusion | flops 414119936 | bytes 8796160 | tf_op jit(solution)/shard_map/transpose(jvp(kah,hq->qka))/dot_general | solution.py:74
  96.3 2.1 %fusion.9 = f32[320,640]{1,0:T(8,128)S(1)} fusion(f32[1024,3]{1,0:T(8,128)} %bitcast.237, f32[1024,512]{1,0:T(8,128)S(1)} %bitcast.226, f32[640]{0:T(1024)S(1)} %copy-done.94, s32[1024]{0:T(1024)S(1)} %bitcast.247), kind=kOutput, calls=%fused_computation.25 | convolution fusion | flops 423690240 | bytes 2935296 | tf_op jit(solution)/shard_map/nr,nw->rw/dot_general | solution.py:161
  99.4 1.6 %collective-permute-start.7 = (f32[16,640]{1,0:T(8,128)S(1)}, f32[16,640]{1,0:T(8,128)S(1)}, u32[]{:S(2)}, u32[]{:S(2)}) collective-permute-start(f32[16,640]{1,0:T(8,128)S(1)} %get-tuple-element.65), channel_id=1, source_target_pairs={{3,0},{0,1},{1,2},{2,3},{7,4},{4,5},{5,6},{6,7},{11,8},{8,9},{9,10... | collective-permute-start | bytes 122888 | tf_op jit(solution)/shard_map/ppermute | solution.py:28
  101.1 2.4 %collective-permute-start.6 = (f32[16,640]{1,0:T(8,128)S(1)}, f32[16,640]{1,0:T(8,128)S(1)}, u32[]{:S(2)}, u32[]{:S(2)}) collective-permute-start(f32[16,640]{1,0:T(8,128)S(1)} %get-tuple-element.64), channel_id=1, source_target_pairs={{1,0},{2,1},{3,2},{0,3},{5,4},{6,5},{7,6},{4,7},{9,8},{10,9},{11,1... | collective-permute-start | bytes 122888 | tf_op jit(solution)/shard_map/ppermute | solution.py:28
  103.4 2.0 %collective-permute-done.7 = f32[16,640]{1,0:T(8,128)S(1)} collective-permute-done((f32[16,640]{1,0:T(8,128)S(1)}, f32[16,640]{1,0:T(8,128)S(1)}, u32[]{:S(2)}, u32[]{:S(2)}) %collective-permute-start.7) | collective-permute-done | bytes 40992 | tf_op jit(solution)/shard_map/ppermute | solution.py:28
  107.1 1.6 %collective-permute-start.8 = (f32[64,640]{1,0:T(8,128)S(1)}, f32[64,640]{1,0:T(8,128)S(1)}, u32[]{:S(2)}, u32[]{:S(2)}) collective-permute-start(f32[64,640]{1,0:T(8,128)S(1)} %get-tuple-element.73), channel_id=1, source_target_pairs={{4,0},{0,4},{5,1},{1,5},{6,2},{2,6},{7,3},{3,7},{12,8},{8,12},{13,... | collective-permute-start | bytes 491528 | tf_op jit(solution)/shard_map/ppermute | solution.py:28
  109.9 3.0 %collective-permute-done.8 = f32[64,640]{1,0:T(8,128)S(1)} collective-permute-done((f32[64,640]{1,0:T(8,128)S(1)}, f32[64,640]{1,0:T(8,128)S(1)}, u32[]{:S(2)}, u32[]{:S(2)}) %collective-permute-start.8) | collective-permute-done | bytes 163872 | tf_op jit(solution)/shard_map/ppermute | solution.py:28
  117.9 1.9 %collective-permute-done.11 = f32[16,640]{1,0:T(8,128)S(1)} collective-permute-done((f32[16,640]{1,0:T(8,128)S(1)}, f32[16,640]{1,0:T(8,128)S(1)}, u32[]{:S(2)}, u32[]{:S(2)}) %collective-permute-start.11) | collective-permute-done | bytes 40992 | tf_op jit(solution)/shard_map/ppermute | solution.py:28
  120.4 1.4 %convolution_add_fusion.7 = f32[128,512]{1,0:T(8,128)} fusion(f32[128,512]{1,0:T(8,128)S(1)} %fusion.149, bf16[512,512]{1,0:T(8,128)(2,1)S(1)} %copy-done.2, f32[128,640]{1,0:T(8,128)S(1)} %fusion.44), kind=kOutput, calls=%fused_computation.46 | convolution fusion | flops 402718720 | bytes 1310720 | tf_op jit(solution)/shard_map/dot_general | solution.py:249
  (346 shorter events, 53.5 us)
Async XLA Ops:
  0.6 47.6 %copy-start = (bf16[512,512]{1,0:T(8,128)(2,1)S(1)}, bf16[512,512]{1,0:T(8,128)(2,1)}, u32[]{:S(2)}) copy-start(bf16[512,512]{1,0:T(8,128)(2,1)} %param.28) | copy-start | bytes 1572868
  0.7 8.0 %copy-start.97 = (s32[128]{0:T(128)S(1)}, s32[128]{0:T(128)}, u32[]{:S(2)}) copy-start(s32[128]{0:T(128)} %param.18) | copy-start | bytes 1540
  0.7 8.3 %copy-start.20 = (bf16[128,512]{1,0:T(8,128)(2,1)S(1)}, bf16[128,512]{1,0:T(8,128)(2,1)}, u32[]{:S(2)}) copy-start(bf16[128,512]{1,0:T(8,128)(2,1)} %param.16) | copy-start | bytes 393220
  0.7 8.0 %copy-start.73 = (f32[5,512]{1,0:T(8,128)S(1)}, f32[5,512]{1,0:T(8,128)}, u32[]{:S(2)}) copy-start(f32[5,512]{1,0:T(8,128)} %param.24) | copy-start | bytes 30724
  0.7 8.3 %copy-start.1 = (bf16[512,512]{1,0:T(8,128)(2,1)S(1)}, bf16[512,512]{1,0:T(8,128)(2,1)}, u32[]{:S(2)}) copy-start(bf16[512,512]{1,0:T(8,128)(2,1)} %param.22) | copy-start | bytes 1572868
  1.6 16.6 %copy-start.78 = (s32[16]{0:T(128)}, s32[16]{0:T(128)S(1)}, u32[]{:S(2)}) copy-start(s32[16]{0:T(128)S(1)} %get-tuple-element.113) | copy-start | bytes 196
  1.6 18.6 %copy-start.80 = (s32[16]{0:T(128)}, s32[16]{0:T(128)S(1)}, u32[]{:S(2)}) copy-start(s32[16]{0:T(128)S(1)} %get-tuple-element.110) | copy-start | bytes 196
  2.3 26.5 %copy-start.53 = (f32[3,128]{1,0:T(4,128)}, f32[3,128]{1,0:T(4,128)S(1)}, u32[]{:S(2)}) copy-start(f32[3,128]{1,0:T(4,128)S(1)} %get-tuple-element.108) | copy-start | bytes 4612
  5.1 5.0 %collective-permute-start = (bf16[16,640]{1,0:T(8,128)(2,1)S(1)}, bf16[16,640]{1,0:T(8,128)(2,1)S(1)}, u32[]{:S(2)}, u32[]{:S(2)}) collective-permute-start(bf16[16,640]{1,0:T(8,128)(2,1)S(1)} %convolution_convert_fusion.7), channel_id=1, source_target_pairs={{24,0},{0,8},{8,16},{16,24},{25,1},{1,9},{9,17},{17,25},{26,2},{2,... | collective-permute-start | bytes 61448 | tf_op jit(solution)/shard_map/ppermute | solution.py:28
  5.8 4.3 %collective-permute-start.1 = (bf16[16,640]{1,0:T(8,128)(2,1)S(1)}, bf16[16,640]{1,0:T(8,128)(2,1)S(1)}, u32[]{:S(2)}, u32[]{:S(2)}) collective-permute-start(bf16[16,640]{1,0:T(8,128)(2,1)S(1)} %convolution_convert_fusion.6), channel_id=1, source_target_pairs={{8,0},{16,8},{24,16},{0,24},{9,1},{17,9},{25,17},{1,25},{10,2},{18... | collective-permute-start | bytes 61448 | tf_op jit(solution)/shard_map/ppermute | solution.py:28
  7.8 21.2 %copy-start.99 = (f32[8]{0:T(128)}, f32[8]{0:T(128)S(1)}, u32[]{:S(2)}) copy-start(f32[8]{0:T(128)S(1)} %convert_multiply_fusion) | copy-start | bytes 100
  9.3 16.7 %copy-start.88 = (f32[128]{0:T(128)}, f32[128]{0:T(128)S(1)}, u32[]{:S(2)}) copy-start(f32[128]{0:T(128)S(1)} %compare_convert_fusion) | copy-start | bytes 1540
  9.4 14.8 %copy-start.67 = (s32[8,128]{1,0:T(8,128)}, s32[8,128]{1,0:T(8,128)S(1)}, u32[]{:S(2)}) copy-start(s32[8,128]{1,0:T(8,128)S(1)} %copy.92) | copy-start | bytes 12292
  10.7 5.5 %collective-permute-start.2 = (bf16[64,640]{1,0:T(8,128)(2,1)S(1)}, bf16[64,640]{1,0:T(8,128)(2,1)S(1)}, u32[]{:S(2)}, u32[]{:S(2)}) collective-permute-start(bf16[64,640]{1,0:T(8,128)(2,1)S(1)} %convolution_convert_fusion.3), channel_id=1, source_target_pairs={{4,0},{0,4},{5,1},{1,5},{6,2},{2,6},{7,3},{3,7},{12,8},{8,12},{13,... | collective-permute-start | bytes 245768 | tf_op jit(solution)/shard_map/ppermute | solution.py:28
  13.1 5.1 %collective-permute-start.3 = (bf16[64,640]{1,0:T(8,128)(2,1)S(1)}, bf16[64,640]{1,0:T(8,128)(2,1)S(1)}, u32[]{:S(2)}, u32[]{:S(2)}) collective-permute-start(bf16[64,640]{1,0:T(8,128)(2,1)S(1)} %convolution_convert_fusion.2), channel_id=1, source_target_pairs={{4,0},{0,4},{5,1},{1,5},{6,2},{2,6},{7,3},{3,7},{12,8},{8,12},{13,... | collective-permute-start | bytes 245768 | tf_op jit(solution)/shard_map/ppermute | solution.py:28
  18.4 5.6 %collective-permute-start.4 = (bf16[16,640]{1,0:T(8,128)(2,1)S(1)}, bf16[16,640]{1,0:T(8,128)(2,1)S(1)}, u32[]{:S(2)}, u32[]{:S(2)}) collective-permute-start(bf16[16,640]{1,0:T(8,128)(2,1)S(1)} %convolution_convert_fusion.5), channel_id=1, source_target_pairs={{3,0},{0,1},{1,2},{2,3},{7,4},{4,5},{5,6},{6,7},{11,8},{8,9},{9,10... | collective-permute-start | bytes 61448 | tf_op jit(solution)/shard_map/ppermute | solution.py:28
  20.4 3.8 %collective-permute-start.5 = (bf16[16,640]{1,0:T(8,128)(2,1)S(1)}, bf16[16,640]{1,0:T(8,128)(2,1)S(1)}, u32[]{:S(2)}, u32[]{:S(2)}) collective-permute-start(bf16[16,640]{1,0:T(8,128)(2,1)S(1)} %convolution_convert_fusion.4), channel_id=1, source_target_pairs={{1,0},{2,1},{3,2},{0,3},{5,4},{6,5},{7,6},{4,7},{9,8},{10,9},{11,1... | collective-permute-start | bytes 61448 | tf_op jit(solution)/shard_map/ppermute | solution.py:28
  36.0 8.4 %copy-start.30 = (f32[8,128]{1,0:T(8,128)S(1)}, f32[8,128]{1,0:T(8,128)}, u32[]{:S(2)}) copy-start(f32[8,128]{1,0:T(8,128)} %copy-done.29) | copy-start | bytes 12292
  36.0 8.4 %copy-start.33 = (f32[8,128]{1,0:T(8,128)S(1)}, f32[8,128]{1,0:T(8,128)}, u32[]{:S(2)}) copy-start(f32[8,128]{1,0:T(8,128)} %copy-done.32) | copy-start | bytes 12292
  36.0 8.3 %copy-start.36 = (f32[8,128]{1,0:T(8,128)S(1)}, f32[8,128]{1,0:T(8,128)}, u32[]{:S(2)}) copy-start(f32[8,128]{1,0:T(8,128)} %copy-done.35) | copy-start | bytes 12292
  36.0 8.3 %copy-start.39 = (f32[8,128]{1,0:T(8,128)S(1)}, f32[8,128]{1,0:T(8,128)}, u32[]{:S(2)}) copy-start(f32[8,128]{1,0:T(8,128)} %copy-done.38) | copy-start | bytes 12292
  36.1 9.2 %copy-start.9 = (f32[64,128]{0,1:T(8,128)}, f32[64,128]{0,1:T(8,128)S(1)}, u32[]{:S(2)}) copy-start(f32[64,128]{0,1:T(8,128)S(1)} %get-tuple-element.127) | copy-start | bytes 98308
  37.5 7.8 %copy-start.11 = (f32[64,128]{0,1:T(8,128)}, f32[64,128]{0,1:T(8,128)S(1)}, u32[]{:S(2)}) copy-start(f32[64,128]{0,1:T(8,128)S(1)} %get-tuple-element.125) | copy-start | bytes 98308
  71.7 13.7 %copy-start.17 = (f32[8,8,8,128]{3,2,1,0:T(8,128)S(1)}, f32[8,8,8,128]{3,2,1,0:T(8,128)}, u32[]{:S(2)}) copy-start(f32[8,8,8,128]{3,2,1,0:T(8,128)} %copy.128) | copy-start | bytes 786436
  99.4 6.0 %collective-permute-start.7 = (f32[16,640]{1,0:T(8,128)S(1)}, f32[16,640]{1,0:T(8,128)S(1)}, u32[]{:S(2)}, u32[]{:S(2)}) collective-permute-start(f32[16,640]{1,0:T(8,128)S(1)} %get-tuple-element.65), channel_id=1, source_target_pairs={{3,0},{0,1},{1,2},{2,3},{7,4},{4,5},{5,6},{6,7},{11,8},{8,9},{9,10... | collective-permute-start | bytes 122888 | tf_op jit(solution)/shard_map/ppermute | solution.py:28
  101.1 5.1 %collective-permute-start.6 = (f32[16,640]{1,0:T(8,128)S(1)}, f32[16,640]{1,0:T(8,128)S(1)}, u32[]{:S(2)}, u32[]{:S(2)}) collective-permute-start(f32[16,640]{1,0:T(8,128)S(1)} %get-tuple-element.64), channel_id=1, source_target_pairs={{1,0},{2,1},{3,2},{0,3},{5,4},{6,5},{7,6},{4,7},{9,8},{10,9},{11,1... | collective-permute-start | bytes 122888 | tf_op jit(solution)/shard_map/ppermute | solution.py:28
  107.0 7.8 %copy-start.91 = (s32[64]{0:T(128)S(1)}, s32[64]{0:T(128)}, u32[]{:S(2)}) copy-start(s32[64]{0:T(128)} %copy-done.90) | copy-start | bytes 772
  107.1 5.8 %collective-permute-start.8 = (f32[64,640]{1,0:T(8,128)S(1)}, f32[64,640]{1,0:T(8,128)S(1)}, u32[]{:S(2)}, u32[]{:S(2)}) collective-permute-start(f32[64,640]{1,0:T(8,128)S(1)} %get-tuple-element.73), channel_id=1, source_target_pairs={{4,0},{0,4},{5,1},{1,5},{6,2},{2,6},{7,3},{3,7},{12,8},{8,12},{13,... | collective-permute-start | bytes 491528 | tf_op jit(solution)/shard_map/ppermute | solution.py:28
  109.4 7.8 %copy-start.87 = (s32[16]{0:T(128)S(1)}, s32[16]{0:T(128)}, u32[]{:S(2)}) copy-start(s32[16]{0:T(128)} %copy-done.86) | copy-start | bytes 196
  109.4 5.4 %collective-permute-start.9 = (f32[64,640]{1,0:T(8,128)S(1)}, f32[64,640]{1,0:T(8,128)S(1)}, u32[]{:S(2)}, u32[]{:S(2)}) collective-permute-start(f32[64,640]{1,0:T(8,128)S(1)} %get-tuple-element.72), channel_id=1, source_target_pairs={{4,0},{0,4},{5,1},{1,5},{6,2},{2,6},{7,3},{3,7},{12,8},{8,12},{13,... | collective-permute-start | bytes 491528 | tf_op jit(solution)/shard_map/ppermute | solution.py:28
  115.5 1.7 %collective-permute-start.10 = (f32[16,640]{1,0:T(8,128)S(1)}, f32[16,640]{1,0:T(8,128)S(1)}, u32[]{:S(2)}, u32[]{:S(2)}) collective-permute-start(f32[16,640]{1,0:T(8,128)S(1)} %get-tuple-element.75), channel_id=1, source_target_pairs={{8,0},{16,8},{24,16},{0,24},{9,1},{17,9},{25,17},{1,25},{10,2},{18... | collective-permute-start | bytes 122888 | tf_op jit(solution)/shard_map/ppermute | solution.py:28
  116.3 3.4 %collective-permute-start.11 = (f32[16,640]{1,0:T(8,128)S(1)}, f32[16,640]{1,0:T(8,128)S(1)}, u32[]{:S(2)}, u32[]{:S(2)}) collective-permute-start(f32[16,640]{1,0:T(8,128)S(1)} %get-tuple-element.74), channel_id=1, source_target_pairs={{24,0},{0,8},{8,16},{16,24},{25,1},{1,9},{9,17},{17,25},{26,2},{2,... | collective-permute-start | bytes 122888 | tf_op jit(solution)/shard_map/ppermute | solution.py:28
  (87 other events, 262.3 us)

commit v3 on v2

--- a/solution.py
+++ b/solution.py
@@ -29,13 +29,12 @@
 
 
 def by_order(values):
-    count = values.shape[1]
-    pairs = values.shape[2]
+    rest = values.shape[1:]
     return jnp.concatenate(
         [
             values[0:1],
-            jnp.broadcast_to(values[1:2], (3, count, pairs)),
-            jnp.broadcast_to(values[2:3], (5, count, pairs)),
+            jnp.broadcast_to(values[1:2], (3,) + rest),
+            jnp.broadcast_to(values[2:3], (5,) + rest),
         ],
         axis=0,
     )
@@ -80,25 +79,25 @@
     root3 = math.sqrt(3.0)
     root15 = math.sqrt(15.0)
     root5 = math.sqrt(5.0)
-    harmonics = [
-        [jnp.ones_like(unit_x)],
-        [root3 * unit_x, root3 * unit_y, root3 * unit_z],
+    harmonics = jnp.stack(
         [
+            jnp.ones_like(unit_x),
+            root3 * unit_x,
+            root3 * unit_y,
+            root3 * unit_z,
             root15 * unit_x * unit_y,
             root15 * unit_y * unit_z,
             0.5 * root5 * (2.0 * unit_z * unit_z - unit_x * unit_x - unit_y * unit_y),
             root15 * unit_x * unit_z,
             0.5 * root15 * (unit_x * unit_x - unit_y * unit_y),
         ],
-    ]
-    scalars = []
-    for order in range(3):
-        total = 0.0
-        for harmonic in harmonics[order]:
-            environment = (weights[order] * harmonic[None]).sum(axis=1) / math.sqrt(K)
-            total = total + harmonic[None] * environment[:, None, :]
-        scalars.append(amplitude[order] * total)
-    scalars = jnp.stack(scalars, axis=0).reshape(3 * CH, K * atoms).astype(jnp.bfloat16)
+        axis=0,
+    )
+    gathered = by_order(weights) * harmonics[:, None]
+    environment = gathered.sum(axis=2) / math.sqrt(K)
+    products = by_order(amplitude) * harmonics[:, None] * environment[:, :, None, :]
+    scalars = jnp.stack([products[0], products[1:4].sum(axis=0), products[4:9].sum(axis=0)], axis=0)
+    scalars = scalars.reshape(3 * CH, K * atoms).astype(jnp.bfloat16)
     flat_low = hidden_low.reshape(K * atoms, width)
     update = jax.nn.silu(
         jnp.dot(flat_low, update_proj, preferred_element_type=jnp.float32)

time: 124 us -> 80.3 us (0.65)
  local copies, waits for them, and re-layouts: 32.2 us -> 13.4 us
  other arithmetic: 25.6 us -> 6.91 us
  matrix products: 31 us -> 26.5 us
    div x18 -> x0, local copies, waits for them, and re-layouts: 14 us -> none  [pair_energy(): environment = (weights[order] * harmonic[None]).sum(axis=1) / math.sqrt(K)]
    div x14 -> x2, other arithmetic: 6.39 us -> 0.06 us  [pair_energy(): environment = gathered.sum(axis=2) / math.sqrt(K)]
    another operation x5 -> x0, local copies, waits for them, and re-layouts: 5.03 us -> none  [pair_energy(): jnp.stack(scalars, axis=0).reshape(3 * CH, K * atoms).astype(jnp.bfloat16)]
    slice x0 -> x8, local copies, waits for them, and re-layouts: none -> 4.83 us  [the longest x3 4.02 us: by_order(): values[0:1]]
    mul x5 -> x1, other arithmetic: 4.57 us -> 0.28 us  [pair_energy(): by_order(amplitude) * harmonics[:, None] * environment[:, :, None, :]]
    reduce_sum x4 -> x9, other arithmetic: 8.87 us -> 4.94 us  [the longest x1 3.59 us: pair_energy(): by_order(amplitude) * harmonics[:, None] * environment[:, :, None, :]]
    unnamed x221 -> x47, local copies, waits for them, and re-layouts: 7.86 us -> 4.45 us
    another operation x4 -> x3, other arithmetic: 3.83 us -> 0.82 us  [the longest x3 3.06 us: pair_energy(): jnp.stack(scalars, axis=0).reshape(3 * CH, K * atoms).astype(jnp.bfloat16)]
  transfers between devices with their start and end apart: 12 -> 12, of which waited for: 9 -> 9; matrix products, arithmetic and copies ran while one was open for 4% -> 6% of each run, Pallas kernels for 0% -> 0%
where the time goes in v3:
time: 80.3 us; the launch traced here: 79.8 us
  matrix products  26.5 us (33%)
  starting transfers between devices  15.4 us (19%)
  waiting for transfers between devices  15.4 us (19%)
  local copies, waits for them, and re-layouts  13.4 us (17%)
  other arithmetic  6.91 us (9%)
  between operations  2.18 us (3%)
    ppermute x12, waiting for transfers between devices, passed_along(): return lax.ppermute(block, axis, route)  15.4 us
    ppermute x12, starting transfers between devices, passed_along(): return lax.ppermute(block, axis, route)  15.4 us
    dot_general x2, matrix products, pair_energy(): jnp.einsum('nka,nh->kah', basis, basis_proj.astype(jnp.float32), precisio...  5.73 us
    unnamed x47, local copies, waits for them, and re-layouts  4.45 us
    slice x3, local copies, waits for them, and re-layouts, by_order(): values[0:1]  4.02 us
    reduce_sum x1, other arithmetic, pair_energy(): by_order(amplitude) * harmonics[:, None] * environment[:, :, None, :]  3.59 us
    dot_general x7, matrix products, spread(): jnp.einsum('nr,nw->rw', onehot, low, preferred_element_type=jnp.float32)  3.06 us
    dot_general x7, matrix products, spread(): jnp.einsum('nr,nw->rw', onehot, high, preferred_element_type=jnp.float32)  3.04 us
  transfers between devices with their start and end apart: 12, of which 9 were waited for; matrix products, arithmetic and copies ran while one was open for 6% of the time, Pallas kernels for 0%

profile of v3, /device:TPU:0, one launch (start us, length us, event | category | flops | bytes accessed | tf_op | source)
XLA Modules:
  0.0 79.8 jit_solution(15431588440595919137)
XLA Ops:
  2.5 1.0 %fusion.64 = f32[128,512]{1,0:T(8,128)S(1)} fusion(f32[5,512]{1,0:T(8,128)} %param.25, s32[128]{0:T(128)} %param.18), kind=kOutput, calls=%fused_computation.128 | convolution fusion | flops 3932800 | bytes 272896 | tf_op jit(solution)/shard_map/dot_general | solution.py:148
  3.5 1.3 %fusion.42 = bf16[128,512]{1,0:T(8,128)(2,1)S(1)} fusion(f32[128,512]{1,0:T(8,128)S(1)} %fusion.64, bf16[128,512]{1,0:T(8,128)(2,1)} %param.16, bf16[512,512]{1,0:T(8,128)(2,1)} %param.23), kind=kOutput, calls=%fused_computation.68 | convolution fusion | flops 67239936 | bytes 1048576 | tf_op jit(solution)/shard_map/dot_general | solution.py:152
  5.8 1.9 %collective-permute-start.1 = (bf16[16,640]{1,0:T(8,128)(2,1)S(1)}, bf16[16,640]{1,0:T(8,128)(2,1)S(1)}, u32[]{:S(2)}, u32[]{:S(2)}) collective-permute-start(bf16[16,640]{1,0:T(8,128)(2,1)S(1)} %convolution_convert_fusion.6), channel_id=1, source_target_pairs={{8,0},{16,8},{24,16},{0,24},{9,1},{17,9},{25,17},{1,25},{10,2},{18... | collective-permute-start | bytes 61448 | tf_op jit(solution)/shard_map/ppermute | solution.py:28
  10.0 2.4 %collective-permute-start.2 = (bf16[64,640]{1,0:T(8,128)(2,1)S(1)}, bf16[64,640]{1,0:T(8,128)(2,1)S(1)}, u32[]{:S(2)}, u32[]{:S(2)}) collective-permute-start(bf16[64,640]{1,0:T(8,128)(2,1)S(1)} %convolution_convert_fusion.3), channel_id=1, source_target_pairs={{4,0},{0,4},{5,1},{1,5},{6,2},{2,6},{7,3},{3,7},{12,8},{8,12},{13,... | collective-permute-start | bytes 245768 | tf_op jit(solution)/shard_map/ppermute | solution.py:28
  12.4 2.4 %collective-permute-done.2 = bf16[64,640]{1,0:T(8,128)(2,1)S(1)} collective-permute-done((bf16[64,640]{1,0:T(8,128)(2,1)S(1)}, bf16[64,640]{1,0:T(8,128)(2,1)S(1)}, u32[]{:S(2)}, u32[]{:S(2)}) %collective-permute-start.2) | collective-permute-done | bytes 81952 | tf_op jit(solution)/shard_map/ppermute | solution.py:28
  14.9 2.7 %collective-permute-done.3 = bf16[64,640]{1,0:T(8,128)(2,1)S(1)} collective-permute-done((bf16[64,640]{1,0:T(8,128)(2,1)S(1)}, bf16[64,640]{1,0:T(8,128)(2,1)S(1)}, u32[]{:S(2)}, u32[]{:S(2)}) %collective-permute-start.3) | collective-permute-done | bytes 81952 | tf_op jit(solution)/shard_map/ppermute | solution.py:28
  17.9 1.7 %collective-permute-start.4 = (bf16[16,640]{1,0:T(8,128)(2,1)S(1)}, bf16[16,640]{1,0:T(8,128)(2,1)S(1)}, u32[]{:S(2)}, u32[]{:S(2)}) collective-permute-start(bf16[16,640]{1,0:T(8,128)(2,1)S(1)} %convolution_convert_fusion.5), channel_id=1, source_target_pairs={{3,0},{0,1},{1,2},{2,3},{7,4},{4,5},{5,6},{6,7},{11,8},{8,9},{9,10... | collective-permute-start | bytes 61448 | tf_op jit(solution)/shard_map/ppermute | solution.py:28
  19.8 2.2 %collective-permute-start.5 = (bf16[16,640]{1,0:T(8,128)(2,1)S(1)}, bf16[16,640]{1,0:T(8,128)(2,1)S(1)}, u32[]{:S(2)}, u32[]{:S(2)}) collective-permute-start(bf16[16,640]{1,0:T(8,128)(2,1)S(1)} %convolution_convert_fusion.4), channel_id=1, source_target_pairs={{1,0},{2,1},{3,2},{0,3},{5,4},{6,5},{7,6},{4,7},{9,8},{10,9},{11,1... | collective-permute-start | bytes 61448 | tf_op jit(solution)/shard_map/ppermute | solution.py:28
  22.0 1.7 %collective-permute-done.4 = bf16[16,640]{1,0:T(8,128)(2,1)S(1)} collective-permute-done((bf16[16,640]{1,0:T(8,128)(2,1)S(1)}, bf16[16,640]{1,0:T(8,128)(2,1)S(1)}, u32[]{:S(2)}, u32[]{:S(2)}) %collective-permute-start.4) | collective-permute-done | bytes 20512 | tf_op jit(solution)/shard_map/ppermute | solution.py:28
  23.9 1.1 %fusion.23 = f32[1024,640]{0,1:T(8,128)S(1)} fusion(bf16[320,640]{1,0:T(8,128)(2,1)S(1)} %constant_dynamic-update-slice_fusion.3, s32[1024]{0:T(1024)S(1)} %bitcast.176), kind=kOutput, calls=%fused_computation.42 | convolution fusion | flops 419758080 | bytes 3035136 | tf_op jit(solution)/shard_map/dot_general | solution.py:197
  25.3 1.8 %copy.74 = f32[1024,512]{1,0:T(8,128)} copy(f32[1024,512]{0,1:T(8,128)S(1)} %slice.168) | data formatting | bytes 4194304 | tf_op jit(solution)/shard_map/jvp()/reshape | solution.py:69
  27.2 4.6 %multiply_convert_fusion = (bf16[8,128,512]{2,1,0:T(8,128)(2,1)S(1)}, f32[8,128,512]{2,1,0:T(8,128)}) fusion(f32[8,128]{1,0:T(8,128)S(1)} %get-tuple-element.57, bf16[8,512]{1,0:T(8,128)(2,1)S(1)} %copy-done.12, f32[8,128]{1,0:T(8,128)S(1)} %get-tuple-element.56, f32[8,128]{1,0:T(8,128)S(1)} %get-tuple-element.60, f32[8]{0:T(128)S(1)} %convert_multiply_fusion, ...), kind=kOutput, calls=%fused_computation.34 | convolution fusion | flops 54542336 | bytes 5525536 | tf_op jit(solution)/shard_map/jvp(nka,nh->kah)/dot_general | solution.py:65
  31.8 1.0 %copy-done.4 = bf16[8,128,512]{2,1,0:T(8,128)(2,1)} copy-done((bf16[8,128,512]{2,1,0:T(8,128)(2,1)}, bf16[8,128,512]{2,1,0:T(8,128)(2,1)S(1)}, u32[]{:S(2)}) %copy-start.4) | copy-done | bytes 1048600
  33.5 1.5 %slice_bitcast_fusion = (f32[1,64,8,128]{1,3,2,0:T(8,128)}, f32[64,8,128]{0,2,1:T(8,128)S(1)}, f32[64,8,128]{0,2,1:T(8,128)S(1)}, f32[64,8,128]{0,2,1:T(8,128)S(...) fusion(f32[384,8,128]{0,2,1:T(8,128)S(1)} %convolution_bitcast_fusion), kind=kLoop, calls=%fused_computation.91 | loop fusion | bytes 3145728 | tf_op jit(solution)/shard_map/jvp()/slice | solution.py:35
  35.1 1.2 %copy.69 = f32[1,64,8,128]{3,2,1,0:T(8,128)S(1)} copy(f32[1,64,8,128]{1,3,2,0:T(8,128)} %get-tuple-element.29) | data formatting | bytes 524288 | tf_op jit(solution)/shard_map/jvp()/slice | solution.py:35
  36.3 1.2 %copy.66 = f32[1,64,8,128]{3,2,1,0:T(8,128)S(1)} copy(f32[1,64,8,128]{1,3,2,0:T(8,128)} %get-tuple-element.34) | data formatting | bytes 524288 | tf_op jit(solution)/shard_map/jvp()/slice | solution.py:35
  41.2 1.0 %fusion.16 = (f32[1024,512]{1,0:T(8,128)S(1)}, f32[1024,512]{1,0:T(8,128)S(1)}) fusion(f32[1024,512]{1,0:T(8,128)S(1)} %fusion.53, bf16[1024,512]{1,0:T(8,128)(2,1)S(1)} %bitcast.157, bf16[512,512]{1,0:T(8,128)(2,1)S(1)} %copy-done), kind=kOutput, calls=%fused_computation.29 | convolution fusion | flops 539492352 | bytes 7864320 | tf_op jit(solution)/shard_map/jvp()/dot_general | solution.py:103
  42.2 1.1 %fusion.41 = f32[192,1024]{1,0:T(8,128)S(1)} fusion(bf16[192,512]{1,0:T(8,128)(2,1)S(1)} %copy-done.9, f32[1024,512]{1,0:T(8,128)S(1)} %get-tuple-element.75, f32[512]{0:T(512)S(1)} %copy-done.16, f32[1024]{0:T(1024)S(1)} %get-tuple-element.59), kind=kOutput, calls=%fused_computation.59 | convolution fusion | flops 206962688 | bytes 3086336 | tf_op jit(solution)/shard_map/transpose(jvp(qp,qh->ph))/dot_general | solution.py:104
  43.3 1.1 %convolution_convert_fusion = bf16[1024,512]{1,0:T(8,128)(2,1)S(1)} fusion(bf16[512,512]{1,0:T(8,128)(2,1)S(1)} %copy-done, f32[1024,512]{1,0:T(8,128)S(1)} %get-tuple-element.75, f32[512]{0:T(512)S(1)} %copy-done.16, f32[1024]{0:T(1024)S(1)} %get-tuple-element.59), kind=kOutput, calls=%fused_computation.43 | convolution fusion | flops 542638080 | bytes 3676160 | tf_op jit(solution)/shard_map/transpose(jvp())/dot_general | solution.py:103
  44.8 3.6 %fusion.4 = (f32[9,64,128]{2,1,0:T(8,128)S(1)}, f32[9,8,128]{2,1,0:T(8,128)S(1)}, f32[9,64,8,128]{3,2,1,0:T(8,128)S(1)}) fusion(f32[5,64,8,128]{3,2,1,0:T(8,128)S(1)} %broadcast_in_dim.138, f32[3,64,8,128]{3,2,1,0:T(8,128)S(1)} %broadcast_in_dim.137, f32[1,64,8,128]{3,2,1,0:T(8,128)S(1)} %copy.66, f32[1,64,8,128]{3,2,1,0:T(8,128)S(1)} %bitcast.158, ...), kind=kLoop, calls=%fused_computation.11 | loop fusion | flops 6405120 | bytes 7741440 | tf_op jit(solution)/shard_map/transpose(jvp())/reduce_sum | solution.py:98
  49.8 1.2 %copy-done.18 = f32[8,128,512]{2,1,0:T(8,128)S(1)} copy-done((f32[8,128,512]{2,1,0:T(8,128)S(1)}, f32[8,128,512]{2,1,0:T(8,128)}, u32[]{:S(2)}) %copy-start.18) | copy-done | bytes 2097176
  51.2 2.3 %fusion.146 = (f32[128,512]{1,0:T(8,128)S(1)}, f32[8,128,512]{2,1,0:T(8,128)S(1)}, f32[8,128]{1,0:T(8,128)S(1)}, f32[8,128]{1,0:T(8,128)S(1)}) fusion(f32[8,128,512]{2,1,0:T(8,128)S(1)} %copy-done.18, f32[512]{0:T(512)S(1)} %copy-done.16, f32[8,128]{1,0:T(8,128)S(1)} %get-tuple-element.57, f32[8,128,512]{2,1,0:T(8,128)S(1)} %bitcast.179, ...), kind=kOutput, calls=%fused_computation.285 | convolution fusion | flops 414119936 | bytes 8796160 | tf_op jit(solution)/shard_map/transpose(jvp(kah,hq->qka))/dot_general | solution.py:73
  53.4 1.1 %fusion.75 = (f32[8,128]{1,0:T(8,128)S(1)}, f32[8,128]{1,0:T(8,128)S(1)}) fusion(f32[8,128]{1,0:T(8,128)S(1)} %get-tuple-element.56, f32[8,128]{1,0:T(8,128)S(1)} %get-tuple-element.60, f32[8]{0:T(128)S(1)} %convert_multiply_fusion, f32[8,128,512]{2,1,0:T(8,128)S(1)} %get-tuple-element.19, bf16[8,512]{1,0:T(8,128)(2,1)S(1)} %copy-done.12), kind=kOutput, calls=%fused_computation.161 | convolution fusion | flops 50386944 | bytes 2121760 | tf_op jit(solution)/shard_map/transpose(jvp(nka,nh->kah))/dot_general | solution.py:65
  55.0 1.0 %fusion.21 = f32[320,640]{1,0:T(8,128)S(1)} fusion(f32[1024,3]{1,0:T(8,128)S(1)} %bitcast.165, f32[1024,512]{1,0:T(8,128)S(1)} %bitcast.153, f32[640]{0:T(1024)S(1)} %pad.63.clone, s32[1024]{0:T(1024)S(1)} %bitcast.177), kind=kOutput, calls=%fused_computation.40 | convolution fusion | flops 423690240 | bytes 2935296 | tf_op jit(solution)/shard_map/nr,nw->rw/dot_general | solution.py:160
  57.0 1.4 %collective-permute-start.7 = (f32[16,640]{1,0:T(8,128)S(1)}, f32[16,640]{1,0:T(8,128)S(1)}, u32[]{:S(2)}, u32[]{:S(2)}) collective-permute-start(f32[16,640]{1,0:T(8,128)S(1)} %get-tuple-element.36), channel_id=1, source_target_pairs={{3,0},{0,1},{1,2},{2,3},{7,4},{4,5},{5,6},{6,7},{11,8},{8,9},{9,10... | collective-permute-start | bytes 122888 | tf_op jit(solution)/shard_map/ppermute | solution.py:28
  58.4 2.5 %collective-permute-start.6 = (f32[16,640]{1,0:T(8,128)S(1)}, f32[16,640]{1,0:T(8,128)S(1)}, u32[]{:S(2)}, u32[]{:S(2)}) collective-permute-start(f32[16,640]{1,0:T(8,128)S(1)} %get-tuple-element.35), channel_id=1, source_target_pairs={{1,0},{2,1},{3,2},{0,3},{5,4},{6,5},{7,6},{4,7},{9,8},{10,9},{11,1... | collective-permute-start | bytes 122888 | tf_op jit(solution)/shard_map/ppermute | solution.py:28
  60.9 2.0 %collective-permute-done.7 = f32[16,640]{1,0:T(8,128)S(1)} collective-permute-done((f32[16,640]{1,0:T(8,128)S(1)}, f32[16,640]{1,0:T(8,128)S(1)}, u32[]{:S(2)}, u32[]{:S(2)}) %collective-permute-start.7) | collective-permute-done | bytes 40992 | tf_op jit(solution)/shard_map/ppermute | solution.py:28
  64.4 1.5 %collective-permute-start.8 = (f32[64,640]{1,0:T(8,128)S(1)}, f32[64,640]{1,0:T(8,128)S(1)}, u32[]{:S(2)}, u32[]{:S(2)}) collective-permute-start(f32[64,640]{1,0:T(8,128)S(1)} %get-tuple-element.41), channel_id=1, source_target_pairs={{4,0},{0,4},{5,1},{1,5},{6,2},{2,6},{7,3},{3,7},{12,8},{8,12},{13,... | collective-permute-start | bytes 491528 | tf_op jit(solution)/shard_map/ppermute | solution.py:28
  67.2 3.2 %collective-permute-done.8 = f32[64,640]{1,0:T(8,128)S(1)} collective-permute-done((f32[64,640]{1,0:T(8,128)S(1)}, f32[64,640]{1,0:T(8,128)S(1)}, u32[]{:S(2)}, u32[]{:S(2)}) %collective-permute-start.8) | collective-permute-done | bytes 163872 | tf_op jit(solution)/shard_map/ppermute | solution.py:28
  71.1 1.1 %collective-permute-done.9 = f32[64,640]{1,0:T(8,128)S(1)} collective-permute-done((f32[64,640]{1,0:T(8,128)S(1)}, f32[64,640]{1,0:T(8,128)S(1)}, u32[]{:S(2)}, u32[]{:S(2)}) %collective-permute-start.9) | collective-permute-done | bytes 163872 | tf_op jit(solution)/shard_map/ppermute | solution.py:28
  75.3 1.9 %collective-permute-done.11 = f32[16,640]{1,0:T(8,128)S(1)} collective-permute-done((f32[16,640]{1,0:T(8,128)S(1)}, f32[16,640]{1,0:T(8,128)S(1)}, u32[]{:S(2)}, u32[]{:S(2)}) %collective-permute-start.11) | collective-permute-done | bytes 40992 | tf_op jit(solution)/shard_map/ppermute | solution.py:28
  77.8 1.4 %convolution_add_fusion.7 = f32[128,512]{1,0:T(8,128)} fusion(f32[128,512]{1,0:T(8,128)S(1)} %fusion.152, bf16[512,512]{1,0:T(8,128)(2,1)S(1)} %copy-done.3, f32[128,640]{1,0:T(8,128)S(1)} %fusion.58), kind=kOutput, calls=%fused_computation.65 | convolution fusion | flops 402718720 | bytes 1310720 | tf_op jit(solution)/shard_map/dot_general | solution.py:248
  (156 shorter events, 20.4 us)
Async XLA Ops:
  0.6 40.5 %copy-start = (bf16[512,512]{1,0:T(8,128)(2,1)S(1)}, bf16[512,512]{1,0:T(8,128)(2,1)}, u32[]{:S(2)}) copy-start(bf16[512,512]{1,0:T(8,128)(2,1)} %param.28) | copy-start | bytes 1572868
  0.6 7.1 %copy-start.11 = (s32[1,192]{1,0:T(1,128)S(1)}, s32[1,192]{1,0:T(1,128)}, u32[]{:S(2)}) copy-start(s32[1,192]{1,0:T(1,128)} %param.19) | copy-start | bytes 2308
  0.7 7.9 %copy-start.14 = (s32[128]{0:T(128)S(1)}, s32[128]{0:T(128)}, u32[]{:S(2)}) copy-start(s32[128]{0:T(128)} %param.18) | copy-start | bytes 1540
  0.7 8.3 %copy-start.6 = (bf16[128,512]{1,0:T(8,128)(2,1)S(1)}, bf16[128,512]{1,0:T(8,128)(2,1)}, u32[]{:S(2)}) copy-start(bf16[128,512]{1,0:T(8,128)(2,1)} %param.16) | copy-start | bytes 393220
  0.7 7.9 %copy-start.10 = (f32[5,512]{1,0:T(8,128)S(1)}, f32[5,512]{1,0:T(8,128)}, u32[]{:S(2)}) copy-start(f32[5,512]{1,0:T(8,128)} %param.24) | copy-start | bytes 30724
  0.7 8.3 %copy-start.1 = (bf16[512,512]{1,0:T(8,128)(2,1)S(1)}, bf16[512,512]{1,0:T(8,128)(2,1)}, u32[]{:S(2)}) copy-start(bf16[512,512]{1,0:T(8,128)(2,1)} %param.22) | copy-start | bytes 1572868
  2.5 6.7 %copy-start.13 = (s32[1024]{0:T(1024)S(1)}, s32[1024]{0:T(1024)}, u32[]{:S(2)}) copy-start(s32[1024]{0:T(1024)} %param.20) | copy-start | bytes 12292
  5.1 4.3 %collective-permute-start = (bf16[16,640]{1,0:T(8,128)(2,1)S(1)}, bf16[16,640]{1,0:T(8,128)(2,1)S(1)}, u32[]{:S(2)}, u32[]{:S(2)}) collective-permute-start(bf16[16,640]{1,0:T(8,128)(2,1)S(1)} %convolution_convert_fusion.7), channel_id=1, source_target_pairs={{24,0},{0,8},{8,16},{16,24},{25,1},{1,9},{9,17},{17,25},{26,2},{2,... | collective-permute-start | bytes 61448 | tf_op jit(solution)/shard_map/ppermute | solution.py:28
  5.8 3.7 %collective-permute-start.1 = (bf16[16,640]{1,0:T(8,128)(2,1)S(1)}, bf16[16,640]{1,0:T(8,128)(2,1)S(1)}, u32[]{:S(2)}, u32[]{:S(2)}) collective-permute-start(bf16[16,640]{1,0:T(8,128)(2,1)S(1)} %convolution_convert_fusion.6), channel_id=1, source_target_pairs={{8,0},{16,8},{24,16},{0,24},{9,1},{17,9},{25,17},{1,25},{10,2},{18... | collective-permute-start | bytes 61448 | tf_op jit(solution)/shard_map/ppermute | solution.py:28
  10.0 4.9 %collective-permute-start.2 = (bf16[64,640]{1,0:T(8,128)(2,1)S(1)}, bf16[64,640]{1,0:T(8,128)(2,1)S(1)}, u32[]{:S(2)}, u32[]{:S(2)}) collective-permute-start(bf16[64,640]{1,0:T(8,128)(2,1)S(1)} %convolution_convert_fusion.3), channel_id=1, source_target_pairs={{4,0},{0,4},{5,1},{1,5},{6,2},{2,6},{7,3},{3,7},{12,8},{8,12},{13,... | collective-permute-start | bytes 245768 | tf_op jit(solution)/shard_map/ppermute | solution.py:28
  12.4 5.3 %collective-permute-start.3 = (bf16[64,640]{1,0:T(8,128)(2,1)S(1)}, bf16[64,640]{1,0:T(8,128)(2,1)S(1)}, u32[]{:S(2)}, u32[]{:S(2)}) collective-permute-start(bf16[64,640]{1,0:T(8,128)(2,1)S(1)} %convolution_convert_fusion.2), channel_id=1, source_target_pairs={{4,0},{0,4},{5,1},{1,5},{6,2},{2,6},{7,3},{3,7},{12,8},{8,12},{13,... | collective-permute-start | bytes 245768 | tf_op jit(solution)/shard_map/ppermute | solution.py:28
  17.9 5.8 %collective-permute-start.4 = (bf16[16,640]{1,0:T(8,128)(2,1)S(1)}, bf16[16,640]{1,0:T(8,128)(2,1)S(1)}, u32[]{:S(2)}, u32[]{:S(2)}) collective-permute-start(bf16[16,640]{1,0:T(8,128)(2,1)S(1)} %convolution_convert_fusion.5), channel_id=1, source_target_pairs={{3,0},{0,1},{1,2},{2,3},{7,4},{4,5},{5,6},{6,7},{11,8},{8,9},{9,10... | collective-permute-start | bytes 61448 | tf_op jit(solution)/shard_map/ppermute | solution.py:28
  19.8 4.0 %collective-permute-start.5 = (bf16[16,640]{1,0:T(8,128)(2,1)S(1)}, bf16[16,640]{1,0:T(8,128)(2,1)S(1)}, u32[]{:S(2)}, u32[]{:S(2)}) collective-permute-start(bf16[16,640]{1,0:T(8,128)(2,1)S(1)} %convolution_convert_fusion.4), channel_id=1, source_target_pairs={{1,0},{2,1},{3,2},{0,3},{5,4},{6,5},{7,6},{4,7},{9,8},{10,9},{11,1... | collective-permute-start | bytes 61448 | tf_op jit(solution)/shard_map/ppermute | solution.py:28
  25.2 1.9 %copy-start.12 = (bf16[8,512]{1,0:T(8,128)(2,1)S(1)}, bf16[8,512]{1,0:T(8,128)(2,1)}, u32[]{:S(2)}) copy-start(bf16[8,512]{1,0:T(8,128)(2,1)} %param.26) | copy-start | bytes 24580
  27.2 5.6 %copy-start.7 = (bf16[512,384]{1,0:T(8,128)(2,1)S(1)}, bf16[512,384]{1,0:T(8,128)(2,1)}, u32[]{:S(2)}) copy-start(bf16[512,384]{1,0:T(8,128)(2,1)} %param.27) | copy-start | bytes 1179652
  31.8 1.0 %copy-start.4 = (bf16[8,128,512]{2,1,0:T(8,128)(2,1)}, bf16[8,128,512]{2,1,0:T(8,128)(2,1)S(1)}, u32[]{:S(2)}) copy-start(bf16[8,128,512]{2,1,0:T(8,128)(2,1)S(1)} %get-tuple-element.72) | copy-start | bytes 3145732
  39.8 0.9 %copy-start.9 = (bf16[192,512]{1,0:T(8,128)(2,1)S(1)}, bf16[192,512]{1,0:T(8,128)(2,1)}, u32[]{:S(2)}) copy-start(bf16[192,512]{1,0:T(8,128)(2,1)} %param.29) | copy-start | bytes 589828
  39.9 1.3 %copy-start.5 = (bf16[8,128,512]{2,1,0:T(8,128)(2,1)S(1)}, bf16[8,128,512]{2,1,0:T(8,128)(2,1)}, u32[]{:S(2)}) copy-start(bf16[8,128,512]{2,1,0:T(8,128)(2,1)} %copy-done.4) | copy-start | bytes 3145732
  41.2 1.0 %copy-start.16 = (f32[512]{0:T(512)S(1)}, f32[512]{0:T(512)}, u32[]{:S(2)}) copy-start(f32[512]{0:T(512)} %param.30) | copy-start | bytes 6148
  48.8 0.7 copy-start.15
  49.5 1.6 %copy-start.18 = (f32[8,128,512]{2,1,0:T(8,128)S(1)}, f32[8,128,512]{2,1,0:T(8,128)}, u32[]{:S(2)}) copy-start(f32[8,128,512]{2,1,0:T(8,128)} %get-tuple-element.73) | copy-start | bytes 6291460
  49.7 1.4 %copy-start.8 = (bf16[512,384]{1,0:T(8,128)(2,1)S(1)}, bf16[512,384]{1,0:T(8,128)(2,1)}, u32[]{:S(2)}) copy-start(bf16[512,384]{1,0:T(8,128)(2,1)} %param.27) | copy-start | bytes 1179652
  57.0 5.9 %collective-permute-start.7 = (f32[16,640]{1,0:T(8,128)S(1)}, f32[16,640]{1,0:T(8,128)S(1)}, u32[]{:S(2)}, u32[]{:S(2)}) collective-permute-start(f32[16,640]{1,0:T(8,128)S(1)} %get-tuple-element.36), channel_id=1, source_target_pairs={{3,0},{0,1},{1,2},{2,3},{7,4},{4,5},{5,6},{6,7},{11,8},{8,9},{9,10... | collective-permute-start | bytes 122888 | tf_op jit(solution)/shard_map/ppermute | solution.py:28
  58.4 5.2 %collective-permute-start.6 = (f32[16,640]{1,0:T(8,128)S(1)}, f32[16,640]{1,0:T(8,128)S(1)}, u32[]{:S(2)}, u32[]{:S(2)}) collective-permute-start(f32[16,640]{1,0:T(8,128)S(1)} %get-tuple-element.35), channel_id=1, source_target_pairs={{1,0},{2,1},{3,2},{0,3},{5,4},{6,5},{7,6},{4,7},{9,8},{10,9},{11,1... | collective-permute-start | bytes 122888 | tf_op jit(solution)/shard_map/ppermute | solution.py:28
  63.6 2.3 %copy-start.2 = (bf16[512,512]{1,0:T(8,128)(2,1)S(1)}, bf16[512,512]{1,0:T(8,128)(2,1)}, u32[]{:S(2)}) copy-start(bf16[512,512]{1,0:T(8,128)(2,1)} %param.22) | copy-start | bytes 1572868
  64.4 6.0 %collective-permute-start.8 = (f32[64,640]{1,0:T(8,128)S(1)}, f32[64,640]{1,0:T(8,128)S(1)}, u32[]{:S(2)}, u32[]{:S(2)}) collective-permute-start(f32[64,640]{1,0:T(8,128)S(1)} %get-tuple-element.41), channel_id=1, source_target_pairs={{4,0},{0,4},{5,1},{1,5},{6,2},{2,6},{7,3},{3,7},{12,8},{8,12},{13,... | collective-permute-start | bytes 491528 | tf_op jit(solution)/shard_map/ppermute | solution.py:28
  66.6 6.4 %copy-start.17 = (f32[5]{0:T(128)S(1)}, f32[5]{0:T(128)}, u32[]{:S(2)}) copy-start(f32[5]{0:T(128)} %param.31) | copy-start | bytes 64
  66.6 5.6 %collective-permute-start.9 = (f32[64,640]{1,0:T(8,128)S(1)}, f32[64,640]{1,0:T(8,128)S(1)}, u32[]{:S(2)}, u32[]{:S(2)}) collective-permute-start(f32[64,640]{1,0:T(8,128)S(1)} %get-tuple-element.40), channel_id=1, source_target_pairs={{4,0},{0,4},{5,1},{1,5},{6,2},{2,6},{7,3},{3,7},{12,8},{8,12},{13,... | collective-permute-start | bytes 491528 | tf_op jit(solution)/shard_map/ppermute | solution.py:28
  72.5 5.3 %copy-start.3 = (bf16[512,512]{1,0:T(8,128)(2,1)S(1)}, bf16[512,512]{1,0:T(8,128)(2,1)}, u32[]{:S(2)}) copy-start(bf16[512,512]{1,0:T(8,128)(2,1)} %param.23) | copy-start | bytes 1572868
  72.9 1.7 %collective-permute-start.10 = (f32[16,640]{1,0:T(8,128)S(1)}, f32[16,640]{1,0:T(8,128)S(1)}, u32[]{:S(2)}, u32[]{:S(2)}) collective-permute-start(f32[16,640]{1,0:T(8,128)S(1)} %get-tuple-element.43), channel_id=1, source_target_pairs={{8,0},{16,8},{24,16},{0,24},{9,1},{17,9},{25,17},{1,25},{10,2},{18... | collective-permute-start | bytes 122888 | tf_op jit(solution)/shard_map/ppermute | solution.py:28
  73.7 3.4 %collective-permute-start.11 = (f32[16,640]{1,0:T(8,128)S(1)}, f32[16,640]{1,0:T(8,128)S(1)}, u32[]{:S(2)}, u32[]{:S(2)}) collective-permute-start(f32[16,640]{1,0:T(8,128)S(1)} %get-tuple-element.42), channel_id=1, source_target_pairs={{24,0},{0,8},{8,16},{16,24},{25,1},{1,9},{9,17},{17,25},{26,2},{2,... | collective-permute-start | bytes 122888 | tf_op jit(solution)/shard_map/ppermute | solution.py:28

commit v4 on v3

--- a/solution.py
+++ b/solution.py
@@ -62,9 +62,10 @@
         jnp.sin(orders[:, None, None] * (math.pi / CUTOFF) * radius[None])
         * (envelope / radius)[None]
     )
-    radial = jnp.einsum(
-        "nka,nh->kah", basis, basis_proj.astype(jnp.float32), precision=lax.Precision.HIGHEST
-    )
+    basis_rows = basis_proj.astype(jnp.float32)
+    radial = basis[0][:, :, None] * basis_rows[0]
+    for order in range(1, NB):
+        radial = radial + basis[order][:, :, None] * basis_rows[order]
     hidden = (
         jax.nn.silu(centre_rows[None] + neigh_rows.reshape(K, atoms, width) + radial)
         * envelope[:, :, None]
@@ -144,8 +145,10 @@
     kinds = jnp.arange(NSPEC, dtype=jnp.int32)
 
     def lookup(codes, table):
-        onehot = (codes[:, None] == kinds[None, :]).astype(jnp.float32)
-        return jnp.dot(onehot, table, precision=lax.Precision.HIGHEST)
+        found = jnp.zeros((codes.shape[0], table.shape[1]), jnp.float32)
+        for kind in range(NSPEC):
+            found = jnp.where(codes[:, None] == kind, table[kind][None, :], found)
+        return found
 
     def project(rows, codes, weight, table):
         return (
@@ -176,14 +179,23 @@
         rows_now = table.shape[0]
         base_rows.append(rows_now)
         parts = [table]
-        for number, (segment, direction) in enumerate(((segs[0], 1), (segs[1], -1))):
+        outs = []
+        for segment in segs:
             picked = send_rows[starts[segment] : starts[segment] + lengths[segment]]
             onehot = (
                 picked[:, None] == jnp.arange(rows_now, dtype=jnp.int32)[None, :]
             ).astype(jnp.bfloat16)
             pickers[segment] = onehot
-            out = jnp.dot(onehot, table, preferred_element_type=jnp.float32).astype(jnp.bfloat16)
-            got = passed_along(out, axis, direction)
+            outs.append(
+                jnp.dot(onehot, table, preferred_element_type=jnp.float32).astype(jnp.bfloat16)
+            )
+        if lax.axis_size(axis) == 2:
+            both = passed_along(jnp.concatenate(outs, axis=0), axis, 1)
+            arrived = [both[: outs[0].shape[0]], both[outs[0].shape[0] :]]
+        else:
+            arrived = [passed_along(outs[0], axis, 1), passed_along(outs[1], axis, -1)]
+        for number in range(2):
+            got = arrived[number]
             coord_axis, offset = shifts[2 * section + number]
             columns = jnp.arange(width + extra, dtype=jnp.int32)[None, :]
             shift = jnp.where(columns == width + coord_axis, offset // 16, 0).astype(jnp.bfloat16)
@@ -194,9 +206,9 @@
     select = (neighbour[:, None] == jnp.arange(total_rows, dtype=jnp.int32)[None, :]).astype(
         jnp.bfloat16
     )
-    gathered = jnp.dot(select, table, preferred_element_type=jnp.float32)
-    neigh_rows = gathered[:, :width]
-    coords_n = (gathered[:, width : width + 3] * 16.0 + gathered[:, width + 3 : width + 6]).T
+    neigh_rows = jnp.dot(select, table[:, :width], preferred_element_type=jnp.float32)
+    gathered = jnp.dot(select, table[:, width:], preferred_element_type=jnp.float32)
+    coords_n = (gathered[:, 0:3] * 16.0 + gathered[:, 3:6]).T
     delta = (coords_n.reshape(3, K, atoms) - positions.astype(jnp.float32)[:, None, :]) * (
         1.0 / 64.0
     )
@@ -219,15 +231,10 @@
     atom_energy, pull = jax.vjp(energy_of, delta, neigh_rows, proj_c.astype(jnp.float32))
     grad_delta, grad_neigh, grad_centre = pull(jnp.ones_like(atom_energy))
     pairs = grad_neigh.shape[0]
-    grads = jnp.concatenate(
-        [
-            grad_neigh,
-            grad_delta.reshape(3, pairs).T,
-            jnp.zeros((pairs, extra - 3), jnp.float32),
-        ],
-        axis=1,
-    )
-    sums = spread(select, grads)
+    pos_grads = jnp.concatenate(
+        [grad_delta.reshape(3, pairs).T, jnp.zeros((pairs, extra - 3), jnp.float32)], axis=1
+    )
+    sums = jnp.concatenate([spread(select, grad_neigh), spread(select, pos_grads)], axis=1)
     own_pos = grad_delta.sum(axis=1)
     sums = sums - jnp.pad(own_pos.T, ((0, total_rows - atoms), (width, extra - 3)))
     for section in (2, 1, 0):
@@ -235,8 +242,13 @@
         rows_now = base_rows[section]
         first = atoms + starts[2 * section]
         second = atoms + starts[2 * section + 1]
-        back_first = passed_along(sums[first : first + lengths[2 * section]], axis, -1)
-        back_second = passed_along(sums[second : second + lengths[2 * section + 1]], axis, 1)
+        if lax.axis_size(axis) == 2:
+            both = passed_along(sums[first : second + lengths[2 * section + 1]], axis, 1)
+            back_first = both[: lengths[2 * section]]
+            back_second = both[lengths[2 * section] :]
+        else:
+            back_first = passed_along(sums[first : first + lengths[2 * section]], axis, -1)
+            back_second = passed_along(sums[second : second + lengths[2 * section + 1]], axis, 1)
         sums = (
             sums[:rows_now]
             + spread(pickers[segs[0]], back_first)

time: 80.3 us -> 94.7 us (1.18)
  other arithmetic: 6.91 us -> 16.1 us
  local copies, waits for them, and re-layouts: 13.4 us -> 19.4 us
  matrix products: 26.5 us -> 25.5 us
    dot_general x6 -> x2, matrix products: 8.91 us -> 4.37 us  [the longest x1 3.81 us: shards(): jnp.dot(select, table[:, :width], preferred_element_type=jnp.float32)]
    mul x0 -> x2, other arithmetic: none -> 3.78 us  [the longest x1 3.59 us: shards(): live * (lookup(species, species_shift[:, None])[:, 0] + atom_energy)]
    slice x2, local copies, waits for them, and re-layouts: 0.4 us -> 3.86 us  [by_order(): values[2:3]]
    add_any x0 -> x1, other arithmetic: none -> 2.46 us  [pair_energy(): jax.nn.silu(centre_rows[None] + neigh_rows.reshape(K, atoms, width) + rad...]
    slice x2, local copies, waits for them, and re-layouts: 0.4 us -> 2.81 us  [by_order(): values[1:2]]
    dot_general x2, matrix products: 2.98 us -> 5.29 us  [pair_energy(): jnp.einsum('kah,hq->qka', hidden_low, split_proj, preferred_element_type=...]
    reshape x2 -> x0, local copies, waits for them, and re-layouts: 2.05 us -> none  [the longest x1 1.83 us: pair_energy(): neigh_rows.reshape(K, atoms, width)]
    reduce_sum x0 -> x2, other arithmetic: none -> 1.51 us  [the longest x1 1.31 us: pair_energy(): centre_rows[None] + neigh_rows.reshape(K, atoms, width) + radial]
  transfers between devices with their start and end apart: 12 -> 10, of which waited for: 9 -> 6; matrix products, arithmetic and copies ran while one was open for 6% -> 8% of each run, Pallas kernels for 0% -> 0%
where the time goes in v4:
time: 94.7 us; the launch traced here: 94 us
  matrix products  25.5 us (27%)
  local copies, waits for them, and re-layouts  19.4 us (20%)
  other arithmetic  16.1 us (17%)
  starting transfers between devices  15.8 us (17%)
  waiting for transfers between devices  14.9 us (16%)
  between operations  2.41 us (3%)
    ppermute x10, starting transfers between devices, passed_along(): return lax.ppermute(block, axis, route)  15.8 us
    ppermute x10, waiting for transfers between devices, passed_along(): return lax.ppermute(block, axis, route)  14.9 us
    dot_general x2, matrix products, pair_energy(): jnp.einsum('kah,hq->qka', hidden_low, split_proj, preferred_element_type=...  5.29 us
    slice x3, local copies, waits for them, and re-layouts, by_order(): values[0:1]  4.55 us
    unnamed x88, local copies, waits for them, and re-layouts  3.94 us
    slice x2, local copies, waits for them, and re-layouts, by_order(): values[2:3]  3.86 us
    dot_general x1, matrix products, shards(): jnp.dot(select, table[:, :width], preferred_element_type=jnp.float32)  3.81 us
    mul x1, other arithmetic, shards(): live * (lookup(species, species_shift[:, None])[:, 0] + atom_energy)  3.59 us
  transfers between devices with their start and end apart: 10, of which 6 were waited for; matrix products, arithmetic and copies ran while one was open for 8% of the time, Pallas kernels for 0%

profile of v4, /device:TPU:0, one launch (start us, length us, event | category | flops | bytes accessed | tf_op | source)
XLA Modules:
  0.0 94.0 jit_solution(9592646684609619503)
XLA Ops:
  1.7 0.9 fusion.154
  4.1 1.4 %fusion.37 = bf16[128,512]{1,0:T(8,128)(2,1)S(1)} fusion(bf16[128,512]{1,0:T(8,128)(2,1)} %param.16, bf16[512,512]{1,0:T(8,128)(2,1)} %param.23, f32[512]{0:T(512)S(1)} %bitcast.315, f32[512]{0:T(512)S(1)} %bitcast.316, f32[512]{0:T(512)S(1)} %bitcast.313, f32[512]{0:T(512)S(1)} %bitcast.314, f32[512]{0:T(512)S(1)} %bitcast.312, ...), kind=kOutput, calls=%fused_computation.78 | convolution fusion | flops 67567616 | bytes 797312 | tf_op jit(solution)/shard_map/dot_general | solution.py:155
  6.3 1.9 %collective-permute-start.1 = (bf16[16,640]{1,0:T(8,128)(2,1)S(1)}, bf16[16,640]{1,0:T(8,128)(2,1)S(1)}, u32[]{:S(2)}, u32[]{:S(2)}) collective-permute-start(bf16[16,640]{1,0:T(8,128)(2,1)S(1)} %convolution_convert_fusion.6), channel_id=1, source_target_pairs={{8,0},{16,8},{24,16},{0,24},{9,1},{17,9},{25,17},{1,25},{10,2},{18... | collective-permute-start | bytes 61448 | tf_op jit(solution)/shard_map/ppermute | solution.py:28
  10.3 2.4 %collective-permute-start.2 = (bf16[128,640]{1,0:T(8,128)(2,1)S(1)}, bf16[128,640]{1,0:T(8,128)(2,1)S(1)}, u32[]{:S(2)}, u32[]{:S(2)}) collective-permute-start(bf16[128,640]{1,0:T(8,128)(2,1)S(1)} %pad_maximum_fusion.4), channel_id=1, source_target_pairs={{4,0},{0,4},{5,1},{1,5},{6,2},{2,6},{7,3},{3,7},{12,8},{8,12},{13,... | collective-permute-start | bytes 491528 | tf_op jit(solution)/shard_map/ppermute | solution.py:28
  12.7 4.1 %collective-permute-done.2 = bf16[128,640]{1,0:T(8,128)(2,1)S(1)} collective-permute-done((bf16[128,640]{1,0:T(8,128)(2,1)S(1)}, bf16[128,640]{1,0:T(8,128)(2,1)S(1)}, u32[]{:S(2)}, u32[]{:S(2)}) %collective-permute-start.2) | collective-permute-done | bytes 163872 | tf_op jit(solution)/shard_map/ppermute | solution.py:28
  17.0 2.6 %collective-permute-start.3 = (bf16[16,640]{1,0:T(8,128)(2,1)S(1)}, bf16[16,640]{1,0:T(8,128)(2,1)S(1)}, u32[]{:S(2)}, u32[]{:S(2)}) collective-permute-start(bf16[16,640]{1,0:T(8,128)(2,1)S(1)} %convolution_convert_fusion.5), channel_id=1, source_target_pairs={{3,0},{0,1},{1,2},{2,3},{7,4},{4,5},{5,6},{6,7},{11,8},{8,9},{9,10... | collective-permute-start | bytes 61448 | tf_op jit(solution)/shard_map/ppermute | solution.py:28
  19.8 2.1 %collective-permute-start.4 = (bf16[16,640]{1,0:T(8,128)(2,1)S(1)}, bf16[16,640]{1,0:T(8,128)(2,1)S(1)}, u32[]{:S(2)}, u32[]{:S(2)}) collective-permute-start(bf16[16,640]{1,0:T(8,128)(2,1)S(1)} %convolution_convert_fusion.4), channel_id=1, source_target_pairs={{1,0},{2,1},{3,2},{0,3},{5,4},{6,5},{7,6},{4,7},{9,8},{10,9},{11,1... | collective-permute-start | bytes 61448 | tf_op jit(solution)/shard_map/ppermute | solution.py:28
  21.9 1.5 %collective-permute-done.3 = bf16[16,640]{1,0:T(8,128)(2,1)S(1)} collective-permute-done((bf16[16,640]{1,0:T(8,128)(2,1)S(1)}, bf16[16,640]{1,0:T(8,128)(2,1)S(1)}, u32[]{:S(2)}, u32[]{:S(2)}) %collective-permute-start.3) | collective-permute-done | bytes 20512 | tf_op jit(solution)/shard_map/ppermute | solution.py:28
  25.2 3.8 %multiply_multiply_fusion.2 = (f32[1024,512]{1,0:T(8,128)}, f32[1024,512]{1,0:T(8,128)S(1)}) fusion(f32[1024]{0:T(1024)S(1)} %get-tuple-element.97, f32[512]{0:T(512)S(1)} %bitcast.290, f32[1024]{0:T(1024)S(1)} %get-tuple-element.65, f32[512]{0:T(512)S(1)} %bitcast.285, f32[1024]{0:T(1024)S(1)} %get-tuple-element.66, f32[512]{0:T(512)S(1)} %bitcast.280, ...), kind=kOutput, calls=%fused_computation.44 | convolution fusion | flops 347406336 | bytes 4841472 | tf_op jit(solution)/shard_map/dot_general | solution.py:209
  29.0 2.0 %convolution_bitcast_fusion = f32[384,8,128]{0,2,1:T(8,128)S(1)} fusion(f32[8,128]{1,0:T(8,128)S(1)} %get-tuple-element.93, bf16[512,384]{1,0:T(8,128)(2,1)S(1)} %copy-done.36, f32[8,128,512]{2,1,0:T(8,128)S(1)} %bitcast.232, f32[512]{0:T(512)S(1)} %bitcast.291, f32[8,128]{1,0:T(8,128)S(1)} %get-tuple-element.64, f32[512]{0:T(512)S(1)} %bitcast.286, ...), kind=kOutput, calls=%fused_computation.57 | convolution fusion | flops 414711808 | bytes 4378624 | tf_op jit(solution)/shard_map/jvp(kah,hq->qka)/dot_general | solution.py:74
  31.0 2.0 %slice_bitcast_fusion = (f32[1,64,8,128]{1,3,2,0:T(8,128)}, f32[64,8,128]{0,2,1:T(8,128)}, f32[64,8,128]{0,2,1:T(8,128)S(1)}, f32[64,8,128]{0,2,1:T(8,128)}, f32...) fusion(f32[384,8,128]{0,2,1:T(8,128)S(1)} %convolution_bitcast_fusion), kind=kLoop, calls=%fused_computation.108 | loop fusion | bytes 3145728 | tf_op jit(solution)/shard_map/jvp()/slice | solution.py:35
  33.0 1.9 %copy.64 = f32[64,8,128]{2,1,0:T(8,128)} copy(f32[64,8,128]{0,2,1:T(8,128)} %get-tuple-element.37) | data formatting | bytes 524288 | tf_op jit(solution)/shard_map/jvp()/slice | solution.py:37
  35.0 1.9 %copy.63 = f32[64,8,128]{2,1,0:T(8,128)} copy(f32[64,8,128]{0,2,1:T(8,128)} %get-tuple-element.38) | data formatting | bytes 524288 | tf_op jit(solution)/shard_map/jvp()/slice | solution.py:36
  36.9 1.2 %copy.65 = f32[1,64,8,128]{3,2,1,0:T(8,128)S(1)} copy(f32[1,64,8,128]{1,3,2,0:T(8,128)} %get-tuple-element.39) | data formatting | bytes 524288 | tf_op jit(solution)/shard_map/jvp()/slice | solution.py:35
  38.1 1.9 %copy.67 = f32[64,8,128]{2,1,0:T(8,128)} copy(f32[64,8,128]{0,2,1:T(8,128)} %get-tuple-element.35) | data formatting | bytes 524288 | tf_op jit(solution)/shard_map/jvp()/slice | solution.py:37
  40.9 1.3 %copy.68 = f32[1,64,8,128]{3,2,1,0:T(8,128)S(1)} copy(f32[1,64,8,128]{1,3,2,0:T(8,128)} %get-tuple-element.34) | data formatting | bytes 524288 | tf_op jit(solution)/shard_map/jvp()/slice | solution.py:35
  42.3 1.0 %broadcast_in_dim.365 = f32[5,64,8,128]{3,2,1,0:T(8,128)S(1)} broadcast(f32[64,8,128]{2,1,0:T(8,128)} %copy.67), dimensions={1,2,3} | broadcast | bytes 1572864 | tf_op jit(solution)/shard_map/jvp()/broadcast_in_dim | solution.py:37
  46.5 1.2 %multiply_reduce_fusion.9 = (f32[1024]{0:T(1024)S(1)}, f32[1024,512]{1,0:T(8,128)S(1)}) fusion(f32[1024,512]{1,0:T(8,128)S(1)} %copy-done.1, f32[512]{0:T(512)S(1)} %copy-done.31, f32[1024,512]{1,0:T(8,128)S(1)} %fusion.55, bf16[512,512]{1,0:T(8,128)(2,1)S(1)} %copy-done), kind=kOutput, calls=%fused_computation.38 | convolution fusion | flops 541588480 | bytes 6821888 | tf_op jit(solution)/shard_map/jvp()/dot_general | solution.py:104
  47.8 1.1 %convolution_convert_fusion = bf16[1024,512]{1,0:T(8,128)(2,1)S(1)} fusion(bf16[512,512]{1,0:T(8,128)(2,1)S(1)} %copy-done, f32[1024,512]{1,0:T(8,128)S(1)} %get-tuple-element.125, f32[1024]{0:T(1024)S(1)} %copy-done.30, f32[512]{0:T(512)S(1)} %copy-done.31), kind=kOutput, calls=%fused_computation.55 | convolution fusion | flops 542638080 | bytes 3676160 | tf_op jit(solution)/shard_map/transpose(jvp())/dot_general | solution.py:104
  48.9 1.1 %fusion.36 = f32[192,1024]{1,0:T(8,128)S(1)} fusion(bf16[192,512]{1,0:T(8,128)(2,1)S(1)} %copy-done.10, f32[1024,512]{1,0:T(8,128)S(1)} %get-tuple-element.125, f32[1024]{0:T(1024)S(1)} %copy-done.30, f32[512]{0:T(512)S(1)} %copy-done.31), kind=kOutput, calls=%fused_computation.69 | convolution fusion | flops 206962688 | bytes 3086336 | tf_op jit(solution)/shard_map/transpose(jvp(qp,qh->ph))/dot_general | solution.py:105
  50.3 3.4 %fusion.4 = (f32[9,64,128]{2,1,0:T(8,128)S(1)}, f32[9,8,128]{2,1,0:T(8,128)S(1)}, f32[9,64,8,128]{3,2,1,0:T(8,128)S(1)}) fusion(f32[5,64,8,128]{3,2,1,0:T(8,128)S(1)} %broadcast_in_dim.363, f32[3,64,8,128]{3,2,1,0:T(8,128)S(1)} %broadcast_in_dim.362, f32[1,64,8,128]{3,2,1,0:T(8,128)S(1)} %copy.65, f32[1,64,8,128]{3,2,1,0:T(8,128)S(1)} %bitcast.237, ...), kind=kLoop, calls=%fused_computation.9 | loop fusion | flops 6405120 | bytes 7741440 | tf_op jit(solution)/shard_map/transpose(jvp())/reduce_sum | solution.py:99
  56.1 3.3 %multiply_reduce_fusion = (f32[8,128]{1,0:T(8,128)S(1)}, bf16[8,128,512]{2,1,0:T(8,128)(2,1)S(1)}) fusion(f32[512]{0:T(512)S(1)} %copy-done.31, f32[8,128]{1,0:T(8,128)S(1)} %get-tuple-element.93, f32[512]{0:T(512)S(1)} %bitcast.292, f32[8,128]{1,0:T(8,128)S(1)} %get-tuple-element.64, f32[512]{0:T(512)S(1)} %bitcast.287, ...), kind=kOutput, calls=%fused_computation.28 | convolution fusion | flops 416807936 | bytes 5695488 | tf_op jit(solution)/shard_map/transpose(jvp(kah,hq->qka))/dot_general | solution.py:74
  59.4 2.5 %fusion.15 = f32[8,128,512]{2,1,0:T(8,128)S(1)} fusion(bf16[8,128,512]{2,1,0:T(8,128)(2,1)S(1)} %get-tuple-element.123, f32[512]{0:T(512)S(1)} %copy-done.31, f32[8,128]{1,0:T(8,128)S(1)} %get-tuple-element.93, f32[512]{0:T(512)S(1)} %bitcast.293, f32[8,128]{1,0:T(8,128)S(1)} %get-tuple-element.64, f32[512]{0:T(512)S(1)} %bitcast.288, ...), kind=kLoop, calls=%fused_computation.22 | loop fusion | flops 15728640 | bytes 5560320 | tf_op jit(solution)/shard_map/transpose(jvp(jit(silu)))/add_any | solution.py:70
  61.9 1.3 %fusion.150 = (f32[128,512]{1,0:T(8,128)S(1)}, f32[8,128]{1,0:T(8,128)S(1)}, f32[8,128]{1,0:T(8,128)S(1)}, f32[8,128]{1,0:T(8,128)S(1)}, f32[8,128]{1,0:T(8,128)...) fusion(f32[8,128,512]{2,1,0:T(8,128)S(1)} %fusion.15, ...), kind=kLoop, calls=%fused_computation.330 | loop fusion | flops 8839168 | bytes 2408448 | tf_op jit(solution)/shard_map/transpose(jvp())/reduce_sum | solution.py:70
  67.3 1.6 %collective-permute-start.6 = (f32[16,640]{1,0:T(8,128)S(1)}, f32[16,640]{1,0:T(8,128)S(1)}, u32[]{:S(2)}, u32[]{:S(2)}) collective-permute-start(f32[16,640]{1,0:T(8,128)S(1)} %get-tuple-element.41), channel_id=1, source_target_pairs={{3,0},{0,1},{1,2},{2,3},{7,4},{4,5},{5,6},{6,7},{11,8},{8,9},{9,10... | collective-permute-start | bytes 122888 | tf_op jit(solution)/shard_map/ppermute | solution.py:28
  69.0 2.3 %collective-permute-start.5 = (f32[16,640]{1,0:T(8,128)S(1)}, f32[16,640]{1,0:T(8,128)S(1)}, u32[]{:S(2)}, u32[]{:S(2)}) collective-permute-start(f32[16,640]{1,0:T(8,128)S(1)} %get-tuple-element.40), channel_id=1, source_target_pairs={{1,0},{2,1},{3,2},{0,3},{5,4},{6,5},{7,6},{4,7},{9,8},{10,9},{11,1... | collective-permute-start | bytes 122888 | tf_op jit(solution)/shard_map/ppermute | solution.py:28
  71.3 2.2 %collective-permute-done.6 = f32[16,640]{1,0:T(8,128)S(1)} collective-permute-done((f32[16,640]{1,0:T(8,128)S(1)}, f32[16,640]{1,0:T(8,128)S(1)}, u32[]{:S(2)}, u32[]{:S(2)}) %collective-permute-start.6) | collective-permute-done | bytes 40992 | tf_op jit(solution)/shard_map/ppermute | solution.py:28
  75.2 1.8 %collective-permute-start.7 = (f32[128,640]{1,0:T(8,128)S(1)}, f32[128,640]{1,0:T(8,128)S(1)}, u32[]{:S(2)}, u32[]{:S(2)}) collective-permute-start(f32[128,640]{1,0:T(8,128)S(1)} %slice.349), channel_id=1, source_target_pairs={{4,0},{0,4},{5,1},{1,5},{6,2},{2,6},{7,3},{3,7},{12,8},{8,12},{13,... | collective-permute-start | bytes 983048 | tf_op jit(solution)/shard_map/ppermute | solution.py:28
  78.2 4.6 %collective-permute-done.7 = f32[128,640]{1,0:T(8,128)S(1)} collective-permute-done((f32[128,640]{1,0:T(8,128)S(1)}, f32[128,640]{1,0:T(8,128)S(1)}, u32[]{:S(2)}, u32[]{:S(2)}) %collective-permute-start.7) | collective-permute-done | bytes 327712 | tf_op jit(solution)/shard_map/ppermute | solution.py:28
  84.3 3.6 %compare_select_fusion = f32[128]{0:T(128)} fusion(f32[128]{0:T(128)S(1)} %get-tuple-element.84, f32[]{:T(128)} %bitcast.5, f32[]{:T(128)} %bitcast.4, f32[]{:T(128)} %bitcast.3, f32[]{:T(128)} %bitcast.2, f32[]{:T(128)} %bitcast.1, s32[]{:T(128)} %bitcast.231, s32[128]{0:T(128)S(1)} %copy-done.34), kind=kLoop, calls=%fused_computation.310 | loop fusion | flops 1664 | bytes 1560 | tf_op jit(solution)/shard_map/mul | solution.py:264
  89.1 2.3 %collective-permute-done.9 = f32[16,640]{1,0:T(8,128)S(1)} collective-permute-done((f32[16,640]{1,0:T(8,128)S(1)}, f32[16,640]{1,0:T(8,128)S(1)}, u32[]{:S(2)}, u32[]{:S(2)}) %collective-permute-start.9) | collective-permute-done | bytes 40992 | tf_op jit(solution)/shard_map/ppermute | solution.py:28
  92.7 1.3 %convolution_add_fusion.7 = f32[128,512]{1,0:T(8,128)} fusion(f32[128,512]{1,0:T(8,128)S(1)} %fusion.158, bf16[512,512]{1,0:T(8,128)(2,1)S(1)} %copy-done.9, f32[128,640]{1,0:T(8,128)S(1)} %fusion.61), kind=kOutput, calls=%fused_computation.75 | convolution fusion | flops 402718720 | bytes 1310720 | tf_op jit(solution)/shard_map/dot_general | solution.py:260
  (201 shorter events, 24.0 us)
Async XLA Ops:
  0.6 45.6 %copy-start = (bf16[512,512]{1,0:T(8,128)(2,1)S(1)}, bf16[512,512]{1,0:T(8,128)(2,1)}, u32[]{:S(2)}) copy-start(bf16[512,512]{1,0:T(8,128)(2,1)} %param.28) | copy-start | bytes 1572868
  0.6 7.7 %copy-start.13 = (s32[1,192]{1,0:T(1,128)S(1)}, s32[1,192]{1,0:T(1,128)}, u32[]{:S(2)}) copy-start(s32[1,192]{1,0:T(1,128)} %param.19) | copy-start | bytes 2308
  0.7 8.6 %copy-start.38 = (bf16[128,512]{1,0:T(8,128)(2,1)S(1)}, bf16[128,512]{1,0:T(8,128)(2,1)}, u32[]{:S(2)}) copy-start(bf16[128,512]{1,0:T(8,128)(2,1)} %param.16) | copy-start | bytes 393220
  0.7 8.5 %copy-start.11 = (bf16[8,512]{1,0:T(8,128)(2,1)S(1)}, bf16[8,512]{1,0:T(8,128)(2,1)}, u32[]{:S(2)}) copy-start(bf16[8,512]{1,0:T(8,128)(2,1)} %param.26) | copy-start | bytes 24580
  0.7 8.6 %copy-start.20 = (f32[5,512]{1,0:T(8,128)S(1)}, f32[5,512]{1,0:T(8,128)}, u32[]{:S(2)}) copy-start(f32[5,512]{1,0:T(8,128)} %param.24) | copy-start | bytes 30724
  0.7 8.6 %copy-start.7 = (bf16[512,512]{1,0:T(8,128)(2,1)S(1)}, bf16[512,512]{1,0:T(8,128)(2,1)}, u32[]{:S(2)}) copy-start(bf16[512,512]{1,0:T(8,128)(2,1)} %param.22) | copy-start | bytes 1572868
  1.5 8.0 %copy-start.29 = (s32[1024]{0:T(1024)S(1)}, s32[1024]{0:T(1024)}, u32[]{:S(2)}) copy-start(s32[1024]{0:T(1024)} %param.20) | copy-start | bytes 12292
  4.1 12.8 %copy-start.16 = (s32[16]{0:T(128)}, s32[16]{0:T(128)S(1)}, u32[]{:S(2)}) copy-start(s32[16]{0:T(128)S(1)} %get-tuple-element.105) | copy-start | bytes 196
  4.1 15.6 %copy-start.18 = (s32[16]{0:T(128)}, s32[16]{0:T(128)S(1)}, u32[]{:S(2)}) copy-start(s32[16]{0:T(128)S(1)} %get-tuple-element.102) | copy-start | bytes 196
  5.6 4.1 %collective-permute-start = (bf16[16,640]{1,0:T(8,128)(2,1)S(1)}, bf16[16,640]{1,0:T(8,128)(2,1)S(1)}, u32[]{:S(2)}, u32[]{:S(2)}) collective-permute-start(bf16[16,640]{1,0:T(8,128)(2,1)S(1)} %convolution_convert_fusion.7), channel_id=1, source_target_pairs={{24,0},{0,8},{8,16},{16,24},{25,1},{1,9},{9,17},{17,25},{26,2},{2,... | collective-permute-start | bytes 61448 | tf_op jit(solution)/shard_map/ppermute | solution.py:28
  6.3 3.4 %collective-permute-start.1 = (bf16[16,640]{1,0:T(8,128)(2,1)S(1)}, bf16[16,640]{1,0:T(8,128)(2,1)S(1)}, u32[]{:S(2)}, u32[]{:S(2)}) collective-permute-start(bf16[16,640]{1,0:T(8,128)(2,1)S(1)} %convolution_convert_fusion.6), channel_id=1, source_target_pairs={{8,0},{16,8},{24,16},{0,24},{9,1},{17,9},{25,17},{1,25},{10,2},{18... | collective-permute-start | bytes 61448 | tf_op jit(solution)/shard_map/ppermute | solution.py:28
  8.5 8.3 %copy-start.23 = (s32[64]{0:T(128)}, s32[64]{0:T(128)S(1)}, u32[]{:S(2)}) copy-start(s32[64]{0:T(128)S(1)} %get-tuple-element.106) | copy-start | bytes 772
  8.5 8.3 %copy-start.27 = (s32[64]{0:T(128)}, s32[64]{0:T(128)S(1)}, u32[]{:S(2)}) copy-start(s32[64]{0:T(128)S(1)} %get-tuple-element.107) | copy-start | bytes 772
  8.5 16.4 %copy-start.32 = (f32[8]{0:T(128)}, f32[8]{0:T(128)S(1)}, u32[]{:S(2)}) copy-start(f32[8]{0:T(128)S(1)} %convert_multiply_fusion) | copy-start | bytes 100
  9.5 19.5 %copy-start.2 = (f32[128,512]{1,0:T(8,128)}, f32[128,512]{1,0:T(8,128)S(1)}, u32[]{:S(2)}) copy-start(f32[128,512]{1,0:T(8,128)S(1)} %fusion.39) | copy-start | bytes 786436
  9.6 14.8 %copy-start.14 = (f32[128]{0:T(128)}, f32[128]{0:T(128)S(1)}, u32[]{:S(2)}) copy-start(f32[128]{0:T(128)S(1)} %compare_convert_fusion) | copy-start | bytes 1540
  10.3 6.5 %collective-permute-start.2 = (bf16[128,640]{1,0:T(8,128)(2,1)S(1)}, bf16[128,640]{1,0:T(8,128)(2,1)S(1)}, u32[]{:S(2)}, u32[]{:S(2)}) collective-permute-start(bf16[128,640]{1,0:T(8,128)(2,1)S(1)} %pad_maximum_fusion.4), channel_id=1, source_target_pairs={{4,0},{0,4},{5,1},{1,5},{6,2},{2,6},{7,3},{3,7},{12,8},{8,12},{13,... | collective-permute-start | bytes 491528 | tf_op jit(solution)/shard_map/ppermute | solution.py:28
  17.0 6.4 %collective-permute-start.3 = (bf16[16,640]{1,0:T(8,128)(2,1)S(1)}, bf16[16,640]{1,0:T(8,128)(2,1)S(1)}, u32[]{:S(2)}, u32[]{:S(2)}) collective-permute-start(bf16[16,640]{1,0:T(8,128)(2,1)S(1)} %convolution_convert_fusion.5), channel_id=1, source_target_pairs={{3,0},{0,1},{1,2},{2,3},{7,4},{4,5},{5,6},{6,7},{11,8},{8,9},{9,10... | collective-permute-start | bytes 61448 | tf_op jit(solution)/shard_map/ppermute | solution.py:28
  19.8 3.8 %collective-permute-start.4 = (bf16[16,640]{1,0:T(8,128)(2,1)S(1)}, bf16[16,640]{1,0:T(8,128)(2,1)S(1)}, u32[]{:S(2)}, u32[]{:S(2)}) collective-permute-start(bf16[16,640]{1,0:T(8,128)(2,1)S(1)} %convolution_convert_fusion.4), channel_id=1, source_target_pairs={{1,0},{2,1},{3,2},{0,3},{5,4},{6,5},{7,6},{4,7},{9,8},{10,9},{11,1... | collective-permute-start | bytes 61448 | tf_op jit(solution)/shard_map/ppermute | solution.py:28
  66.4 7.2 %copy-start.19 = (s32[16]{0:T(128)S(1)}, s32[16]{0:T(128)}, u32[]{:S(2)}) copy-start(s32[16]{0:T(128)} %copy-done.18) | copy-start | bytes 196
  67.3 7.0 %copy-start.17 = (s32[16]{0:T(128)S(1)}, s32[16]{0:T(128)}, u32[]{:S(2)}) copy-start(s32[16]{0:T(128)} %copy-done.16) | copy-start | bytes 196
  67.3 6.2 %collective-permute-start.6 = (f32[16,640]{1,0:T(8,128)S(1)}, f32[16,640]{1,0:T(8,128)S(1)}, u32[]{:S(2)}, u32[]{:S(2)}) collective-permute-start(f32[16,640]{1,0:T(8,128)S(1)} %get-tuple-element.41), channel_id=1, source_target_pairs={{3,0},{0,1},{1,2},{2,3},{7,4},{4,5},{5,6},{6,7},{11,8},{8,9},{9,10... | collective-permute-start | bytes 122888 | tf_op jit(solution)/shard_map/ppermute | solution.py:28
  69.0 5.3 %collective-permute-start.5 = (f32[16,640]{1,0:T(8,128)S(1)}, f32[16,640]{1,0:T(8,128)S(1)}, u32[]{:S(2)}, u32[]{:S(2)}) collective-permute-start(f32[16,640]{1,0:T(8,128)S(1)} %get-tuple-element.40), channel_id=1, source_target_pairs={{1,0},{2,1},{3,2},{0,3},{5,4},{6,5},{7,6},{4,7},{9,8},{10,9},{11,1... | collective-permute-start | bytes 122888 | tf_op jit(solution)/shard_map/ppermute | solution.py:28
  74.7 8.1 %copy-start.24 = (s32[64]{0:T(128)S(1)}, s32[64]{0:T(128)}, u32[]{:S(2)}) copy-start(s32[64]{0:T(128)} %copy-done.23) | copy-start | bytes 772
  74.7 8.5 %copy-start.28 = (s32[64]{0:T(128)S(1)}, s32[64]{0:T(128)}, u32[]{:S(2)}) copy-start(s32[64]{0:T(128)} %copy-done.27) | copy-start | bytes 772
  75.2 7.7 %collective-permute-start.7 = (f32[128,640]{1,0:T(8,128)S(1)}, f32[128,640]{1,0:T(8,128)S(1)}, u32[]{:S(2)}, u32[]{:S(2)}) collective-permute-start(f32[128,640]{1,0:T(8,128)S(1)} %slice.349), channel_id=1, source_target_pairs={{4,0},{0,4},{5,1},{1,5},{6,2},{2,6},{7,3},{3,7},{12,8},{8,12},{13,... | collective-permute-start | bytes 983048 | tf_op jit(solution)/shard_map/ppermute | solution.py:28
  78.2 6.1 %copy-start.34 = (s32[128]{0:T(128)S(1)}, s32[128]{0:T(128)}, u32[]{:S(2)}) copy-start(s32[128]{0:T(128)} %param.18) | copy-start | bytes 1540
  78.2 10.2 %copy-start.26 = (s32[16]{0:T(128)S(1)}, s32[16]{0:T(128)}, u32[]{:S(2)}) copy-start(s32[16]{0:T(128)} %copy-done.25) | copy-start | bytes 196
  83.5 7.8 %copy-start.22 = (s32[16]{0:T(128)S(1)}, s32[16]{0:T(128)}, u32[]{:S(2)}) copy-start(s32[16]{0:T(128)} %copy-done.21) | copy-start | bytes 196
  83.9 8.8 %copy-start.9 = (bf16[512,512]{1,0:T(8,128)(2,1)S(1)}, bf16[512,512]{1,0:T(8,128)(2,1)}, u32[]{:S(2)}) copy-start(bf16[512,512]{1,0:T(8,128)(2,1)} %param.23) | copy-start | bytes 1572868
  84.3 4.2 %collective-permute-start.8 = (f32[16,640]{1,0:T(8,128)S(1)}, f32[16,640]{1,0:T(8,128)S(1)}, u32[]{:S(2)}, u32[]{:S(2)}) collective-permute-start(f32[16,640]{1,0:T(8,128)S(1)} %get-tuple-element.46), channel_id=1, source_target_pairs={{8,0},{16,8},{24,16},{0,24},{9,1},{17,9},{25,17},{1,25},{10,2},{18... | collective-permute-start | bytes 122888 | tf_op jit(solution)/shard_map/ppermute | solution.py:28
  87.9 3.4 %collective-permute-start.9 = (f32[16,640]{1,0:T(8,128)S(1)}, f32[16,640]{1,0:T(8,128)S(1)}, u32[]{:S(2)}, u32[]{:S(2)}) collective-permute-start(f32[16,640]{1,0:T(8,128)S(1)} %get-tuple-element.45), channel_id=1, source_target_pairs={{24,0},{0,8},{8,16},{16,24},{25,1},{1,9},{9,17},{17,25},{26,2},{2,... | collective-permute-start | bytes 122888 | tf_op jit(solution)/shard_map/ppermute | solution.py:28
  (17 other events, 32.4 us)

commit v5 on v3

--- a/solution.py
+++ b/solution.py
@@ -42,8 +42,8 @@
 
 def pair_energy(
     delta,
-    neigh_rows,
-    centre_rows,
+    neigh_cols,
+    centre_cols,
     valid_pair,
     basis_proj,
     split_proj,
@@ -51,8 +51,7 @@
     tensor_proj,
     energy_proj,
 ):
-    atoms = centre_rows.shape[0]
-    width = centre_rows.shape[1]
+    atoms = centre_cols.shape[1]
     radius = jnp.sqrt(jnp.sum(delta * delta, axis=0) + SOFTEN)
     unit = delta / radius
     ratio = radius / CUTOFF
@@ -63,14 +62,11 @@
         * (envelope / radius)[None]
     )
     radial = jnp.einsum(
-        "nka,nh->kah", basis, basis_proj.astype(jnp.float32), precision=lax.Precision.HIGHEST
-    )
-    hidden = (
-        jax.nn.silu(centre_rows[None] + neigh_rows.reshape(K, atoms, width) + radial)
-        * envelope[:, :, None]
-    )
+        "nka,nh->hka", basis, basis_proj.astype(jnp.float32), precision=lax.Precision.HIGHEST
+    )
+    hidden = jax.nn.silu(centre_cols[:, None, :] + neigh_cols + radial) * envelope[None]
     hidden_low = hidden.astype(jnp.bfloat16)
-    mixed = jnp.einsum("kah,hq->qka", hidden_low, split_proj, preferred_element_type=jnp.float32)
+    mixed = jnp.einsum("hka,hq->qka", hidden_low, split_proj, preferred_element_type=jnp.float32)
     amplitude = mixed[: 3 * CH].reshape(3, CH, K, atoms)
     weights = mixed[3 * CH :].reshape(3, CH, K, atoms)
     unit_x = unit[0]
@@ -97,15 +93,12 @@
     environment = gathered.sum(axis=2) / math.sqrt(K)
     products = by_order(amplitude) * harmonics[:, None] * environment[:, :, None, :]
     scalars = jnp.stack([products[0], products[1:4].sum(axis=0), products[4:9].sum(axis=0)], axis=0)
-    scalars = scalars.reshape(3 * CH, K * atoms).astype(jnp.bfloat16)
-    flat_low = hidden_low.reshape(K * atoms, width)
+    scalars = scalars.reshape(3 * CH, K, atoms).astype(jnp.bfloat16)
     update = jax.nn.silu(
-        jnp.dot(flat_low, update_proj, preferred_element_type=jnp.float32)
-        + jnp.einsum("qp,qh->ph", scalars, tensor_proj, preferred_element_type=jnp.float32)
-    )
-    energy = envelope * jnp.sum(
-        (hidden + update.reshape(K, atoms, width)) * energy_proj, axis=-1
-    )
+        jnp.einsum("hka,hi->ika", hidden_low, update_proj, preferred_element_type=jnp.float32)
+        + jnp.einsum("qka,qi->ika", scalars, tensor_proj, preferred_element_type=jnp.float32)
+    )
+    energy = envelope * jnp.sum((hidden + update) * energy_proj[:, None, None], axis=0)
     return energy.sum(axis=0)
 
 
@@ -152,6 +145,13 @@
             jnp.dot(rows, weight, preferred_element_type=jnp.float32) + lookup(codes, table)
         ).astype(jnp.bfloat16)
 
+    def spread_cols(onehot, values):
+        high = values.astype(jnp.bfloat16)
+        low = (values - high.astype(jnp.float32)).astype(jnp.bfloat16)
+        return jnp.einsum(
+            "wn,nr->wr", high, onehot, preferred_element_type=jnp.float32
+        ) + jnp.einsum("wn,nr->wr", low, onehot, preferred_element_type=jnp.float32)
+
     def spread(onehot, values):
         high = values.astype(jnp.bfloat16)
         low = (values - high.astype(jnp.float32)).astype(jnp.bfloat16)
@@ -194,9 +194,9 @@
     select = (neighbour[:, None] == jnp.arange(total_rows, dtype=jnp.int32)[None, :]).astype(
         jnp.bfloat16
     )
-    gathered = jnp.dot(select, table, preferred_element_type=jnp.float32)
-    neigh_rows = gathered[:, :width]
-    coords_n = (gathered[:, width : width + 3] * 16.0 + gathered[:, width + 3 : width + 6]).T
+    gathered = jnp.einsum("tw,pt->wp", table, select, preferred_element_type=jnp.float32)
+    neigh_cols = gathered[:width].reshape(width, K, atoms)
+    coords_n = gathered[width : width + 3] * 16.0 + gathered[width + 3 : width + 6]
     delta = (coords_n.reshape(3, K, atoms) - positions.astype(jnp.float32)[:, None, :]) * (
         1.0 / 64.0
     )
@@ -216,18 +216,18 @@
             energy_proj,
         )
 
-    atom_energy, pull = jax.vjp(energy_of, delta, neigh_rows, proj_c.astype(jnp.float32))
+    atom_energy, pull = jax.vjp(energy_of, delta, neigh_cols, proj_c.astype(jnp.float32).T)
     grad_delta, grad_neigh, grad_centre = pull(jnp.ones_like(atom_energy))
-    pairs = grad_neigh.shape[0]
+    pairs = K * atoms
     grads = jnp.concatenate(
         [
-            grad_neigh,
-            grad_delta.reshape(3, pairs).T,
-            jnp.zeros((pairs, extra - 3), jnp.float32),
+            grad_neigh.reshape(width, pairs),
+            grad_delta.reshape(3, pairs),
+            jnp.zeros((extra - 3, pairs), jnp.float32),
         ],
-        axis=1,
-    )
-    sums = spread(select, grads)
+        axis=0,
+    )
+    sums = spread_cols(select, grads).T
     own_pos = grad_delta.sum(axis=1)
     sums = sums - jnp.pad(own_pos.T, ((0, total_rows - atoms), (width, extra - 3)))
     for section in (2, 1, 0):
@@ -244,7 +244,7 @@
         )
     back_neigh = neigh_proj.astype(jnp.float32).T
     back_centre = centre_proj.astype(jnp.float32).T
-    latent_grad = jnp.dot(grad_centre, back_centre, precision=lax.Precision.HIGHEST)
+    latent_grad = jnp.dot(grad_centre.T, back_centre, precision=lax.Precision.HIGHEST)
     latent_grad = latent_grad + jnp.dot(
         sums[:, :width], back_neigh, precision=lax.Precision.HIGHEST
     )

time: 80.3 us -> 81.7 us (1.017)
  local copies, waits for them, and re-layouts: 13.4 us -> 20.4 us
  matrix products: 26.5 us -> 24 us
  other arithmetic: 6.91 us -> 4.41 us
  waiting for transfers between devices: 15.4 us -> 14.5 us
    reduce_sum x1, other arithmetic: 3.59 us -> 1 us  [pair_energy(): by_order(amplitude) * harmonics[:, None] * environment[:, :, None, :]]
    slice x2, local copies, waits for them, and re-layouts: 0.4 us -> 2.11 us  [by_order(): values[1:2]]
    slice x2, local copies, waits for them, and re-layouts: 0.4 us -> 2.11 us  [by_order(): values[2:3]]
    slice x1, local copies, waits for them, and re-layouts: 0.24 us -> 1.48 us  [shards(): neigh_cols = gathered[:width].reshape(width, K, atoms)]
    broadcast_in_dim x2, local copies, waits for them, and re-layouts: 0.17 us -> 1.23 us  [by_order(): jnp.broadcast_to(values[2:3], (5,) + rest)]
    dot_general x7 -> x6, matrix products: 3.06 us -> 2.04 us  [spread(): jnp.einsum('nr,nw->rw', onehot, low, preferred_element_type=jnp.float32)]
    broadcast_in_dim x2, local copies, waits for them, and re-layouts: 0.11 us -> 1.11 us  [by_order(): jnp.broadcast_to(values[1:2], (3,) + rest)]
    slice x3, local copies, waits for them, and re-layouts: 4.02 us -> 3.04 us  [by_order(): values[0:1]]
  transfers between devices with their start and end apart: 12 -> 12, of which waited for: 9 -> 9; matrix products, arithmetic and copies ran while one was open for 6% -> 8% of each run, Pallas kernels for 0% -> 0%
where the time goes in v5:
time: 81.7 us; the launch traced here: 81.2 us
  matrix products  24 us (29%)
  local copies, waits for them, and re-layouts  20.4 us (25%)
  starting transfers between devices  15.5 us (19%)
  waiting for transfers between devices  14.5 us (18%)
  other arithmetic  4.41 us (5%)
  between operations  2.35 us (3%)
    ppermute x12, starting transfers between devices, passed_along(): return lax.ppermute(block, axis, route)  15.5 us
    ppermute x12, waiting for transfers between devices, passed_along(): return lax.ppermute(block, axis, route)  14.5 us
    dot_general x2, matrix products, pair_energy(): jnp.einsum('hka,hq->qka', hidden_low, split_proj, preferred_element_type=...  3.77 us
    unnamed x65, local copies, waits for them, and re-layouts  3.59 us
    slice x3, local copies, waits for them, and re-layouts, by_order(): values[0:1]  3.04 us
    dot_general x2, matrix products, pair_energy(): jnp.einsum('nka,nh->hka', basis, basis_proj.astype(jnp.float32), precisio...  2.32 us
    dot_general x3, matrix products, lookup(): return jnp.dot(onehot, table, precision=lax.Precision.HIGHEST)  2.25 us
    slice x2, local copies, waits for them, and re-layouts, by_order(): values[1:2]  2.11 us
  transfers between devices with their start and end apart: 12, of which 9 were waited for; matrix products, arithmetic and copies ran while one was open for 8% of the time, Pallas kernels for 0%

profile of v5, /device:TPU:0, one launch (start us, length us, event | category | flops | bytes accessed | tf_op | source)
XLA Modules:
  0.0 81.2 jit_solution(18036454852963517904)
XLA Ops:
  2.5 1.1 %fusion.75 = f32[128,512]{1,0:T(8,128)S(1)} fusion(f32[5,512]{1,0:T(8,128)} %param.25, s32[128]{0:T(128)} %param.18), kind=kOutput, calls=%fused_computation.137 | convolution fusion | flops 3932800 | bytes 272896 | tf_op jit(solution)/shard_map/dot_general | solution.py:141
  3.5 1.3 %fusion.52 = bf16[128,512]{1,0:T(8,128)(2,1)S(1)} fusion(f32[128,512]{1,0:T(8,128)S(1)} %fusion.75, bf16[128,512]{1,0:T(8,128)(2,1)} %param.16, bf16[512,512]{1,0:T(8,128)(2,1)} %param.23), kind=kOutput, calls=%fused_computation.78 | convolution fusion | flops 67239936 | bytes 1048576 | tf_op jit(solution)/shard_map/dot_general | solution.py:145
  5.8 1.9 %collective-permute-start.1 = (bf16[16,640]{1,0:T(8,128)(2,1)S(1)}, bf16[16,640]{1,0:T(8,128)(2,1)S(1)}, u32[]{:S(2)}, u32[]{:S(2)}) collective-permute-start(bf16[16,640]{1,0:T(8,128)(2,1)S(1)} %convolution_convert_fusion.6), channel_id=1, source_target_pairs={{8,0},{16,8},{24,16},{0,24},{9,1},{17,9},{25,17},{1,25},{10,2},{18... | collective-permute-start | bytes 61448 | tf_op jit(solution)/shard_map/ppermute | solution.py:28
  10.7 2.4 %collective-permute-start.2 = (bf16[64,640]{1,0:T(8,128)(2,1)S(1)}, bf16[64,640]{1,0:T(8,128)(2,1)S(1)}, u32[]{:S(2)}, u32[]{:S(2)}) collective-permute-start(bf16[64,640]{1,0:T(8,128)(2,1)S(1)} %convolution_convert_fusion.3), channel_id=1, source_target_pairs={{4,0},{0,4},{5,1},{1,5},{6,2},{2,6},{7,3},{3,7},{12,8},{8,12},{13,... | collective-permute-start | bytes 245768 | tf_op jit(solution)/shard_map/ppermute | solution.py:28
  13.4 3.0 %collective-permute-done.2 = bf16[64,640]{1,0:T(8,128)(2,1)S(1)} collective-permute-done((bf16[64,640]{1,0:T(8,128)(2,1)S(1)}, bf16[64,640]{1,0:T(8,128)(2,1)S(1)}, u32[]{:S(2)}, u32[]{:S(2)}) %collective-permute-start.2) | collective-permute-done | bytes 81952 | tf_op jit(solution)/shard_map/ppermute | solution.py:28
  16.4 1.5 %collective-permute-done.3 = bf16[64,640]{1,0:T(8,128)(2,1)S(1)} collective-permute-done((bf16[64,640]{1,0:T(8,128)(2,1)S(1)}, bf16[64,640]{1,0:T(8,128)(2,1)S(1)}, u32[]{:S(2)}, u32[]{:S(2)}) %collective-permute-start.3) | collective-permute-done | bytes 81952 | tf_op jit(solution)/shard_map/ppermute | solution.py:28
  18.2 1.6 %collective-permute-start.4 = (bf16[16,640]{1,0:T(8,128)(2,1)S(1)}, bf16[16,640]{1,0:T(8,128)(2,1)S(1)}, u32[]{:S(2)}, u32[]{:S(2)}) collective-permute-start(bf16[16,640]{1,0:T(8,128)(2,1)S(1)} %convolution_convert_fusion.5), channel_id=1, source_target_pairs={{3,0},{0,1},{1,2},{2,3},{7,4},{4,5},{5,6},{6,7},{11,8},{8,9},{9,10... | collective-permute-start | bytes 61448 | tf_op jit(solution)/shard_map/ppermute | solution.py:28
  20.1 2.3 %collective-permute-start.5 = (bf16[16,640]{1,0:T(8,128)(2,1)S(1)}, bf16[16,640]{1,0:T(8,128)(2,1)S(1)}, u32[]{:S(2)}, u32[]{:S(2)}) collective-permute-start(bf16[16,640]{1,0:T(8,128)(2,1)S(1)} %convolution_convert_fusion.4), channel_id=1, source_target_pairs={{1,0},{2,1},{3,2},{0,3},{5,4},{6,5},{7,6},{4,7},{9,8},{10,9},{11,1... | collective-permute-start | bytes 61448 | tf_op jit(solution)/shard_map/ppermute | solution.py:28
  22.4 1.5 %collective-permute-done.4 = bf16[16,640]{1,0:T(8,128)(2,1)S(1)} collective-permute-done((bf16[16,640]{1,0:T(8,128)(2,1)S(1)}, bf16[16,640]{1,0:T(8,128)(2,1)S(1)}, u32[]{:S(2)}, u32[]{:S(2)}) %collective-permute-start.4) | collective-permute-done | bytes 20512 | tf_op jit(solution)/shard_map/ppermute | solution.py:28
  24.1 1.0 %fusion.33 = f32[640,1024]{1,0:T(8,128)S(1)} fusion(bf16[320,640]{1,0:T(8,128)(2,1)S(1)} %constant_dynamic-update-slice_fusion.3, s32[1024]{0:T(1024)S(1)} %bitcast.197), kind=kOutput, calls=%fused_computation.51 | convolution fusion | flops 419758080 | bytes 3035136 | tf_op jit(solution)/shard_map/tw,pt->wp/dot_general | solution.py:197
  25.1 1.5 %slice.168 = f32[512,1024]{1,0:T(8,128)} slice(f32[640,1024]{1,0:T(8,128)S(1)} %fusion.33), slice={[0:512], [0:1024]} | slice | bytes 4194304 | tf_op jit(solution)/shard_map/slice | solution.py:198
  26.8 2.1 %copy.94 = f32[512,1024]{0,1:T(8,128)S(1)} copy(f32[512,1024]{1,0:T(8,128)} %slice.168) | data formatting | bytes 4194304 | tf_op jit(solution)/shard_map/reshape | solution.py:198
  29.0 1.2 %bitcast_add_fusion = f32[512,8,128]{0,2,1:T(8,128)S(1)} fusion(f32[512,8,128]{0,2,1:T(8,128)S(1)} %bitcast.176, f32[512,128]{0,1:T(8,128)S(1)} %copy.74, f32[8,128]{1,0:T(8,128)S(1)} %get-tuple-element.58, f32[8,128]{1,0:T(8,128)S(1)} %sqrt_bitcast_fusion, f32[8]{0:T(128)S(1)} %convert_multiply_fusion, bf16[8,512]{1,0:T(8,128)(2,1)S(1)} %copy-done.8), kind=kOutput, calls=%fused_computation.33 | convolution fusion | flops 51396608 | bytes 4472864 | tf_op jit(solution)/shard_map/jvp(nka,nh->hka)/dot_general | solution.py:64
  30.2 1.3 %copy-done.1 = f32[512,8,128]{0,2,1:T(8,128)} copy-done((f32[512,8,128]{0,2,1:T(8,128)}, f32[512,8,128]{0,2,1:T(8,128)S(1)}, u32[]{:S(2)}) %copy-start.1) | copy-done | bytes 2097176
  32.5 1.6 %slice_bitcast_fusion = (f32[1,64,8,128]{1,3,2,0:T(8,128)S(1)}, f32[64,8,128]{0,2,1:T(8,128)S(1)}, f32[64,8,128]{0,2,1:T(8,128)S(1)}, f32[64,8,128]{0,2,1:T(8,12...) fusion(f32[384,8,128]{0,2,1:T(8,128)S(1)} %convolution_bitcast_fusion), kind=kLoop, calls=%fused_computation.101 | loop fusion | bytes 3145728 | tf_op jit(solution)/shard_map/jvp()/slice | solution.py:35
  35.3 1.9 %copy.77 = f32[64,8,128]{2,0,1:T(8,128)} copy(f32[64,8,128]{0,2,1:T(8,128)} %get-tuple-element.34) | data formatting | bytes 524288 | tf_op jit(solution)/shard_map/jvp()/slice | solution.py:37
  37.2 1.9 %copy.76 = f32[64,8,128]{2,0,1:T(8,128)} copy(f32[64,8,128]{0,2,1:T(8,128)} %get-tuple-element.35) | data formatting | bytes 524288 | tf_op jit(solution)/shard_map/jvp()/slice | solution.py:36
  39.2 1.2 %copy.78 = f32[1,64,8,128]{3,1,2,0:T(8,128)S(1)} copy(f32[1,64,8,128]{1,3,2,0:T(8,128)} %get-tuple-element.36) | data formatting | bytes 524288 | tf_op jit(solution)/shard_map/jvp()/slice | solution.py:35
  40.4 1.1 %broadcast_in_dim.70 = f32[5,64,8,128]{3,1,2,0:T(8,128)S(1)} broadcast(f32[64,8,128]{2,0,1:T(8,128)} %copy.77), dimensions={1,2,3} | broadcast | bytes 1572864 | tf_op jit(solution)/shard_map/jvp()/broadcast_in_dim | solution.py:37
  41.5 1.0 %broadcast_in_dim.69 = f32[3,64,8,128]{3,1,2,0:T(8,128)S(1)} broadcast(f32[64,8,128]{2,0,1:T(8,128)} %copy.76), dimensions={1,2,3} | broadcast | bytes 1048576 | tf_op jit(solution)/shard_map/jvp()/broadcast_in_dim | solution.py:36
  45.7 1.1 %fusion.51 = f32[192,8,128]{2,0,1:T(8,128)S(1)} fusion(bf16[192,512]{1,0:T(8,128)(2,1)S(1)} %copy-done.7, f32[8,128,512]{2,1,0:T(8,128)S(1)} %convolution_add_fusion, f32[512]{0:T(512)S(1)} %copy-done.28, f32[8,128]{1,0:T(8,128)S(1)} %copy-done.18), kind=kOutput, calls=%fused_computation.68 | convolution fusion | flops 206962688 | bytes 3086336 | tf_op jit(solution)/shard_map/transpose(jvp(qka,qi->ika))/dot_general | solution.py:99
  49.0 1.1 %convolution_convert_fusion = bf16[8,128,512]{2,1,0:T(8,128)(2,1)S(1)} fusion(bf16[512,512]{1,0:T(8,128)(2,1)S(1)} %copy-done, f32[8,128,512]{2,1,0:T(8,128)S(1)} %convolution_add_fusion, f32[512]{0:T(512)S(1)} %copy-done.28, f32[8,128]{1,0:T(8,128)S(1)} %copy-done.18), kind=kOutput, calls=%fused_computation.52 | convolution fusion | flops 542638080 | bytes 3676160 | tf_op jit(solution)/shard_map/transpose(jvp(hka,hi->ika))/dot_general | solution.py:98
  51.9 2.8 %fusion.158 = (f32[512,128]{0,1:T(8,128)S(1)}, f32[512,8,128]{0,2,1:T(8,128)S(1)}, f32[8,128]{1,0:T(8,128)S(1)}, f32[8,128]{1,0:T(8,128)S(1)}) fusion(f32[512,8,128]{0,2,1:T(8,128)S(1)} %copy-done.2, f32[512]{0:T(512)S(1)} %copy-done.28, f32[8,128]{1,0:T(8,128)S(1)} %copy-done.18, f32[8,128,512]{2,1,0:T(8,128)S(1)} %convolution_add_fusion, ...), kind=kOutput, calls=%fused_computation.292 | convolution fusion | flops 416217088 | bytes 8796160 | tf_op jit(solution)/shard_map/transpose(jvp(hka,hq->qka))/dot_general | solution.py:69
  54.8 1.1 %fusion.86 = (f32[8,128]{1,0:T(8,128)S(1)}, f32[8,128]{1,0:T(8,128)S(1)}) fusion(f32[8,128]{1,0:T(8,128)S(1)} %get-tuple-element.58, f32[8,128]{1,0:T(8,128)S(1)} %sqrt_bitcast_fusion, f32[8]{0:T(128)S(1)} %copy-done.22, f32[512,8,128]{0,2,1:T(8,128)S(1)} %get-tuple-element.19, bf16[8,512]{1,0:T(8,128)(2,1)S(1)} %copy-done.8), kind=kOutput, calls=%fused_computation.170 | convolution fusion | flops 50386944 | bytes 2121760 | tf_op jit(solution)/shard_map/transpose(jvp(nka,nh->hka))/dot_general | solution.py:64
  58.3 1.4 %collective-permute-start.7 = (f32[16,640]{1,0:T(8,128)S(1)}, f32[16,640]{1,0:T(8,128)S(1)}, u32[]{:S(2)}, u32[]{:S(2)}) collective-permute-start(f32[16,640]{1,0:T(8,128)S(1)} %get-tuple-element.38), channel_id=1, source_target_pairs={{3,0},{0,1},{1,2},{2,3},{7,4},{4,5},{5,6},{6,7},{11,8},{8,9},{9,10... | collective-permute-start | bytes 122888 | tf_op jit(solution)/shard_map/ppermute | solution.py:28
  59.8 2.5 %collective-permute-start.6 = (f32[16,640]{1,0:T(8,128)S(1)}, f32[16,640]{1,0:T(8,128)S(1)}, u32[]{:S(2)}, u32[]{:S(2)}) collective-permute-start(f32[16,640]{1,0:T(8,128)S(1)} %get-tuple-element.37), channel_id=1, source_target_pairs={{1,0},{2,1},{3,2},{0,3},{5,4},{6,5},{7,6},{4,7},{9,8},{10,9},{11,1... | collective-permute-start | bytes 122888 | tf_op jit(solution)/shard_map/ppermute | solution.py:28
  62.3 1.9 %collective-permute-done.7 = f32[16,640]{1,0:T(8,128)S(1)} collective-permute-done((f32[16,640]{1,0:T(8,128)S(1)}, f32[16,640]{1,0:T(8,128)S(1)}, u32[]{:S(2)}, u32[]{:S(2)}) %collective-permute-start.7) | collective-permute-done | bytes 40992 | tf_op jit(solution)/shard_map/ppermute | solution.py:28
  65.8 1.6 %collective-permute-start.8 = (f32[64,640]{1,0:T(8,128)S(1)}, f32[64,640]{1,0:T(8,128)S(1)}, u32[]{:S(2)}, u32[]{:S(2)}) collective-permute-start(f32[64,640]{1,0:T(8,128)S(1)} %get-tuple-element.43), channel_id=1, source_target_pairs={{4,0},{0,4},{5,1},{1,5},{6,2},{2,6},{7,3},{3,7},{12,8},{8,12},{13,... | collective-permute-start | bytes 491528 | tf_op jit(solution)/shard_map/ppermute | solution.py:28
  68.7 2.6 %collective-permute-done.8 = f32[64,640]{1,0:T(8,128)S(1)} collective-permute-done((f32[64,640]{1,0:T(8,128)S(1)}, f32[64,640]{1,0:T(8,128)S(1)}, u32[]{:S(2)}, u32[]{:S(2)}) %collective-permute-start.8) | collective-permute-done | bytes 163872 | tf_op jit(solution)/shard_map/ppermute | solution.py:28
  71.9 1.6 %collective-permute-done.9 = f32[64,640]{1,0:T(8,128)S(1)} collective-permute-done((f32[64,640]{1,0:T(8,128)S(1)}, f32[64,640]{1,0:T(8,128)S(1)}, u32[]{:S(2)}, u32[]{:S(2)}) %collective-permute-start.9) | collective-permute-done | bytes 163872 | tf_op jit(solution)/shard_map/ppermute | solution.py:28
  76.6 1.9 %collective-permute-done.11 = f32[16,640]{1,0:T(8,128)S(1)} collective-permute-done((f32[16,640]{1,0:T(8,128)S(1)}, f32[16,640]{1,0:T(8,128)S(1)}, u32[]{:S(2)}, u32[]{:S(2)}) %collective-permute-start.11) | collective-permute-done | bytes 40992 | tf_op jit(solution)/shard_map/ppermute | solution.py:28
  79.2 1.4 %convolution_add_fusion.7 = f32[128,512]{1,0:T(8,128)} fusion(f32[128,512]{1,0:T(8,128)S(1)} %fusion.165, bf16[512,512]{1,0:T(8,128)(2,1)S(1)} %copy-done.5, f32[128,640]{1,0:T(8,128)S(1)} %fusion.67), kind=kOutput, calls=%fused_computation.74 | convolution fusion | flops 402718720 | bytes 1310720 | tf_op jit(solution)/shard_map/dot_general | solution.py:248
  (178 shorter events, 25.1 us)
Async XLA Ops:
  0.6 43.7 %copy-start = (bf16[512,512]{1,0:T(8,128)(2,1)S(1)}, bf16[512,512]{1,0:T(8,128)(2,1)}, u32[]{:S(2)}) copy-start(bf16[512,512]{1,0:T(8,128)(2,1)} %param.28) | copy-start | bytes 1572868
  0.6 7.2 %copy-start.10 = (s32[1,192]{1,0:T(1,128)S(1)}, s32[1,192]{1,0:T(1,128)}, u32[]{:S(2)}) copy-start(s32[1,192]{1,0:T(1,128)} %param.19) | copy-start | bytes 2308
  0.7 8.0 %copy-start.19 = (s32[128]{0:T(128)S(1)}, s32[128]{0:T(128)}, u32[]{:S(2)}) copy-start(s32[128]{0:T(128)} %param.18) | copy-start | bytes 1540
  0.7 8.4 %copy-start.6 = (bf16[128,512]{1,0:T(8,128)(2,1)S(1)}, bf16[128,512]{1,0:T(8,128)(2,1)}, u32[]{:S(2)}) copy-start(bf16[128,512]{1,0:T(8,128)(2,1)} %param.16) | copy-start | bytes 393220
  0.7 8.0 %copy-start.9 = (f32[5,512]{1,0:T(8,128)S(1)}, f32[5,512]{1,0:T(8,128)}, u32[]{:S(2)}) copy-start(f32[5,512]{1,0:T(8,128)} %param.24) | copy-start | bytes 30724
  0.7 8.4 %copy-start.3 = (bf16[512,512]{1,0:T(8,128)(2,1)S(1)}, bf16[512,512]{1,0:T(8,128)(2,1)}, u32[]{:S(2)}) copy-start(bf16[512,512]{1,0:T(8,128)(2,1)} %param.22) | copy-start | bytes 1572868
  2.5 5.3 %copy-start.11 = (s32[16]{0:T(128)}, s32[16]{0:T(128)S(1)}, u32[]{:S(2)}) copy-start(s32[16]{0:T(128)S(1)} %get-tuple-element.66) | copy-start | bytes 196
  2.5 7.0 %copy-start.15 = (s32[1024]{0:T(1024)S(1)}, s32[1024]{0:T(1024)}, u32[]{:S(2)}) copy-start(s32[1024]{0:T(1024)} %param.20) | copy-start | bytes 12292
  5.1 5.3 %collective-permute-start = (bf16[16,640]{1,0:T(8,128)(2,1)S(1)}, bf16[16,640]{1,0:T(8,128)(2,1)S(1)}, u32[]{:S(2)}, u32[]{:S(2)}) collective-permute-start(bf16[16,640]{1,0:T(8,128)(2,1)S(1)} %convolution_convert_fusion.7), channel_id=1, source_target_pairs={{24,0},{0,8},{8,16},{16,24},{25,1},{1,9},{9,17},{17,25},{26,2},{2,... | collective-permute-start | bytes 61448 | tf_op jit(solution)/shard_map/ppermute | solution.py:28
  5.8 4.7 %collective-permute-start.1 = (bf16[16,640]{1,0:T(8,128)(2,1)S(1)}, bf16[16,640]{1,0:T(8,128)(2,1)S(1)}, u32[]{:S(2)}, u32[]{:S(2)}) collective-permute-start(bf16[16,640]{1,0:T(8,128)(2,1)S(1)} %convolution_convert_fusion.6), channel_id=1, source_target_pairs={{8,0},{16,8},{24,16},{0,24},{9,1},{17,9},{25,17},{1,25},{10,2},{18... | collective-permute-start | bytes 61448 | tf_op jit(solution)/shard_map/ppermute | solution.py:28
  7.9 5.4 %copy-start.13 = (s32[64]{0:T(128)}, s32[64]{0:T(128)S(1)}, u32[]{:S(2)}) copy-start(s32[64]{0:T(128)S(1)} %get-tuple-element.68) | copy-start | bytes 772
  8.0 21.0 %copy-start.21 = (f32[8]{0:T(128)}, f32[8]{0:T(128)S(1)}, u32[]{:S(2)}) copy-start(f32[8]{0:T(128)S(1)} %convert_multiply_fusion) | copy-start | bytes 100
  9.5 19.4 %copy-start.23 = (f32[128]{0:T(128)}, f32[128]{0:T(128)S(1)}, u32[]{:S(2)}) copy-start(f32[128]{0:T(128)S(1)} %compare_convert_fusion) | copy-start | bytes 1540
  10.7 5.7 %collective-permute-start.2 = (bf16[64,640]{1,0:T(8,128)(2,1)S(1)}, bf16[64,640]{1,0:T(8,128)(2,1)S(1)}, u32[]{:S(2)}, u32[]{:S(2)}) collective-permute-start(bf16[64,640]{1,0:T(8,128)(2,1)S(1)} %convolution_convert_fusion.3), channel_id=1, source_target_pairs={{4,0},{0,4},{5,1},{1,5},{6,2},{2,6},{7,3},{3,7},{12,8},{8,12},{13,... | collective-permute-start | bytes 245768 | tf_op jit(solution)/shard_map/ppermute | solution.py:28
  13.4 4.6 %collective-permute-start.3 = (bf16[64,640]{1,0:T(8,128)(2,1)S(1)}, bf16[64,640]{1,0:T(8,128)(2,1)S(1)}, u32[]{:S(2)}, u32[]{:S(2)}) collective-permute-start(bf16[64,640]{1,0:T(8,128)(2,1)S(1)} %convolution_convert_fusion.2), channel_id=1, source_target_pairs={{4,0},{0,4},{5,1},{1,5},{6,2},{2,6},{7,3},{3,7},{12,8},{8,12},{13,... | collective-permute-start | bytes 245768 | tf_op jit(solution)/shard_map/ppermute | solution.py:28
  18.2 5.7 %collective-permute-start.4 = (bf16[16,640]{1,0:T(8,128)(2,1)S(1)}, bf16[16,640]{1,0:T(8,128)(2,1)S(1)}, u32[]{:S(2)}, u32[]{:S(2)}) collective-permute-start(bf16[16,640]{1,0:T(8,128)(2,1)S(1)} %convolution_convert_fusion.5), channel_id=1, source_target_pairs={{3,0},{0,1},{1,2},{2,3},{7,4},{4,5},{5,6},{6,7},{11,8},{8,9},{9,10... | collective-permute-start | bytes 61448 | tf_op jit(solution)/shard_map/ppermute | solution.py:28
  20.1 4.0 %collective-permute-start.5 = (bf16[16,640]{1,0:T(8,128)(2,1)S(1)}, bf16[16,640]{1,0:T(8,128)(2,1)S(1)}, u32[]{:S(2)}, u32[]{:S(2)}) collective-permute-start(bf16[16,640]{1,0:T(8,128)(2,1)S(1)} %convolution_convert_fusion.4), channel_id=1, source_target_pairs={{1,0},{2,1},{3,2},{0,3},{5,4},{6,5},{7,6},{4,7},{9,8},{10,9},{11,1... | collective-permute-start | bytes 61448 | tf_op jit(solution)/shard_map/ppermute | solution.py:28
  26.8 2.2 %copy-start.8 = (bf16[8,512]{1,0:T(8,128)(2,1)S(1)}, bf16[8,512]{1,0:T(8,128)(2,1)}, u32[]{:S(2)}) copy-start(bf16[8,512]{1,0:T(8,128)(2,1)} %param.26) | copy-start | bytes 24580
  29.0 2.6 %copy-start.26 = (bf16[512,384]{1,0:T(8,128)(2,1)S(1)}, bf16[512,384]{1,0:T(8,128)(2,1)}, u32[]{:S(2)}) copy-start(bf16[512,384]{1,0:T(8,128)(2,1)} %param.27) | copy-start | bytes 1179652
  51.9 2.9 %copy-start.22 = (f32[8]{0:T(128)S(1)}, f32[8]{0:T(128)}, u32[]{:S(2)}) copy-start(f32[8]{0:T(128)} %copy-done.21) | copy-start | bytes 100
  58.3 5.9 %collective-permute-start.7 = (f32[16,640]{1,0:T(8,128)S(1)}, f32[16,640]{1,0:T(8,128)S(1)}, u32[]{:S(2)}, u32[]{:S(2)}) collective-permute-start(f32[16,640]{1,0:T(8,128)S(1)} %get-tuple-element.38), channel_id=1, source_target_pairs={{3,0},{0,1},{1,2},{2,3},{7,4},{4,5},{5,6},{6,7},{11,8},{8,9},{9,10... | collective-permute-start | bytes 122888 | tf_op jit(solution)/shard_map/ppermute | solution.py:28
  59.8 5.2 %collective-permute-start.6 = (f32[16,640]{1,0:T(8,128)S(1)}, f32[16,640]{1,0:T(8,128)S(1)}, u32[]{:S(2)}, u32[]{:S(2)}) collective-permute-start(f32[16,640]{1,0:T(8,128)S(1)} %get-tuple-element.37), channel_id=1, source_target_pairs={{1,0},{2,1},{3,2},{0,3},{5,4},{6,5},{7,6},{4,7},{9,8},{10,9},{11,1... | collective-permute-start | bytes 122888 | tf_op jit(solution)/shard_map/ppermute | solution.py:28
  65.0 2.4 %copy-start.4 = (bf16[512,512]{1,0:T(8,128)(2,1)S(1)}, bf16[512,512]{1,0:T(8,128)(2,1)}, u32[]{:S(2)}) copy-start(bf16[512,512]{1,0:T(8,128)(2,1)} %param.22) | copy-start | bytes 1572868
  65.8 7.7 %copy-start.14 = (s32[64]{0:T(128)S(1)}, s32[64]{0:T(128)}, u32[]{:S(2)}) copy-start(s32[64]{0:T(128)} %copy-done.13) | copy-start | bytes 772
  65.8 5.4 %collective-permute-start.8 = (f32[64,640]{1,0:T(8,128)S(1)}, f32[64,640]{1,0:T(8,128)S(1)}, u32[]{:S(2)}, u32[]{:S(2)}) collective-permute-start(f32[64,640]{1,0:T(8,128)S(1)} %get-tuple-element.43), channel_id=1, source_target_pairs={{4,0},{0,4},{5,1},{1,5},{6,2},{2,6},{7,3},{3,7},{12,8},{8,12},{13,... | collective-permute-start | bytes 491528 | tf_op jit(solution)/shard_map/ppermute | solution.py:28
  68.1 6.2 %copy-start.20 = (s32[128]{0:T(128)S(1)}, s32[128]{0:T(128)}, u32[]{:S(2)}) copy-start(s32[128]{0:T(128)} %param.18) | copy-start | bytes 1540
  68.1 6.2 %copy-start.29 = (f32[5]{0:T(128)S(1)}, f32[5]{0:T(128)}, u32[]{:S(2)}) copy-start(f32[5]{0:T(128)} %param.31) | copy-start | bytes 64
  68.1 7.9 %copy-start.12 = (s32[16]{0:T(128)S(1)}, s32[16]{0:T(128)}, u32[]{:S(2)}) copy-start(s32[16]{0:T(128)} %copy-done.11) | copy-start | bytes 196
  68.1 5.4 %collective-permute-start.9 = (f32[64,640]{1,0:T(8,128)S(1)}, f32[64,640]{1,0:T(8,128)S(1)}, u32[]{:S(2)}, u32[]{:S(2)}) collective-permute-start(f32[64,640]{1,0:T(8,128)S(1)} %get-tuple-element.42), channel_id=1, source_target_pairs={{4,0},{0,4},{5,1},{1,5},{6,2},{2,6},{7,3},{3,7},{12,8},{8,12},{13,... | collective-permute-start | bytes 491528 | tf_op jit(solution)/shard_map/ppermute | solution.py:28
  73.8 5.3 %copy-start.5 = (bf16[512,512]{1,0:T(8,128)(2,1)S(1)}, bf16[512,512]{1,0:T(8,128)(2,1)}, u32[]{:S(2)}) copy-start(bf16[512,512]{1,0:T(8,128)(2,1)} %param.23) | copy-start | bytes 1572868
  74.2 1.7 %collective-permute-start.10 = (f32[16,640]{1,0:T(8,128)S(1)}, f32[16,640]{1,0:T(8,128)S(1)}, u32[]{:S(2)}, u32[]{:S(2)}) collective-permute-start(f32[16,640]{1,0:T(8,128)S(1)} %get-tuple-element.45), channel_id=1, source_target_pairs={{8,0},{16,8},{24,16},{0,24},{9,1},{17,9},{25,17},{1,25},{10,2},{18... | collective-permute-start | bytes 122888 | tf_op jit(solution)/shard_map/ppermute | solution.py:28
  75.1 3.4 %collective-permute-start.11 = (f32[16,640]{1,0:T(8,128)S(1)}, f32[16,640]{1,0:T(8,128)S(1)}, u32[]{:S(2)}, u32[]{:S(2)}) collective-permute-start(f32[16,640]{1,0:T(8,128)S(1)} %get-tuple-element.44), channel_id=1, source_target_pairs={{24,0},{0,8},{8,16},{16,24},{25,1},{1,9},{9,17},{17,25},{26,2},{2,... | collective-permute-start | bytes 122888 | tf_op jit(solution)/shard_map/ppermute | solution.py:28
  (10 other events, 12.6 us)

commit v6 on v3

--- a/solution.py
+++ b/solution.py
@@ -3,6 +3,8 @@
 import jax
 import jax.numpy as jnp
 from jax import lax
+from jax.experimental import pallas as pl
+from jax.experimental.pallas import tpu as pltpu
 from jax.sharding import PartitionSpec as P
 
 K = 8
@@ -40,19 +42,12 @@
     )
 
 
-def pair_energy(
-    delta,
-    neigh_rows,
-    centre_rows,
-    valid_pair,
-    basis_proj,
-    split_proj,
-    update_proj,
-    tensor_proj,
-    energy_proj,
-):
-    atoms = centre_rows.shape[0]
-    width = centre_rows.shape[1]
+ORDER_OF = (0, 1, 1, 1, 2, 2, 2, 2, 2)
+GROUPS = ((0,), (1, 2, 3), (4, 5, 6, 7, 8))
+
+
+def geometry(delta, valid_pair):
+    atoms = delta.shape[2]
     radius = jnp.sqrt(jnp.sum(delta * delta, axis=0) + SOFTEN)
     unit = delta / radius
     ratio = radius / CUTOFF
@@ -62,51 +57,225 @@
         jnp.sin(orders[:, None, None] * (math.pi / CUTOFF) * radius[None])
         * (envelope / radius)[None]
     )
-    radial = jnp.einsum(
-        "nka,nh->kah", basis, basis_proj.astype(jnp.float32), precision=lax.Precision.HIGHEST
-    )
-    hidden = (
-        jax.nn.silu(centre_rows[None] + neigh_rows.reshape(K, atoms, width) + radial)
-        * envelope[:, :, None]
-    )
-    hidden_low = hidden.astype(jnp.bfloat16)
-    mixed = jnp.einsum("kah,hq->qka", hidden_low, split_proj, preferred_element_type=jnp.float32)
-    amplitude = mixed[: 3 * CH].reshape(3, CH, K, atoms)
-    weights = mixed[3 * CH :].reshape(3, CH, K, atoms)
-    unit_x = unit[0]
-    unit_y = unit[1]
-    unit_z = unit[2]
-    root3 = math.sqrt(3.0)
-    root15 = math.sqrt(15.0)
-    root5 = math.sqrt(5.0)
+    ux, uy, uz = unit[0], unit[1], unit[2]
+    r3 = math.sqrt(3.0)
+    r15 = math.sqrt(15.0)
+    r5 = math.sqrt(5.0)
     harmonics = jnp.stack(
         [
-            jnp.ones_like(unit_x),
-            root3 * unit_x,
-            root3 * unit_y,
-            root3 * unit_z,
-            root15 * unit_x * unit_y,
-            root15 * unit_y * unit_z,
-            0.5 * root5 * (2.0 * unit_z * unit_z - unit_x * unit_x - unit_y * unit_y),
-            root15 * unit_x * unit_z,
-            0.5 * root15 * (unit_x * unit_x - unit_y * unit_y),
+            jnp.ones_like(ux),
+            r3 * ux,
+            r3 * uy,
+            r3 * uz,
+            r15 * ux * uy,
+            r15 * uy * uz,
+            0.5 * r5 * (2.0 * uz * uz - ux * ux - uy * uy),
+            r15 * ux * uz,
+            0.5 * r15 * (ux * ux - uy * uy),
         ],
         axis=0,
     )
-    gathered = by_order(weights) * harmonics[:, None]
-    environment = gathered.sum(axis=2) / math.sqrt(K)
-    products = by_order(amplitude) * harmonics[:, None] * environment[:, :, None, :]
-    scalars = jnp.stack([products[0], products[1:4].sum(axis=0), products[4:9].sum(axis=0)], axis=0)
-    scalars = scalars.reshape(3 * CH, K * atoms).astype(jnp.bfloat16)
-    flat_low = hidden_low.reshape(K * atoms, width)
-    update = jax.nn.silu(
-        jnp.dot(flat_low, update_proj, preferred_element_type=jnp.float32)
-        + jnp.einsum("qp,qh->ph", scalars, tensor_proj, preferred_element_type=jnp.float32)
-    )
-    energy = envelope * jnp.sum(
-        (hidden + update.reshape(K, atoms, width)) * energy_proj, axis=-1
-    )
-    return energy.sum(axis=0)
+    cols = jnp.concatenate([basis, envelope[None], harmonics], axis=0).reshape(18, K * atoms)
+    cols = jnp.concatenate([cols, jnp.zeros((128 - 18, K * atoms), jnp.float32)], axis=0)
+    return cols.T
+
+
+def _mm(a, b):
+    return jnp.dot(a, b, preferred_element_type=jnp.float32)
+
+
+def _sigmoid(v):
+    return 1.0 / (1.0 + jnp.exp(-v))
+
+
+def _pair_kernel(
+    rows_ref, centre_ref, geo_ref, basis_ref, split_ref, split_t_ref, update_ref,
+    update_t_ref, tensor_ref, tensor_t_ref, basis_t_ref, energy_w_ref,
+    grad_rows_ref, grad_centre_ref, grad_geo_ref, energy_ref,
+    pre_s, hidden_s, mixed_s, damp_s, dlow_s, dgeo_s, env_s, denv_s,
+):
+    atoms = centre_ref.shape[0]
+    f32 = jnp.float32
+    bf16 = jnp.bfloat16
+    lane = lax.broadcasted_iota(jnp.int32, (atoms, 128), 1)
+    inv_root = 1.0 / math.sqrt(K)
+    env_s[...] = jnp.zeros_like(env_s)
+    denv_s[...] = jnp.zeros_like(denv_s)
+
+    def block(k):
+        return pl.ds(pl.multiple_of(k * atoms, atoms), atoms)
+
+    def split_dot(values, weight_ref):
+        high = values.astype(bf16)
+        low = (values - high.astype(f32)).astype(bf16)
+        return _mm(high, weight_ref[...]) + _mm(low, weight_ref[...])
+
+    def first(k, carry):
+        at = block(k)
+        geo = geo_ref[at, :]
+        radial = split_dot(geo, basis_ref)
+        pre = centre_ref[...] + rows_ref[at, :].astype(f32) + radial
+        envelope = geo[:, 8:9]
+        hidden = pre * _sigmoid(pre) * envelope
+        pre_s[at, :] = pre
+        hidden_s[at, :] = hidden
+        mixed = _mm(hidden.astype(bf16), split_ref[...])
+        mixed_s[at, :] = mixed
+        for m in range(9):
+            l = ORDER_OF[m]
+            weight = mixed[:, (2 * l + 1) * 128 : (2 * l + 2) * 128]
+            env_s[m] = env_s[m] + weight * geo[:, 9 + m : 10 + m] * inv_root
+        return carry
+
+    lax.fori_loop(0, K, first, 0)
+
+    def second(k, energy):
+        at = block(k)
+        geo = geo_ref[at, :]
+        envelope = geo[:, 8:9]
+        hidden = hidden_s[at, :]
+        mixed = mixed_s[at, :]
+        parts = []
+        totals = []
+        for l in range(3):
+            total = 0.0
+            for m in GROUPS[l]:
+                total = total + geo[:, 9 + m : 10 + m] * env_s[m]
+            totals.append(total)
+            parts.append((mixed[:, 2 * l * 128 : (2 * l + 1) * 128] * total).astype(bf16))
+        scalars = jnp.concatenate(parts, axis=1)
+        z = _mm(hidden.astype(bf16), update_ref[...]) + _mm(scalars, tensor_ref[...])
+        gate = _sigmoid(z)
+        update = z * gate
+        readout = jnp.sum((hidden + update) * energy_w_ref[...], axis=1, keepdims=True)
+        energy = energy + envelope * readout
+        grad_sum = envelope * energy_w_ref[...]
+        dz = grad_sum * (gate * (1.0 + z * (1.0 - gate)))
+        dz_low = dz.astype(bf16)
+        dscalars = _mm(dz_low, tensor_t_ref[...])
+        dscalars = dscalars.astype(bf16).astype(f32)
+        dlow_s[at, :] = _mm(dz_low, update_t_ref[...])
+        dgeo = jnp.where(lane == 8, readout, 0.0)
+        for l in range(3):
+            ds = dscalars[:, l * 128 : (l + 1) * 128]
+            damp_s[at, l * 128 : (l + 1) * 128] = ds * totals[l]
+            dtotal = ds * mixed[:, 2 * l * 128 : (2 * l + 1) * 128]
+            for m in GROUPS[l]:
+                dgeo = dgeo + jnp.where(
+                    lane == 9 + m, jnp.sum(dtotal * env_s[m], axis=1, keepdims=True), 0.0
+                )
+                denv_s[m] = denv_s[m] + dtotal * geo[:, 9 + m : 10 + m]
+        dgeo_s[at, :] = dgeo
+        return energy
+
+    energy = lax.fori_loop(0, K, second, jnp.zeros((atoms, 1), f32))
+    energy_ref[...] = jnp.broadcast_to(energy, (atoms, 128))
+
+    def third(k, centre_grad):
+        at = block(k)
+        geo = geo_ref[at, :]
+        envelope = geo[:, 8:9]
+        mixed = mixed_s[at, :]
+        dgeo = dgeo_s[at, :]
+        dmixed = []
+        for l in range(3):
+            weight = mixed[:, (2 * l + 1) * 128 : (2 * l + 2) * 128]
+            dweight = 0.0
+            for m in GROUPS[l]:
+                y = geo[:, 9 + m : 10 + m]
+                dweight = dweight + denv_s[m] * y * inv_root
+                dgeo = dgeo + jnp.where(
+                    lane == 9 + m,
+                    jnp.sum(denv_s[m] * weight, axis=1, keepdims=True) * inv_root,
+                    0.0,
+                )
+            dmixed.append(damp_s[at, l * 128 : (l + 1) * 128])
+            dmixed.append(dweight)
+        dmixed = jnp.concatenate(dmixed, axis=1).astype(bf16)
+        dlow = dlow_s[at, :] + _mm(dmixed, split_t_ref[...])
+        dhidden = envelope * energy_w_ref[...] + dlow
+        pre = pre_s[at, :]
+        sig = _sigmoid(pre)
+        act = pre * sig
+        dgeo = dgeo + jnp.where(lane == 8, jnp.sum(dhidden * act, axis=1, keepdims=True), 0.0)
+        dpre = dhidden * envelope * (sig * (1.0 + pre * (1.0 - sig)))
+        grad_rows_ref[at, :] = dpre
+        dgeo = dgeo + split_dot(dpre, basis_t_ref)
+        grad_geo_ref[at, :] = dgeo
+        return centre_grad + dpre
+
+    grad_centre_ref[...] = lax.fori_loop(
+        0, K, third, jnp.zeros(grad_centre_ref.shape, f32)
+    )
+
+
+def pair_terms(rows, centre, geo, basis_proj, split_proj, update_proj, tensor_proj, energy_proj):
+    pairs, width = rows.shape
+    atoms = centre.shape[0]
+    f32 = jnp.float32
+    bf16 = jnp.bfloat16
+    blocks = []
+    for l in range(3):
+        blocks.append(split_proj[:, l * CH : (l + 1) * CH])
+        blocks.append(jnp.zeros((width, 128 - CH), bf16))
+        blocks.append(split_proj[:, 3 * CH + l * CH : 3 * CH + (l + 1) * CH])
+        blocks.append(jnp.zeros((width, 128 - CH), bf16))
+    split_pad = jnp.concatenate(blocks, axis=1)
+    tensor_pad = jnp.concatenate(
+        sum(
+            [
+                [tensor_proj[l * CH : (l + 1) * CH], jnp.zeros((128 - CH, width), bf16)]
+                for l in range(3)
+            ],
+            [],
+        ),
+        axis=0,
+    )
+    basis_pad = jnp.concatenate(
+        [basis_proj, jnp.zeros((128 - NB, width), bf16)], axis=0
+    )
+    vmem = pl.BlockSpec(memory_space=pltpu.VMEM)
+    outs = pl.pallas_call(
+        _pair_kernel,
+        out_shape=(
+            jax.ShapeDtypeStruct((pairs, width), f32),
+            jax.ShapeDtypeStruct((atoms, width), f32),
+            jax.ShapeDtypeStruct((pairs, 128), f32),
+            jax.ShapeDtypeStruct((atoms, 128), f32),
+        ),
+        in_specs=[vmem] * 12,
+        out_specs=(vmem, vmem, vmem, vmem),
+        scratch_shapes=[
+            pltpu.VMEM((pairs, width), f32),
+            pltpu.VMEM((pairs, width), f32),
+            pltpu.VMEM((pairs, 6 * 128), f32),
+            pltpu.VMEM((pairs, 3 * 128), f32),
+            pltpu.VMEM((pairs, width), f32),
+            pltpu.VMEM((pairs, 128), f32),
+            pltpu.VMEM((9, atoms, 128), f32),
+            pltpu.VMEM((9, atoms, 128), f32),
+        ],
+        compiler_params=pltpu.CompilerParams(vmem_limit_bytes=60 * 1024 * 1024),
+        cost_estimate=pl.CostEstimate(
+            flops=int(40 * pairs * width * 128), transcendentals=int(3 * pairs * width),
+            bytes_accessed=int(16 * pairs * width),
+        ),
+    )(
+        rows,
+        centre,
+        geo,
+        basis_pad,
+        split_pad,
+        split_pad.T,
+        update_proj,
+        update_proj.T,
+        tensor_pad,
+        tensor_pad.T,
+        basis_pad.T,
+        energy_proj.astype(f32)[None, :],
+    )
+    grad_rows, grad_centre, grad_geo, energy = outs
+    return grad_rows, grad_centre, grad_geo, energy[:, 0]
 
 
 def shards(
@@ -194,30 +363,29 @@
     select = (neighbour[:, None] == jnp.arange(total_rows, dtype=jnp.int32)[None, :]).astype(
         jnp.bfloat16
     )
-    gathered = jnp.dot(select, table, preferred_element_type=jnp.float32)
-    neigh_rows = gathered[:, :width]
-    coords_n = (gathered[:, width : width + 3] * 16.0 + gathered[:, width + 3 : width + 6]).T
+    neigh_rows = jnp.dot(select, table[:, :width], preferred_element_type=jnp.float32).astype(
+        jnp.bfloat16
+    )
+    gathered = jnp.dot(select, table[:, width:], preferred_element_type=jnp.float32)
+    coords_n = (gathered[:, 0:3] * 16.0 + gathered[:, 3:6]).T
     delta = (coords_n.reshape(3, K, atoms) - positions.astype(jnp.float32)[:, None, :]) * (
         1.0 / 64.0
     )
     live = (jnp.arange(atoms) < atom_count[0]).astype(jnp.float32)
     valid_pair = live[None, :]
 
-    def energy_of(delta_in, neigh_in, centre_in):
-        return pair_energy(
-            delta_in,
-            neigh_in,
-            centre_in,
-            valid_pair,
-            basis_proj,
-            split_proj,
-            update_proj,
-            tensor_proj,
-            energy_proj,
-        )
-
-    atom_energy, pull = jax.vjp(energy_of, delta, neigh_rows, proj_c.astype(jnp.float32))
-    grad_delta, grad_neigh, grad_centre = pull(jnp.ones_like(atom_energy))
+    geo, geo_pull = jax.vjp(lambda d: geometry(d, valid_pair), delta)
+    grad_neigh, grad_centre, grad_geo, atom_energy = pair_terms(
+        neigh_rows,
+        proj_c.astype(jnp.float32),
+        geo,
+        basis_proj,
+        split_proj,
+        update_proj,
+        tensor_proj,
+        energy_proj,
+    )
+    (grad_delta,) = geo_pull(grad_geo)
     pairs = grad_neigh.shape[0]
     grads = jnp.concatenate(
         [

time: 80.3 us -> 116 us (1.44)
  Pallas kernels: 0 us -> 23.8 us
  other arithmetic: 6.91 us -> 17.1 us
  local copies, waits for them, and re-layouts: 13.4 us -> 23.3 us
  matrix products: 26.5 us -> 19 us
  waiting for transfers between devices: 15.4 us -> 13.8 us
    pallas_call x0 -> x1, Pallas kernels: none -> 23.8 us  [pair_terms(): pl.pallas_call(_pair_kernel, out_shape=(jax.ShapeDtypeStruct((pairs, widt...]
    concatenate x0 -> x14, local copies, waits for them, and re-layouts: none -> 12 us  [the longest x9 8.77 us: geometry(): jnp.concatenate([basis, envelope[None], harmonics], axis=0)]
    dot_general x9 -> x2, matrix products: 13.4 us -> 2.31 us  [the longest x1 1.75 us: shards(): jnp.dot(select, table[:, :width], preferred_element_type=jnp.float32)]
    split x0 -> x1, other arithmetic: none -> 5.87 us  [geometry(): jnp.concatenate([basis, envelope[None], harmonics], axis=0)]
    slice x9 -> x3, local copies, waits for them, and re-layouts: 5.07 us -> 0.31 us  [the longest x1 0.19 us: pair_terms(): blocks.append(split_proj[:, 3 * CH + l * CH:3 * CH + (l + 1) * CH])]
    mul x4 -> x5, other arithmetic: 0.33 us -> 3.26 us  [the longest x1 2.67 us: geometry(): jnp.sin(orders[:, None, None] * (math.pi / CUTOFF) * radius[None])]
    transpose x0 -> x2, local copies, waits for them, and re-layouts: none -> 2.59 us  [the longest x1 1.88 us: geometry(): return cols.T]
    unnamed x13 -> x6, other arithmetic: 0.22 us -> 2.28 us
  transfers between devices with their start and end apart: 12 -> 12, of which waited for: 9 -> 9; matrix products, arithmetic and copies ran while one was open for 6% -> 15% of each run, Pallas kernels for 0% -> 0%
where the time goes in v6:
time: 116 us; the launch traced here: 115 us
  Pallas kernels  23.8 us (21%)
  local copies, waits for them, and re-layouts  23.3 us (20%)
  matrix products  19 us (16%)
  other arithmetic  17.1 us (15%)
  starting transfers between devices  16 us (14%)
  waiting for transfers between devices  13.8 us (12%)
  between operations  2.28 us (2%)
    pallas_call x1, Pallas kernels, pair_terms(): pl.pallas_call(_pair_kernel, out_shape=(jax.ShapeDtypeStruct((pairs, widt...  23.8 us
    ppermute x12, starting transfers between devices, passed_along(): return lax.ppermute(block, axis, route)  16 us
    ppermute x12, waiting for transfers between devices, passed_along(): return lax.ppermute(block, axis, route)  13.8 us
    concatenate x9, local copies, waits for them, and re-layouts, geometry(): jnp.concatenate([basis, envelope[None], harmonics], axis=0)  8.77 us
    split x1, other arithmetic, geometry(): jnp.concatenate([basis, envelope[None], harmonics], axis=0)  5.87 us
    dot_general x7, matrix products, spread(): jnp.einsum('nr,nw->rw', onehot, low, preferred_element_type=jnp.float32)  4.78 us
    unnamed x117, local copies, waits for them, and re-layouts  3.13 us
    dot_general x7, matrix products, spread(): jnp.einsum('nr,nw->rw', onehot, high, preferred_element_type=jnp.float32)  3.04 us
  transfers between devices with their start and end apart: 12, of which 9 were waited for; matrix products, arithmetic and copies ran while one was open for 15% of the time, Pallas kernels for 0%

profile of v6, /device:TPU:0, one launch (start us, length us, event | category | flops | bytes accessed | tf_op | source)
XLA Modules:
  0.0 115.2 jit_solution(12273377330813128991)
XLA Ops:
  1.6 1.4 %slice_bitcast_fusion = (s32[16]{0:T(128)}, s32[16]{0:T(128)S(1)}, s32[16]{0:T(128)S(1)}, s32[16]{0:T(128)}) fusion(s32[1,192]{1,0:T(1,128)} %param.19), kind=kLoop, calls=%fused_computation.250 | loop fusion | bytes 512 | tf_op jit(solution)/shard_map/eq | solution.py:351
  3.0 1.0 fusion.45
  4.0 1.3 %fusion.16 = bf16[128,512]{1,0:T(8,128)(2,1)S(1)} fusion(f32[128,512]{1,0:T(8,128)S(1)} %fusion.45, bf16[128,512]{1,0:T(8,128)(2,1)} %param.16, bf16[512,512]{1,0:T(8,128)(2,1)} %param.23), kind=kOutput, calls=%fused_computation.23 | convolution fusion | flops 67239936 | bytes 1048576 | tf_op jit(solution)/shard_map/dot_general | solution.py:321
  7.5 1.9 %collective-permute-start.1 = (bf16[16,640]{1,0:T(8,128)(2,1)}, bf16[16,640]{1,0:T(8,128)(2,1)}, u32[]{:S(2)}, u32[]{:S(2)}) collective-permute-start(bf16[16,640]{1,0:T(8,128)(2,1)} %convolution_convert_fusion.4), channel_id=1, source_target_pairs={{8,0},{16,8},{24,16},{0,24},{9,1},{17,9},{25,17},{1,25},{10,2},{18... | collective-permute-start | bytes 61448 | tf_op jit(solution)/shard_map/ppermute | solution.py:30
  17.3 1.2 %copy.156.split_ref = bf16[512,768]{1,0:T(8,128)(2,1)} copy(bf16[512,768]{0,1:T(8,128)(2,1)S(1)} %constant_dynamic-update-slice_fusion.8) | data formatting | bytes 1572864 | tf_op jit(solution)/shard_map/concatenate | solution.py:223
  21.0 1.0 copy.151
  24.5 2.4 %collective-permute-start.2 = (bf16[64,640]{1,0:T(8,128)(2,1)S(1)}, bf16[64,640]{1,0:T(8,128)(2,1)S(1)}, u32[]{:S(2)}, u32[]{:S(2)}) collective-permute-start(bf16[64,640]{1,0:T(8,128)(2,1)S(1)} %convolution_convert_fusion.1), channel_id=1, source_target_pairs={{4,0},{0,4},{5,1},{1,5},{6,2},{2,6},{7,3},{3,7},{12,8},{8,12},{13,... | collective-permute-start | bytes 245768 | tf_op jit(solution)/shard_map/ppermute | solution.py:30
  27.2 2.6 %collective-permute-done.2 = bf16[64,640]{1,0:T(8,128)(2,1)S(1)} collective-permute-done((bf16[64,640]{1,0:T(8,128)(2,1)S(1)}, bf16[64,640]{1,0:T(8,128)(2,1)S(1)}, u32[]{:S(2)}, u32[]{:S(2)}) %collective-permute-start.2) | collective-permute-done | bytes 81952 | tf_op jit(solution)/shard_map/ppermute | solution.py:30
  29.8 1.8 %collective-permute-done.3 = bf16[64,640]{1,0:T(8,128)(2,1)S(1)} collective-permute-done((bf16[64,640]{1,0:T(8,128)(2,1)S(1)}, bf16[64,640]{1,0:T(8,128)(2,1)S(1)}, u32[]{:S(2)}, u32[]{:S(2)}) %collective-permute-start.3) | collective-permute-done | bytes 81952 | tf_op jit(solution)/shard_map/ppermute | solution.py:30
  31.9 1.6 %collective-permute-start.4 = (bf16[16,640]{1,0:T(8,128)(2,1)S(1)}, bf16[16,640]{1,0:T(8,128)(2,1)S(1)}, u32[]{:S(2)}, u32[]{:S(2)}) collective-permute-start(bf16[16,640]{1,0:T(8,128)(2,1)S(1)} %convolution_convert_fusion.3), channel_id=1, source_target_pairs={{3,0},{0,1},{1,2},{2,3},{7,4},{4,5},{5,6},{6,7},{11,8},{8,9},{9,10... | collective-permute-start | bytes 61448 | tf_op jit(solution)/shard_map/ppermute | solution.py:30
  33.7 2.5 %collective-permute-start.5 = (bf16[16,640]{1,0:T(8,128)(2,1)S(1)}, bf16[16,640]{1,0:T(8,128)(2,1)S(1)}, u32[]{:S(2)}, u32[]{:S(2)}) collective-permute-start(bf16[16,640]{1,0:T(8,128)(2,1)S(1)} %convolution_convert_fusion.2), channel_id=1, source_target_pairs={{1,0},{2,1},{3,2},{0,3},{5,4},{6,5},{7,6},{4,7},{9,8},{10,9},{11,1... | collective-permute-start | bytes 61448 | tf_op jit(solution)/shard_map/ppermute | solution.py:30
  36.2 1.4 %collective-permute-done.4 = bf16[16,640]{1,0:T(8,128)(2,1)S(1)} collective-permute-done((bf16[16,640]{1,0:T(8,128)(2,1)S(1)}, bf16[16,640]{1,0:T(8,128)(2,1)S(1)}, u32[]{:S(2)}, u32[]{:S(2)}) %collective-permute-start.4) | collective-permute-done | bytes 20512 | tf_op jit(solution)/shard_map/ppermute | solution.py:30
  38.4 1.7 %fusion.5.rows_ref = bf16[1024,512]{1,0:T(8,128)(2,1)} fusion(s32[1024]{0:T(1024)S(1)} %bitcast.214, bf16[320,640]{1,0:T(8,128)(2,1)S(1)} %constant_dynamic-update-slice_fusion.3), kind=kOutput, calls=%fused_computation.8 | convolution fusion | flops 336396288 | bytes 1380352 | tf_op jit(solution)/shard_map/dot_general | solution.py:366
  41.5 1.0 copy.141
  42.5 1.0 copy.142
  43.6 1.0 copy.143
  44.6 1.0 copy.135
  45.6 2.7 %fusion.26 = f32[8,1024]{0,1:T(8,128)} fusion(f32[8]{0:T(128)S(1)} %copy-done.42, f32[1024]{0:T(1024)S(1)} %get-tuple-element.77, f32[1024]{0:T(1024)S(1)} %get-tuple-element.78), kind=kLoop, calls=%fused_computation.42 | loop fusion | flops 16384 | bytes 40992 | tf_op jit(solution)/shard_map/jvp()/mul | solution.py:57
  49.2 4.5 %concatenate.66 = f32[18,1024]{0,1:T(8,128)} concatenate(f32[8,1024]{0,1:T(8,128)} %fusion.26, f32[1,1024]{0,1:T(8,128)} %copy.135, f32[1,1024]{0,1:T(8,128)} %broadcast.366, f32[1,1024]{0,1:T(8,128)S(1)} %copy.136, f32[1,1024]{0,1:T(8,128)S(1)} %copy.137, f32[1,1024]{0,1:T(8,128)S(1)} %copy.138, f32[1,1024]{0,1:T(8,128)S(1)} %copy.139, f32[1,1024]{0,1:T(8,128)S(1)} %copy.140, ...), dimensions={0} | concatenate | bytes 147456 | tf_op jit(solution)/shard_map/jvp()/concatenate | solution.py:78
  53.7 1.9 %pad_bitcast_fusion.geo_ref = f32[1024,128]{1,0:T(8,128)} fusion(f32[18,1024]{0,1:T(8,128)} %concatenate.66), kind=kLoop, calls=%fused_computation.61 | loop fusion | bytes 598016 | tf_op jit(solution)/shard_map/jvp()/transpose | solution.py:80
  55.6 23.8 %shard_map.175 = (f32[1024,512]{1,0:T(8,128)}, f32[128,512]{1,0:T(8,128)}, f32[1024,128]{1,0:T(8,128)}, f32[128,128]{1,0:T(8,128)}) custom-call(bf16[1024,512]{1,0:T(8,128)(2,1)} %fusion.5.rows_ref, f32[128,512]{1,0:T(8,128)} %fusion.18.centre_ref, f32[1024,128]{1,0:T(8,128)} %pad_bitcast_fusion.geo_ref, bf16[128,512]{1,0:T(8,128)(2,1)} %concatenate.68.clone.basis_ref, ...), custom_call_target="tpu_custom_call" | custom-call | flops 2684354560 | bytes 8388608 | tf_op jit(solution)/shard_map/pallas_call | solution.py:238
  79.4 5.9 %slice_reduce_fusion = (f32[1024]{0:T(1024)S(1)}, f32[1024]{0:T(1024)S(1)}, f32[1024]{0:T(1024)S(1)}, f32[1024]{0:T(1024)S(1)}, f32[1024]{0:T(1024)S(1)}, /*inde...) fusion(f32[128,1024]{0,1:T(8,128)} %bitcast.189), kind=kLoop, calls=%fused_computation.47 | loop fusion | flops 5120 | bytes 73728 | tf_op jit(solution)/shard_map/transpose(jvp())/split | solution.py:78
  85.3 2.9 %fusion.27 = (f32[1024]{0:T(1024)S(1)}, f32[1024]{0:T(1024)S(1)}) fusion(f32[128,1024]{0,1:T(8,128)S(1)} %bitcast.190, f32[8]{0:T(128)S(1)} %copy-done.42, f32[1024]{0:T(1024)S(1)} %get-tuple-element.78, f32[1024]{0:T(1024)S(1)} %get-tuple-element.77), kind=kLoop, calls=%fused_computation.43 | loop fusion | flops 55296 | bytes 49184 | tf_op jit(solution)/shard_map/transpose(jvp())/reduce_sum | solution.py:57
  88.7 2.7 %fusion.1 = f32[320,640]{1,0:T(8,128)S(1)} fusion(f32[1024,3]{1,0:T(8,128)S(1)} %bitcast.194, f32[1024,512]{1,0:T(8,128)} %get-tuple-element.8, f32[640]{0:T(1024)S(1)} %copy-done.39, s32[1024]{0:T(1024)S(1)} %bitcast.215), kind=kOutput, calls=%fused_computation.4 | convolution fusion | flops 423690240 | bytes 2935296 | tf_op jit(solution)/shard_map/nr,nw->rw/dot_general | solution.py:329
  92.4 1.6 %collective-permute-start.7 = (f32[16,640]{1,0:T(8,128)S(1)}, f32[16,640]{1,0:T(8,128)S(1)}, u32[]{:S(2)}, u32[]{:S(2)}) collective-permute-start(f32[16,640]{1,0:T(8,128)S(1)} %get-tuple-element.44), channel_id=1, source_target_pairs={{3,0},{0,1},{1,2},{2,3},{7,4},{4,5},{5,6},{6,7},{11,8},{8,9},{9,10... | collective-permute-start | bytes 122888 | tf_op jit(solution)/shard_map/ppermute | solution.py:30
  94.0 2.8 %collective-permute-start.6 = (f32[16,640]{1,0:T(8,128)S(1)}, f32[16,640]{1,0:T(8,128)S(1)}, u32[]{:S(2)}, u32[]{:S(2)}) collective-permute-start(f32[16,640]{1,0:T(8,128)S(1)} %get-tuple-element.43), channel_id=1, source_target_pairs={{1,0},{2,1},{3,2},{0,3},{5,4},{6,5},{7,6},{4,7},{9,8},{10,9},{11,1... | collective-permute-start | bytes 122888 | tf_op jit(solution)/shard_map/ppermute | solution.py:30
  96.7 1.7 %collective-permute-done.7 = f32[16,640]{1,0:T(8,128)S(1)} collective-permute-done((f32[16,640]{1,0:T(8,128)S(1)}, f32[16,640]{1,0:T(8,128)S(1)}, u32[]{:S(2)}, u32[]{:S(2)}) %collective-permute-start.7) | collective-permute-done | bytes 40992 | tf_op jit(solution)/shard_map/ppermute | solution.py:30
  100.0 1.3 %collective-permute-start.8 = (f32[64,640]{1,0:T(8,128)S(1)}, f32[64,640]{1,0:T(8,128)S(1)}, u32[]{:S(2)}, u32[]{:S(2)}) collective-permute-start(f32[64,640]{1,0:T(8,128)S(1)} %get-tuple-element.46), channel_id=1, source_target_pairs={{4,0},{0,4},{5,1},{1,5},{6,2},{2,6},{7,3},{3,7},{12,8},{8,12},{13,... | collective-permute-start | bytes 491528 | tf_op jit(solution)/shard_map/ppermute | solution.py:30
  103.0 2.4 %collective-permute-done.8 = f32[64,640]{1,0:T(8,128)S(1)} collective-permute-done((f32[64,640]{1,0:T(8,128)S(1)}, f32[64,640]{1,0:T(8,128)S(1)}, u32[]{:S(2)}, u32[]{:S(2)}) %collective-permute-start.8) | collective-permute-done | bytes 163872 | tf_op jit(solution)/shard_map/ppermute | solution.py:30
  106.1 1.4 %collective-permute-done.9 = f32[64,640]{1,0:T(8,128)S(1)} collective-permute-done((f32[64,640]{1,0:T(8,128)S(1)}, f32[64,640]{1,0:T(8,128)S(1)}, u32[]{:S(2)}, u32[]{:S(2)}) %collective-permute-start.9) | collective-permute-done | bytes 163872 | tf_op jit(solution)/shard_map/ppermute | solution.py:30
  110.6 1.9 %collective-permute-done.11 = f32[16,640]{1,0:T(8,128)S(1)} collective-permute-done((f32[16,640]{1,0:T(8,128)S(1)}, f32[16,640]{1,0:T(8,128)S(1)}, u32[]{:S(2)}, u32[]{:S(2)}) %collective-permute-start.11) | collective-permute-done | bytes 40992 | tf_op jit(solution)/shard_map/ppermute | solution.py:30
  113.2 1.4 %convolution_add_fusion.6 = f32[128,512]{1,0:T(8,128)} fusion(f32[128,512]{1,0:T(8,128)S(1)} %fusion.136, bf16[512,512]{1,0:T(8,128)(2,1)S(1)} %copy-done.2, f32[128,640]{1,0:T(8,128)S(1)} %fusion.37), kind=kOutput, calls=%fused_computation.20 | convolution fusion | flops 402718720 | bytes 1310720 | tf_op jit(solution)/shard_map/dot_general | solution.py:416
  (207 shorter events, 28.1 us)
Async XLA Ops:
  0.6 15.5 %copy-start = (bf16[512,512]{1,0:T(8,128)(2,1)S(1)}, bf16[512,512]{1,0:T(8,128)(2,1)}, u32[]{:S(2)}) copy-start(bf16[512,512]{1,0:T(8,128)(2,1)} %param.22) | copy-start | bytes 1572868
  0.6 10.1 %copy-start.17 = (s32[1,192]{1,0:T(1,128)S(1)}, s32[1,192]{1,0:T(1,128)}, u32[]{:S(2)}) copy-start(s32[1,192]{1,0:T(1,128)} %param.19) | copy-start | bytes 2308
  0.7 13.1 %copy-start.3 = (bf16[512,384]{1,0:T(8,128)(2,1)S(1)}, bf16[512,384]{1,0:T(8,128)(2,1)}, u32[]{:S(2)}) copy-start(bf16[512,384]{1,0:T(8,128)(2,1)} %param.27) | copy-start | bytes 1179652
  1.6 11.5 %copy-start.10 = (bf16[6,128]{0,1:T(8,128)(2,1)}, bf16[6,128]{0,1:T(8,128)(2,1)S(1)}, u32[]{:S(2)}) copy-start(bf16[6,128]{0,1:T(8,128)(2,1)S(1)} %copy.133) | copy-start | bytes 4612
  3.0 11.0 %copy-start.26 = (s32[16]{0:T(128)}, s32[16]{0:T(128)S(1)}, u32[]{:S(2)}) copy-start(s32[16]{0:T(128)S(1)} %get-tuple-element.83) | copy-start | bytes 196
  3.0 11.0 %copy-start.30 = (s32[16]{0:T(128)}, s32[16]{0:T(128)S(1)}, u32[]{:S(2)}) copy-start(s32[16]{0:T(128)S(1)} %get-tuple-element.84) | copy-start | bytes 196
  5.4 7.7 %copy-start.12 = (bf16[128,122]{1,0:T(8,128)(2,1)}, bf16[128,122]{1,0:T(8,128)(2,1)S(1)}, u32[]{:S(2)}) copy-start(bf16[128,122]{1,0:T(8,128)(2,1)S(1)} %broadcast_in_dim.43) | copy-start | bytes 93700
  6.2 16.5 %collective-permute-start = (bf16[16,640]{1,0:T(8,128)(2,1)}, bf16[16,640]{1,0:T(8,128)(2,1)}, u32[]{:S(2)}, u32[]{:S(2)}) collective-permute-start(bf16[16,640]{1,0:T(8,128)(2,1)} %convolution_convert_fusion.5), channel_id=1, source_target_pairs={{24,0},{0,8},{8,16},{16,24},{25,1},{1,9},{9,17},{17,25},{26,2},{2,... | collective-permute-start | bytes 61448 | tf_op jit(solution)/shard_map/ppermute | solution.py:30
  7.5 15.9 %collective-permute-start.1 = (bf16[16,640]{1,0:T(8,128)(2,1)}, bf16[16,640]{1,0:T(8,128)(2,1)}, u32[]{:S(2)}, u32[]{:S(2)}) collective-permute-start(bf16[16,640]{1,0:T(8,128)(2,1)} %convolution_convert_fusion.4), channel_id=1, source_target_pairs={{8,0},{16,8},{24,16},{0,24},{9,1},{17,9},{25,17},{1,25},{10,2},{18... | collective-permute-start | bytes 61448 | tf_op jit(solution)/shard_map/ppermute | solution.py:30
  17.1 23.1 %copy-start.32 = (f32[128]{0:T(128)}, f32[128]{0:T(128)S(1)}, u32[]{:S(2)}) copy-start(f32[128]{0:T(128)S(1)} %compare_convert_fusion) | copy-start | bytes 1540
  17.3 21.1 %copy-start.37 = (s32[8,128]{1,0:T(8,128)}, s32[8,128]{1,0:T(8,128)S(1)}, u32[]{:S(2)}) copy-start(s32[8,128]{1,0:T(8,128)S(1)} %copy.132) | copy-start | bytes 12292
  18.9 7.9 %copy-start.14 = (bf16[320,640]{1,0:T(8,128)(2,1)S(1)}, bf16[320,640]{1,0:T(8,128)(2,1)}, u32[]{:S(2)}) copy-start(bf16[320,640]{1,0:T(8,128)(2,1)} %get-tuple-element.59) | copy-start | bytes 1228804
  18.9 8.0 %copy-start.34 = (s32[64]{0:T(128)S(1)}, s32[64]{0:T(128)}, u32[]{:S(2)}) copy-start(s32[64]{0:T(128)} %get-tuple-element.86) | copy-start | bytes 772
  19.4 10.4 %copy-start.4 = (bf16[384,512]{0,1:T(8,128)(2,1)}, bf16[384,512]{0,1:T(8,128)(2,1)S(1)}, u32[]{:S(2)}) copy-start(bf16[384,512]{0,1:T(8,128)(2,1)S(1)} %concatenate.70) | copy-start | bytes 1179652
  20.3 11.3 %copy-start.22 = (s32[16]{0:T(128)S(1)}, s32[16]{0:T(128)}, u32[]{:S(2)}) copy-start(s32[16]{0:T(128)} %get-tuple-element.85) | copy-start | bytes 196
  20.3 13.2 %copy-start.24 = (s32[16]{0:T(128)S(1)}, s32[16]{0:T(128)}, u32[]{:S(2)}) copy-start(s32[16]{0:T(128)} %get-tuple-element.82) | copy-start | bytes 196
  21.0 16.6 %copy-start.21 = (bf16[640]{0:T(1024)(128)(2,1)S(1)}, bf16[640]{0:T(1024)(128)(2,1)}, u32[]{:S(2)}) copy-start(bf16[640]{0:T(1024)(128)(2,1)} %select_convert_fusion.1) | copy-start | bytes 3844
  21.0 16.8 %copy-start.20 = (bf16[640]{0:T(1024)(128)(2,1)S(1)}, bf16[640]{0:T(1024)(128)(2,1)}, u32[]{:S(2)}) copy-start(bf16[640]{0:T(1024)(128)(2,1)} %select_convert_fusion) | copy-start | bytes 3844
  24.5 5.3 %collective-permute-start.2 = (bf16[64,640]{1,0:T(8,128)(2,1)S(1)}, bf16[64,640]{1,0:T(8,128)(2,1)S(1)}, u32[]{:S(2)}, u32[]{:S(2)}) collective-permute-start(bf16[64,640]{1,0:T(8,128)(2,1)S(1)} %convolution_convert_fusion.1), channel_id=1, source_target_pairs={{4,0},{0,4},{5,1},{1,5},{6,2},{2,6},{7,3},{3,7},{12,8},{8,12},{13,... | collective-permute-start | bytes 245768 | tf_op jit(solution)/shard_map/ppermute | solution.py:30
  27.1 4.5 %collective-permute-start.3 = (bf16[64,640]{1,0:T(8,128)(2,1)S(1)}, bf16[64,640]{1,0:T(8,128)(2,1)S(1)}, u32[]{:S(2)}, u32[]{:S(2)}) collective-permute-start(bf16[64,640]{1,0:T(8,128)(2,1)S(1)} %convolution_convert_fusion), channel_id=1, source_target_pairs={{4,0},{0,4},{5,1},{1,5},{6,2},{2,6},{7,3},{3,7},{12,8},{8,12},{13,... | collective-permute-start | bytes 245768 | tf_op jit(solution)/shard_map/ppermute | solution.py:30
  31.9 5.7 %collective-permute-start.4 = (bf16[16,640]{1,0:T(8,128)(2,1)S(1)}, bf16[16,640]{1,0:T(8,128)(2,1)S(1)}, u32[]{:S(2)}, u32[]{:S(2)}) collective-permute-start(bf16[16,640]{1,0:T(8,128)(2,1)S(1)} %convolution_convert_fusion.3), channel_id=1, source_target_pairs={{3,0},{0,1},{1,2},{2,3},{7,4},{4,5},{5,6},{6,7},{11,8},{8,9},{9,10... | collective-permute-start | bytes 61448 | tf_op jit(solution)/shard_map/ppermute | solution.py:30
  33.7 4.1 %collective-permute-start.5 = (bf16[16,640]{1,0:T(8,128)(2,1)S(1)}, bf16[16,640]{1,0:T(8,128)(2,1)S(1)}, u32[]{:S(2)}, u32[]{:S(2)}) collective-permute-start(bf16[16,640]{1,0:T(8,128)(2,1)S(1)} %convolution_convert_fusion.2), channel_id=1, source_target_pairs={{1,0},{2,1},{3,2},{0,3},{5,4},{6,5},{7,6},{4,7},{9,8},{10,9},{11,1... | collective-permute-start | bytes 61448 | tf_op jit(solution)/shard_map/ppermute | solution.py:30
  79.4 9.3 %copy-start.38 = (s32[8,128]{1,0:T(8,128)S(1)}, s32[8,128]{1,0:T(8,128)}, u32[]{:S(2)}) copy-start(s32[8,128]{1,0:T(8,128)} %copy-done.37) | copy-start | bytes 12292
  79.4 9.3 %copy-start.39 = (f32[640]{0:T(1024)S(1)}, f32[640]{0:T(1024)}, u32[]{:S(2)}) copy-start(f32[640]{0:T(1024)} %pad.21.clone) | copy-start | bytes 7684
  92.4 6.0 %collective-permute-start.7 = (f32[16,640]{1,0:T(8,128)S(1)}, f32[16,640]{1,0:T(8,128)S(1)}, u32[]{:S(2)}, u32[]{:S(2)}) collective-permute-start(f32[16,640]{1,0:T(8,128)S(1)} %get-tuple-element.44), channel_id=1, source_target_pairs={{3,0},{0,1},{1,2},{2,3},{7,4},{4,5},{5,6},{6,7},{11,8},{8,9},{9,10... | collective-permute-start | bytes 122888 | tf_op jit(solution)/shard_map/ppermute | solution.py:30
  94.0 5.2 %collective-permute-start.6 = (f32[16,640]{1,0:T(8,128)S(1)}, f32[16,640]{1,0:T(8,128)S(1)}, u32[]{:S(2)}, u32[]{:S(2)}) collective-permute-start(f32[16,640]{1,0:T(8,128)S(1)} %get-tuple-element.43), channel_id=1, source_target_pairs={{1,0},{2,1},{3,2},{0,3},{5,4},{6,5},{7,6},{4,7},{9,8},{10,9},{11,1... | collective-permute-start | bytes 122888 | tf_op jit(solution)/shard_map/ppermute | solution.py:30
  100.0 7.5 %copy-start.35 = (s32[64]{0:T(128)S(1)}, s32[64]{0:T(128)}, u32[]{:S(2)}) copy-start(s32[64]{0:T(128)} %get-tuple-element.86) | copy-start | bytes 772
  100.0 5.4 %collective-permute-start.8 = (f32[64,640]{1,0:T(8,128)S(1)}, f32[64,640]{1,0:T(8,128)S(1)}, u32[]{:S(2)}, u32[]{:S(2)}) collective-permute-start(f32[64,640]{1,0:T(8,128)S(1)} %get-tuple-element.46), channel_id=1, source_target_pairs={{4,0},{0,4},{5,1},{1,5},{6,2},{2,6},{7,3},{3,7},{12,8},{8,12},{13,... | collective-permute-start | bytes 491528 | tf_op jit(solution)/shard_map/ppermute | solution.py:30
  102.1 7.8 %copy-start.31 = (s32[16]{0:T(128)S(1)}, s32[16]{0:T(128)}, u32[]{:S(2)}) copy-start(s32[16]{0:T(128)} %copy-done.30) | copy-start | bytes 196
  102.1 5.4 %collective-permute-start.9 = (f32[64,640]{1,0:T(8,128)S(1)}, f32[64,640]{1,0:T(8,128)S(1)}, u32[]{:S(2)}, u32[]{:S(2)}) collective-permute-start(f32[64,640]{1,0:T(8,128)S(1)} %get-tuple-element.45), channel_id=1, source_target_pairs={{4,0},{0,4},{5,1},{1,5},{6,2},{2,6},{7,3},{3,7},{12,8},{8,12},{13,... | collective-permute-start | bytes 491528 | tf_op jit(solution)/shard_map/ppermute | solution.py:30
  108.2 1.7 %collective-permute-start.10 = (f32[16,640]{1,0:T(8,128)S(1)}, f32[16,640]{1,0:T(8,128)S(1)}, u32[]{:S(2)}, u32[]{:S(2)}) collective-permute-start(f32[16,640]{1,0:T(8,128)S(1)} %get-tuple-element.48), channel_id=1, source_target_pairs={{8,0},{16,8},{24,16},{0,24},{9,1},{17,9},{25,17},{1,25},{10,2},{18... | collective-permute-start | bytes 122888 | tf_op jit(solution)/shard_map/ppermute | solution.py:30
  109.1 3.4 %collective-permute-start.11 = (f32[16,640]{1,0:T(8,128)S(1)}, f32[16,640]{1,0:T(8,128)S(1)}, u32[]{:S(2)}, u32[]{:S(2)}) collective-permute-start(f32[16,640]{1,0:T(8,128)S(1)} %get-tuple-element.47), channel_id=1, source_target_pairs={{24,0},{0,8},{8,16},{16,24},{25,1},{1,9},{9,17},{17,25},{26,2},{2,... | collective-permute-start | bytes 122888 | tf_op jit(solution)/shard_map/ppermute | solution.py:30
  (25 other events, 110.6 us)

commit v7 on v6

v7 whole, which is shorter than its diff:
```python
import math

import jax
import jax.numpy as jnp
from jax import lax
from jax.experimental import pallas as pl
from jax.experimental.pallas import tpu as pltpu
from jax.sharding import PartitionSpec as P

K = 8
CH = 64
NB = 8
NSPEC = 5
LX_FIX = 1024
LY_FIX = 512
LZ_FIX = 1280


CUTOFF = 6.0
SOFTEN = 0.25


def shortened(shard):
    return jax.tree.map(lambda a: a.astype(jnp.bfloat16) if a.dtype == jnp.float32 else a, shard)


def passed_along(block, axis, distance):
    devices = range(lax.axis_size(axis))
    route = [((i - distance) % len(devices), i) for i in devices]
    return lax.ppermute(block, axis, route)


def by_order(values):
    rest = values.shape[1:]
    return jnp.concatenate(
        [
            values[0:1],
            jnp.broadcast_to(values[1:2], (3,) + rest),
            jnp.broadcast_to(values[2:3], (5,) + rest),
        ],
        axis=0,
    )


ORDER_OF = (0, 1, 1, 1, 2, 2, 2, 2, 2)
GROUPS = ((0,), (1, 2, 3), (4, 5, 6, 7, 8))


def geometry(delta, valid_pair):
    atoms = delta.shape[2]
    radius = jnp.sqrt(jnp.sum(delta * delta, axis=0) + SOFTEN)
    unit = delta / radius
    ratio = radius / CUTOFF
    envelope = jnp.where(ratio < 1.0, (1.0 - ratio * ratio) ** 2, 0.0) * valid_pair
    orders = jnp.arange(1, NB + 1).astype(jnp.float32)
    basis = (
        jnp.sin(orders[:, None, None] * (math.pi / CUTOFF) * radius[None])
        * (envelope / radius)[None]
    )
    ux, uy, uz = unit[0], unit[1], unit[2]
    r3 = math.sqrt(3.0)
    r15 = math.sqrt(15.0)
    r5 = math.sqrt(5.0)
    harmonics = jnp.stack(
        [
            jnp.ones_like(ux),
            r3 * ux,
            r3 * uy,
            r3 * uz,
            r15 * ux * uy,
            r15 * uy * uz,
            0.5 * r5 * (2.0 * uz * uz - ux * ux - uy * uy),
            r15 * ux * uz,
            0.5 * r15 * (ux * ux - uy * uy),
        ],
        axis=0,
    )
    rows = jnp.concatenate([basis, envelope[None], harmonics], axis=0).reshape(18, K * atoms)
    return jnp.concatenate([rows, jnp.zeros((128 - 18, K * atoms), jnp.float32)], axis=0)


def _mm(a, b):
    return jnp.dot(a, b, preferred_element_type=jnp.float32)


def _sigmoid(v):
    return 1.0 / (1.0 + jnp.exp(-v))


def _pair_kernel(
    rows_ref, centre_ref, geo_ref, basis_t_ref, split_t_ref, split_ref, update_t_ref,
    update_ref, tensor_t_ref, tensor_ref, basis_ref, energy_w_ref,
    grad_rows_ref, grad_centre_ref, grad_geo_ref, energy_ref,
    pre_s, hidden_s, mixed_s, damp_s, dlow_s, dgeo_s, env_s, denv_s,
):
    atoms = centre_ref.shape[1]
    f32 = jnp.float32
    bf16 = jnp.bfloat16
    sub = lax.broadcasted_iota(jnp.int32, (128, atoms), 0)
    inv_root = 1.0 / math.sqrt(K)
    env_s[...] = jnp.zeros_like(env_s)
    denv_s[...] = jnp.zeros_like(denv_s)

    def block(k):
        return pl.ds(pl.multiple_of(k * atoms, atoms), atoms)

    def split_mm(weight, values):
        high = values.astype(bf16)
        low = (values - high.astype(f32)).astype(bf16)
        return _mm(weight, high) + _mm(weight, low)

    def first(k, carry):
        at = block(k)
        geo = geo_ref[:, at]
        radial = split_mm(basis_t_ref[...], geo)
        pre = centre_ref[...] + rows_ref[:, at].astype(f32) + radial
        envelope = geo[8:9, :]
        hidden = pre * _sigmoid(pre) * envelope
        pre_s[:, at] = pre
        hidden_s[:, at] = hidden
        mixed = _mm(split_t_ref[...], hidden.astype(bf16))
        mixed_s[:, at] = mixed
        for m in range(9):
            l = ORDER_OF[m]
            weight = mixed[3 * CH + l * CH : 3 * CH + (l + 1) * CH, :]
            env_s[m] = env_s[m] + weight * (geo[9 + m : 10 + m, :] * inv_root)
        return carry

    lax.fori_loop(0, K, first, 0)

    def second(k, energy):
        at = block(k)
        geo = geo_ref[:, at]
        envelope = geo[8:9, :]
        hidden = hidden_s[:, at]
        mixed = mixed_s[:, at]
        parts = []
        totals = []
        for l in range(3):
            total = 0.0
            for m in GROUPS[l]:
                total = total + geo[9 + m : 10 + m, :] * env_s[m]
            totals.append(total)
            parts.append(mixed[l * CH : (l + 1) * CH, :] * total)
        scalars = jnp.concatenate(parts, axis=0).astype(bf16)
        z = _mm(update_t_ref[...], hidden.astype(bf16)) + _mm(tensor_t_ref[...], scalars)
        gate = _sigmoid(z)
        update = z * gate
        readout = jnp.sum((hidden + update) * energy_w_ref[...], axis=0, keepdims=True)
        energy = energy + envelope * readout
        dz = (envelope * energy_w_ref[...]) * (gate * (1.0 + z * (1.0 - gate)))
        dz_low = dz.astype(bf16)
        dscalars = _mm(tensor_ref[...], dz_low).astype(bf16).astype(f32)
        dlow_s[:, at] = _mm(update_ref[...], dz_low)
        dgeo = jnp.where(sub == 8, readout, 0.0)
        for l in range(3):
            ds = dscalars[l * CH : (l + 1) * CH, :]
            damp_s[l * CH : (l + 1) * CH, at] = ds * totals[l]
            dtotal = ds * mixed[l * CH : (l + 1) * CH, :]
            for m in GROUPS[l]:
                dgeo = dgeo + jnp.where(
                    sub == 9 + m, jnp.sum(dtotal * env_s[m], axis=0, keepdims=True), 0.0
                )
                denv_s[m] = denv_s[m] + dtotal * geo[9 + m : 10 + m, :]
        dgeo_s[:, at] = dgeo
        return energy

    energy = lax.fori_loop(0, K, second, jnp.zeros((1, atoms), f32))
    energy_ref[...] = jnp.broadcast_to(energy, energy_ref.shape)

    def third(k, centre_grad):
        at = block(k)
        geo = geo_ref[:, at]
        envelope = geo[8:9, :]
        mixed = mixed_s[:, at]
        dgeo = dgeo_s[:, at]
        dweights = []
        for l in range(3):
            weight = mixed[3 * CH + l * CH : 3 * CH + (l + 1) * CH, :]
            dweight = 0.0
            for m in GROUPS[l]:
                dweight = dweight + denv_s[m] * (geo[9 + m : 10 + m, :] * inv_root)
                dgeo = dgeo + jnp.where(
                    sub == 9 + m,
                    jnp.sum(denv_s[m] * weight, axis=0, keepdims=True) * inv_root,
                    0.0,
                )
            dweights.append(dweight)
        dmixed = jnp.concatenate([damp_s[:, at]] + dweights, axis=0).astype(bf16)
        dlow = dlow_s[:, at] + _mm(split_ref[...], dmixed)
        dhidden = envelope * energy_w_ref[...] + dlow
        pre = pre_s[:, at]
        sig = _sigmoid(pre)
        act = pre * sig
        dgeo = dgeo + jnp.where(sub == 8, jnp.sum(dhidden * act, axis=0, keepdims=True), 0.0)
        dpre = dhidden * envelope * (sig * (1.0 + pre * (1.0 - sig)))
        grad_rows_ref[:, at] = dpre
        dgeo = dgeo + split_mm(basis_ref[...], dpre)
        grad_geo_ref[:, at] = dgeo
        return centre_grad + dpre

    grad_centre_ref[...] = lax.fori_loop(0, K, third, jnp.zeros(grad_centre_ref.shape, f32))


def pair_terms(rows_t, centre_t, geo, basis_proj, split_proj, update_proj, tensor_proj, energy_proj):
    width, pairs = rows_t.shape
    atoms = centre_t.shape[1]
    f32 = jnp.float32
    bf16 = jnp.bfloat16
    basis_pad = jnp.concatenate([basis_proj, jnp.zeros((128 - NB, width), bf16)], axis=0)
    vmem = pl.BlockSpec(memory_space=pltpu.VMEM)
    outs = pl.pallas_call(
        _pair_kernel,
        out_shape=(
            jax.ShapeDtypeStruct((width, pairs), f32),
            jax.ShapeDtypeStruct((width, atoms), f32),
            jax.ShapeDtypeStruct((128, pairs), f32),
            jax.ShapeDtypeStruct((8, atoms), f32),
        ),
        in_specs=[vmem] * 12,
        out_specs=(vmem, vmem, vmem, vmem),
        scratch_shapes=[
            pltpu.VMEM((width, pairs), f32),
            pltpu.VMEM((width, pairs), f32),
            pltpu.VMEM((6 * CH, pairs), f32),
            pltpu.VMEM((3 * CH, pairs), f32),
            pltpu.VMEM((width, pairs), f32),
            pltpu.VMEM((128, pairs), f32),
            pltpu.VMEM((9, CH, atoms), f32),
            pltpu.VMEM((9, CH, atoms), f32),
        ],
        compiler_params=pltpu.CompilerParams(vmem_limit_bytes=60 * 1024 * 1024),
        cost_estimate=pl.CostEstimate(
            flops=int(24 * pairs * width * 128),
            transcendentals=int(3 * pairs * width),
            bytes_accessed=int(16 * pairs * width),
        ),
    )(
        rows_t,
        centre_t,
        geo,
        basis_pad.T,
        split_proj.T,
        split_proj,
        update_proj.T,
        update_proj,
        tensor_proj.T,
        tensor_proj,
        basis_pad,
        jnp.broadcast_to(energy_proj.astype(f32)[:, None], (width, atoms)),
    )
    grad_rows_t, grad_centre_t, grad_geo, energy = outs
    return grad_rows_t, grad_centre_t, grad_geo, energy[0]


def shards(
    latent,
    positions,
    species,
    send_list,
    neighbour,
    atom_count,
    centre_proj,
    neigh_proj,
    centre_table,
    neigh_table,
    basis_proj,
    split_proj,
    update_proj,
    tensor_proj,
    energy_proj,
    species_shift,
):
    atoms, width = latent.shape
    extra = 128
    face_x = atoms // 8
    face_y = atoms // 2
    face_z = atoms // 8
    lengths = [face_x, face_x, face_y, face_y, face_z, face_z]
    starts = [
        0,
        face_x,
        2 * face_x,
        2 * face_x + face_y,
        2 * face_x + 2 * face_y,
        2 * face_x + 2 * face_y + face_z,
    ]
    kinds = jnp.arange(NSPEC, dtype=jnp.int32)

    def lookup(codes, table):
        onehot = (codes[:, None] == kinds[None, :]).astype(jnp.float32)
        return jnp.dot(onehot, table, precision=lax.Precision.HIGHEST)

    def project(rows, codes, weight, table):
        return (
            jnp.dot(rows, weight, preferred_element_type=jnp.float32) + lookup(codes, table)
        ).astype(jnp.bfloat16)

    def spread_cols(onehot, values):
        high = values.astype(jnp.bfloat16)
        low = (values - high.astype(jnp.float32)).astype(jnp.bfloat16)
        return jnp.einsum(
            "wn,nr->wr", high, onehot, preferred_element_type=jnp.float32
        ) + jnp.einsum("wn,nr->wr", low, onehot, preferred_element_type=jnp.float32)

    def spread(onehot, values):
        high = values.astype(jnp.bfloat16)
        low = (values - high.astype(jnp.float32)).astype(jnp.bfloat16)
        return jnp.einsum(
            "nr,nw->rw", onehot, high, preferred_element_type=jnp.float32
        ) + jnp.einsum("nr,nw->rw", onehot, low, preferred_element_type=jnp.float32)

    proj_c = project(latent, species, centre_proj, centre_table)
    proj_n = project(latent, species, neigh_proj, neigh_table)
    send_rows = send_list[0]
    coarse = positions // 16
    fine = positions - coarse * 16
    coord_cols = jnp.concatenate([coarse, fine], axis=0).T.astype(jnp.bfloat16)
    table = jnp.concatenate(
        [proj_n, coord_cols, jnp.zeros((atoms, extra - 6), jnp.bfloat16)], axis=1
    )
    shifts = [(0, -LX_FIX), (0, LX_FIX), (1, -LY_FIX), (1, LY_FIX), (2, -LZ_FIX), (2, LZ_FIX)]
    sections = (("gx", (1, 0)), ("gy", (3, 2)), ("gz", (5, 4)))
    pickers = {}
    base_rows = []
    for section, (axis, segs) in enumerate(sections):
        rows_now = table.shape[0]
        base_rows.append(rows_now)
        parts = [table]
        for number, (segment, direction) in enumerate(((segs[0], 1), (segs[1], -1))):
            picked = send_rows[starts[segment] : starts[segment] + lengths[segment]]
            onehot = (
                picked[:, None] == jnp.arange(rows_now, dtype=jnp.int32)[None, :]
            ).astype(jnp.bfloat16)
            pickers[segment] = onehot
            out = jnp.dot(onehot, table, preferred_element_type=jnp.float32).astype(jnp.bfloat16)
            got = passed_along(out, axis, direction)
            coord_axis, offset = shifts[2 * section + number]
            columns = jnp.arange(width + extra, dtype=jnp.int32)[None, :]
            shift = jnp.where(columns == width + coord_axis, offset // 16, 0).astype(jnp.bfloat16)
            parts.append(got + shift)
        table = jnp.concatenate(parts, axis=0)
    total_rows = table.shape[0]
    neighbour = neighbour.reshape(atoms, K).T.reshape(-1)
    select = (neighbour[:, None] == jnp.arange(total_rows, dtype=jnp.int32)[None, :]).astype(
        jnp.bfloat16
    )
    gathered = jnp.einsum("tw,pt->wp", table, select, preferred_element_type=jnp.float32)
    neigh_cols = gathered[:width].astype(jnp.bfloat16)
    coords_n = gathered[width : width + 3] * 16.0 + gathered[width + 3 : width + 6]
    delta = (coords_n.reshape(3, K, atoms) - positions.astype(jnp.float32)[:, None, :]) * (
        1.0 / 64.0
    )
    live = (jnp.arange(atoms) < atom_count[0]).astype(jnp.float32)
    valid_pair = live[None, :]

    geo, geo_pull = jax.vjp(lambda d: geometry(d, valid_pair), delta)
    grad_neigh, grad_centre, grad_geo, atom_energy = pair_terms(
        neigh_cols,
        proj_c.astype(jnp.float32).T,
        geo,
        basis_proj,
        split_proj,
        update_proj,
        tensor_proj,
        energy_proj,
    )
    (grad_delta,) = geo_pull(grad_geo)
    pairs = grad_neigh.shape[1]
    grads = jnp.concatenate(
        [
            grad_neigh,
            grad_delta.reshape(3, pairs),
            jnp.zeros((extra - 3, pairs), jnp.float32),
        ],
        axis=0,
    )
    sums = spread_cols(select, grads).T
    own_pos = grad_delta.sum(axis=1)
    sums = sums - jnp.pad(own_pos.T, ((0, total_rows - atoms), (width, extra - 3)))
    for section in (2, 1, 0):
        axis, segs = sections[section]
        rows_now = base_rows[section]
        first = atoms + starts[2 * section]
        second = atoms + starts[2 * section + 1]
        back_first = passed_along(sums[first : first + lengths[2 * section]], axis, -1)
        back_second = passed_along(sums[second : second + lengths[2 * section + 1]], axis, 1)
        sums = (
            sums[:rows_now]
            + spread(pickers[segs[0]], back_first)
            + spread(pickers[segs[1]], back_second)
        )
    back_neigh = neigh_proj.astype(jnp.float32).T
    back_centre = centre_proj.astype(jnp.float32).T
    latent_grad = jnp.dot(grad_centre.T, back_centre, precision=lax.Precision.HIGHEST)
    latent_grad = latent_grad + jnp.dot(
        sums[:, :width], back_neigh, precision=lax.Precision.HIGHEST
    )
    forces = -sums[:, width : width + 3].T
    energies = live * (lookup(species, species_shift[:, None])[:, 0] + atom_energy)
    return (energies, forces, latent_grad)


def solution(mesh):
    in_specs = (
        P(("gx", "gy", "gz"), None),
        P(None, ("gx", "gy", "gz")),
        P(("gx", "gy", "gz")),
        P(("gx", "gy", "gz"), None),
        P(("gx", "gy", "gz")),
        P(("gx", "gy", "gz")),
        P(),
        P(),
        P(),
        P(),
        P(),
        P(),
        P(),
        P(),
        P(),
        P(),
    )
    out_specs = (P(("gx", "gy", "gz")), P(None, ("gx", "gy", "gz")), P(("gx", "gy", "gz"), None))
    return jax.shard_map(shards, mesh=mesh, in_specs=in_specs, out_specs=out_specs, check_vma=False)
```

time: 116 us -> 82.6 us (0.71)
  local copies, waits for them, and re-layouts: 23.3 us -> 9.33 us
  other arithmetic: 17.1 us -> 3.43 us
  Pallas kernels: 23.8 us -> 21 us
  matrix products: 19 us -> 17.1 us
    concatenate x9 -> x1, local copies, waits for them, and re-layouts: 8.77 us -> 0.09 us  [geometry(): jnp.concatenate([basis, envelope[None], harmonics], axis=0)]
    split x1 -> x0, other arithmetic: 5.87 us -> none  [geometry(): jnp.concatenate([basis, envelope[None], harmonics], axis=0)]
    pallas_call x1, Pallas kernels: 23.8 us -> 21 us  [pair_terms(): pl.pallas_call(_pair_kernel, out_shape=(jax.ShapeDtypeStruct((width, pair...]
    dot_general x7 -> x6, matrix products: 4.78 us -> 2.04 us  [spread(): jnp.einsum('nr,nw->rw', onehot, low, preferred_element_type=jnp.float32)]
    dot_general x3 -> x4, matrix products: 2.96 us -> 5.65 us  [the longest x1 2.82 us: spread_cols(): jnp.einsum('wn,nr->wr', high, onehot, preferred_element_type=jnp.float32)]
    mul x1, other arithmetic: 2.67 us -> 0.19 us  [geometry(): jnp.sin(orders[:, None, None] * (math.pi / CUTOFF) * radius[None])]
    concatenate x5 -> x2, local copies, waits for them, and re-layouts: 3.21 us -> 0.93 us  [the longest x1 0.85 us: geometry(): jnp.concatenate([rows, jnp.zeros((128 - 18, K * atoms), jnp.float32)], ax...]
    unnamed x6, other arithmetic: 2.28 us -> 0.18 us
  transfers between devices with their start and end apart: 12 -> 12, of which waited for: 9 -> 9; matrix products, arithmetic and copies ran while one was open for 15% -> 13% of each run, Pallas kernels for 0% -> 0%
where the time goes in v7:
time: 82.6 us; the launch traced here: 82.2 us
  Pallas kernels  21 us (25%)
  matrix products  17.1 us (21%)
  starting transfers between devices  15.5 us (19%)
  waiting for transfers between devices  14.1 us (17%)
  local copies, waits for them, and re-layouts  9.33 us (11%)
  other arithmetic  3.43 us (4%)
  between operations  1.83 us (2%)
    pallas_call x1, Pallas kernels, pair_terms(): pl.pallas_call(_pair_kernel, out_shape=(jax.ShapeDtypeStruct((width, pair...  21 us
    ppermute x12, starting transfers between devices, passed_along(): return lax.ppermute(block, axis, route)  15.5 us
    ppermute x12, waiting for transfers between devices, passed_along(): return lax.ppermute(block, axis, route)  14.1 us
    unnamed x40, local copies, waits for them, and re-layouts  3.57 us
    dot_general x1, matrix products, spread_cols(): jnp.einsum('wn,nr->wr', high, onehot, preferred_element_type=jnp.float32)  2.82 us
    dot_general x2, matrix products, project(): jnp.dot(rows, weight, preferred_element_type=jnp.float32)  2.45 us
    dot_general x3, matrix products, lookup(): return jnp.dot(onehot, table, precision=lax.Precision.HIGHEST)  2.24 us
    dot_general x6, matrix products, spread(): jnp.einsum('nr,nw->rw', onehot, high, preferred_element_type=jnp.float32)  2.09 us
  transfers between devices with their start and end apart: 12, of which 9 were waited for; matrix products, arithmetic and copies ran while one was open for 13% of the time, Pallas kernels for 0%

profile of v7, /device:TPU:0, one launch (start us, length us, event | category | flops | bytes accessed | tf_op | source)
XLA Modules:
  0.0 82.2 jit_solution(14506209038942432517)
XLA Ops:
  1.7 0.8 slice_bitcast_fusion
  2.5 1.0 %fusion.27 = f32[128,512]{1,0:T(8,128)S(1)} fusion(f32[5,512]{1,0:T(8,128)} %param.25, s32[128]{0:T(128)} %param.18), kind=kOutput, calls=%fused_computation.59 | convolution fusion | flops 3932800 | bytes 272896 | tf_op jit(solution)/shard_map/dot_general | solution.py:292
  3.5 1.4 %fusion.11 = bf16[128,512]{1,0:T(8,128)(2,1)S(1)} fusion(f32[128,512]{1,0:T(8,128)S(1)} %fusion.27, bf16[128,512]{1,0:T(8,128)(2,1)} %param.16, bf16[512,512]{1,0:T(8,128)(2,1)} %param.23), kind=kOutput, calls=%fused_computation.24 | convolution fusion | flops 67239936 | bytes 1048576 | tf_op jit(solution)/shard_map/dot_general | solution.py:296
  5.8 2.0 %collective-permute-start.1 = (bf16[16,640]{1,0:T(8,128)(2,1)S(1)}, bf16[16,640]{1,0:T(8,128)(2,1)S(1)}, u32[]{:S(2)}, u32[]{:S(2)}) collective-permute-start(bf16[16,640]{1,0:T(8,128)(2,1)S(1)} %convolution_convert_fusion.4), channel_id=1, source_target_pairs={{8,0},{16,8},{24,16},{0,24},{9,1},{17,9},{25,17},{1,25},{10,2},{18... | collective-permute-start | bytes 61448 | tf_op jit(solution)/shard_map/ppermute | solution.py:30
  9.8 1.1 %fusion.13.centre_ref = f32[512,128]{1,0:T(8,128)} fusion(f32[512,128]{1,0:T(8,128)S(1)} %convolution_bitcast_fusion, bf16[512,512]{1,0:T(8,128)(2,1)S(1)} %copy-done, bf16[128,512]{1,0:T(8,128)(2,1)S(1)} %copy-done.3), kind=kOutput, calls=%fused_computation.26 | convolution fusion | flops 67305472 | bytes 1179648 | tf_op jit(solution)/shard_map/dot_general | solution.py:296
  11.8 1.0 %copy.56 = bf16[512,512]{0,1:T(8,128)(2,1)} copy(bf16[512,512]{1,0:T(8,128)(2,1)S(1)} %copy-done.2) | data formatting | bytes 1048576 | tf_op args[12]
  12.8 1.0 %copy.55 = bf16[512,384]{0,1:T(8,128)(2,1)} copy(bf16[512,384]{1,0:T(8,128)(2,1)S(1)} %copy-done.4) | data formatting | bytes 786432 | tf_op args[11]
  13.8 0.8 %copy.57 = bf16[192,512]{0,1:T(8,128)(2,1)} copy(bf16[192,512]{1,0:T(8,128)(2,1)S(1)} %copy-done.6) | data formatting | bytes 393216 | tf_op args[13]
  15.0 2.4 %collective-permute-start.2 = (bf16[64,640]{1,0:T(8,128)(2,1)S(1)}, bf16[64,640]{1,0:T(8,128)(2,1)S(1)}, u32[]{:S(2)}, u32[]{:S(2)}) collective-permute-start(bf16[64,640]{1,0:T(8,128)(2,1)S(1)} %convolution_convert_fusion.1), channel_id=1, source_target_pairs={{4,0},{0,4},{5,1},{1,5},{6,2},{2,6},{7,3},{3,7},{12,8},{8,12},{13,... | collective-permute-start | bytes 245768 | tf_op jit(solution)/shard_map/ppermute | solution.py:30
  17.7 2.6 %collective-permute-done.2 = bf16[64,640]{1,0:T(8,128)(2,1)S(1)} collective-permute-done((bf16[64,640]{1,0:T(8,128)(2,1)S(1)}, bf16[64,640]{1,0:T(8,128)(2,1)S(1)}, u32[]{:S(2)}, u32[]{:S(2)}) %collective-permute-start.2) | collective-permute-done | bytes 81952 | tf_op jit(solution)/shard_map/ppermute | solution.py:30
  20.3 1.8 %collective-permute-done.3 = bf16[64,640]{1,0:T(8,128)(2,1)S(1)} collective-permute-done((bf16[64,640]{1,0:T(8,128)(2,1)S(1)}, bf16[64,640]{1,0:T(8,128)(2,1)S(1)}, u32[]{:S(2)}, u32[]{:S(2)}) %collective-permute-start.3) | collective-permute-done | bytes 81952 | tf_op jit(solution)/shard_map/ppermute | solution.py:30
  22.3 1.6 %collective-permute-start.4 = (bf16[16,640]{1,0:T(8,128)(2,1)S(1)}, bf16[16,640]{1,0:T(8,128)(2,1)S(1)}, u32[]{:S(2)}, u32[]{:S(2)}) collective-permute-start(bf16[16,640]{1,0:T(8,128)(2,1)S(1)} %convolution_convert_fusion.3), channel_id=1, source_target_pairs={{3,0},{0,1},{1,2},{2,3},{7,4},{4,5},{5,6},{6,7},{11,8},{8,9},{9,10... | collective-permute-start | bytes 61448 | tf_op jit(solution)/shard_map/ppermute | solution.py:30
  24.2 2.3 %collective-permute-start.5 = (bf16[16,640]{1,0:T(8,128)(2,1)S(1)}, bf16[16,640]{1,0:T(8,128)(2,1)S(1)}, u32[]{:S(2)}, u32[]{:S(2)}) collective-permute-start(bf16[16,640]{1,0:T(8,128)(2,1)S(1)} %convolution_convert_fusion.2), channel_id=1, source_target_pairs={{1,0},{2,1},{3,2},{0,3},{5,4},{6,5},{7,6},{4,7},{9,8},{10,9},{11,1... | collective-permute-start | bytes 61448 | tf_op jit(solution)/shard_map/ppermute | solution.py:30
  26.5 1.5 %collective-permute-done.4 = bf16[16,640]{1,0:T(8,128)(2,1)S(1)} collective-permute-done((bf16[16,640]{1,0:T(8,128)(2,1)S(1)}, bf16[16,640]{1,0:T(8,128)(2,1)S(1)}, u32[]{:S(2)}, u32[]{:S(2)}) %collective-permute-start.4) | collective-permute-done | bytes 20512 | tf_op jit(solution)/shard_map/ppermute | solution.py:30
  28.2 1.0 %fusion.2 = f32[640,1024]{1,0:T(8,128)S(1)} fusion(bf16[320,640]{1,0:T(8,128)(2,1)S(1)} %constant_dynamic-update-slice_fusion.3, s32[1024]{0:T(1024)S(1)} %bitcast.151), kind=kOutput, calls=%fused_computation.6 | convolution fusion | flops 419758080 | bytes 3035136 | tf_op jit(solution)/shard_map/tw,pt->wp/dot_general | solution.py:348
  29.3 1.1 %slice.197.rows_ref = bf16[512,1024]{1,0:T(8,128)(2,1)} slice(f32[640,1024]{1,0:T(8,128)S(1)} %fusion.2), slice={[0:512], [0:1024]} | slice | bytes 2097152 | tf_op jit(solution)/shard_map/slice | solution.py:349
  30.8 0.8 %concatenate.61.geo_ref = f32[128,1024]{1,0:T(8,128)} pad(f32[18,1024]{1,0:T(8,128)S(1)} %concatenate.60, f32[]{:T(128)} %constant.27.clone.1), padding=0_110x0_0 | pad | bytes 598020 | tf_op jit(solution)/shard_map/jvp()/concatenate | solution.py:79
  31.7 0.8 %broadcast_in_dim.99.energy_w_ref = f32[512,128]{1,0:T(8,128)} broadcast(f32[512]{0:T(512)S(1)} %copy-done.11), dimensions={0} | broadcast | bytes 264192 | tf_op jit(solution)/shard_map/broadcast_in_dim | solution.py:250
  32.5 21.0 %shard_map.175 = (f32[512,1024]{1,0:T(8,128)}, f32[512,128]{1,0:T(8,128)}, f32[128,1024]{1,0:T(8,128)}, f32[8,128]{1,0:T(8,128)}) custom-call(bf16[512,1024]{1,0:T(8,128)(2,1)} %slice.197.rows_ref, f32[512,128]{1,0:T(8,128)} %fusion.13.centre_ref, f32[128,1024]{1,0:T(8,128)} %concatenate.61.geo_ref, bf16[512,128]{1,0:T(8,128)(2,1)} %copy.58.basis_t_ref, ...), custom_call_target="tpu_custom_call" | custom-call | flops 1610612736 | bytes 8388608 | tf_op jit(solution)/shard_map/pallas_call | solution.py:212
  53.5 1.1 %slice_multiply_fusion.4 = (f32[1,1024]{1,0:T(1,128)S(1)}, f32[1,1024]{1,0:T(1,128)S(1)}, f32[1,1024]{1,0:T(1,128)S(1)}, f32[1,1024]{1,0:T(1,128)S(1)}, f32[1,10...) fusion(f32[128,1024]{1,0:T(8,128)} %get-tuple-element.9), kind=kLoop, calls=%fused_computation.173 | loop fusion | flops 5120 | bytes 73728 | tf_op jit(solution)/shard_map/transpose(jvp())/mul | solution.py:69
  54.5 1.0 %fusion.34 = (f32[1024]{0:T(1024)S(1)}, f32[1024]{0:T(1024)S(1)}) fusion(f32[128,1024]{1,0:T(8,128)} %get-tuple-element.9, f32[1024]{0:T(1024)S(1)} %get-tuple-element.67, f32[8]{0:T(128)S(1)} %convert_multiply_fusion, f32[1024]{0:T(1024)S(1)} %get-tuple-element.66), kind=kLoop, calls=%fused_computation.73 | loop fusion | flops 55296 | bytes 49184 | tf_op jit(solution)/shard_map/transpose(jvp())/reduce_sum | solution.py:57
  55.7 2.8 %fusion.3 = f32[320,640]{1,0:T(8,128)S(1)} fusion(f32[3,1024]{1,0:T(4,128)S(1)} %bitcast.163, f32[512,1024]{1,0:T(8,128)} %get-tuple-element.8, f32[640]{0:T(1024)S(1)} %pad.21.clone, s32[1024]{0:T(1024)S(1)} %bitcast.152), kind=kOutput, calls=%fused_computation.7 | convolution fusion | flops 424017920 | bytes 2935296 | tf_op jit(solution)/shard_map/wn,nr->wr/dot_general | solution.py:302
  58.6 1.1 %fusion.8 = f32[320,640]{1,0:T(8,128)S(1)} fusion(f32[320,640]{1,0:T(8,128)S(1)} %fusion.3, f32[3,1024]{1,0:T(4,128)S(1)} %bitcast.164, f32[512,1024]{1,0:T(8,128)S(1)} %copy-done.15, f32[640]{0:T(1024)S(1)} %pad.21.clone, f32[128,3]{1,0:T(8,128)S(1)} %bitcast.149, s32[1024]{0:T(1024)S(1)} %bitcast.153), kind=kOutput, calls=%fused_computation.11 | convolution fusion | flops 424427520 | bytes 3756032 | tf_op jit(solution)/shard_map/wn,nr->wr/dot_general | solution.py:304
  59.7 1.5 %collective-permute-start.7 = (f32[16,640]{1,0:T(8,128)S(1)}, f32[16,640]{1,0:T(8,128)S(1)}, u32[]{:S(2)}, u32[]{:S(2)}) collective-permute-start(f32[16,640]{1,0:T(8,128)S(1)} %get-tuple-element.31), channel_id=1, source_target_pairs={{3,0},{0,1},{1,2},{2,3},{7,4},{4,5},{5,6},{6,7},{11,8},{8,9},{9,10... | collective-permute-start | bytes 122888 | tf_op jit(solution)/shard_map/ppermute | solution.py:30
  61.1 2.5 %collective-permute-start.6 = (f32[16,640]{1,0:T(8,128)S(1)}, f32[16,640]{1,0:T(8,128)S(1)}, u32[]{:S(2)}, u32[]{:S(2)}) collective-permute-start(f32[16,640]{1,0:T(8,128)S(1)} %get-tuple-element.30), channel_id=1, source_target_pairs={{1,0},{2,1},{3,2},{0,3},{5,4},{6,5},{7,6},{4,7},{9,8},{10,9},{11,1... | collective-permute-start | bytes 122888 | tf_op jit(solution)/shard_map/ppermute | solution.py:30
  63.7 1.9 %collective-permute-done.7 = f32[16,640]{1,0:T(8,128)S(1)} collective-permute-done((f32[16,640]{1,0:T(8,128)S(1)}, f32[16,640]{1,0:T(8,128)S(1)}, u32[]{:S(2)}, u32[]{:S(2)}) %collective-permute-start.7) | collective-permute-done | bytes 40992 | tf_op jit(solution)/shard_map/ppermute | solution.py:30
  67.2 1.3 %collective-permute-start.8 = (f32[64,640]{1,0:T(8,128)S(1)}, f32[64,640]{1,0:T(8,128)S(1)}, u32[]{:S(2)}, u32[]{:S(2)}) collective-permute-start(f32[64,640]{1,0:T(8,128)S(1)} %get-tuple-element.33), channel_id=1, source_target_pairs={{4,0},{0,4},{5,1},{1,5},{6,2},{2,6},{7,3},{3,7},{12,8},{8,12},{13,... | collective-permute-start | bytes 491528 | tf_op jit(solution)/shard_map/ppermute | solution.py:30
  69.2 0.9 %collective-permute-start.9 = (f32[64,640]{1,0:T(8,128)S(1)}, f32[64,640]{1,0:T(8,128)S(1)}, u32[]{:S(2)}, u32[]{:S(2)}) collective-permute-start(f32[64,640]{1,0:T(8,128)S(1)} %get-tuple-element.32), channel_id=1, source_target_pairs={{4,0},{0,4},{5,1},{1,5},{6,2},{2,6},{7,3},{3,7},{12,8},{8,12},{13,... | collective-permute-start | bytes 491528 | tf_op jit(solution)/shard_map/ppermute | solution.py:30
  70.0 2.5 %collective-permute-done.8 = f32[64,640]{1,0:T(8,128)S(1)} collective-permute-done((f32[64,640]{1,0:T(8,128)S(1)}, f32[64,640]{1,0:T(8,128)S(1)}, u32[]{:S(2)}, u32[]{:S(2)}) %collective-permute-start.8) | collective-permute-done | bytes 163872 | tf_op jit(solution)/shard_map/ppermute | solution.py:30
  73.2 1.3 %collective-permute-done.9 = f32[64,640]{1,0:T(8,128)S(1)} collective-permute-done((f32[64,640]{1,0:T(8,128)S(1)}, f32[64,640]{1,0:T(8,128)S(1)}, u32[]{:S(2)}, u32[]{:S(2)}) %collective-permute-start.9) | collective-permute-done | bytes 163872 | tf_op jit(solution)/shard_map/ppermute | solution.py:30
  77.7 1.9 %collective-permute-done.11 = f32[16,640]{1,0:T(8,128)S(1)} collective-permute-done((f32[16,640]{1,0:T(8,128)S(1)}, f32[16,640]{1,0:T(8,128)S(1)}, u32[]{:S(2)}, u32[]{:S(2)}) %collective-permute-start.11) | collective-permute-done | bytes 40992 | tf_op jit(solution)/shard_map/ppermute | solution.py:30
  80.2 1.3 %convolution_add_fusion.6 = f32[128,512]{1,0:T(8,128)} fusion(f32[128,512]{1,0:T(8,128)S(1)} %fusion.118, bf16[512,512]{1,0:T(8,128)(2,1)S(1)} %copy-done.1, f32[128,640]{1,0:T(8,128)S(1)} %fusion.22), kind=kOutput, calls=%fused_computation.20 | convolution fusion | flops 402718720 | bytes 1310720 | tf_op jit(solution)/shard_map/dot_general | solution.py:396
  (112 shorter events, 13.2 us)
Async XLA Ops:
  0.6 9.2 %copy-start = (bf16[512,512]{1,0:T(8,128)(2,1)S(1)}, bf16[512,512]{1,0:T(8,128)(2,1)}, u32[]{:S(2)}) copy-start(bf16[512,512]{1,0:T(8,128)(2,1)} %param.22) | copy-start | bytes 1572868
  0.6 7.3 %copy-start.8 = (s32[1,192]{1,0:T(1,128)S(1)}, s32[1,192]{1,0:T(1,128)}, u32[]{:S(2)}) copy-start(s32[1,192]{1,0:T(1,128)} %param.19) | copy-start | bytes 2308
  0.7 8.7 %copy-start.12 = (s32[128]{0:T(128)S(1)}, s32[128]{0:T(128)}, u32[]{:S(2)}) copy-start(s32[128]{0:T(128)} %param.18) | copy-start | bytes 1540
  0.7 9.1 %copy-start.3 = (bf16[128,512]{1,0:T(8,128)(2,1)S(1)}, bf16[128,512]{1,0:T(8,128)(2,1)}, u32[]{:S(2)}) copy-start(bf16[128,512]{1,0:T(8,128)(2,1)} %param.16) | copy-start | bytes 393220
  0.7 8.0 %copy-start.9 = (bf16[8,512]{1,0:T(8,128)(2,1)S(1)}, bf16[8,512]{1,0:T(8,128)(2,1)}, u32[]{:S(2)}) copy-start(bf16[8,512]{1,0:T(8,128)(2,1)} %param.26) | copy-start | bytes 24580
  0.7 8.7 %copy-start.7 = (f32[5,512]{1,0:T(8,128)S(1)}, f32[5,512]{1,0:T(8,128)}, u32[]{:S(2)}) copy-start(f32[5,512]{1,0:T(8,128)} %param.24) | copy-start | bytes 30724
  3.5 7.4 %copy-start.10 = (s32[1024]{0:T(1024)S(1)}, s32[1024]{0:T(1024)}, u32[]{:S(2)}) copy-start(s32[1024]{0:T(1024)} %param.20) | copy-start | bytes 12292
  3.5 8.3 %copy-start.2 = (bf16[512,512]{1,0:T(8,128)(2,1)S(1)}, bf16[512,512]{1,0:T(8,128)(2,1)}, u32[]{:S(2)}) copy-start(bf16[512,512]{1,0:T(8,128)(2,1)} %update_ref.1) | copy-start | bytes 1572868
  5.2 7.7 %copy-start.4 = (bf16[512,384]{1,0:T(8,128)(2,1)S(1)}, bf16[512,384]{1,0:T(8,128)(2,1)}, u32[]{:S(2)}) copy-start(bf16[512,384]{1,0:T(8,128)(2,1)} %split_ref.1) | copy-start | bytes 1179652
  5.2 9.5 %collective-permute-start = (bf16[16,640]{1,0:T(8,128)(2,1)S(1)}, bf16[16,640]{1,0:T(8,128)(2,1)S(1)}, u32[]{:S(2)}, u32[]{:S(2)}) collective-permute-start(bf16[16,640]{1,0:T(8,128)(2,1)S(1)} %convolution_convert_fusion.5), channel_id=1, source_target_pairs={{24,0},{0,8},{8,16},{16,24},{25,1},{1,9},{9,17},{17,25},{26,2},{2,... | collective-permute-start | bytes 61448 | tf_op jit(solution)/shard_map/ppermute | solution.py:30
  5.8 8.9 %collective-permute-start.1 = (bf16[16,640]{1,0:T(8,128)(2,1)S(1)}, bf16[16,640]{1,0:T(8,128)(2,1)S(1)}, u32[]{:S(2)}, u32[]{:S(2)}) collective-permute-start(bf16[16,640]{1,0:T(8,128)(2,1)S(1)} %convolution_convert_fusion.4), channel_id=1, source_target_pairs={{8,0},{16,8},{24,16},{0,24},{9,1},{17,9},{25,17},{1,25},{10,2},{18... | collective-permute-start | bytes 61448 | tf_op jit(solution)/shard_map/ppermute | solution.py:30
  7.9 5.9 %copy-start.6 = (bf16[192,512]{1,0:T(8,128)(2,1)S(1)}, bf16[192,512]{1,0:T(8,128)(2,1)}, u32[]{:S(2)}) copy-start(bf16[192,512]{1,0:T(8,128)(2,1)} %tensor_ref.1) | copy-start | bytes 589828
  15.0 5.3 %collective-permute-start.2 = (bf16[64,640]{1,0:T(8,128)(2,1)S(1)}, bf16[64,640]{1,0:T(8,128)(2,1)S(1)}, u32[]{:S(2)}, u32[]{:S(2)}) collective-permute-start(bf16[64,640]{1,0:T(8,128)(2,1)S(1)} %convolution_convert_fusion.1), channel_id=1, source_target_pairs={{4,0},{0,4},{5,1},{1,5},{6,2},{2,6},{7,3},{3,7},{12,8},{8,12},{13,... | collective-permute-start | bytes 245768 | tf_op jit(solution)/shard_map/ppermute | solution.py:30
  17.6 4.5 %collective-permute-start.3 = (bf16[64,640]{1,0:T(8,128)(2,1)S(1)}, bf16[64,640]{1,0:T(8,128)(2,1)S(1)}, u32[]{:S(2)}, u32[]{:S(2)}) collective-permute-start(bf16[64,640]{1,0:T(8,128)(2,1)S(1)} %convolution_convert_fusion), channel_id=1, source_target_pairs={{4,0},{0,4},{5,1},{1,5},{6,2},{2,6},{7,3},{3,7},{12,8},{8,12},{13,... | collective-permute-start | bytes 245768 | tf_op jit(solution)/shard_map/ppermute | solution.py:30
  22.3 5.6 %collective-permute-start.4 = (bf16[16,640]{1,0:T(8,128)(2,1)S(1)}, bf16[16,640]{1,0:T(8,128)(2,1)S(1)}, u32[]{:S(2)}, u32[]{:S(2)}) collective-permute-start(bf16[16,640]{1,0:T(8,128)(2,1)S(1)} %convolution_convert_fusion.3), channel_id=1, source_target_pairs={{3,0},{0,1},{1,2},{2,3},{7,4},{4,5},{5,6},{6,7},{11,8},{8,9},{9,10... | collective-permute-start | bytes 61448 | tf_op jit(solution)/shard_map/ppermute | solution.py:30
  24.2 4.0 %collective-permute-start.5 = (bf16[16,640]{1,0:T(8,128)(2,1)S(1)}, bf16[16,640]{1,0:T(8,128)(2,1)S(1)}, u32[]{:S(2)}, u32[]{:S(2)}) collective-permute-start(bf16[16,640]{1,0:T(8,128)(2,1)S(1)} %convolution_convert_fusion.2), channel_id=1, source_target_pairs={{1,0},{2,1},{3,2},{0,3},{5,4},{6,5},{7,6},{4,7},{9,8},{10,9},{11,1... | collective-permute-start | bytes 61448 | tf_op jit(solution)/shard_map/ppermute | solution.py:30
  29.3 2.4 %copy-start.11 = (f32[512]{0:T(512)S(1)}, f32[512]{0:T(512)}, u32[]{:S(2)}) copy-start(f32[512]{0:T(512)} %param.30) | copy-start | bytes 6148
  55.7 2.8 %copy-start.15 = (f32[512,1024]{1,0:T(8,128)S(1)}, f32[512,1024]{1,0:T(8,128)}, u32[]{:S(2)}) copy-start(f32[512,1024]{1,0:T(8,128)} %get-tuple-element.8) | copy-start | bytes 6291460
  59.7 5.9 %collective-permute-start.7 = (f32[16,640]{1,0:T(8,128)S(1)}, f32[16,640]{1,0:T(8,128)S(1)}, u32[]{:S(2)}, u32[]{:S(2)}) collective-permute-start(f32[16,640]{1,0:T(8,128)S(1)} %get-tuple-element.31), channel_id=1, source_target_pairs={{3,0},{0,1},{1,2},{2,3},{7,4},{4,5},{5,6},{6,7},{11,8},{8,9},{9,10... | collective-permute-start | bytes 122888 | tf_op jit(solution)/shard_map/ppermute | solution.py:30
  61.1 5.2 %collective-permute-start.6 = (f32[16,640]{1,0:T(8,128)S(1)}, f32[16,640]{1,0:T(8,128)S(1)}, u32[]{:S(2)}, u32[]{:S(2)}) collective-permute-start(f32[16,640]{1,0:T(8,128)S(1)} %get-tuple-element.30), channel_id=1, source_target_pairs={{1,0},{2,1},{3,2},{0,3},{5,4},{6,5},{7,6},{4,7},{9,8},{10,9},{11,1... | collective-permute-start | bytes 122888 | tf_op jit(solution)/shard_map/ppermute | solution.py:30
  66.3 2.1 %copy-start.5 = (f32[512,128]{1,0:T(8,128)S(1)}, f32[512,128]{1,0:T(8,128)}, u32[]{:S(2)}) copy-start(f32[512,128]{1,0:T(8,128)} %get-tuple-element.10) | copy-start | bytes 786436
  67.2 5.4 %collective-permute-start.8 = (f32[64,640]{1,0:T(8,128)S(1)}, f32[64,640]{1,0:T(8,128)S(1)}, u32[]{:S(2)}, u32[]{:S(2)}) collective-permute-start(f32[64,640]{1,0:T(8,128)S(1)} %get-tuple-element.33), channel_id=1, source_target_pairs={{4,0},{0,4},{5,1},{1,5},{6,2},{2,6},{7,3},{3,7},{12,8},{8,12},{13,... | collective-permute-start | bytes 491528 | tf_op jit(solution)/shard_map/ppermute | solution.py:30
  69.2 6.2 %copy-start.13 = (f32[5]{0:T(128)S(1)}, f32[5]{0:T(128)}, u32[]{:S(2)}) copy-start(f32[5]{0:T(128)} %param.31) | copy-start | bytes 64
  69.2 6.2 %copy-start.14 = (f32[8,128]{1,0:T(8,128)S(1)}, f32[8,128]{1,0:T(8,128)}, u32[]{:S(2)}) copy-start(f32[8,128]{1,0:T(8,128)} %get-tuple-element.7) | copy-start | bytes 12292
  69.2 5.4 %collective-permute-start.9 = (f32[64,640]{1,0:T(8,128)S(1)}, f32[64,640]{1,0:T(8,128)S(1)}, u32[]{:S(2)}, u32[]{:S(2)}) collective-permute-start(f32[64,640]{1,0:T(8,128)S(1)} %get-tuple-element.32), channel_id=1, source_target_pairs={{4,0},{0,4},{5,1},{1,5},{6,2},{2,6},{7,3},{3,7},{12,8},{8,12},{13,... | collective-permute-start | bytes 491528 | tf_op jit(solution)/shard_map/ppermute | solution.py:30
  74.9 5.3 %copy-start.1 = (bf16[512,512]{1,0:T(8,128)(2,1)S(1)}, bf16[512,512]{1,0:T(8,128)(2,1)}, u32[]{:S(2)}) copy-start(bf16[512,512]{1,0:T(8,128)(2,1)} %param.23) | copy-start | bytes 1572868
  75.3 1.7 %collective-permute-start.10 = (f32[16,640]{1,0:T(8,128)S(1)}, f32[16,640]{1,0:T(8,128)S(1)}, u32[]{:S(2)}, u32[]{:S(2)}) collective-permute-start(f32[16,640]{1,0:T(8,128)S(1)} %get-tuple-element.44), channel_id=1, source_target_pairs={{8,0},{16,8},{24,16},{0,24},{9,1},{17,9},{25,17},{1,25},{10,2},{18... | collective-permute-start | bytes 122888 | tf_op jit(solution)/shard_map/ppermute | solution.py:30
  76.1 3.4 %collective-permute-start.11 = (f32[16,640]{1,0:T(8,128)S(1)}, f32[16,640]{1,0:T(8,128)S(1)}, u32[]{:S(2)}, u32[]{:S(2)}) collective-permute-start(f32[16,640]{1,0:T(8,128)S(1)} %get-tuple-element.43), channel_id=1, source_target_pairs={{24,0},{0,8},{8,16},{16,24},{25,1},{1,9},{9,17},{17,25},{26,2},{2,... | collective-permute-start | bytes 122888 | tf_op jit(solution)/shard_map/ppermute | solution.py:30

commit v8 on v7

--- a/solution.py
+++ b/solution.py
@@ -84,7 +84,7 @@
 
 
 def _sigmoid(v):
-    return 1.0 / (1.0 + jnp.exp(-v))
+    return 0.5 + 0.5 * jnp.tanh(0.5 * v)
 
 
 def _pair_kernel(
@@ -96,13 +96,20 @@
     atoms = centre_ref.shape[1]
     f32 = jnp.float32
     bf16 = jnp.bfloat16
-    sub = lax.broadcasted_iota(jnp.int32, (128, atoms), 0)
+    span = 2 * atoms
+    sub = lax.broadcasted_iota(jnp.int32, (128, span), 0)
     inv_root = 1.0 / math.sqrt(K)
     env_s[...] = jnp.zeros_like(env_s)
     denv_s[...] = jnp.zeros_like(denv_s)
 
     def block(k):
-        return pl.ds(pl.multiple_of(k * atoms, atoms), atoms)
+        return pl.ds(pl.multiple_of(k * span, span), span)
+
+    def twice(v):
+        return jnp.concatenate([v, v], axis=1)
+
+    def fold(v):
+        return v[:, :atoms] + v[:, atoms:]
 
     def split_mm(weight, values):
         high = values.astype(bf16)
@@ -113,7 +120,7 @@
         at = block(k)
         geo = geo_ref[:, at]
         radial = split_mm(basis_t_ref[...], geo)
-        pre = centre_ref[...] + rows_ref[:, at].astype(f32) + radial
+        pre = twice(centre_ref[...]) + rows_ref[:, at].astype(f32) + radial
         envelope = geo[8:9, :]
         hidden = pre * _sigmoid(pre) * envelope
         pre_s[:, at] = pre
@@ -123,10 +130,10 @@
         for m in range(9):
             l = ORDER_OF[m]
             weight = mixed[3 * CH + l * CH : 3 * CH + (l + 1) * CH, :]
-            env_s[m] = env_s[m] + weight * (geo[9 + m : 10 + m, :] * inv_root)
+            env_s[m] = env_s[m] + fold(weight * (geo[9 + m : 10 + m, :] * inv_root))
         return carry
 
-    lax.fori_loop(0, K, first, 0)
+    lax.fori_loop(0, K // 2, first, 0)
 
     def second(k, energy):
         at = block(k)
@@ -139,7 +146,7 @@
         for l in range(3):
             total = 0.0
             for m in GROUPS[l]:
-                total = total + geo[9 + m : 10 + m, :] * env_s[m]
+                total = total + geo[9 + m : 10 + m, :] * twice(env_s[m])
             totals.append(total)
             parts.append(mixed[l * CH : (l + 1) * CH, :] * total)
         scalars = jnp.concatenate(parts, axis=0).astype(bf16)
@@ -159,14 +166,14 @@
             dtotal = ds * mixed[l * CH : (l + 1) * CH, :]
             for m in GROUPS[l]:
                 dgeo = dgeo + jnp.where(
-                    sub == 9 + m, jnp.sum(dtotal * env_s[m], axis=0, keepdims=True), 0.0
+                    sub == 9 + m, jnp.sum(dtotal * twice(env_s[m]), axis=0, keepdims=True), 0.0
                 )
-                denv_s[m] = denv_s[m] + dtotal * geo[9 + m : 10 + m, :]
+                denv_s[m] = denv_s[m] + fold(dtotal * geo[9 + m : 10 + m, :])
         dgeo_s[:, at] = dgeo
         return energy
 
-    energy = lax.fori_loop(0, K, second, jnp.zeros((1, atoms), f32))
-    energy_ref[...] = jnp.broadcast_to(energy, energy_ref.shape)
+    energy = lax.fori_loop(0, K // 2, second, jnp.zeros((1, span), f32))
+    energy_ref[...] = jnp.broadcast_to(fold(energy), energy_ref.shape)
 
     def third(k, centre_grad):
         at = block(k)
@@ -179,10 +186,11 @@
             weight = mixed[3 * CH + l * CH : 3 * CH + (l + 1) * CH, :]
             dweight = 0.0
             for m in GROUPS[l]:
-                dweight = dweight + denv_s[m] * (geo[9 + m : 10 + m, :] * inv_root)
+                denv = twice(denv_s[m])
+                dweight = dweight + denv * (geo[9 + m : 10 + m, :] * inv_root)
                 dgeo = dgeo + jnp.where(
                     sub == 9 + m,
-                    jnp.sum(denv_s[m] * weight, axis=0, keepdims=True) * inv_root,
+                    jnp.sum(denv * weight, axis=0, keepdims=True) * inv_root,
                     0.0,
                 )
             dweights.append(dweight)
@@ -197,9 +205,11 @@
         grad_rows_ref[:, at] = dpre
         dgeo = dgeo + split_mm(basis_ref[...], dpre)
         grad_geo_ref[:, at] = dgeo
-        return centre_grad + dpre
-
-    grad_centre_ref[...] = lax.fori_loop(0, K, third, jnp.zeros(grad_centre_ref.shape, f32))
+        return centre_grad + fold(dpre)
+
+    grad_centre_ref[...] = lax.fori_loop(
+        0, K // 2, third, jnp.zeros(grad_centre_ref.shape, f32)
+    )
 
 
 def pair_terms(rows_t, centre_t, geo, basis_proj, split_proj, update_proj, tensor_proj, energy_proj):
@@ -247,7 +257,7 @@
         tensor_proj.T,
         tensor_proj,
         basis_pad,
-        jnp.broadcast_to(energy_proj.astype(f32)[:, None], (width, atoms)),
+        jnp.broadcast_to(energy_proj.astype(f32)[:, None], (width, 2 * atoms)),
     )
     grad_rows_t, grad_centre_t, grad_geo, energy = outs
     return grad_rows_t, grad_centre_t, grad_geo, energy[0]

time: 82.6 us -> 75.9 us (0.919)
  Pallas kernels: 21 us -> 14.1 us
    pallas_call x1, Pallas kernels: 21 us -> 14.1 us  [pair_terms(): pl.pallas_call(_pair_kernel, out_shape=(jax.ShapeDtypeStruct((width, pair...]
  transfers between devices with their start and end apart: 12 -> 12, of which waited for: 9 -> 9; matrix products, arithmetic and copies ran while one was open for 13% -> 14% of each run, Pallas kernels for 0% -> 0%
where the time goes in v8:
time: 75.9 us; the launch traced here: 75.5 us
  matrix products  17.1 us (23%)
  starting transfers between devices  15.5 us (20%)
  waiting for transfers between devices  14.1 us (19%)
  Pallas kernels  14.1 us (19%)
  local copies, waits for them, and re-layouts  9.41 us (12%)
  other arithmetic  3.43 us (5%)
  between operations  1.83 us (2%)
    ppermute x12, starting transfers between devices, passed_along(): return lax.ppermute(block, axis, route)  15.5 us
    pallas_call x1, Pallas kernels, pair_terms(): pl.pallas_call(_pair_kernel, out_shape=(jax.ShapeDtypeStruct((width, pair...  14.1 us
    ppermute x12, waiting for transfers between devices, passed_along(): return lax.ppermute(block, axis, route)  14.1 us
    unnamed x40, local copies, waits for them, and re-layouts  3.55 us
    dot_general x1, matrix products, spread_cols(): jnp.einsum('wn,nr->wr', high, onehot, preferred_element_type=jnp.float32)  2.82 us
    dot_general x2, matrix products, project(): jnp.dot(rows, weight, preferred_element_type=jnp.float32)  2.44 us
    dot_general x3, matrix products, lookup(): return jnp.dot(onehot, table, precision=lax.Precision.HIGHEST)  2.24 us
    dot_general x6, matrix products, spread(): jnp.einsum('nr,nw->rw', onehot, high, preferred_element_type=jnp.float32)  2.09 us
  transfers between devices with their start and end apart: 12, of which 9 were waited for; matrix products, arithmetic and copies ran while one was open for 14% of the time, Pallas kernels for 0%

profile of v8, /device:TPU:0, one launch (start us, length us, event | category | flops | bytes accessed | tf_op | source)
XLA Modules:
  0.0 75.5 jit_solution(2132766607354244699)
XLA Ops:
  1.7 0.8 %slice_bitcast_fusion = (s32[16]{0:T(128)S(1)}, s32[16]{0:T(128)S(1)}, s32[16]{0:T(128)S(1)}, s32[16]{0:T(128)S(1)}) fusion(s32[1,192]{1,0:T(1,128)} %param.19), kind=kLoop, calls=%fused_computation.211 | loop fusion | bytes 512 | tf_op jit(solution)/shard_map/eq | solution.py:343
  2.5 1.0 %fusion.27 = f32[128,512]{1,0:T(8,128)S(1)} fusion(f32[5,512]{1,0:T(8,128)} %param.25, s32[128]{0:T(128)} %param.18), kind=kOutput, calls=%fused_computation.59 | convolution fusion | flops 3932800 | bytes 272896 | tf_op jit(solution)/shard_map/dot_general | solution.py:302
  3.5 1.4 %fusion.11 = bf16[128,512]{1,0:T(8,128)(2,1)S(1)} fusion(f32[128,512]{1,0:T(8,128)S(1)} %fusion.27, bf16[128,512]{1,0:T(8,128)(2,1)} %param.16, bf16[512,512]{1,0:T(8,128)(2,1)} %param.23), kind=kOutput, calls=%fused_computation.24 | convolution fusion | flops 67239936 | bytes 1048576 | tf_op jit(solution)/shard_map/dot_general | solution.py:306
  5.8 2.0 %collective-permute-start.1 = (bf16[16,640]{1,0:T(8,128)(2,1)S(1)}, bf16[16,640]{1,0:T(8,128)(2,1)S(1)}, u32[]{:S(2)}, u32[]{:S(2)}) collective-permute-start(bf16[16,640]{1,0:T(8,128)(2,1)S(1)} %convolution_convert_fusion.4), channel_id=1, source_target_pairs={{8,0},{16,8},{24,16},{0,24},{9,1},{17,9},{25,17},{1,25},{10,2},{18... | collective-permute-start | bytes 61448 | tf_op jit(solution)/shard_map/ppermute | solution.py:30
  9.8 1.0 %fusion.13.centre_ref = f32[512,128]{1,0:T(8,128)} fusion(f32[512,128]{1,0:T(8,128)S(1)} %convolution_bitcast_fusion, bf16[512,512]{1,0:T(8,128)(2,1)S(1)} %copy-done, bf16[128,512]{1,0:T(8,128)(2,1)S(1)} %copy-done.3), kind=kOutput, calls=%fused_computation.26 | convolution fusion | flops 67305472 | bytes 1179648 | tf_op jit(solution)/shard_map/dot_general | solution.py:306
  11.8 1.0 %copy.56 = bf16[512,512]{0,1:T(8,128)(2,1)} copy(bf16[512,512]{1,0:T(8,128)(2,1)S(1)} %copy-done.2) | data formatting | bytes 1048576 | tf_op args[12]
  12.8 0.9 %copy.55 = bf16[512,384]{0,1:T(8,128)(2,1)} copy(bf16[512,384]{1,0:T(8,128)(2,1)S(1)} %copy-done.4) | data formatting | bytes 786432 | tf_op args[11]
  13.7 0.8 %copy.57 = bf16[192,512]{0,1:T(8,128)(2,1)} copy(bf16[192,512]{1,0:T(8,128)(2,1)S(1)} %copy-done.6) | data formatting | bytes 393216 | tf_op args[13]
  14.9 2.4 %collective-permute-start.2 = (bf16[64,640]{1,0:T(8,128)(2,1)S(1)}, bf16[64,640]{1,0:T(8,128)(2,1)S(1)}, u32[]{:S(2)}, u32[]{:S(2)}) collective-permute-start(bf16[64,640]{1,0:T(8,128)(2,1)S(1)} %convolution_convert_fusion.1), channel_id=1, source_target_pairs={{4,0},{0,4},{5,1},{1,5},{6,2},{2,6},{7,3},{3,7},{12,8},{8,12},{13,... | collective-permute-start | bytes 245768 | tf_op jit(solution)/shard_map/ppermute | solution.py:30
  17.7 2.6 %collective-permute-done.2 = bf16[64,640]{1,0:T(8,128)(2,1)S(1)} collective-permute-done((bf16[64,640]{1,0:T(8,128)(2,1)S(1)}, bf16[64,640]{1,0:T(8,128)(2,1)S(1)}, u32[]{:S(2)}, u32[]{:S(2)}) %collective-permute-start.2) | collective-permute-done | bytes 81952 | tf_op jit(solution)/shard_map/ppermute | solution.py:30
  20.3 1.8 %collective-permute-done.3 = bf16[64,640]{1,0:T(8,128)(2,1)S(1)} collective-permute-done((bf16[64,640]{1,0:T(8,128)(2,1)S(1)}, bf16[64,640]{1,0:T(8,128)(2,1)S(1)}, u32[]{:S(2)}, u32[]{:S(2)}) %collective-permute-start.3) | collective-permute-done | bytes 81952 | tf_op jit(solution)/shard_map/ppermute | solution.py:30
  22.3 1.6 %collective-permute-start.4 = (bf16[16,640]{1,0:T(8,128)(2,1)S(1)}, bf16[16,640]{1,0:T(8,128)(2,1)S(1)}, u32[]{:S(2)}, u32[]{:S(2)}) collective-permute-start(bf16[16,640]{1,0:T(8,128)(2,1)S(1)} %convolution_convert_fusion.3), channel_id=1, source_target_pairs={{3,0},{0,1},{1,2},{2,3},{7,4},{4,5},{5,6},{6,7},{11,8},{8,9},{9,10... | collective-permute-start | bytes 61448 | tf_op jit(solution)/shard_map/ppermute | solution.py:30
  24.2 2.3 %collective-permute-start.5 = (bf16[16,640]{1,0:T(8,128)(2,1)S(1)}, bf16[16,640]{1,0:T(8,128)(2,1)S(1)}, u32[]{:S(2)}, u32[]{:S(2)}) collective-permute-start(bf16[16,640]{1,0:T(8,128)(2,1)S(1)} %convolution_convert_fusion.2), channel_id=1, source_target_pairs={{1,0},{2,1},{3,2},{0,3},{5,4},{6,5},{7,6},{4,7},{9,8},{10,9},{11,1... | collective-permute-start | bytes 61448 | tf_op jit(solution)/shard_map/ppermute | solution.py:30
  26.5 1.5 %collective-permute-done.4 = bf16[16,640]{1,0:T(8,128)(2,1)S(1)} collective-permute-done((bf16[16,640]{1,0:T(8,128)(2,1)S(1)}, bf16[16,640]{1,0:T(8,128)(2,1)S(1)}, u32[]{:S(2)}, u32[]{:S(2)}) %collective-permute-start.4) | collective-permute-done | bytes 20512 | tf_op jit(solution)/shard_map/ppermute | solution.py:30
  28.2 1.1 %fusion.2 = f32[640,1024]{1,0:T(8,128)S(1)} fusion(bf16[320,640]{1,0:T(8,128)(2,1)S(1)} %constant_dynamic-update-slice_fusion.3, s32[1024]{0:T(1024)S(1)} %bitcast.151), kind=kOutput, calls=%fused_computation.6 | convolution fusion | flops 419758080 | bytes 3035136 | tf_op jit(solution)/shard_map/tw,pt->wp/dot_general | solution.py:358
  29.3 1.1 %slice.197.rows_ref = bf16[512,1024]{1,0:T(8,128)(2,1)} slice(f32[640,1024]{1,0:T(8,128)S(1)} %fusion.2), slice={[0:512], [0:1024]} | slice | bytes 2097152 | tf_op jit(solution)/shard_map/slice | solution.py:359
  30.8 0.8 %concatenate.61.geo_ref = f32[128,1024]{1,0:T(8,128)} pad(f32[18,1024]{1,0:T(8,128)S(1)} %concatenate.60, f32[]{:T(128)} %constant.27.clone.1), padding=0_110x0_0 | pad | bytes 598020 | tf_op jit(solution)/shard_map/jvp()/concatenate | solution.py:79
  31.7 0.9 %broadcast_in_dim.99.energy_w_ref = f32[512,256]{1,0:T(8,128)} broadcast(f32[512]{0:T(512)S(1)} %copy-done.11), dimensions={0} | broadcast | bytes 526336 | tf_op jit(solution)/shard_map/broadcast_in_dim | solution.py:260
  32.6 14.1 %shard_map.175 = (f32[512,1024]{1,0:T(8,128)}, f32[512,128]{1,0:T(8,128)}, f32[128,1024]{1,0:T(8,128)}, f32[8,128]{1,0:T(8,128)}) custom-call(bf16[512,1024]{1,0:T(8,128)(2,1)} %slice.197.rows_ref, f32[512,128]{1,0:T(8,128)} %fusion.13.centre_ref, f32[128,1024]{1,0:T(8,128)} %concatenate.61.geo_ref, bf16[512,128]{1,0:T(8,128)(2,1)} %copy.58.basis_t_ref, ...), custom_call_target="tpu_custom_call" | custom-call | flops 1610612736 | bytes 8388608 | tf_op jit(solution)/shard_map/pallas_call | solution.py:222
  46.7 1.1 %slice_multiply_fusion.4 = (f32[1,1024]{1,0:T(1,128)S(1)}, f32[1,1024]{1,0:T(1,128)S(1)}, f32[1,1024]{1,0:T(1,128)S(1)}, f32[1,1024]{1,0:T(1,128)S(1)}, f32[1,10...) fusion(f32[128,1024]{1,0:T(8,128)} %get-tuple-element.9), kind=kLoop, calls=%fused_computation.173 | loop fusion | flops 5120 | bytes 73728 | tf_op jit(solution)/shard_map/transpose(jvp())/mul | solution.py:69
  47.8 1.0 %fusion.34 = (f32[1024]{0:T(1024)S(1)}, f32[1024]{0:T(1024)S(1)}) fusion(f32[128,1024]{1,0:T(8,128)} %get-tuple-element.9, f32[1024]{0:T(1024)S(1)} %get-tuple-element.67, f32[8]{0:T(128)S(1)} %convert_multiply_fusion, f32[1024]{0:T(1024)S(1)} %get-tuple-element.66), kind=kLoop, calls=%fused_computation.73 | loop fusion | flops 55296 | bytes 49184 | tf_op jit(solution)/shard_map/transpose(jvp())/reduce_sum | solution.py:57
  49.0 2.8 %fusion.3 = f32[320,640]{1,0:T(8,128)S(1)} fusion(f32[3,1024]{1,0:T(4,128)S(1)} %bitcast.163, f32[512,1024]{1,0:T(8,128)} %get-tuple-element.8, f32[640]{0:T(1024)S(1)} %pad.21.clone, s32[1024]{0:T(1024)S(1)} %bitcast.152), kind=kOutput, calls=%fused_computation.7 | convolution fusion | flops 424017920 | bytes 2935296 | tf_op jit(solution)/shard_map/wn,nr->wr/dot_general | solution.py:312
  51.8 1.1 %fusion.8 = f32[320,640]{1,0:T(8,128)S(1)} fusion(f32[320,640]{1,0:T(8,128)S(1)} %fusion.3, f32[3,1024]{1,0:T(4,128)S(1)} %bitcast.164, f32[512,1024]{1,0:T(8,128)S(1)} %copy-done.14, f32[640]{0:T(1024)S(1)} %pad.21.clone, f32[128,3]{1,0:T(8,128)S(1)} %bitcast.149, s32[1024]{0:T(1024)S(1)} %bitcast.153), kind=kOutput, calls=%fused_computation.11 | convolution fusion | flops 424427520 | bytes 3756032 | tf_op jit(solution)/shard_map/wn,nr->wr/dot_general | solution.py:314
  52.9 1.4 %collective-permute-start.7 = (f32[16,640]{1,0:T(8,128)S(1)}, f32[16,640]{1,0:T(8,128)S(1)}, u32[]{:S(2)}, u32[]{:S(2)}) collective-permute-start(f32[16,640]{1,0:T(8,128)S(1)} %get-tuple-element.31), channel_id=1, source_target_pairs={{3,0},{0,1},{1,2},{2,3},{7,4},{4,5},{5,6},{6,7},{11,8},{8,9},{9,10... | collective-permute-start | bytes 122888 | tf_op jit(solution)/shard_map/ppermute | solution.py:30
  54.4 2.5 %collective-permute-start.6 = (f32[16,640]{1,0:T(8,128)S(1)}, f32[16,640]{1,0:T(8,128)S(1)}, u32[]{:S(2)}, u32[]{:S(2)}) collective-permute-start(f32[16,640]{1,0:T(8,128)S(1)} %get-tuple-element.30), channel_id=1, source_target_pairs={{1,0},{2,1},{3,2},{0,3},{5,4},{6,5},{7,6},{4,7},{9,8},{10,9},{11,1... | collective-permute-start | bytes 122888 | tf_op jit(solution)/shard_map/ppermute | solution.py:30
  56.9 1.9 %collective-permute-done.7 = f32[16,640]{1,0:T(8,128)S(1)} collective-permute-done((f32[16,640]{1,0:T(8,128)S(1)}, f32[16,640]{1,0:T(8,128)S(1)}, u32[]{:S(2)}, u32[]{:S(2)}) %collective-permute-start.7) | collective-permute-done | bytes 40992 | tf_op jit(solution)/shard_map/ppermute | solution.py:30
  60.4 1.3 %collective-permute-start.8 = (f32[64,640]{1,0:T(8,128)S(1)}, f32[64,640]{1,0:T(8,128)S(1)}, u32[]{:S(2)}, u32[]{:S(2)}) collective-permute-start(f32[64,640]{1,0:T(8,128)S(1)} %get-tuple-element.33), channel_id=1, source_target_pairs={{4,0},{0,4},{5,1},{1,5},{6,2},{2,6},{7,3},{3,7},{12,8},{8,12},{13,... | collective-permute-start | bytes 491528 | tf_op jit(solution)/shard_map/ppermute | solution.py:30
  62.4 0.9 %collective-permute-start.9 = (f32[64,640]{1,0:T(8,128)S(1)}, f32[64,640]{1,0:T(8,128)S(1)}, u32[]{:S(2)}, u32[]{:S(2)}) collective-permute-start(f32[64,640]{1,0:T(8,128)S(1)} %get-tuple-element.32), channel_id=1, source_target_pairs={{4,0},{0,4},{5,1},{1,5},{6,2},{2,6},{7,3},{3,7},{12,8},{8,12},{13,... | collective-permute-start | bytes 491528 | tf_op jit(solution)/shard_map/ppermute | solution.py:30
  63.3 2.5 %collective-permute-done.8 = f32[64,640]{1,0:T(8,128)S(1)} collective-permute-done((f32[64,640]{1,0:T(8,128)S(1)}, f32[64,640]{1,0:T(8,128)S(1)}, u32[]{:S(2)}, u32[]{:S(2)}) %collective-permute-start.8) | collective-permute-done | bytes 163872 | tf_op jit(solution)/shard_map/ppermute | solution.py:30
  66.5 1.3 %collective-permute-done.9 = f32[64,640]{1,0:T(8,128)S(1)} collective-permute-done((f32[64,640]{1,0:T(8,128)S(1)}, f32[64,640]{1,0:T(8,128)S(1)}, u32[]{:S(2)}, u32[]{:S(2)}) %collective-permute-start.9) | collective-permute-done | bytes 163872 | tf_op jit(solution)/shard_map/ppermute | solution.py:30
  70.9 1.9 %collective-permute-done.11 = f32[16,640]{1,0:T(8,128)S(1)} collective-permute-done((f32[16,640]{1,0:T(8,128)S(1)}, f32[16,640]{1,0:T(8,128)S(1)}, u32[]{:S(2)}, u32[]{:S(2)}) %collective-permute-start.11) | collective-permute-done | bytes 40992 | tf_op jit(solution)/shard_map/ppermute | solution.py:30
  73.5 1.3 %convolution_add_fusion.6 = f32[128,512]{1,0:T(8,128)} fusion(f32[128,512]{1,0:T(8,128)S(1)} %fusion.118, bf16[512,512]{1,0:T(8,128)(2,1)S(1)} %copy-done.1, f32[128,640]{1,0:T(8,128)S(1)} %fusion.22), kind=kOutput, calls=%fused_computation.20 | convolution fusion | flops 402718720 | bytes 1310720 | tf_op jit(solution)/shard_map/dot_general | solution.py:406
  (112 shorter events, 13.2 us)
Async XLA Ops:
  0.6 9.2 %copy-start = (bf16[512,512]{1,0:T(8,128)(2,1)S(1)}, bf16[512,512]{1,0:T(8,128)(2,1)}, u32[]{:S(2)}) copy-start(bf16[512,512]{1,0:T(8,128)(2,1)} %param.22) | copy-start | bytes 1572868
  0.6 7.3 %copy-start.8 = (s32[1,192]{1,0:T(1,128)S(1)}, s32[1,192]{1,0:T(1,128)}, u32[]{:S(2)}) copy-start(s32[1,192]{1,0:T(1,128)} %param.19) | copy-start | bytes 2308
  0.7 8.7 %copy-start.12 = (s32[128]{0:T(128)S(1)}, s32[128]{0:T(128)}, u32[]{:S(2)}) copy-start(s32[128]{0:T(128)} %param.18) | copy-start | bytes 1540
  0.7 9.1 %copy-start.3 = (bf16[128,512]{1,0:T(8,128)(2,1)S(1)}, bf16[128,512]{1,0:T(8,128)(2,1)}, u32[]{:S(2)}) copy-start(bf16[128,512]{1,0:T(8,128)(2,1)} %param.16) | copy-start | bytes 393220
  0.7 8.0 %copy-start.9 = (bf16[8,512]{1,0:T(8,128)(2,1)S(1)}, bf16[8,512]{1,0:T(8,128)(2,1)}, u32[]{:S(2)}) copy-start(bf16[8,512]{1,0:T(8,128)(2,1)} %param.26) | copy-start | bytes 24580
  0.7 8.7 %copy-start.7 = (f32[5,512]{1,0:T(8,128)S(1)}, f32[5,512]{1,0:T(8,128)}, u32[]{:S(2)}) copy-start(f32[5,512]{1,0:T(8,128)} %param.24) | copy-start | bytes 30724
  3.5 7.4 %copy-start.10 = (s32[1024]{0:T(1024)S(1)}, s32[1024]{0:T(1024)}, u32[]{:S(2)}) copy-start(s32[1024]{0:T(1024)} %param.20) | copy-start | bytes 12292
  3.5 8.3 %copy-start.2 = (bf16[512,512]{1,0:T(8,128)(2,1)S(1)}, bf16[512,512]{1,0:T(8,128)(2,1)}, u32[]{:S(2)}) copy-start(bf16[512,512]{1,0:T(8,128)(2,1)} %update_ref.1) | copy-start | bytes 1572868
  5.2 7.6 %copy-start.4 = (bf16[512,384]{1,0:T(8,128)(2,1)S(1)}, bf16[512,384]{1,0:T(8,128)(2,1)}, u32[]{:S(2)}) copy-start(bf16[512,384]{1,0:T(8,128)(2,1)} %split_ref.1) | copy-start | bytes 1179652
  5.2 9.5 %collective-permute-start = (bf16[16,640]{1,0:T(8,128)(2,1)S(1)}, bf16[16,640]{1,0:T(8,128)(2,1)S(1)}, u32[]{:S(2)}, u32[]{:S(2)}) collective-permute-start(bf16[16,640]{1,0:T(8,128)(2,1)S(1)} %convolution_convert_fusion.5), channel_id=1, source_target_pairs={{24,0},{0,8},{8,16},{16,24},{25,1},{1,9},{9,17},{17,25},{26,2},{2,... | collective-permute-start | bytes 61448 | tf_op jit(solution)/shard_map/ppermute | solution.py:30
  5.8 8.9 %collective-permute-start.1 = (bf16[16,640]{1,0:T(8,128)(2,1)S(1)}, bf16[16,640]{1,0:T(8,128)(2,1)S(1)}, u32[]{:S(2)}, u32[]{:S(2)}) collective-permute-start(bf16[16,640]{1,0:T(8,128)(2,1)S(1)} %convolution_convert_fusion.4), channel_id=1, source_target_pairs={{8,0},{16,8},{24,16},{0,24},{9,1},{17,9},{25,17},{1,25},{10,2},{18... | collective-permute-start | bytes 61448 | tf_op jit(solution)/shard_map/ppermute | solution.py:30
  7.9 5.9 %copy-start.6 = (bf16[192,512]{1,0:T(8,128)(2,1)S(1)}, bf16[192,512]{1,0:T(8,128)(2,1)}, u32[]{:S(2)}) copy-start(bf16[192,512]{1,0:T(8,128)(2,1)} %tensor_ref.1) | copy-start | bytes 589828
  14.9 5.3 %collective-permute-start.2 = (bf16[64,640]{1,0:T(8,128)(2,1)S(1)}, bf16[64,640]{1,0:T(8,128)(2,1)S(1)}, u32[]{:S(2)}, u32[]{:S(2)}) collective-permute-start(bf16[64,640]{1,0:T(8,128)(2,1)S(1)} %convolution_convert_fusion.1), channel_id=1, source_target_pairs={{4,0},{0,4},{5,1},{1,5},{6,2},{2,6},{7,3},{3,7},{12,8},{8,12},{13,... | collective-permute-start | bytes 245768 | tf_op jit(solution)/shard_map/ppermute | solution.py:30
  17.6 4.5 %collective-permute-start.3 = (bf16[64,640]{1,0:T(8,128)(2,1)S(1)}, bf16[64,640]{1,0:T(8,128)(2,1)S(1)}, u32[]{:S(2)}, u32[]{:S(2)}) collective-permute-start(bf16[64,640]{1,0:T(8,128)(2,1)S(1)} %convolution_convert_fusion), channel_id=1, source_target_pairs={{4,0},{0,4},{5,1},{1,5},{6,2},{2,6},{7,3},{3,7},{12,8},{8,12},{13,... | collective-permute-start | bytes 245768 | tf_op jit(solution)/shard_map/ppermute | solution.py:30
  22.3 5.6 %collective-permute-start.4 = (bf16[16,640]{1,0:T(8,128)(2,1)S(1)}, bf16[16,640]{1,0:T(8,128)(2,1)S(1)}, u32[]{:S(2)}, u32[]{:S(2)}) collective-permute-start(bf16[16,640]{1,0:T(8,128)(2,1)S(1)} %convolution_convert_fusion.3), channel_id=1, source_target_pairs={{3,0},{0,1},{1,2},{2,3},{7,4},{4,5},{5,6},{6,7},{11,8},{8,9},{9,10... | collective-permute-start | bytes 61448 | tf_op jit(solution)/shard_map/ppermute | solution.py:30
  24.2 4.0 %collective-permute-start.5 = (bf16[16,640]{1,0:T(8,128)(2,1)S(1)}, bf16[16,640]{1,0:T(8,128)(2,1)S(1)}, u32[]{:S(2)}, u32[]{:S(2)}) collective-permute-start(bf16[16,640]{1,0:T(8,128)(2,1)S(1)} %convolution_convert_fusion.2), channel_id=1, source_target_pairs={{1,0},{2,1},{3,2},{0,3},{5,4},{6,5},{7,6},{4,7},{9,8},{10,9},{11,1... | collective-permute-start | bytes 61448 | tf_op jit(solution)/shard_map/ppermute | solution.py:30
  29.2 2.4 %copy-start.11 = (f32[512]{0:T(512)S(1)}, f32[512]{0:T(512)}, u32[]{:S(2)}) copy-start(f32[512]{0:T(512)} %param.30) | copy-start | bytes 6148
  49.0 2.8 %copy-start.14 = (f32[512,1024]{1,0:T(8,128)S(1)}, f32[512,1024]{1,0:T(8,128)}, u32[]{:S(2)}) copy-start(f32[512,1024]{1,0:T(8,128)} %get-tuple-element.8) | copy-start | bytes 6291460
  52.9 5.9 %collective-permute-start.7 = (f32[16,640]{1,0:T(8,128)S(1)}, f32[16,640]{1,0:T(8,128)S(1)}, u32[]{:S(2)}, u32[]{:S(2)}) collective-permute-start(f32[16,640]{1,0:T(8,128)S(1)} %get-tuple-element.31), channel_id=1, source_target_pairs={{3,0},{0,1},{1,2},{2,3},{7,4},{4,5},{5,6},{6,7},{11,8},{8,9},{9,10... | collective-permute-start | bytes 122888 | tf_op jit(solution)/shard_map/ppermute | solution.py:30
  54.4 5.2 %collective-permute-start.6 = (f32[16,640]{1,0:T(8,128)S(1)}, f32[16,640]{1,0:T(8,128)S(1)}, u32[]{:S(2)}, u32[]{:S(2)}) collective-permute-start(f32[16,640]{1,0:T(8,128)S(1)} %get-tuple-element.30), channel_id=1, source_target_pairs={{1,0},{2,1},{3,2},{0,3},{5,4},{6,5},{7,6},{4,7},{9,8},{10,9},{11,1... | collective-permute-start | bytes 122888 | tf_op jit(solution)/shard_map/ppermute | solution.py:30
  59.6 2.1 %copy-start.5 = (f32[512,128]{1,0:T(8,128)S(1)}, f32[512,128]{1,0:T(8,128)}, u32[]{:S(2)}) copy-start(f32[512,128]{1,0:T(8,128)} %get-tuple-element.10) | copy-start | bytes 786436
  60.4 5.4 %collective-permute-start.8 = (f32[64,640]{1,0:T(8,128)S(1)}, f32[64,640]{1,0:T(8,128)S(1)}, u32[]{:S(2)}, u32[]{:S(2)}) collective-permute-start(f32[64,640]{1,0:T(8,128)S(1)} %get-tuple-element.33), channel_id=1, source_target_pairs={{4,0},{0,4},{5,1},{1,5},{6,2},{2,6},{7,3},{3,7},{12,8},{8,12},{13,... | collective-permute-start | bytes 491528 | tf_op jit(solution)/shard_map/ppermute | solution.py:30
  62.4 6.2 %copy-start.13 = (f32[5]{0:T(128)S(1)}, f32[5]{0:T(128)}, u32[]{:S(2)}) copy-start(f32[5]{0:T(128)} %param.31) | copy-start | bytes 64
  62.4 6.2 %copy-start.15 = (f32[8,128]{1,0:T(8,128)S(1)}, f32[8,128]{1,0:T(8,128)}, u32[]{:S(2)}) copy-start(f32[8,128]{1,0:T(8,128)} %get-tuple-element.7) | copy-start | bytes 12292
  62.4 5.4 %collective-permute-start.9 = (f32[64,640]{1,0:T(8,128)S(1)}, f32[64,640]{1,0:T(8,128)S(1)}, u32[]{:S(2)}, u32[]{:S(2)}) collective-permute-start(f32[64,640]{1,0:T(8,128)S(1)} %get-tuple-element.32), channel_id=1, source_target_pairs={{4,0},{0,4},{5,1},{1,5},{6,2},{2,6},{7,3},{3,7},{12,8},{8,12},{13,... | collective-permute-start | bytes 491528 | tf_op jit(solution)/shard_map/ppermute | solution.py:30
  68.2 5.3 %copy-start.1 = (bf16[512,512]{1,0:T(8,128)(2,1)S(1)}, bf16[512,512]{1,0:T(8,128)(2,1)}, u32[]{:S(2)}) copy-start(bf16[512,512]{1,0:T(8,128)(2,1)} %param.23) | copy-start | bytes 1572868
  68.5 1.7 %collective-permute-start.10 = (f32[16,640]{1,0:T(8,128)S(1)}, f32[16,640]{1,0:T(8,128)S(1)}, u32[]{:S(2)}, u32[]{:S(2)}) collective-permute-start(f32[16,640]{1,0:T(8,128)S(1)} %get-tuple-element.44), channel_id=1, source_target_pairs={{8,0},{16,8},{24,16},{0,24},{9,1},{17,9},{25,17},{1,25},{10,2},{18... | collective-permute-start | bytes 122888 | tf_op jit(solution)/shard_map/ppermute | solution.py:30
  69.4 3.4 %collective-permute-start.11 = (f32[16,640]{1,0:T(8,128)S(1)}, f32[16,640]{1,0:T(8,128)S(1)}, u32[]{:S(2)}, u32[]{:S(2)}) collective-permute-start(f32[16,640]{1,0:T(8,128)S(1)} %get-tuple-element.43), channel_id=1, source_target_pairs={{24,0},{0,8},{8,16},{16,24},{25,1},{1,9},{9,17},{17,25},{26,2},{2,... | collective-permute-start | bytes 122888 | tf_op jit(solution)/shard_map/ppermute | solution.py:30

commit v9 on v8

--- a/solution.py
+++ b/solution.py
@@ -42,6 +42,7 @@
     )
 
 
+SLOTS = 4
 ORDER_OF = (0, 1, 1, 1, 2, 2, 2, 2, 2)
 GROUPS = ((0,), (1, 2, 3), (4, 5, 6, 7, 8))
 
@@ -96,7 +97,7 @@
     atoms = centre_ref.shape[1]
     f32 = jnp.float32
     bf16 = jnp.bfloat16
-    span = 2 * atoms
+    span = SLOTS * atoms
     sub = lax.broadcasted_iota(jnp.int32, (128, span), 0)
     inv_root = 1.0 / math.sqrt(K)
     env_s[...] = jnp.zeros_like(env_s)
@@ -106,10 +107,13 @@
         return pl.ds(pl.multiple_of(k * span, span), span)
 
     def twice(v):
-        return jnp.concatenate([v, v], axis=1)
+        return jnp.concatenate([v] * SLOTS, axis=1)
 
     def fold(v):
-        return v[:, :atoms] + v[:, atoms:]
+        total = v[:, :atoms]
+        for slot in range(1, SLOTS):
+            total = total + v[:, slot * atoms : (slot + 1) * atoms]
+        return total
 
     def split_mm(weight, values):
         high = values.astype(bf16)
@@ -133,7 +137,7 @@
             env_s[m] = env_s[m] + fold(weight * (geo[9 + m : 10 + m, :] * inv_root))
         return carry
 
-    lax.fori_loop(0, K // 2, first, 0)
+    lax.fori_loop(0, K // SLOTS, first, 0)
 
     def second(k, energy):
         at = block(k)
@@ -172,7 +176,7 @@
         dgeo_s[:, at] = dgeo
         return energy
 
-    energy = lax.fori_loop(0, K // 2, second, jnp.zeros((1, span), f32))
+    energy = lax.fori_loop(0, K // SLOTS, second, jnp.zeros((1, span), f32))
     energy_ref[...] = jnp.broadcast_to(fold(energy), energy_ref.shape)
 
     def third(k, centre_grad):
@@ -208,7 +212,7 @@
         return centre_grad + fold(dpre)
 
     grad_centre_ref[...] = lax.fori_loop(
-        0, K // 2, third, jnp.zeros(grad_centre_ref.shape, f32)
+        0, K // SLOTS, third, jnp.zeros(grad_centre_ref.shape, f32)
     )
 
 
@@ -257,7 +261,7 @@
         tensor_proj.T,
         tensor_proj,
         basis_pad,
-        jnp.broadcast_to(energy_proj.astype(f32)[:, None], (width, 2 * atoms)),
+        jnp.broadcast_to(energy_proj.astype(f32)[:, None], (width, SLOTS * atoms)),
     )
     grad_rows_t, grad_centre_t, grad_geo, energy = outs
     return grad_rows_t, grad_centre_t, grad_geo, energy[0]

time: 75.9 us -> 73.8 us (0.972)
  Pallas kernels: 14.1 us -> 11.9 us
    pallas_call x1, Pallas kernels: 14.1 us -> 11.9 us  [pair_terms(): pl.pallas_call(_pair_kernel, out_shape=(jax.ShapeDtypeStruct((width, pair...]
where the time goes in v9:
time: 73.8 us; the launch traced here: 73.4 us
  matrix products  17.1 us (23%)
  starting transfers between devices  15.7 us (21%)
  waiting for transfers between devices  13.9 us (19%)
  Pallas kernels  11.9 us (16%)
  local copies, waits for them, and re-layouts  9.64 us (13%)
  other arithmetic  3.43 us (5%)
  between operations  1.83 us (2%)
    ppermute x12, starting transfers between devices, passed_along(): return lax.ppermute(block, axis, route)  15.7 us
    ppermute x12, waiting for transfers between devices, passed_along(): return lax.ppermute(block, axis, route)  13.9 us
    pallas_call x1, Pallas kernels, pair_terms(): pl.pallas_call(_pair_kernel, out_shape=(jax.ShapeDtypeStruct((width, pair...  11.9 us
    unnamed x40, local copies, waits for them, and re-layouts  3.6 us
    dot_general x1, matrix products, spread_cols(): jnp.einsum('wn,nr->wr', high, onehot, preferred_element_type=jnp.float32)  2.82 us
    dot_general x2, matrix products, project(): jnp.dot(rows, weight, preferred_element_type=jnp.float32)  2.45 us
    dot_general x3, matrix products, lookup(): return jnp.dot(onehot, table, precision=lax.Precision.HIGHEST)  2.24 us
    dot_general x6, matrix products, spread(): jnp.einsum('nr,nw->rw', onehot, high, preferred_element_type=jnp.float32)  2.09 us
  transfers between devices with their start and end apart: 12, of which 9 were waited for; matrix products, arithmetic and copies ran while one was open for 14% of the time, Pallas kernels for 0%

profile of v9, /device:TPU:0, one launch (start us, length us, event | category | flops | bytes accessed | tf_op | source)
XLA Modules:
  0.0 73.4 jit_solution(14081188918520907910)
XLA Ops:
  1.7 0.8 %slice_bitcast_fusion = (s32[16]{0:T(128)S(1)}, s32[16]{0:T(128)S(1)}, s32[16]{0:T(128)S(1)}, s32[16]{0:T(128)S(1)}) fusion(s32[1,192]{1,0:T(1,128)} %param.19), kind=kLoop, calls=%fused_computation.211 | loop fusion | bytes 512 | tf_op jit(solution)/shard_map/eq | solution.py:347
  2.5 1.0 %fusion.27 = f32[128,512]{1,0:T(8,128)S(1)} fusion(f32[5,512]{1,0:T(8,128)} %param.25, s32[128]{0:T(128)} %param.18), kind=kOutput, calls=%fused_computation.59 | convolution fusion | flops 3932800 | bytes 272896 | tf_op jit(solution)/shard_map/dot_general | solution.py:306
  3.5 1.4 %fusion.11 = bf16[128,512]{1,0:T(8,128)(2,1)S(1)} fusion(f32[128,512]{1,0:T(8,128)S(1)} %fusion.27, bf16[128,512]{1,0:T(8,128)(2,1)} %param.16, bf16[512,512]{1,0:T(8,128)(2,1)} %param.23), kind=kOutput, calls=%fused_computation.24 | convolution fusion | flops 67239936 | bytes 1048576 | tf_op jit(solution)/shard_map/dot_general | solution.py:310
  5.8 2.0 %collective-permute-start.1 = (bf16[16,640]{1,0:T(8,128)(2,1)S(1)}, bf16[16,640]{1,0:T(8,128)(2,1)S(1)}, u32[]{:S(2)}, u32[]{:S(2)}) collective-permute-start(bf16[16,640]{1,0:T(8,128)(2,1)S(1)} %convolution_convert_fusion.4), channel_id=1, source_target_pairs={{8,0},{16,8},{24,16},{0,24},{9,1},{17,9},{25,17},{1,25},{10,2},{18... | collective-permute-start | bytes 61448 | tf_op jit(solution)/shard_map/ppermute | solution.py:30
  9.8 1.1 %fusion.13.centre_ref = f32[512,128]{1,0:T(8,128)} fusion(f32[512,128]{1,0:T(8,128)S(1)} %convolution_bitcast_fusion, bf16[512,512]{1,0:T(8,128)(2,1)S(1)} %copy-done, bf16[128,512]{1,0:T(8,128)(2,1)S(1)} %copy-done.3), kind=kOutput, calls=%fused_computation.26 | convolution fusion | flops 67305472 | bytes 1179648 | tf_op jit(solution)/shard_map/dot_general | solution.py:310
  11.8 1.0 %copy.56 = bf16[512,512]{0,1:T(8,128)(2,1)} copy(bf16[512,512]{1,0:T(8,128)(2,1)S(1)} %copy-done.2) | data formatting | bytes 1048576 | tf_op args[12]
  12.8 1.0 %copy.55 = bf16[512,384]{0,1:T(8,128)(2,1)} copy(bf16[512,384]{1,0:T(8,128)(2,1)S(1)} %copy-done.4) | data formatting | bytes 786432 | tf_op args[11]
  13.8 0.9 %copy.57 = bf16[192,512]{0,1:T(8,128)(2,1)} copy(bf16[192,512]{1,0:T(8,128)(2,1)S(1)} %copy-done.6) | data formatting | bytes 393216 | tf_op args[13]
  15.0 2.4 %collective-permute-start.2 = (bf16[64,640]{1,0:T(8,128)(2,1)S(1)}, bf16[64,640]{1,0:T(8,128)(2,1)S(1)}, u32[]{:S(2)}, u32[]{:S(2)}) collective-permute-start(bf16[64,640]{1,0:T(8,128)(2,1)S(1)} %convolution_convert_fusion.1), channel_id=1, source_target_pairs={{4,0},{0,4},{5,1},{1,5},{6,2},{2,6},{7,3},{3,7},{12,8},{8,12},{13,... | collective-permute-start | bytes 245768 | tf_op jit(solution)/shard_map/ppermute | solution.py:30
  17.7 2.6 %collective-permute-done.2 = bf16[64,640]{1,0:T(8,128)(2,1)S(1)} collective-permute-done((bf16[64,640]{1,0:T(8,128)(2,1)S(1)}, bf16[64,640]{1,0:T(8,128)(2,1)S(1)}, u32[]{:S(2)}, u32[]{:S(2)}) %collective-permute-start.2) | collective-permute-done | bytes 81952 | tf_op jit(solution)/shard_map/ppermute | solution.py:30
  20.3 1.8 %collective-permute-done.3 = bf16[64,640]{1,0:T(8,128)(2,1)S(1)} collective-permute-done((bf16[64,640]{1,0:T(8,128)(2,1)S(1)}, bf16[64,640]{1,0:T(8,128)(2,1)S(1)}, u32[]{:S(2)}, u32[]{:S(2)}) %collective-permute-start.3) | collective-permute-done | bytes 81952 | tf_op jit(solution)/shard_map/ppermute | solution.py:30
  22.4 1.6 %collective-permute-start.4 = (bf16[16,640]{1,0:T(8,128)(2,1)S(1)}, bf16[16,640]{1,0:T(8,128)(2,1)S(1)}, u32[]{:S(2)}, u32[]{:S(2)}) collective-permute-start(bf16[16,640]{1,0:T(8,128)(2,1)S(1)} %convolution_convert_fusion.3), channel_id=1, source_target_pairs={{3,0},{0,1},{1,2},{2,3},{7,4},{4,5},{5,6},{6,7},{11,8},{8,9},{9,10... | collective-permute-start | bytes 61448 | tf_op jit(solution)/shard_map/ppermute | solution.py:30
  24.2 2.3 %collective-permute-start.5 = (bf16[16,640]{1,0:T(8,128)(2,1)S(1)}, bf16[16,640]{1,0:T(8,128)(2,1)S(1)}, u32[]{:S(2)}, u32[]{:S(2)}) collective-permute-start(bf16[16,640]{1,0:T(8,128)(2,1)S(1)} %convolution_convert_fusion.2), channel_id=1, source_target_pairs={{1,0},{2,1},{3,2},{0,3},{5,4},{6,5},{7,6},{4,7},{9,8},{10,9},{11,1... | collective-permute-start | bytes 61448 | tf_op jit(solution)/shard_map/ppermute | solution.py:30
  26.5 1.5 %collective-permute-done.4 = bf16[16,640]{1,0:T(8,128)(2,1)S(1)} collective-permute-done((bf16[16,640]{1,0:T(8,128)(2,1)S(1)}, bf16[16,640]{1,0:T(8,128)(2,1)S(1)}, u32[]{:S(2)}, u32[]{:S(2)}) %collective-permute-start.4) | collective-permute-done | bytes 20512 | tf_op jit(solution)/shard_map/ppermute | solution.py:30
  28.2 1.0 %fusion.2 = f32[640,1024]{1,0:T(8,128)S(1)} fusion(bf16[320,640]{1,0:T(8,128)(2,1)S(1)} %constant_dynamic-update-slice_fusion.3, s32[1024]{0:T(1024)S(1)} %bitcast.151), kind=kOutput, calls=%fused_computation.6 | convolution fusion | flops 419758080 | bytes 3035136 | tf_op jit(solution)/shard_map/tw,pt->wp/dot_general | solution.py:362
  29.3 1.1 %slice.197.rows_ref = bf16[512,1024]{1,0:T(8,128)(2,1)} slice(f32[640,1024]{1,0:T(8,128)S(1)} %fusion.2), slice={[0:512], [0:1024]} | slice | bytes 2097152 | tf_op jit(solution)/shard_map/slice | solution.py:363
  30.9 0.9 %concatenate.61.geo_ref = f32[128,1024]{1,0:T(8,128)} pad(f32[18,1024]{1,0:T(8,128)S(1)} %concatenate.60, f32[]{:T(128)} %constant.27.clone.1), padding=0_110x0_0 | pad | bytes 598020 | tf_op jit(solution)/shard_map/jvp()/concatenate | solution.py:80
  31.7 1.1 %broadcast_in_dim.99.energy_w_ref = f32[512,512]{1,0:T(8,128)} broadcast(f32[512]{0:T(512)S(1)} %copy-done.11), dimensions={0} | broadcast | bytes 1050624 | tf_op jit(solution)/shard_map/broadcast_in_dim | solution.py:264
  32.8 11.9 %shard_map.175 = (f32[512,1024]{1,0:T(8,128)}, f32[512,128]{1,0:T(8,128)}, f32[128,1024]{1,0:T(8,128)}, f32[8,128]{1,0:T(8,128)}) custom-call(bf16[512,1024]{1,0:T(8,128)(2,1)} %slice.197.rows_ref, f32[512,128]{1,0:T(8,128)} %fusion.13.centre_ref, f32[128,1024]{1,0:T(8,128)} %concatenate.61.geo_ref, bf16[512,128]{1,0:T(8,128)(2,1)} %copy.58.basis_t_ref, ...), custom_call_target="tpu_custom_call" | custom-call | flops 1610612736 | bytes 8388608 | tf_op jit(solution)/shard_map/pallas_call | solution.py:226
  44.7 1.1 %slice_multiply_fusion.4 = (f32[1,1024]{1,0:T(1,128)S(1)}, f32[1,1024]{1,0:T(1,128)S(1)}, f32[1,1024]{1,0:T(1,128)S(1)}, f32[1,1024]{1,0:T(1,128)S(1)}, f32[1,10...) fusion(f32[128,1024]{1,0:T(8,128)} %get-tuple-element.9), kind=kLoop, calls=%fused_computation.173 | loop fusion | flops 5120 | bytes 73728 | tf_op jit(solution)/shard_map/transpose(jvp())/mul | solution.py:70
  45.7 1.0 %fusion.34 = (f32[1024]{0:T(1024)S(1)}, f32[1024]{0:T(1024)S(1)}) fusion(f32[128,1024]{1,0:T(8,128)} %get-tuple-element.9, f32[1024]{0:T(1024)S(1)} %get-tuple-element.67, f32[8]{0:T(128)S(1)} %convert_multiply_fusion, f32[1024]{0:T(1024)S(1)} %get-tuple-element.66), kind=kLoop, calls=%fused_computation.73 | loop fusion | flops 55296 | bytes 49184 | tf_op jit(solution)/shard_map/transpose(jvp())/reduce_sum | solution.py:58
  46.9 2.8 %fusion.3 = f32[320,640]{1,0:T(8,128)S(1)} fusion(f32[3,1024]{1,0:T(4,128)S(1)} %bitcast.163, f32[512,1024]{1,0:T(8,128)} %get-tuple-element.8, f32[640]{0:T(1024)S(1)} %pad.21.clone, s32[1024]{0:T(1024)S(1)} %bitcast.152), kind=kOutput, calls=%fused_computation.7 | convolution fusion | flops 424017920 | bytes 2935296 | tf_op jit(solution)/shard_map/wn,nr->wr/dot_general | solution.py:316
  49.8 1.1 %fusion.8 = f32[320,640]{1,0:T(8,128)S(1)} fusion(f32[320,640]{1,0:T(8,128)S(1)} %fusion.3, f32[3,1024]{1,0:T(4,128)S(1)} %bitcast.164, f32[512,1024]{1,0:T(8,128)S(1)} %copy-done.14, f32[640]{0:T(1024)S(1)} %pad.21.clone, f32[128,3]{1,0:T(8,128)S(1)} %bitcast.149, s32[1024]{0:T(1024)S(1)} %bitcast.153), kind=kOutput, calls=%fused_computation.11 | convolution fusion | flops 424427520 | bytes 3756032 | tf_op jit(solution)/shard_map/wn,nr->wr/dot_general | solution.py:318
  50.9 1.5 %collective-permute-start.7 = (f32[16,640]{1,0:T(8,128)S(1)}, f32[16,640]{1,0:T(8,128)S(1)}, u32[]{:S(2)}, u32[]{:S(2)}) collective-permute-start(f32[16,640]{1,0:T(8,128)S(1)} %get-tuple-element.31), channel_id=1, source_target_pairs={{3,0},{0,1},{1,2},{2,3},{7,4},{4,5},{5,6},{6,7},{11,8},{8,9},{9,10... | collective-permute-start | bytes 122888 | tf_op jit(solution)/shard_map/ppermute | solution.py:30
  52.3 2.7 %collective-permute-start.6 = (f32[16,640]{1,0:T(8,128)S(1)}, f32[16,640]{1,0:T(8,128)S(1)}, u32[]{:S(2)}, u32[]{:S(2)}) collective-permute-start(f32[16,640]{1,0:T(8,128)S(1)} %get-tuple-element.30), channel_id=1, source_target_pairs={{1,0},{2,1},{3,2},{0,3},{5,4},{6,5},{7,6},{4,7},{9,8},{10,9},{11,1... | collective-permute-start | bytes 122888 | tf_op jit(solution)/shard_map/ppermute | solution.py:30
  55.0 1.7 %collective-permute-done.7 = f32[16,640]{1,0:T(8,128)S(1)} collective-permute-done((f32[16,640]{1,0:T(8,128)S(1)}, f32[16,640]{1,0:T(8,128)S(1)}, u32[]{:S(2)}, u32[]{:S(2)}) %collective-permute-start.7) | collective-permute-done | bytes 40992 | tf_op jit(solution)/shard_map/ppermute | solution.py:30
  58.4 1.3 %collective-permute-start.8 = (f32[64,640]{1,0:T(8,128)S(1)}, f32[64,640]{1,0:T(8,128)S(1)}, u32[]{:S(2)}, u32[]{:S(2)}) collective-permute-start(f32[64,640]{1,0:T(8,128)S(1)} %get-tuple-element.33), channel_id=1, source_target_pairs={{4,0},{0,4},{5,1},{1,5},{6,2},{2,6},{7,3},{3,7},{12,8},{8,12},{13,... | collective-permute-start | bytes 491528 | tf_op jit(solution)/shard_map/ppermute | solution.py:30
  60.4 0.9 %collective-permute-start.9 = (f32[64,640]{1,0:T(8,128)S(1)}, f32[64,640]{1,0:T(8,128)S(1)}, u32[]{:S(2)}, u32[]{:S(2)}) collective-permute-start(f32[64,640]{1,0:T(8,128)S(1)} %get-tuple-element.32), channel_id=1, source_target_pairs={{4,0},{0,4},{5,1},{1,5},{6,2},{2,6},{7,3},{3,7},{12,8},{8,12},{13,... | collective-permute-start | bytes 491528 | tf_op jit(solution)/shard_map/ppermute | solution.py:30
  61.2 2.5 %collective-permute-done.8 = f32[64,640]{1,0:T(8,128)S(1)} collective-permute-done((f32[64,640]{1,0:T(8,128)S(1)}, f32[64,640]{1,0:T(8,128)S(1)}, u32[]{:S(2)}, u32[]{:S(2)}) %collective-permute-start.8) | collective-permute-done | bytes 163872 | tf_op jit(solution)/shard_map/ppermute | solution.py:30
  64.4 1.3 %collective-permute-done.9 = f32[64,640]{1,0:T(8,128)S(1)} collective-permute-done((f32[64,640]{1,0:T(8,128)S(1)}, f32[64,640]{1,0:T(8,128)S(1)}, u32[]{:S(2)}, u32[]{:S(2)}) %collective-permute-start.9) | collective-permute-done | bytes 163872 | tf_op jit(solution)/shard_map/ppermute | solution.py:30
  68.9 1.9 %collective-permute-done.11 = f32[16,640]{1,0:T(8,128)S(1)} collective-permute-done((f32[16,640]{1,0:T(8,128)S(1)}, f32[16,640]{1,0:T(8,128)S(1)}, u32[]{:S(2)}, u32[]{:S(2)}) %collective-permute-start.11) | collective-permute-done | bytes 40992 | tf_op jit(solution)/shard_map/ppermute | solution.py:30
  71.4 1.3 %convolution_add_fusion.6 = f32[128,512]{1,0:T(8,128)} fusion(f32[128,512]{1,0:T(8,128)S(1)} %fusion.118, bf16[512,512]{1,0:T(8,128)(2,1)S(1)} %copy-done.1, f32[128,640]{1,0:T(8,128)S(1)} %fusion.22), kind=kOutput, calls=%fused_computation.20 | convolution fusion | flops 402718720 | bytes 1310720 | tf_op jit(solution)/shard_map/dot_general | solution.py:410
  (112 shorter events, 13.2 us)
Async XLA Ops:
  0.6 9.2 %copy-start = (bf16[512,512]{1,0:T(8,128)(2,1)S(1)}, bf16[512,512]{1,0:T(8,128)(2,1)}, u32[]{:S(2)}) copy-start(bf16[512,512]{1,0:T(8,128)(2,1)} %param.22) | copy-start | bytes 1572868
  0.6 7.3 %copy-start.8 = (s32[1,192]{1,0:T(1,128)S(1)}, s32[1,192]{1,0:T(1,128)}, u32[]{:S(2)}) copy-start(s32[1,192]{1,0:T(1,128)} %param.19) | copy-start | bytes 2308
  0.7 8.7 %copy-start.12 = (s32[128]{0:T(128)S(1)}, s32[128]{0:T(128)}, u32[]{:S(2)}) copy-start(s32[128]{0:T(128)} %param.18) | copy-start | bytes 1540
  0.7 9.1 %copy-start.3 = (bf16[128,512]{1,0:T(8,128)(2,1)S(1)}, bf16[128,512]{1,0:T(8,128)(2,1)}, u32[]{:S(2)}) copy-start(bf16[128,512]{1,0:T(8,128)(2,1)} %param.16) | copy-start | bytes 393220
  0.7 8.0 %copy-start.9 = (bf16[8,512]{1,0:T(8,128)(2,1)S(1)}, bf16[8,512]{1,0:T(8,128)(2,1)}, u32[]{:S(2)}) copy-start(bf16[8,512]{1,0:T(8,128)(2,1)} %param.26) | copy-start | bytes 24580
  0.7 8.7 %copy-start.7 = (f32[5,512]{1,0:T(8,128)S(1)}, f32[5,512]{1,0:T(8,128)}, u32[]{:S(2)}) copy-start(f32[5,512]{1,0:T(8,128)} %param.24) | copy-start | bytes 30724
  3.5 7.4 %copy-start.10 = (s32[1024]{0:T(1024)S(1)}, s32[1024]{0:T(1024)}, u32[]{:S(2)}) copy-start(s32[1024]{0:T(1024)} %param.20) | copy-start | bytes 12292
  3.5 8.3 %copy-start.2 = (bf16[512,512]{1,0:T(8,128)(2,1)S(1)}, bf16[512,512]{1,0:T(8,128)(2,1)}, u32[]{:S(2)}) copy-start(bf16[512,512]{1,0:T(8,128)(2,1)} %update_ref.1) | copy-start | bytes 1572868
  5.2 7.7 %copy-start.4 = (bf16[512,384]{1,0:T(8,128)(2,1)S(1)}, bf16[512,384]{1,0:T(8,128)(2,1)}, u32[]{:S(2)}) copy-start(bf16[512,384]{1,0:T(8,128)(2,1)} %split_ref.1) | copy-start | bytes 1179652
  5.2 9.6 %collective-permute-start = (bf16[16,640]{1,0:T(8,128)(2,1)S(1)}, bf16[16,640]{1,0:T(8,128)(2,1)S(1)}, u32[]{:S(2)}, u32[]{:S(2)}) collective-permute-start(bf16[16,640]{1,0:T(8,128)(2,1)S(1)} %convolution_convert_fusion.5), channel_id=1, source_target_pairs={{24,0},{0,8},{8,16},{16,24},{25,1},{1,9},{9,17},{17,25},{26,2},{2,... | collective-permute-start | bytes 61448 | tf_op jit(solution)/shard_map/ppermute | solution.py:30
  5.8 8.9 %collective-permute-start.1 = (bf16[16,640]{1,0:T(8,128)(2,1)S(1)}, bf16[16,640]{1,0:T(8,128)(2,1)S(1)}, u32[]{:S(2)}, u32[]{:S(2)}) collective-permute-start(bf16[16,640]{1,0:T(8,128)(2,1)S(1)} %convolution_convert_fusion.4), channel_id=1, source_target_pairs={{8,0},{16,8},{24,16},{0,24},{9,1},{17,9},{25,17},{1,25},{10,2},{18... | collective-permute-start | bytes 61448 | tf_op jit(solution)/shard_map/ppermute | solution.py:30
  7.9 5.9 %copy-start.6 = (bf16[192,512]{1,0:T(8,128)(2,1)S(1)}, bf16[192,512]{1,0:T(8,128)(2,1)}, u32[]{:S(2)}) copy-start(bf16[192,512]{1,0:T(8,128)(2,1)} %tensor_ref.1) | copy-start | bytes 589828
  15.0 5.3 %collective-permute-start.2 = (bf16[64,640]{1,0:T(8,128)(2,1)S(1)}, bf16[64,640]{1,0:T(8,128)(2,1)S(1)}, u32[]{:S(2)}, u32[]{:S(2)}) collective-permute-start(bf16[64,640]{1,0:T(8,128)(2,1)S(1)} %convolution_convert_fusion.1), channel_id=1, source_target_pairs={{4,0},{0,4},{5,1},{1,5},{6,2},{2,6},{7,3},{3,7},{12,8},{8,12},{13,... | collective-permute-start | bytes 245768 | tf_op jit(solution)/shard_map/ppermute | solution.py:30
  17.6 4.5 %collective-permute-start.3 = (bf16[64,640]{1,0:T(8,128)(2,1)S(1)}, bf16[64,640]{1,0:T(8,128)(2,1)S(1)}, u32[]{:S(2)}, u32[]{:S(2)}) collective-permute-start(bf16[64,640]{1,0:T(8,128)(2,1)S(1)} %convolution_convert_fusion), channel_id=1, source_target_pairs={{4,0},{0,4},{5,1},{1,5},{6,2},{2,6},{7,3},{3,7},{12,8},{8,12},{13,... | collective-permute-start | bytes 245768 | tf_op jit(solution)/shard_map/ppermute | solution.py:30
  22.4 5.6 %collective-permute-start.4 = (bf16[16,640]{1,0:T(8,128)(2,1)S(1)}, bf16[16,640]{1,0:T(8,128)(2,1)S(1)}, u32[]{:S(2)}, u32[]{:S(2)}) collective-permute-start(bf16[16,640]{1,0:T(8,128)(2,1)S(1)} %convolution_convert_fusion.3), channel_id=1, source_target_pairs={{3,0},{0,1},{1,2},{2,3},{7,4},{4,5},{5,6},{6,7},{11,8},{8,9},{9,10... | collective-permute-start | bytes 61448 | tf_op jit(solution)/shard_map/ppermute | solution.py:30
  24.2 4.0 %collective-permute-start.5 = (bf16[16,640]{1,0:T(8,128)(2,1)S(1)}, bf16[16,640]{1,0:T(8,128)(2,1)S(1)}, u32[]{:S(2)}, u32[]{:S(2)}) collective-permute-start(bf16[16,640]{1,0:T(8,128)(2,1)S(1)} %convolution_convert_fusion.2), channel_id=1, source_target_pairs={{1,0},{2,1},{3,2},{0,3},{5,4},{6,5},{7,6},{4,7},{9,8},{10,9},{11,1... | collective-permute-start | bytes 61448 | tf_op jit(solution)/shard_map/ppermute | solution.py:30
  29.3 2.4 %copy-start.11 = (f32[512]{0:T(512)S(1)}, f32[512]{0:T(512)}, u32[]{:S(2)}) copy-start(f32[512]{0:T(512)} %param.30) | copy-start | bytes 6148
  46.9 2.8 %copy-start.14 = (f32[512,1024]{1,0:T(8,128)S(1)}, f32[512,1024]{1,0:T(8,128)}, u32[]{:S(2)}) copy-start(f32[512,1024]{1,0:T(8,128)} %get-tuple-element.8) | copy-start | bytes 6291460
  50.9 5.9 %collective-permute-start.7 = (f32[16,640]{1,0:T(8,128)S(1)}, f32[16,640]{1,0:T(8,128)S(1)}, u32[]{:S(2)}, u32[]{:S(2)}) collective-permute-start(f32[16,640]{1,0:T(8,128)S(1)} %get-tuple-element.31), channel_id=1, source_target_pairs={{3,0},{0,1},{1,2},{2,3},{7,4},{4,5},{5,6},{6,7},{11,8},{8,9},{9,10... | collective-permute-start | bytes 122888 | tf_op jit(solution)/shard_map/ppermute | solution.py:30
  52.3 5.2 %collective-permute-start.6 = (f32[16,640]{1,0:T(8,128)S(1)}, f32[16,640]{1,0:T(8,128)S(1)}, u32[]{:S(2)}, u32[]{:S(2)}) collective-permute-start(f32[16,640]{1,0:T(8,128)S(1)} %get-tuple-element.30), channel_id=1, source_target_pairs={{1,0},{2,1},{3,2},{0,3},{5,4},{6,5},{7,6},{4,7},{9,8},{10,9},{11,1... | collective-permute-start | bytes 122888 | tf_op jit(solution)/shard_map/ppermute | solution.py:30
  57.5 2.1 %copy-start.5 = (f32[512,128]{1,0:T(8,128)S(1)}, f32[512,128]{1,0:T(8,128)}, u32[]{:S(2)}) copy-start(f32[512,128]{1,0:T(8,128)} %get-tuple-element.10) | copy-start | bytes 786436
  58.4 5.4 %collective-permute-start.8 = (f32[64,640]{1,0:T(8,128)S(1)}, f32[64,640]{1,0:T(8,128)S(1)}, u32[]{:S(2)}, u32[]{:S(2)}) collective-permute-start(f32[64,640]{1,0:T(8,128)S(1)} %get-tuple-element.33), channel_id=1, source_target_pairs={{4,0},{0,4},{5,1},{1,5},{6,2},{2,6},{7,3},{3,7},{12,8},{8,12},{13,... | collective-permute-start | bytes 491528 | tf_op jit(solution)/shard_map/ppermute | solution.py:30
  60.3 6.2 %copy-start.13 = (f32[5]{0:T(128)S(1)}, f32[5]{0:T(128)}, u32[]{:S(2)}) copy-start(f32[5]{0:T(128)} %param.31) | copy-start | bytes 64
  60.4 6.2 %copy-start.15 = (f32[8,128]{1,0:T(8,128)S(1)}, f32[8,128]{1,0:T(8,128)}, u32[]{:S(2)}) copy-start(f32[8,128]{1,0:T(8,128)} %get-tuple-element.7) | copy-start | bytes 12292
  60.4 5.4 %collective-permute-start.9 = (f32[64,640]{1,0:T(8,128)S(1)}, f32[64,640]{1,0:T(8,128)S(1)}, u32[]{:S(2)}, u32[]{:S(2)}) collective-permute-start(f32[64,640]{1,0:T(8,128)S(1)} %get-tuple-element.32), channel_id=1, source_target_pairs={{4,0},{0,4},{5,1},{1,5},{6,2},{2,6},{7,3},{3,7},{12,8},{8,12},{13,... | collective-permute-start | bytes 491528 | tf_op jit(solution)/shard_map/ppermute | solution.py:30
  66.1 5.3 %copy-start.1 = (bf16[512,512]{1,0:T(8,128)(2,1)S(1)}, bf16[512,512]{1,0:T(8,128)(2,1)}, u32[]{:S(2)}) copy-start(bf16[512,512]{1,0:T(8,128)(2,1)} %param.23) | copy-start | bytes 1572868
  66.5 1.7 %collective-permute-start.10 = (f32[16,640]{1,0:T(8,128)S(1)}, f32[16,640]{1,0:T(8,128)S(1)}, u32[]{:S(2)}, u32[]{:S(2)}) collective-permute-start(f32[16,640]{1,0:T(8,128)S(1)} %get-tuple-element.44), channel_id=1, source_target_pairs={{8,0},{16,8},{24,16},{0,24},{9,1},{17,9},{25,17},{1,25},{10,2},{18... | collective-permute-start | bytes 122888 | tf_op jit(solution)/shard_map/ppermute | solution.py:30
  67.3 3.4 %collective-permute-start.11 = (f32[16,640]{1,0:T(8,128)S(1)}, f32[16,640]{1,0:T(8,128)S(1)}, u32[]{:S(2)}, u32[]{:S(2)}) collective-permute-start(f32[16,640]{1,0:T(8,128)S(1)} %get-tuple-element.43), channel_id=1, source_target_pairs={{24,0},{0,8},{8,16},{16,24},{25,1},{1,9},{9,17},{17,25},{26,2},{2,... | collective-permute-start | bytes 122888 | tf_op jit(solution)/shard_map/ppermute | solution.py:30

commit v10 on v9

--- a/solution.py
+++ b/solution.py
@@ -42,7 +42,7 @@
     )
 
 
-SLOTS = 4
+SLOTS = 8
 ORDER_OF = (0, 1, 1, 1, 2, 2, 2, 2, 2)
 GROUPS = ((0,), (1, 2, 3), (4, 5, 6, 7, 8))
 

time: 73.8 us -> 72.3 us (0.980)
  Pallas kernels: 11.9 us -> 9.68 us
    pallas_call x1, Pallas kernels: 11.9 us -> 9.68 us  [pair_terms(): pl.pallas_call(_pair_kernel, out_shape=(jax.ShapeDtypeStruct((width, pair...]
where the time goes in v10:
time: 72.3 us; the launch traced here: 71.9 us
  matrix products  17.1 us (24%)
  starting transfers between devices  15.7 us (22%)
  waiting for transfers between devices  14.1 us (20%)
  local copies, waits for them, and re-layouts  10.1 us (14%)
  Pallas kernels  9.68 us (13%)
  other arithmetic  3.43 us (5%)
  between operations  1.83 us (3%)
    ppermute x12, starting transfers between devices, passed_along(): return lax.ppermute(block, axis, route)  15.7 us
    ppermute x12, waiting for transfers between devices, passed_along(): return lax.ppermute(block, axis, route)  14.1 us
    pallas_call x1, Pallas kernels, pair_terms(): pl.pallas_call(_pair_kernel, out_shape=(jax.ShapeDtypeStruct((width, pair...  9.68 us
    unnamed x40, local copies, waits for them, and re-layouts  3.55 us
    dot_general x1, matrix products, spread_cols(): jnp.einsum('wn,nr->wr', high, onehot, preferred_element_type=jnp.float32)  2.82 us
    dot_general x2, matrix products, project(): jnp.dot(rows, weight, preferred_element_type=jnp.float32)  2.44 us
    dot_general x3, matrix products, lookup(): return jnp.dot(onehot, table, precision=lax.Precision.HIGHEST)  2.24 us
    dot_general x6, matrix products, spread(): jnp.einsum('nr,nw->rw', onehot, high, preferred_element_type=jnp.float32)  2.09 us
  transfers between devices with their start and end apart: 12, of which 9 were waited for; matrix products, arithmetic and copies ran while one was open for 14% of the time, Pallas kernels for 0%

profile of v10, /device:TPU:0, one launch (start us, length us, event | category | flops | bytes accessed | tf_op | source)
XLA Modules:
  0.0 71.9 jit_solution(1845261255919990178)
XLA Ops:
  1.7 0.8 %slice_bitcast_fusion = (s32[16]{0:T(128)S(1)}, s32[16]{0:T(128)S(1)}, s32[16]{0:T(128)S(1)}, s32[16]{0:T(128)S(1)}) fusion(s32[1,192]{1,0:T(1,128)} %param.19), kind=kLoop, calls=%fused_computation.211 | loop fusion | bytes 512 | tf_op jit(solution)/shard_map/eq | solution.py:347
  2.5 1.0 %fusion.27 = f32[128,512]{1,0:T(8,128)S(1)} fusion(f32[5,512]{1,0:T(8,128)} %param.25, s32[128]{0:T(128)} %param.18), kind=kOutput, calls=%fused_computation.59 | convolution fusion | flops 3932800 | bytes 272896 | tf_op jit(solution)/shard_map/dot_general | solution.py:306
  3.5 1.4 %fusion.11 = bf16[128,512]{1,0:T(8,128)(2,1)S(1)} fusion(f32[128,512]{1,0:T(8,128)S(1)} %fusion.27, bf16[128,512]{1,0:T(8,128)(2,1)} %param.16, bf16[512,512]{1,0:T(8,128)(2,1)} %param.23), kind=kOutput, calls=%fused_computation.24 | convolution fusion | flops 67239936 | bytes 1048576 | tf_op jit(solution)/shard_map/dot_general | solution.py:310
  5.8 2.0 %collective-permute-start.1 = (bf16[16,640]{1,0:T(8,128)(2,1)S(1)}, bf16[16,640]{1,0:T(8,128)(2,1)S(1)}, u32[]{:S(2)}, u32[]{:S(2)}) collective-permute-start(bf16[16,640]{1,0:T(8,128)(2,1)S(1)} %convolution_convert_fusion.4), channel_id=1, source_target_pairs={{8,0},{16,8},{24,16},{0,24},{9,1},{17,9},{25,17},{1,25},{10,2},{18... | collective-permute-start | bytes 61448 | tf_op jit(solution)/shard_map/ppermute | solution.py:30
  9.8 1.0 %fusion.13.centre_ref = f32[512,128]{1,0:T(8,128)} fusion(f32[512,128]{1,0:T(8,128)S(1)} %convolution_bitcast_fusion, bf16[512,512]{1,0:T(8,128)(2,1)S(1)} %copy-done, bf16[128,512]{1,0:T(8,128)(2,1)S(1)} %copy-done.5), kind=kOutput, calls=%fused_computation.26 | convolution fusion | flops 67305472 | bytes 1179648 | tf_op jit(solution)/shard_map/dot_general | solution.py:310
  11.8 1.0 %copy.56 = bf16[512,512]{0,1:T(8,128)(2,1)} copy(bf16[512,512]{1,0:T(8,128)(2,1)S(1)} %copy-done.1) | data formatting | bytes 1048576 | tf_op args[12]
  12.8 0.9 %copy.55 = bf16[512,384]{0,1:T(8,128)(2,1)} copy(bf16[512,384]{1,0:T(8,128)(2,1)S(1)} %copy-done.3) | data formatting | bytes 786432 | tf_op args[11]
  13.8 0.8 %copy.57 = bf16[192,512]{0,1:T(8,128)(2,1)} copy(bf16[192,512]{1,0:T(8,128)(2,1)S(1)} %copy-done.4) | data formatting | bytes 393216 | tf_op args[13]
  14.9 2.4 %collective-permute-start.2 = (bf16[64,640]{1,0:T(8,128)(2,1)S(1)}, bf16[64,640]{1,0:T(8,128)(2,1)S(1)}, u32[]{:S(2)}, u32[]{:S(2)}) collective-permute-start(bf16[64,640]{1,0:T(8,128)(2,1)S(1)} %convolution_convert_fusion.1), channel_id=1, source_target_pairs={{4,0},{0,4},{5,1},{1,5},{6,2},{2,6},{7,3},{3,7},{12,8},{8,12},{13,... | collective-permute-start | bytes 245768 | tf_op jit(solution)/shard_map/ppermute | solution.py:30
  17.7 2.6 %collective-permute-done.2 = bf16[64,640]{1,0:T(8,128)(2,1)S(1)} collective-permute-done((bf16[64,640]{1,0:T(8,128)(2,1)S(1)}, bf16[64,640]{1,0:T(8,128)(2,1)S(1)}, u32[]{:S(2)}, u32[]{:S(2)}) %collective-permute-start.2) | collective-permute-done | bytes 81952 | tf_op jit(solution)/shard_map/ppermute | solution.py:30
  20.3 1.8 %collective-permute-done.3 = bf16[64,640]{1,0:T(8,128)(2,1)S(1)} collective-permute-done((bf16[64,640]{1,0:T(8,128)(2,1)S(1)}, bf16[64,640]{1,0:T(8,128)(2,1)S(1)}, u32[]{:S(2)}, u32[]{:S(2)}) %collective-permute-start.3) | collective-permute-done | bytes 81952 | tf_op jit(solution)/shard_map/ppermute | solution.py:30
  22.3 1.6 %collective-permute-start.4 = (bf16[16,640]{1,0:T(8,128)(2,1)S(1)}, bf16[16,640]{1,0:T(8,128)(2,1)S(1)}, u32[]{:S(2)}, u32[]{:S(2)}) collective-permute-start(bf16[16,640]{1,0:T(8,128)(2,1)S(1)} %convolution_convert_fusion.3), channel_id=1, source_target_pairs={{3,0},{0,1},{1,2},{2,3},{7,4},{4,5},{5,6},{6,7},{11,8},{8,9},{9,10... | collective-permute-start | bytes 61448 | tf_op jit(solution)/shard_map/ppermute | solution.py:30
  24.2 2.3 %collective-permute-start.5 = (bf16[16,640]{1,0:T(8,128)(2,1)S(1)}, bf16[16,640]{1,0:T(8,128)(2,1)S(1)}, u32[]{:S(2)}, u32[]{:S(2)}) collective-permute-start(bf16[16,640]{1,0:T(8,128)(2,1)S(1)} %convolution_convert_fusion.2), channel_id=1, source_target_pairs={{1,0},{2,1},{3,2},{0,3},{5,4},{6,5},{7,6},{4,7},{9,8},{10,9},{11,1... | collective-permute-start | bytes 61448 | tf_op jit(solution)/shard_map/ppermute | solution.py:30
  26.5 1.5 %collective-permute-done.4 = bf16[16,640]{1,0:T(8,128)(2,1)S(1)} collective-permute-done((bf16[16,640]{1,0:T(8,128)(2,1)S(1)}, bf16[16,640]{1,0:T(8,128)(2,1)S(1)}, u32[]{:S(2)}, u32[]{:S(2)}) %collective-permute-start.4) | collective-permute-done | bytes 20512 | tf_op jit(solution)/shard_map/ppermute | solution.py:30
  28.2 1.0 %fusion.2 = f32[640,1024]{1,0:T(8,128)S(1)} fusion(bf16[320,640]{1,0:T(8,128)(2,1)S(1)} %constant_dynamic-update-slice_fusion.3, s32[1024]{0:T(1024)S(1)} %bitcast.151), kind=kOutput, calls=%fused_computation.6 | convolution fusion | flops 419758080 | bytes 3035136 | tf_op jit(solution)/shard_map/tw,pt->wp/dot_general | solution.py:362
  29.3 1.2 %slice.197.rows_ref = bf16[512,1024]{1,0:T(8,128)(2,1)} slice(f32[640,1024]{1,0:T(8,128)S(1)} %fusion.2), slice={[0:512], [0:1024]} | slice | bytes 2097152 | tf_op jit(solution)/shard_map/slice | solution.py:363
  30.9 0.8 %concatenate.61.geo_ref = f32[128,1024]{1,0:T(8,128)} pad(f32[18,1024]{1,0:T(8,128)S(1)} %concatenate.60, f32[]{:T(128)} %constant.27.clone.1), padding=0_110x0_0 | pad | bytes 598020 | tf_op jit(solution)/shard_map/jvp()/concatenate | solution.py:80
  31.7 1.6 %broadcast_in_dim.99.energy_w_ref = f32[512,1024]{1,0:T(8,128)} broadcast(f32[512]{0:T(512)S(1)} %copy-done.11), dimensions={0} | broadcast | bytes 2099200 | tf_op jit(solution)/shard_map/broadcast_in_dim | solution.py:264
  33.3 9.7 %shard_map.175 = (f32[512,1024]{1,0:T(8,128)}, f32[512,128]{1,0:T(8,128)}, f32[128,1024]{1,0:T(8,128)}, f32[8,128]{1,0:T(8,128)}) custom-call(bf16[512,1024]{1,0:T(8,128)(2,1)} %slice.197.rows_ref, f32[512,128]{1,0:T(8,128)} %fusion.13.centre_ref, f32[128,1024]{1,0:T(8,128)} %concatenate.61.geo_ref, bf16[512,128]{1,0:T(8,128)(2,1)} %copy.58.basis_t_ref, ...), custom_call_target="tpu_custom_call" | custom-call | flops 1610612736 | bytes 8388608 | tf_op jit(solution)/shard_map/pallas_call | solution.py:226
  42.9 1.1 %slice_multiply_fusion.4 = (f32[1,1024]{1,0:T(1,128)S(1)}, f32[1,1024]{1,0:T(1,128)S(1)}, f32[1,1024]{1,0:T(1,128)S(1)}, f32[1,1024]{1,0:T(1,128)S(1)}, f32[1,10...) fusion(f32[128,1024]{1,0:T(8,128)} %get-tuple-element.9), kind=kLoop, calls=%fused_computation.173 | loop fusion | flops 5120 | bytes 73728 | tf_op jit(solution)/shard_map/transpose(jvp())/mul | solution.py:70
  44.0 1.0 %fusion.34 = (f32[1024]{0:T(1024)S(1)}, f32[1024]{0:T(1024)S(1)}) fusion(f32[128,1024]{1,0:T(8,128)} %get-tuple-element.9, f32[1024]{0:T(1024)S(1)} %get-tuple-element.67, f32[8]{0:T(128)S(1)} %convert_multiply_fusion, f32[1024]{0:T(1024)S(1)} %get-tuple-element.66), kind=kLoop, calls=%fused_computation.73 | loop fusion | flops 55296 | bytes 49184 | tf_op jit(solution)/shard_map/transpose(jvp())/reduce_sum | solution.py:58
  45.2 2.8 %fusion.3 = f32[320,640]{1,0:T(8,128)S(1)} fusion(f32[3,1024]{1,0:T(4,128)S(1)} %bitcast.163, f32[512,1024]{1,0:T(8,128)} %get-tuple-element.8, f32[640]{0:T(1024)S(1)} %pad.21.clone, s32[1024]{0:T(1024)S(1)} %bitcast.152), kind=kOutput, calls=%fused_computation.7 | convolution fusion | flops 424017920 | bytes 2935296 | tf_op jit(solution)/shard_map/wn,nr->wr/dot_general | solution.py:316
  48.0 1.1 %fusion.8 = f32[320,640]{1,0:T(8,128)S(1)} fusion(f32[320,640]{1,0:T(8,128)S(1)} %fusion.3, f32[3,1024]{1,0:T(4,128)S(1)} %bitcast.164, f32[512,1024]{1,0:T(8,128)S(1)} %copy-done.13, f32[640]{0:T(1024)S(1)} %pad.21.clone, f32[128,3]{1,0:T(8,128)S(1)} %bitcast.149, s32[1024]{0:T(1024)S(1)} %bitcast.153), kind=kOutput, calls=%fused_computation.11 | convolution fusion | flops 424427520 | bytes 3756032 | tf_op jit(solution)/shard_map/wn,nr->wr/dot_general | solution.py:318
  49.1 1.6 %collective-permute-start.7 = (f32[16,640]{1,0:T(8,128)S(1)}, f32[16,640]{1,0:T(8,128)S(1)}, u32[]{:S(2)}, u32[]{:S(2)}) collective-permute-start(f32[16,640]{1,0:T(8,128)S(1)} %get-tuple-element.31), channel_id=1, source_target_pairs={{3,0},{0,1},{1,2},{2,3},{7,4},{4,5},{5,6},{6,7},{11,8},{8,9},{9,10... | collective-permute-start | bytes 122888 | tf_op jit(solution)/shard_map/ppermute | solution.py:30
  50.8 2.5 %collective-permute-start.6 = (f32[16,640]{1,0:T(8,128)S(1)}, f32[16,640]{1,0:T(8,128)S(1)}, u32[]{:S(2)}, u32[]{:S(2)}) collective-permute-start(f32[16,640]{1,0:T(8,128)S(1)} %get-tuple-element.30), channel_id=1, source_target_pairs={{1,0},{2,1},{3,2},{0,3},{5,4},{6,5},{7,6},{4,7},{9,8},{10,9},{11,1... | collective-permute-start | bytes 122888 | tf_op jit(solution)/shard_map/ppermute | solution.py:30
  53.3 1.9 %collective-permute-done.7 = f32[16,640]{1,0:T(8,128)S(1)} collective-permute-done((f32[16,640]{1,0:T(8,128)S(1)}, f32[16,640]{1,0:T(8,128)S(1)}, u32[]{:S(2)}, u32[]{:S(2)}) %collective-permute-start.7) | collective-permute-done | bytes 40992 | tf_op jit(solution)/shard_map/ppermute | solution.py:30
  56.8 1.3 %collective-permute-start.8 = (f32[64,640]{1,0:T(8,128)S(1)}, f32[64,640]{1,0:T(8,128)S(1)}, u32[]{:S(2)}, u32[]{:S(2)}) collective-permute-start(f32[64,640]{1,0:T(8,128)S(1)} %get-tuple-element.33), channel_id=1, source_target_pairs={{4,0},{0,4},{5,1},{1,5},{6,2},{2,6},{7,3},{3,7},{12,8},{8,12},{13,... | collective-permute-start | bytes 491528 | tf_op jit(solution)/shard_map/ppermute | solution.py:30
  58.8 0.9 %collective-permute-start.9 = (f32[64,640]{1,0:T(8,128)S(1)}, f32[64,640]{1,0:T(8,128)S(1)}, u32[]{:S(2)}, u32[]{:S(2)}) collective-permute-start(f32[64,640]{1,0:T(8,128)S(1)} %get-tuple-element.32), channel_id=1, source_target_pairs={{4,0},{0,4},{5,1},{1,5},{6,2},{2,6},{7,3},{3,7},{12,8},{8,12},{13,... | collective-permute-start | bytes 491528 | tf_op jit(solution)/shard_map/ppermute | solution.py:30
  59.7 2.5 %collective-permute-done.8 = f32[64,640]{1,0:T(8,128)S(1)} collective-permute-done((f32[64,640]{1,0:T(8,128)S(1)}, f32[64,640]{1,0:T(8,128)S(1)}, u32[]{:S(2)}, u32[]{:S(2)}) %collective-permute-start.8) | collective-permute-done | bytes 163872 | tf_op jit(solution)/shard_map/ppermute | solution.py:30
  62.9 1.3 %collective-permute-done.9 = f32[64,640]{1,0:T(8,128)S(1)} collective-permute-done((f32[64,640]{1,0:T(8,128)S(1)}, f32[64,640]{1,0:T(8,128)S(1)}, u32[]{:S(2)}, u32[]{:S(2)}) %collective-permute-start.9) | collective-permute-done | bytes 163872 | tf_op jit(solution)/shard_map/ppermute | solution.py:30
  67.3 1.9 %collective-permute-done.11 = f32[16,640]{1,0:T(8,128)S(1)} collective-permute-done((f32[16,640]{1,0:T(8,128)S(1)}, f32[16,640]{1,0:T(8,128)S(1)}, u32[]{:S(2)}, u32[]{:S(2)}) %collective-permute-start.11) | collective-permute-done | bytes 40992 | tf_op jit(solution)/shard_map/ppermute | solution.py:30
  69.9 1.3 %convolution_add_fusion.6 = f32[128,512]{1,0:T(8,128)} fusion(f32[128,512]{1,0:T(8,128)S(1)} %fusion.118, bf16[512,512]{1,0:T(8,128)(2,1)S(1)} %copy-done.2, f32[128,640]{1,0:T(8,128)S(1)} %fusion.22), kind=kOutput, calls=%fused_computation.20 | convolution fusion | flops 402718720 | bytes 1310720 | tf_op jit(solution)/shard_map/dot_general | solution.py:410
  (112 shorter events, 13.3 us)
Async XLA Ops:
  0.6 9.2 %copy-start = (bf16[512,512]{1,0:T(8,128)(2,1)S(1)}, bf16[512,512]{1,0:T(8,128)(2,1)}, u32[]{:S(2)}) copy-start(bf16[512,512]{1,0:T(8,128)(2,1)} %param.22) | copy-start | bytes 1572868
  0.6 7.3 %copy-start.8 = (s32[1,192]{1,0:T(1,128)S(1)}, s32[1,192]{1,0:T(1,128)}, u32[]{:S(2)}) copy-start(s32[1,192]{1,0:T(1,128)} %param.19) | copy-start | bytes 2308
  0.7 8.7 %copy-start.12 = (s32[128]{0:T(128)S(1)}, s32[128]{0:T(128)}, u32[]{:S(2)}) copy-start(s32[128]{0:T(128)} %param.18) | copy-start | bytes 1540
  0.7 9.2 %copy-start.5 = (bf16[128,512]{1,0:T(8,128)(2,1)S(1)}, bf16[128,512]{1,0:T(8,128)(2,1)}, u32[]{:S(2)}) copy-start(bf16[128,512]{1,0:T(8,128)(2,1)} %param.16) | copy-start | bytes 393220
  0.7 8.0 %copy-start.9 = (bf16[8,512]{1,0:T(8,128)(2,1)S(1)}, bf16[8,512]{1,0:T(8,128)(2,1)}, u32[]{:S(2)}) copy-start(bf16[8,512]{1,0:T(8,128)(2,1)} %param.26) | copy-start | bytes 24580
  0.7 8.7 %copy-start.7 = (f32[5,512]{1,0:T(8,128)S(1)}, f32[5,512]{1,0:T(8,128)}, u32[]{:S(2)}) copy-start(f32[5,512]{1,0:T(8,128)} %param.24) | copy-start | bytes 30724
  3.5 7.4 %copy-start.10 = (s32[1024]{0:T(1024)S(1)}, s32[1024]{0:T(1024)}, u32[]{:S(2)}) copy-start(s32[1024]{0:T(1024)} %param.20) | copy-start | bytes 12292
  3.5 8.3 %copy-start.1 = (bf16[512,512]{1,0:T(8,128)(2,1)S(1)}, bf16[512,512]{1,0:T(8,128)(2,1)}, u32[]{:S(2)}) copy-start(bf16[512,512]{1,0:T(8,128)(2,1)} %update_ref.1) | copy-start | bytes 1572868
  5.2 7.7 %copy-start.3 = (bf16[512,384]{1,0:T(8,128)(2,1)S(1)}, bf16[512,384]{1,0:T(8,128)(2,1)}, u32[]{:S(2)}) copy-start(bf16[512,384]{1,0:T(8,128)(2,1)} %split_ref.1) | copy-start | bytes 1179652
  5.2 9.5 %collective-permute-start = (bf16[16,640]{1,0:T(8,128)(2,1)S(1)}, bf16[16,640]{1,0:T(8,128)(2,1)S(1)}, u32[]{:S(2)}, u32[]{:S(2)}) collective-permute-start(bf16[16,640]{1,0:T(8,128)(2,1)S(1)} %convolution_convert_fusion.5), channel_id=1, source_target_pairs={{24,0},{0,8},{8,16},{16,24},{25,1},{1,9},{9,17},{17,25},{26,2},{2,... | collective-permute-start | bytes 61448 | tf_op jit(solution)/shard_map/ppermute | solution.py:30
  5.8 8.9 %collective-permute-start.1 = (bf16[16,640]{1,0:T(8,128)(2,1)S(1)}, bf16[16,640]{1,0:T(8,128)(2,1)S(1)}, u32[]{:S(2)}, u32[]{:S(2)}) collective-permute-start(bf16[16,640]{1,0:T(8,128)(2,1)S(1)} %convolution_convert_fusion.4), channel_id=1, source_target_pairs={{8,0},{16,8},{24,16},{0,24},{9,1},{17,9},{25,17},{1,25},{10,2},{18... | collective-permute-start | bytes 61448 | tf_op jit(solution)/shard_map/ppermute | solution.py:30
  7.9 5.9 %copy-start.4 = (bf16[192,512]{1,0:T(8,128)(2,1)S(1)}, bf16[192,512]{1,0:T(8,128)(2,1)}, u32[]{:S(2)}) copy-start(bf16[192,512]{1,0:T(8,128)(2,1)} %tensor_ref.1) | copy-start | bytes 589828
  14.9 5.3 %collective-permute-start.2 = (bf16[64,640]{1,0:T(8,128)(2,1)S(1)}, bf16[64,640]{1,0:T(8,128)(2,1)S(1)}, u32[]{:S(2)}, u32[]{:S(2)}) collective-permute-start(bf16[64,640]{1,0:T(8,128)(2,1)S(1)} %convolution_convert_fusion.1), channel_id=1, source_target_pairs={{4,0},{0,4},{5,1},{1,5},{6,2},{2,6},{7,3},{3,7},{12,8},{8,12},{13,... | collective-permute-start | bytes 245768 | tf_op jit(solution)/shard_map/ppermute | solution.py:30
  17.6 4.5 %collective-permute-start.3 = (bf16[64,640]{1,0:T(8,128)(2,1)S(1)}, bf16[64,640]{1,0:T(8,128)(2,1)S(1)}, u32[]{:S(2)}, u32[]{:S(2)}) collective-permute-start(bf16[64,640]{1,0:T(8,128)(2,1)S(1)} %convolution_convert_fusion), channel_id=1, source_target_pairs={{4,0},{0,4},{5,1},{1,5},{6,2},{2,6},{7,3},{3,7},{12,8},{8,12},{13,... | collective-permute-start | bytes 245768 | tf_op jit(solution)/shard_map/ppermute | solution.py:30
  22.3 5.6 %collective-permute-start.4 = (bf16[16,640]{1,0:T(8,128)(2,1)S(1)}, bf16[16,640]{1,0:T(8,128)(2,1)S(1)}, u32[]{:S(2)}, u32[]{:S(2)}) collective-permute-start(bf16[16,640]{1,0:T(8,128)(2,1)S(1)} %convolution_convert_fusion.3), channel_id=1, source_target_pairs={{3,0},{0,1},{1,2},{2,3},{7,4},{4,5},{5,6},{6,7},{11,8},{8,9},{9,10... | collective-permute-start | bytes 61448 | tf_op jit(solution)/shard_map/ppermute | solution.py:30
  24.2 4.0 %collective-permute-start.5 = (bf16[16,640]{1,0:T(8,128)(2,1)S(1)}, bf16[16,640]{1,0:T(8,128)(2,1)S(1)}, u32[]{:S(2)}, u32[]{:S(2)}) collective-permute-start(bf16[16,640]{1,0:T(8,128)(2,1)S(1)} %convolution_convert_fusion.2), channel_id=1, source_target_pairs={{1,0},{2,1},{3,2},{0,3},{5,4},{6,5},{7,6},{4,7},{9,8},{10,9},{11,1... | collective-permute-start | bytes 61448 | tf_op jit(solution)/shard_map/ppermute | solution.py:30
  29.2 2.5 %copy-start.11 = (f32[512]{0:T(512)S(1)}, f32[512]{0:T(512)}, u32[]{:S(2)}) copy-start(f32[512]{0:T(512)} %param.30) | copy-start | bytes 6148
  45.2 2.8 %copy-start.13 = (f32[512,1024]{1,0:T(8,128)S(1)}, f32[512,1024]{1,0:T(8,128)}, u32[]{:S(2)}) copy-start(f32[512,1024]{1,0:T(8,128)} %get-tuple-element.8) | copy-start | bytes 6291460
  49.1 6.1 %collective-permute-start.7 = (f32[16,640]{1,0:T(8,128)S(1)}, f32[16,640]{1,0:T(8,128)S(1)}, u32[]{:S(2)}, u32[]{:S(2)}) collective-permute-start(f32[16,640]{1,0:T(8,128)S(1)} %get-tuple-element.31), channel_id=1, source_target_pairs={{3,0},{0,1},{1,2},{2,3},{7,4},{4,5},{5,6},{6,7},{11,8},{8,9},{9,10... | collective-permute-start | bytes 122888 | tf_op jit(solution)/shard_map/ppermute | solution.py:30
  50.8 5.2 %collective-permute-start.6 = (f32[16,640]{1,0:T(8,128)S(1)}, f32[16,640]{1,0:T(8,128)S(1)}, u32[]{:S(2)}, u32[]{:S(2)}) collective-permute-start(f32[16,640]{1,0:T(8,128)S(1)} %get-tuple-element.30), channel_id=1, source_target_pairs={{1,0},{2,1},{3,2},{0,3},{5,4},{6,5},{7,6},{4,7},{9,8},{10,9},{11,1... | collective-permute-start | bytes 122888 | tf_op jit(solution)/shard_map/ppermute | solution.py:30
  56.0 2.1 %copy-start.6 = (f32[512,128]{1,0:T(8,128)S(1)}, f32[512,128]{1,0:T(8,128)}, u32[]{:S(2)}) copy-start(f32[512,128]{1,0:T(8,128)} %get-tuple-element.10) | copy-start | bytes 786436
  56.8 5.4 %collective-permute-start.8 = (f32[64,640]{1,0:T(8,128)S(1)}, f32[64,640]{1,0:T(8,128)S(1)}, u32[]{:S(2)}, u32[]{:S(2)}) collective-permute-start(f32[64,640]{1,0:T(8,128)S(1)} %get-tuple-element.33), channel_id=1, source_target_pairs={{4,0},{0,4},{5,1},{1,5},{6,2},{2,6},{7,3},{3,7},{12,8},{8,12},{13,... | collective-permute-start | bytes 491528 | tf_op jit(solution)/shard_map/ppermute | solution.py:30
  58.8 6.2 %copy-start.14 = (f32[8,128]{1,0:T(8,128)S(1)}, f32[8,128]{1,0:T(8,128)}, u32[]{:S(2)}) copy-start(f32[8,128]{1,0:T(8,128)} %get-tuple-element.7) | copy-start | bytes 12292
  58.8 6.2 %copy-start.15 = (f32[5]{0:T(128)S(1)}, f32[5]{0:T(128)}, u32[]{:S(2)}) copy-start(f32[5]{0:T(128)} %param.31) | copy-start | bytes 64
  58.8 5.4 %collective-permute-start.9 = (f32[64,640]{1,0:T(8,128)S(1)}, f32[64,640]{1,0:T(8,128)S(1)}, u32[]{:S(2)}, u32[]{:S(2)}) collective-permute-start(f32[64,640]{1,0:T(8,128)S(1)} %get-tuple-element.32), channel_id=1, source_target_pairs={{4,0},{0,4},{5,1},{1,5},{6,2},{2,6},{7,3},{3,7},{12,8},{8,12},{13,... | collective-permute-start | bytes 491528 | tf_op jit(solution)/shard_map/ppermute | solution.py:30
  64.6 5.3 %copy-start.2 = (bf16[512,512]{1,0:T(8,128)(2,1)S(1)}, bf16[512,512]{1,0:T(8,128)(2,1)}, u32[]{:S(2)}) copy-start(bf16[512,512]{1,0:T(8,128)(2,1)} %param.23) | copy-start | bytes 1572868
  64.9 1.7 %collective-permute-start.10 = (f32[16,640]{1,0:T(8,128)S(1)}, f32[16,640]{1,0:T(8,128)S(1)}, u32[]{:S(2)}, u32[]{:S(2)}) collective-permute-start(f32[16,640]{1,0:T(8,128)S(1)} %get-tuple-element.44), channel_id=1, source_target_pairs={{8,0},{16,8},{24,16},{0,24},{9,1},{17,9},{25,17},{1,25},{10,2},{18... | collective-permute-start | bytes 122888 | tf_op jit(solution)/shard_map/ppermute | solution.py:30
  65.8 3.4 %collective-permute-start.11 = (f32[16,640]{1,0:T(8,128)S(1)}, f32[16,640]{1,0:T(8,128)S(1)}, u32[]{:S(2)}, u32[]{:S(2)}) collective-permute-start(f32[16,640]{1,0:T(8,128)S(1)} %get-tuple-element.43), channel_id=1, source_target_pairs={{24,0},{0,8},{8,16},{16,24},{25,1},{1,9},{9,17},{17,25},{26,2},{2,... | collective-permute-start | bytes 122888 | tf_op jit(solution)/shard_map/ppermute | solution.py:30

commit v11 on v10

--- a/solution.py
+++ b/solution.py
@@ -124,7 +124,7 @@
         at = block(k)
         geo = geo_ref[:, at]
         radial = split_mm(basis_t_ref[...], geo)
-        pre = twice(centre_ref[...]) + rows_ref[:, at].astype(f32) + radial
+        pre = twice(centre_ref[...]) + rows_ref[0 : centre_ref.shape[0], at] + radial
         envelope = geo[8:9, :]
         hidden = pre * _sigmoid(pre) * envelope
         pre_s[:, at] = pre
@@ -157,9 +157,9 @@
         z = _mm(update_t_ref[...], hidden.astype(bf16)) + _mm(tensor_t_ref[...], scalars)
         gate = _sigmoid(z)
         update = z * gate
-        readout = jnp.sum((hidden + update) * energy_w_ref[...], axis=0, keepdims=True)
+        readout = jnp.sum((hidden + update) * twice(energy_w_ref[...]), axis=0, keepdims=True)
         energy = energy + envelope * readout
-        dz = (envelope * energy_w_ref[...]) * (gate * (1.0 + z * (1.0 - gate)))
+        dz = (envelope * twice(energy_w_ref[...])) * (gate * (1.0 + z * (1.0 - gate)))
         dz_low = dz.astype(bf16)
         dscalars = _mm(tensor_ref[...], dz_low).astype(bf16).astype(f32)
         dlow_s[:, at] = _mm(update_ref[...], dz_low)
@@ -200,7 +200,7 @@
             dweights.append(dweight)
         dmixed = jnp.concatenate([damp_s[:, at]] + dweights, axis=0).astype(bf16)
         dlow = dlow_s[:, at] + _mm(split_ref[...], dmixed)
-        dhidden = envelope * energy_w_ref[...] + dlow
+        dhidden = envelope * twice(energy_w_ref[...]) + dlow
         pre = pre_s[:, at]
         sig = _sigmoid(pre)
         act = pre * sig
@@ -217,8 +217,8 @@
 
 
 def pair_terms(rows_t, centre_t, geo, basis_proj, split_proj, update_proj, tensor_proj, energy_proj):
-    width, pairs = rows_t.shape
-    atoms = centre_t.shape[1]
+    width, atoms = centre_t.shape
+    pairs = rows_t.shape[1]
     f32 = jnp.float32
     bf16 = jnp.bfloat16
     basis_pad = jnp.concatenate([basis_proj, jnp.zeros((128 - NB, width), bf16)], axis=0)
@@ -261,7 +261,7 @@
         tensor_proj.T,
         tensor_proj,
         basis_pad,
-        jnp.broadcast_to(energy_proj.astype(f32)[:, None], (width, SLOTS * atoms)),
+        jnp.broadcast_to(energy_proj.astype(f32)[:, None], (width, atoms)),
     )
     grad_rows_t, grad_centre_t, grad_geo, energy = outs
     return grad_rows_t, grad_centre_t, grad_geo, energy[0]
@@ -360,7 +360,7 @@
         jnp.bfloat16
     )
     gathered = jnp.einsum("tw,pt->wp", table, select, preferred_element_type=jnp.float32)
-    neigh_cols = gathered[:width].astype(jnp.bfloat16)
+    neigh_cols = gathered
     coords_n = gathered[width : width + 3] * 16.0 + gathered[width + 3 : width + 6]
     delta = (coords_n.reshape(3, K, atoms) - positions.astype(jnp.float32)[:, None, :]) * (
         1.0 / 64.0

time: 72.3 us -> 74.2 us (1.026)
  other arithmetic: 3.43 us -> 4.52 us
  local copies, waits for them, and re-layouts: 10.1 us -> 11.1 us
    slice x1 -> x0, local copies, waits for them, and re-layouts: 1.18 us -> none  [shards(): neigh_cols = gathered[:width].astype(jnp.bfloat16)]
    unnamed x40 -> x88, local copies, waits for them, and re-layouts: 3.55 us -> 4.24 us
  transfers between devices with their start and end apart: 12 -> 12, of which waited for: 9 -> 9; matrix products, arithmetic and copies ran while one was open for 14% -> 18% of each run, Pallas kernels for 0% -> 0%
where the time goes in v11:
time: 74.2 us; the launch traced here: 73.8 us
  matrix products  17.1 us (23%)
  starting transfers between devices  15.7 us (21%)
  waiting for transfers between devices  13.9 us (19%)
  local copies, waits for them, and re-layouts  11.1 us (15%)
  Pallas kernels  9.42 us (13%)
  other arithmetic  4.52 us (6%)
  between operations  2.08 us (3%)
    ppermute x12, starting transfers between devices, passed_along(): return lax.ppermute(block, axis, route)  15.7 us
    ppermute x12, waiting for transfers between devices, passed_along(): return lax.ppermute(block, axis, route)  13.9 us
    pallas_call x1, Pallas kernels, pair_terms(): pl.pallas_call(_pair_kernel, out_shape=(jax.ShapeDtypeStruct((width, pair...  9.42 us
    unnamed x88, local copies, waits for them, and re-layouts  4.24 us
    dot_general x1, matrix products, spread_cols(): jnp.einsum('wn,nr->wr', high, onehot, preferred_element_type=jnp.float32)  2.82 us
    dot_general x2, matrix products, project(): jnp.dot(rows, weight, preferred_element_type=jnp.float32)  2.44 us
    dot_general x3, matrix products, lookup(): return jnp.dot(onehot, table, precision=lax.Precision.HIGHEST)  2.24 us
    dot_general x6, matrix products, spread(): jnp.einsum('nr,nw->rw', onehot, high, preferred_element_type=jnp.float32)  2.09 us
  transfers between devices with their start and end apart: 12, of which 9 were waited for; matrix products, arithmetic and copies ran while one was open for 18% of the time, Pallas kernels for 0%

profile of v11, /device:TPU:0, one launch (start us, length us, event | category | flops | bytes accessed | tf_op | source)
XLA Modules:
  0.0 73.8 jit_solution(7188920042826956561)
XLA Ops:
  0.7 0.8 %fusion.117 = (f32[3,128]{1,0:T(4,128)S(1)}, bf16[3,128]{1,0:T(4,128)(2,1)S(1)}, bf16[3,128]{1,0:T(4,128)(2,1)S(1)}) fusion(s32[3,128]{1,0:T(4,128)} %param.17), kind=kLoop, calls=%fused_computation.226 | loop fusion | flops 7680 | bytes 4608 | tf_op jit(solution)/shard_map/convert_element_type | solution.py:365
  1.7 0.8 %slice_bitcast_fusion = (s32[16]{0:T(128)S(1)}, s32[16]{0:T(128)S(1)}, s32[16]{0:T(128)S(1)}, s32[16]{0:T(128)S(1)}) fusion(s32[1,192]{1,0:T(1,128)} %param.19), kind=kLoop, calls=%fused_computation.210 | loop fusion | bytes 512 | tf_op jit(solution)/shard_map/eq | solution.py:347
  2.5 1.0 %fusion.27 = f32[128,512]{1,0:T(8,128)S(1)} fusion(f32[5,512]{1,0:T(8,128)} %param.25, s32[128]{0:T(128)} %param.18), kind=kOutput, calls=%fused_computation.58 | convolution fusion | flops 3932800 | bytes 272896 | tf_op jit(solution)/shard_map/dot_general | solution.py:306
  3.6 1.4 %fusion.11 = bf16[128,512]{1,0:T(8,128)(2,1)S(1)} fusion(f32[128,512]{1,0:T(8,128)S(1)} %fusion.27, bf16[128,512]{1,0:T(8,128)(2,1)} %param.16, bf16[512,512]{1,0:T(8,128)(2,1)} %param.23), kind=kOutput, calls=%fused_computation.23 | convolution fusion | flops 67239936 | bytes 1048576 | tf_op jit(solution)/shard_map/dot_general | solution.py:310
  5.9 2.0 %collective-permute-start.1 = (bf16[16,640]{1,0:T(8,128)(2,1)S(1)}, bf16[16,640]{1,0:T(8,128)(2,1)S(1)}, u32[]{:S(2)}, u32[]{:S(2)}) collective-permute-start(bf16[16,640]{1,0:T(8,128)(2,1)S(1)} %convolution_convert_fusion.4), channel_id=1, source_target_pairs={{8,0},{16,8},{24,16},{0,24},{9,1},{17,9},{25,17},{1,25},{10,2},{18... | collective-permute-start | bytes 61448 | tf_op jit(solution)/shard_map/ppermute | solution.py:30
  11.0 1.0 %fusion.13.centre_ref = f32[512,128]{1,0:T(8,128)} fusion(f32[512,128]{1,0:T(8,128)S(1)} %convolution_bitcast_fusion, bf16[512,512]{1,0:T(8,128)(2,1)S(1)} %copy-done, bf16[128,512]{1,0:T(8,128)(2,1)S(1)} %copy-done.6), kind=kOutput, calls=%fused_computation.25 | convolution fusion | flops 67305472 | bytes 1179648 | tf_op jit(solution)/shard_map/dot_general | solution.py:310
  14.1 1.0 %copy.56 = bf16[512,512]{0,1:T(8,128)(2,1)} copy(bf16[512,512]{1,0:T(8,128)(2,1)S(1)} %copy-done.2) | data formatting | bytes 1048576 | tf_op args[12]
  15.1 0.9 %copy.55 = bf16[512,384]{0,1:T(8,128)(2,1)} copy(bf16[512,384]{1,0:T(8,128)(2,1)S(1)} %copy-done.4) | data formatting | bytes 786432 | tf_op args[11]
  16.1 0.8 %copy.57 = bf16[192,512]{0,1:T(8,128)(2,1)} copy(bf16[192,512]{1,0:T(8,128)(2,1)S(1)} %copy-done.5) | data formatting | bytes 393216 | tf_op args[13]
  17.9 2.4 %collective-permute-start.2 = (bf16[64,640]{1,0:T(8,128)(2,1)S(1)}, bf16[64,640]{1,0:T(8,128)(2,1)S(1)}, u32[]{:S(2)}, u32[]{:S(2)}) collective-permute-start(bf16[64,640]{1,0:T(8,128)(2,1)S(1)} %convolution_convert_fusion.1), channel_id=1, source_target_pairs={{4,0},{0,4},{5,1},{1,5},{6,2},{2,6},{7,3},{3,7},{12,8},{8,12},{13,... | collective-permute-start | bytes 245768 | tf_op jit(solution)/shard_map/ppermute | solution.py:30
  20.6 2.6 %collective-permute-done.2 = bf16[64,640]{1,0:T(8,128)(2,1)S(1)} collective-permute-done((bf16[64,640]{1,0:T(8,128)(2,1)S(1)}, bf16[64,640]{1,0:T(8,128)(2,1)S(1)}, u32[]{:S(2)}, u32[]{:S(2)}) %collective-permute-start.2) | collective-permute-done | bytes 81952 | tf_op jit(solution)/shard_map/ppermute | solution.py:30
  23.2 1.8 %collective-permute-done.3 = bf16[64,640]{1,0:T(8,128)(2,1)S(1)} collective-permute-done((bf16[64,640]{1,0:T(8,128)(2,1)S(1)}, bf16[64,640]{1,0:T(8,128)(2,1)S(1)}, u32[]{:S(2)}, u32[]{:S(2)}) %collective-permute-start.3) | collective-permute-done | bytes 81952 | tf_op jit(solution)/shard_map/ppermute | solution.py:30
  25.3 1.6 %collective-permute-start.4 = (bf16[16,640]{1,0:T(8,128)(2,1)S(1)}, bf16[16,640]{1,0:T(8,128)(2,1)S(1)}, u32[]{:S(2)}, u32[]{:S(2)}) collective-permute-start(bf16[16,640]{1,0:T(8,128)(2,1)S(1)} %convolution_convert_fusion.3), channel_id=1, source_target_pairs={{3,0},{0,1},{1,2},{2,3},{7,4},{4,5},{5,6},{6,7},{11,8},{8,9},{9,10... | collective-permute-start | bytes 61448 | tf_op jit(solution)/shard_map/ppermute | solution.py:30
  27.1 2.3 %collective-permute-start.5 = (bf16[16,640]{1,0:T(8,128)(2,1)S(1)}, bf16[16,640]{1,0:T(8,128)(2,1)S(1)}, u32[]{:S(2)}, u32[]{:S(2)}) collective-permute-start(bf16[16,640]{1,0:T(8,128)(2,1)S(1)} %convolution_convert_fusion.2), channel_id=1, source_target_pairs={{1,0},{2,1},{3,2},{0,3},{5,4},{6,5},{7,6},{4,7},{9,8},{10,9},{11,1... | collective-permute-start | bytes 61448 | tf_op jit(solution)/shard_map/ppermute | solution.py:30
  29.4 1.5 %collective-permute-done.4 = bf16[16,640]{1,0:T(8,128)(2,1)S(1)} collective-permute-done((bf16[16,640]{1,0:T(8,128)(2,1)S(1)}, bf16[16,640]{1,0:T(8,128)(2,1)S(1)}, u32[]{:S(2)}, u32[]{:S(2)}) %collective-permute-start.4) | collective-permute-done | bytes 20512 | tf_op jit(solution)/shard_map/ppermute | solution.py:30
  31.1 1.1 %fusion.2.rows_ref = f32[640,1024]{1,0:T(8,128)S(1)} fusion(bf16[320,640]{1,0:T(8,128)(2,1)S(1)} %constant_dynamic-update-slice_fusion.3, s32[1024]{0:T(1024)S(1)} %bitcast.151), kind=kOutput, calls=%fused_computation.5 | convolution fusion | flops 419758080 | bytes 3035136 | tf_op jit(solution)/shard_map/tw,pt->wp/dot_general | solution.py:362
  32.7 1.2 %concatenate.61.geo_ref = f32[128,1024]{1,0:T(8,128)} pad(f32[18,1024]{1,0:T(8,128)S(1)} %concatenate.60, f32[]{:T(128)} %constant.27.clone.1), padding=0_110x0_0 | pad | bytes 598020 | tf_op jit(solution)/shard_map/jvp()/concatenate | solution.py:80
  33.8 1.5 %broadcast_in_dim.99.energy_w_ref = f32[512,128]{1,0:T(8,128)} broadcast(f32[512]{0:T(512)} %param.30), dimensions={0} | broadcast | bytes 264192 | tf_op jit(solution)/shard_map/broadcast_in_dim | solution.py:264
  35.4 9.4 %shard_map.175 = (f32[512,1024]{1,0:T(8,128)}, f32[512,128]{1,0:T(8,128)}, f32[128,1024]{1,0:T(8,128)}, f32[8,128]{1,0:T(8,128)}) custom-call(f32[640,1024]{1,0:T(8,128)} %copy-done.1, f32[512,128]{1,0:T(8,128)} %fusion.13.centre_ref, f32[128,1024]{1,0:T(8,128)} %concatenate.61.geo_ref, bf16[512,128]{1,0:T(8,128)(2,1)} %copy.58.basis_t_ref, ...), custom_call_target="tpu_custom_call" | custom-call | flops 1610612736 | bytes 8388608 | tf_op jit(solution)/shard_map/pallas_call | solution.py:226
  44.8 1.1 %slice_multiply_fusion.4 = (f32[1,1024]{1,0:T(1,128)S(1)}, f32[1,1024]{1,0:T(1,128)S(1)}, f32[1,1024]{1,0:T(1,128)S(1)}, f32[1,1024]{1,0:T(1,128)S(1)}, f32[1,10...) fusion(f32[128,1024]{1,0:T(8,128)} %get-tuple-element.9), kind=kLoop, calls=%fused_computation.172 | loop fusion | flops 5120 | bytes 73728 | tf_op jit(solution)/shard_map/transpose(jvp())/mul | solution.py:70
  45.9 1.0 %fusion.34 = (f32[1024]{0:T(1024)S(1)}, f32[1024]{0:T(1024)S(1)}) fusion(f32[128,1024]{1,0:T(8,128)} %get-tuple-element.9, f32[1024]{0:T(1024)S(1)} %get-tuple-element.67, f32[8]{0:T(128)S(1)} %copy-done.36, f32[1024]{0:T(1024)S(1)} %get-tuple-element.66), kind=kLoop, calls=%fused_computation.72 | loop fusion | flops 55296 | bytes 49184 | tf_op jit(solution)/shard_map/transpose(jvp())/reduce_sum | solution.py:58
  47.1 2.8 %fusion.3 = f32[320,640]{1,0:T(8,128)S(1)} fusion(f32[3,1024]{1,0:T(4,128)S(1)} %bitcast.163, f32[512,1024]{1,0:T(8,128)} %get-tuple-element.8, f32[640]{0:T(1024)S(1)} %copy-done.32, s32[1024]{0:T(1024)S(1)} %bitcast.152), kind=kOutput, calls=%fused_computation.6 | convolution fusion | flops 424017920 | bytes 2935296 | tf_op jit(solution)/shard_map/wn,nr->wr/dot_general | solution.py:316
  50.0 1.1 %fusion.8 = f32[320,640]{1,0:T(8,128)S(1)} fusion(f32[320,640]{1,0:T(8,128)S(1)} %fusion.3, f32[3,1024]{1,0:T(4,128)S(1)} %bitcast.164, f32[512,1024]{1,0:T(8,128)S(1)} %copy-done.37, f32[640]{0:T(1024)S(1)} %copy-done.32, f32[128,3]{1,0:T(8,128)S(1)} %bitcast.149, s32[1024]{0:T(1024)S(1)} %bitcast.153), kind=kOutput, calls=%fused_computation.10 | convolution fusion | flops 424427520 | bytes 3756032 | tf_op jit(solution)/shard_map/wn,nr->wr/dot_general | solution.py:318
  51.1 1.5 %collective-permute-start.7 = (f32[16,640]{1,0:T(8,128)S(1)}, f32[16,640]{1,0:T(8,128)S(1)}, u32[]{:S(2)}, u32[]{:S(2)}) collective-permute-start(f32[16,640]{1,0:T(8,128)S(1)} %get-tuple-element.31), channel_id=1, source_target_pairs={{3,0},{0,1},{1,2},{2,3},{7,4},{4,5},{5,6},{6,7},{11,8},{8,9},{9,10... | collective-permute-start | bytes 122888 | tf_op jit(solution)/shard_map/ppermute | solution.py:30
  52.6 2.7 %collective-permute-start.6 = (f32[16,640]{1,0:T(8,128)S(1)}, f32[16,640]{1,0:T(8,128)S(1)}, u32[]{:S(2)}, u32[]{:S(2)}) collective-permute-start(f32[16,640]{1,0:T(8,128)S(1)} %get-tuple-element.30), channel_id=1, source_target_pairs={{1,0},{2,1},{3,2},{0,3},{5,4},{6,5},{7,6},{4,7},{9,8},{10,9},{11,1... | collective-permute-start | bytes 122888 | tf_op jit(solution)/shard_map/ppermute | solution.py:30
  55.3 1.7 %collective-permute-done.7 = f32[16,640]{1,0:T(8,128)S(1)} collective-permute-done((f32[16,640]{1,0:T(8,128)S(1)}, f32[16,640]{1,0:T(8,128)S(1)}, u32[]{:S(2)}, u32[]{:S(2)}) %collective-permute-start.7) | collective-permute-done | bytes 40992 | tf_op jit(solution)/shard_map/ppermute | solution.py:30
  58.6 1.3 %collective-permute-start.8 = (f32[64,640]{1,0:T(8,128)S(1)}, f32[64,640]{1,0:T(8,128)S(1)}, u32[]{:S(2)}, u32[]{:S(2)}) collective-permute-start(f32[64,640]{1,0:T(8,128)S(1)} %get-tuple-element.33), channel_id=1, source_target_pairs={{4,0},{0,4},{5,1},{1,5},{6,2},{2,6},{7,3},{3,7},{12,8},{8,12},{13,... | collective-permute-start | bytes 491528 | tf_op jit(solution)/shard_map/ppermute | solution.py:30
  60.7 0.9 %collective-permute-start.9 = (f32[64,640]{1,0:T(8,128)S(1)}, f32[64,640]{1,0:T(8,128)S(1)}, u32[]{:S(2)}, u32[]{:S(2)}) collective-permute-start(f32[64,640]{1,0:T(8,128)S(1)} %get-tuple-element.32), channel_id=1, source_target_pairs={{4,0},{0,4},{5,1},{1,5},{6,2},{2,6},{7,3},{3,7},{12,8},{8,12},{13,... | collective-permute-start | bytes 491528 | tf_op jit(solution)/shard_map/ppermute | solution.py:30
  61.6 2.5 %collective-permute-done.8 = f32[64,640]{1,0:T(8,128)S(1)} collective-permute-done((f32[64,640]{1,0:T(8,128)S(1)}, f32[64,640]{1,0:T(8,128)S(1)}, u32[]{:S(2)}, u32[]{:S(2)}) %collective-permute-start.8) | collective-permute-done | bytes 163872 | tf_op jit(solution)/shard_map/ppermute | solution.py:30
  64.7 1.3 %collective-permute-done.9 = f32[64,640]{1,0:T(8,128)S(1)} collective-permute-done((f32[64,640]{1,0:T(8,128)S(1)}, f32[64,640]{1,0:T(8,128)S(1)}, u32[]{:S(2)}, u32[]{:S(2)}) %collective-permute-start.9) | collective-permute-done | bytes 163872 | tf_op jit(solution)/shard_map/ppermute | solution.py:30
  69.2 1.9 %collective-permute-done.11 = f32[16,640]{1,0:T(8,128)S(1)} collective-permute-done((f32[16,640]{1,0:T(8,128)S(1)}, f32[16,640]{1,0:T(8,128)S(1)}, u32[]{:S(2)}, u32[]{:S(2)}) %collective-permute-start.11) | collective-permute-done | bytes 40992 | tf_op jit(solution)/shard_map/ppermute | solution.py:30
  71.8 1.4 %convolution_add_fusion.6 = f32[128,512]{1,0:T(8,128)} fusion(f32[128,512]{1,0:T(8,128)S(1)} %fusion.118, bf16[512,512]{1,0:T(8,128)(2,1)S(1)} %copy-done.3, f32[128,640]{1,0:T(8,128)S(1)} %fusion.22), kind=kOutput, calls=%fused_computation.19 | convolution fusion | flops 402718720 | bytes 1310720 | tf_op jit(solution)/shard_map/dot_general | solution.py:410
  (159 shorter events, 15.4 us)
Async XLA Ops:
  0.6 10.4 %copy-start = (bf16[512,512]{1,0:T(8,128)(2,1)S(1)}, bf16[512,512]{1,0:T(8,128)(2,1)}, u32[]{:S(2)}) copy-start(bf16[512,512]{1,0:T(8,128)(2,1)} %param.22) | copy-start | bytes 1572868
  0.7 9.9 %copy-start.33 = (s32[128]{0:T(128)S(1)}, s32[128]{0:T(128)}, u32[]{:S(2)}) copy-start(s32[128]{0:T(128)} %param.18) | copy-start | bytes 1540
  0.7 10.4 %copy-start.6 = (bf16[128,512]{1,0:T(8,128)(2,1)S(1)}, bf16[128,512]{1,0:T(8,128)(2,1)}, u32[]{:S(2)}) copy-start(bf16[128,512]{1,0:T(8,128)(2,1)} %param.16) | copy-start | bytes 393220
  0.7 9.2 %copy-start.16 = (bf16[8,512]{1,0:T(8,128)(2,1)S(1)}, bf16[8,512]{1,0:T(8,128)(2,1)}, u32[]{:S(2)}) copy-start(bf16[8,512]{1,0:T(8,128)(2,1)} %param.26) | copy-start | bytes 24580
  0.7 9.9 %copy-start.14 = (f32[5,512]{1,0:T(8,128)S(1)}, f32[5,512]{1,0:T(8,128)}, u32[]{:S(2)}) copy-start(f32[5,512]{1,0:T(8,128)} %param.24) | copy-start | bytes 30724
  2.5 22.6 %copy-start.17 = (s32[16]{0:T(128)}, s32[16]{0:T(128)S(1)}, u32[]{:S(2)}) copy-start(s32[16]{0:T(128)S(1)} %get-tuple-element.74) | copy-start | bytes 196
  2.5 24.4 %copy-start.19 = (s32[16]{0:T(128)}, s32[16]{0:T(128)S(1)}, u32[]{:S(2)}) copy-start(s32[16]{0:T(128)S(1)} %get-tuple-element.71) | copy-start | bytes 196
  3.5 9.1 %copy-start.31 = (s32[1024]{0:T(1024)S(1)}, s32[1024]{0:T(1024)}, u32[]{:S(2)}) copy-start(s32[1024]{0:T(1024)} %param.20) | copy-start | bytes 12292
  3.6 10.6 %copy-start.2 = (bf16[512,512]{1,0:T(8,128)(2,1)S(1)}, bf16[512,512]{1,0:T(8,128)(2,1)}, u32[]{:S(2)}) copy-start(bf16[512,512]{1,0:T(8,128)(2,1)} %update_ref.1) | copy-start | bytes 1572868
  5.2 9.9 %copy-start.4 = (bf16[512,384]{1,0:T(8,128)(2,1)S(1)}, bf16[512,384]{1,0:T(8,128)(2,1)}, u32[]{:S(2)}) copy-start(bf16[512,384]{1,0:T(8,128)(2,1)} %split_ref.1) | copy-start | bytes 1179652
  5.2 12.4 %collective-permute-start = (bf16[16,640]{1,0:T(8,128)(2,1)S(1)}, bf16[16,640]{1,0:T(8,128)(2,1)S(1)}, u32[]{:S(2)}, u32[]{:S(2)}) collective-permute-start(bf16[16,640]{1,0:T(8,128)(2,1)S(1)} %convolution_convert_fusion.5), channel_id=1, source_target_pairs={{24,0},{0,8},{8,16},{16,24},{25,1},{1,9},{9,17},{17,25},{26,2},{2,... | collective-permute-start | bytes 61448 | tf_op jit(solution)/shard_map/ppermute | solution.py:30
  5.9 11.7 %collective-permute-start.1 = (bf16[16,640]{1,0:T(8,128)(2,1)S(1)}, bf16[16,640]{1,0:T(8,128)(2,1)S(1)}, u32[]{:S(2)}, u32[]{:S(2)}) collective-permute-start(bf16[16,640]{1,0:T(8,128)(2,1)S(1)} %convolution_convert_fusion.4), channel_id=1, source_target_pairs={{8,0},{16,8},{24,16},{0,24},{9,1},{17,9},{25,17},{1,25},{10,2},{18... | collective-permute-start | bytes 61448 | tf_op jit(solution)/shard_map/ppermute | solution.py:30
  7.9 8.2 %copy-start.5 = (bf16[192,512]{1,0:T(8,128)(2,1)S(1)}, bf16[192,512]{1,0:T(8,128)(2,1)}, u32[]{:S(2)}) copy-start(bf16[192,512]{1,0:T(8,128)(2,1)} %tensor_ref.1) | copy-start | bytes 589828
  8.0 9.6 %copy-start.23 = (s32[64]{0:T(128)}, s32[64]{0:T(128)S(1)}, u32[]{:S(2)}) copy-start(s32[64]{0:T(128)S(1)} %get-tuple-element.76) | copy-start | bytes 772
  8.0 12.2 %copy-start.29 = (s32[64]{0:T(128)}, s32[64]{0:T(128)S(1)}, u32[]{:S(2)}) copy-start(s32[64]{0:T(128)S(1)} %get-tuple-element.75) | copy-start | bytes 772
  16.9 14.2 %copy-start.12 = (s32[8,128]{1,0:T(8,128)S(1)}, s32[8,128]{1,0:T(8,128)}, u32[]{:S(2)}) copy-start(s32[8,128]{1,0:T(8,128)} %copy.53) | copy-start | bytes 12292
  17.9 5.3 %collective-permute-start.2 = (bf16[64,640]{1,0:T(8,128)(2,1)S(1)}, bf16[64,640]{1,0:T(8,128)(2,1)S(1)}, u32[]{:S(2)}, u32[]{:S(2)}) collective-permute-start(bf16[64,640]{1,0:T(8,128)(2,1)S(1)} %convolution_convert_fusion.1), channel_id=1, source_target_pairs={{4,0},{0,4},{5,1},{1,5},{6,2},{2,6},{7,3},{3,7},{12,8},{8,12},{13,... | collective-permute-start | bytes 245768 | tf_op jit(solution)/shard_map/ppermute | solution.py:30
  20.5 4.5 %collective-permute-start.3 = (bf16[64,640]{1,0:T(8,128)(2,1)S(1)}, bf16[64,640]{1,0:T(8,128)(2,1)S(1)}, u32[]{:S(2)}, u32[]{:S(2)}) collective-permute-start(bf16[64,640]{1,0:T(8,128)(2,1)S(1)} %convolution_convert_fusion), channel_id=1, source_target_pairs={{4,0},{0,4},{5,1},{1,5},{6,2},{2,6},{7,3},{3,7},{12,8},{8,12},{13,... | collective-permute-start | bytes 245768 | tf_op jit(solution)/shard_map/ppermute | solution.py:30
  23.2 9.0 %copy-start.11 = (f32[1,3,8,128]{3,2,1,0:T(8,128)S(1)}, f32[1,3,8,128]{3,2,1,0:T(8,128)}, u32[]{:S(2)}) copy-start(f32[1,3,8,128]{3,2,1,0:T(8,128)} %broadcast_bitcast_fusion) | copy-start | bytes 36868
  25.3 5.6 %collective-permute-start.4 = (bf16[16,640]{1,0:T(8,128)(2,1)S(1)}, bf16[16,640]{1,0:T(8,128)(2,1)S(1)}, u32[]{:S(2)}, u32[]{:S(2)}) collective-permute-start(bf16[16,640]{1,0:T(8,128)(2,1)S(1)} %convolution_convert_fusion.3), channel_id=1, source_target_pairs={{3,0},{0,1},{1,2},{2,3},{7,4},{4,5},{5,6},{6,7},{11,8},{8,9},{9,10... | collective-permute-start | bytes 61448 | tf_op jit(solution)/shard_map/ppermute | solution.py:30
  27.1 4.0 %collective-permute-start.5 = (bf16[16,640]{1,0:T(8,128)(2,1)S(1)}, bf16[16,640]{1,0:T(8,128)(2,1)S(1)}, u32[]{:S(2)}, u32[]{:S(2)}) collective-permute-start(bf16[16,640]{1,0:T(8,128)(2,1)S(1)} %convolution_convert_fusion.2), channel_id=1, source_target_pairs={{1,0},{2,1},{3,2},{0,3},{5,4},{6,5},{7,6},{4,7},{9,8},{10,9},{11,1... | collective-permute-start | bytes 61448 | tf_op jit(solution)/shard_map/ppermute | solution.py:30
  35.4 10.5 %copy-start.36 = (f32[8]{0:T(128)S(1)}, f32[8]{0:T(128)}, u32[]{:S(2)}) copy-start(f32[8]{0:T(128)} %convert_multiply_fusion) | copy-start | bytes 100
  35.4 11.5 %copy-start.10 = (f32[3,128]{1,0:T(4,128)S(1)}, f32[3,128]{1,0:T(4,128)}, u32[]{:S(2)}) copy-start(f32[3,128]{1,0:T(4,128)} %copy-done.8) | copy-start | bytes 4612
  35.4 11.5 %copy-start.28 = (f32[128]{0:T(128)S(1)}, f32[128]{0:T(128)}, u32[]{:S(2)}) copy-start(f32[128]{0:T(128)} %compare_convert_fusion) | copy-start | bytes 1540
  35.4 11.7 %copy-start.13 = (s32[8,128]{1,0:T(8,128)S(1)}, s32[8,128]{1,0:T(8,128)}, u32[]{:S(2)}) copy-start(s32[8,128]{1,0:T(8,128)} %copy.53) | copy-start | bytes 12292
  35.4 11.7 %copy-start.32 = (f32[640]{0:T(1024)S(1)}, f32[640]{0:T(1024)}, u32[]{:S(2)}) copy-start(f32[640]{0:T(1024)} %pad.21.clone) | copy-start | bytes 7684
  51.1 5.9 %collective-permute-start.7 = (f32[16,640]{1,0:T(8,128)S(1)}, f32[16,640]{1,0:T(8,128)S(1)}, u32[]{:S(2)}, u32[]{:S(2)}) collective-permute-start(f32[16,640]{1,0:T(8,128)S(1)} %get-tuple-element.31), channel_id=1, source_target_pairs={{3,0},{0,1},{1,2},{2,3},{7,4},{4,5},{5,6},{6,7},{11,8},{8,9},{9,10... | collective-permute-start | bytes 122888 | tf_op jit(solution)/shard_map/ppermute | solution.py:30
  52.6 5.2 %collective-permute-start.6 = (f32[16,640]{1,0:T(8,128)S(1)}, f32[16,640]{1,0:T(8,128)S(1)}, u32[]{:S(2)}, u32[]{:S(2)}) collective-permute-start(f32[16,640]{1,0:T(8,128)S(1)} %get-tuple-element.30), channel_id=1, source_target_pairs={{1,0},{2,1},{3,2},{0,3},{5,4},{6,5},{7,6},{4,7},{9,8},{10,9},{11,1... | collective-permute-start | bytes 122888 | tf_op jit(solution)/shard_map/ppermute | solution.py:30
  58.6 5.4 %collective-permute-start.8 = (f32[64,640]{1,0:T(8,128)S(1)}, f32[64,640]{1,0:T(8,128)S(1)}, u32[]{:S(2)}, u32[]{:S(2)}) collective-permute-start(f32[64,640]{1,0:T(8,128)S(1)} %get-tuple-element.33), channel_id=1, source_target_pairs={{4,0},{0,4},{5,1},{1,5},{6,2},{2,6},{7,3},{3,7},{12,8},{8,12},{13,... | collective-permute-start | bytes 491528 | tf_op jit(solution)/shard_map/ppermute | solution.py:30
  60.7 5.4 %collective-permute-start.9 = (f32[64,640]{1,0:T(8,128)S(1)}, f32[64,640]{1,0:T(8,128)S(1)}, u32[]{:S(2)}, u32[]{:S(2)}) collective-permute-start(f32[64,640]{1,0:T(8,128)S(1)} %get-tuple-element.32), channel_id=1, source_target_pairs={{4,0},{0,4},{5,1},{1,5},{6,2},{2,6},{7,3},{3,7},{12,8},{8,12},{13,... | collective-permute-start | bytes 491528 | tf_op jit(solution)/shard_map/ppermute | solution.py:30
  66.8 1.7 %collective-permute-start.10 = (f32[16,640]{1,0:T(8,128)S(1)}, f32[16,640]{1,0:T(8,128)S(1)}, u32[]{:S(2)}, u32[]{:S(2)}) collective-permute-start(f32[16,640]{1,0:T(8,128)S(1)} %get-tuple-element.44), channel_id=1, source_target_pairs={{8,0},{16,8},{24,16},{0,24},{9,1},{17,9},{25,17},{1,25},{10,2},{18... | collective-permute-start | bytes 122888 | tf_op jit(solution)/shard_map/ppermute | solution.py:30
  67.7 3.4 %collective-permute-start.11 = (f32[16,640]{1,0:T(8,128)S(1)}, f32[16,640]{1,0:T(8,128)S(1)}, u32[]{:S(2)}, u32[]{:S(2)}) collective-permute-start(f32[16,640]{1,0:T(8,128)S(1)} %get-tuple-element.43), channel_id=1, source_target_pairs={{24,0},{0,8},{8,16},{16,24},{25,1},{1,9},{9,17},{17,25},{26,2},{2,... | collective-permute-start | bytes 122888 | tf_op jit(solution)/shard_map/ppermute | solution.py:30
  (20 other events, 120.0 us)

commit v12 on v10

--- a/solution.py
+++ b/solution.py
@@ -347,7 +347,22 @@
                 picked[:, None] == jnp.arange(rows_now, dtype=jnp.int32)[None, :]
             ).astype(jnp.bfloat16)
             pickers[segment] = onehot
-            out = jnp.dot(onehot, table, preferred_element_type=jnp.float32).astype(jnp.bfloat16)
+            if section == 0:
+                chosen = jnp.dot(onehot, latent, preferred_element_type=jnp.float32)
+                kinds_of = jnp.take(species, picked, axis=0)
+                out = jnp.concatenate(
+                    [
+                        project(chosen.astype(jnp.bfloat16), kinds_of, neigh_proj, neigh_table),
+                        jnp.dot(
+                            onehot, table[:, width:], preferred_element_type=jnp.float32
+                        ).astype(jnp.bfloat16),
+                    ],
+                    axis=1,
+                )
+            else:
+                out = jnp.dot(onehot, table, preferred_element_type=jnp.float32).astype(
+                    jnp.bfloat16
+                )
             got = passed_along(out, axis, direction)
             coord_axis, offset = shifts[2 * section + number]
             columns = jnp.arange(width + extra, dtype=jnp.int32)[None, :]

time: 72.3 us -> 79.2 us (1.095)
  local copies, waits for them, and re-layouts: 10.1 us -> 12.8 us
  other arithmetic: 3.43 us -> 5.69 us
  matrix products: 17.1 us -> 18.7 us
    gather x0 -> x2, local copies, waits for them, and re-layouts: none -> 2.64 us  [shards(): kinds_of = jnp.take(species, picked, axis=0)]
    select_n x0 -> x2, other arithmetic: none -> 1.62 us  [shards(): kinds_of = jnp.take(species, picked, axis=0)]
    dot_general x2 -> x4, matrix products: 2.44 us -> 3.75 us  [project(): jnp.dot(rows, weight, preferred_element_type=jnp.float32)]
    dot_general x3 -> x5, matrix products: 2.24 us -> 2.63 us  [lookup(): return jnp.dot(onehot, table, precision=lax.Precision.HIGHEST)]
    unnamed x40 -> x44, local copies, waits for them, and re-layouts: 3.55 us -> 3.59 us
  transfers between devices with their start and end apart: 12 -> 12, of which waited for: 9 -> 9; matrix products, arithmetic and copies ran while one was open for 14% -> 16% of each run, Pallas kernels for 0% -> 0%
where the time goes in v12:
time: 79.2 us; the launch traced here: 78.7 us
  matrix products  18.7 us (24%)
  starting transfers between devices  15.8 us (20%)
  waiting for transfers between devices  14.1 us (18%)
  local copies, waits for them, and re-layouts  12.8 us (16%)
  Pallas kernels  9.67 us (12%)
  other arithmetic  5.69 us (7%)
  between operations  1.89 us (2%)
    ppermute x12, starting transfers between devices, passed_along(): return lax.ppermute(block, axis, route)  15.8 us
    ppermute x12, waiting for transfers between devices, passed_along(): return lax.ppermute(block, axis, route)  14.1 us
    pallas_call x1, Pallas kernels, pair_terms(): pl.pallas_call(_pair_kernel, out_shape=(jax.ShapeDtypeStruct((width, pair...  9.67 us
    dot_general x4, matrix products, project(): jnp.dot(rows, weight, preferred_element_type=jnp.float32)  3.75 us
    unnamed x44, local copies, waits for them, and re-layouts  3.59 us
    dot_general x1, matrix products, spread_cols(): jnp.einsum('wn,nr->wr', high, onehot, preferred_element_type=jnp.float32)  2.82 us
    gather x2, local copies, waits for them, and re-layouts, shards(): kinds_of = jnp.take(species, picked, axis=0)  2.64 us
    dot_general x5, matrix products, lookup(): return jnp.dot(onehot, table, precision=lax.Precision.HIGHEST)  2.63 us
  transfers between devices with their start and end apart: 12, of which 9 were waited for; matrix products, arithmetic and copies ran while one was open for 16% of the time, Pallas kernels for 0%

profile of v12, /device:TPU:0, one launch (start us, length us, event | category | flops | bytes accessed | tf_op | source)
XLA Modules:
  0.0 78.7 jit_solution(5075949462111365173)
XLA Ops:
  3.3 1.3 %gather_fusion = s32[16]{0:T(128)S(1)} fusion(s32[128]{0:T(128)} %param.20, s32[1024]{0:T(1024)S(1)} %get-tuple-element.83), kind=kCustom, calls=%fused_computation.clone | custom fusion | bytes 192 | tf_op jit(solution)/shard_map/jit(_take)/gather | solution.py:352
  4.6 1.3 %gather_fusion.1 = s32[16]{0:T(128)S(1)} fusion(s32[128]{0:T(128)} %param.20, s32[1024]{0:T(1024)S(1)} %get-tuple-element.82), kind=kCustom, calls=%fused_computation.1.clone | custom fusion | bytes 192 | tf_op jit(solution)/shard_map/jit(_take)/gather | solution.py:352
  6.9 1.2 %fusion.16 = f32[16,512]{1,0:T(8,128)S(1)} fusion(bf16[512,512]{1,0:T(8,128)(2,1)S(1)} %copy-done, bf16[128,512]{1,0:T(8,128)(2,1)} %param.18, s32[16]{0:T(128)S(1)} %get-tuple-element.74), kind=kOutput, calls=%fused_computation.39 | convolution fusion | flops 10496000 | bytes 688192 | tf_op jit(solution)/shard_map/dot_general | solution.py:310
  8.2 0.9 %fusion.14 = bf16[16,512]{1,0:T(8,128)(2,1)S(1)} fusion(f32[16,512]{1,0:T(8,128)S(1)} %fusion.16, f32[5,512]{1,0:T(8,128)} %param.27, s32[16]{0:T(128)S(1)} %get-tuple-element.79), kind=kOutput, calls=%fused_computation.35 | convolution fusion | flops 507984 | bytes 59456 | tf_op jit(solution)/shard_map/dot_general | solution.py:306
  9.8 1.2 %fusion.17 = f32[16,512]{1,0:T(8,128)S(1)} fusion(bf16[512,512]{1,0:T(8,128)(2,1)S(1)} %copy-done, bf16[128,512]{1,0:T(8,128)(2,1)} %param.18, s32[16]{0:T(128)S(1)} %get-tuple-element.73), kind=kOutput, calls=%fused_computation.40 | convolution fusion | flops 10496000 | bytes 688192 | tf_op jit(solution)/shard_map/dot_general | solution.py:310
  11.3 2.0 %collective-permute-start.1 = (bf16[16,640]{1,0:T(8,128)(2,1)S(1)}, bf16[16,640]{1,0:T(8,128)(2,1)S(1)}, u32[]{:S(2)}, u32[]{:S(2)}) collective-permute-start(bf16[16,640]{1,0:T(8,128)(2,1)S(1)} %pad_maximum_fusion.3), channel_id=1, source_target_pairs={{8,0},{16,8},{24,16},{0,24},{9,1},{17,9},{25,17},{1,25},{10,2},{18... | collective-permute-start | bytes 61448 | tf_op jit(solution)/shard_map/ppermute | solution.py:30
  16.4 1.0 %fusion.13.centre_ref = f32[512,128]{1,0:T(8,128)} fusion(f32[512,128]{1,0:T(8,128)S(1)} %convolution_bitcast_fusion, bf16[512,512]{1,0:T(8,128)(2,1)S(1)} %copy-done.3, bf16[128,512]{1,0:T(8,128)(2,1)S(1)} %copy-done.4), kind=kOutput, calls=%fused_computation.28 | convolution fusion | flops 67305472 | bytes 1179648 | tf_op jit(solution)/shard_map/dot_general | solution.py:310
  18.4 1.0 %copy.56 = bf16[512,512]{0,1:T(8,128)(2,1)} copy(bf16[512,512]{1,0:T(8,128)(2,1)S(1)} %copy-done.2) | data formatting | bytes 1048576 | tf_op args[12]
  19.4 0.9 %copy.55 = bf16[512,384]{0,1:T(8,128)(2,1)} copy(bf16[512,384]{1,0:T(8,128)(2,1)S(1)} %copy-done.5) | data formatting | bytes 786432 | tf_op args[11]
  21.6 2.4 %collective-permute-start.2 = (bf16[64,640]{1,0:T(8,128)(2,1)S(1)}, bf16[64,640]{1,0:T(8,128)(2,1)S(1)}, u32[]{:S(2)}, u32[]{:S(2)}) collective-permute-start(bf16[64,640]{1,0:T(8,128)(2,1)S(1)} %convolution_convert_fusion.1), channel_id=1, source_target_pairs={{4,0},{0,4},{5,1},{1,5},{6,2},{2,6},{7,3},{3,7},{12,8},{8,12},{13,... | collective-permute-start | bytes 245768 | tf_op jit(solution)/shard_map/ppermute | solution.py:30
  24.3 2.6 %collective-permute-done.2 = bf16[64,640]{1,0:T(8,128)(2,1)S(1)} collective-permute-done((bf16[64,640]{1,0:T(8,128)(2,1)S(1)}, bf16[64,640]{1,0:T(8,128)(2,1)S(1)}, u32[]{:S(2)}, u32[]{:S(2)}) %collective-permute-start.2) | collective-permute-done | bytes 81952 | tf_op jit(solution)/shard_map/ppermute | solution.py:30
  26.9 1.8 %collective-permute-done.3 = bf16[64,640]{1,0:T(8,128)(2,1)S(1)} collective-permute-done((bf16[64,640]{1,0:T(8,128)(2,1)S(1)}, bf16[64,640]{1,0:T(8,128)(2,1)S(1)}, u32[]{:S(2)}, u32[]{:S(2)}) %collective-permute-start.3) | collective-permute-done | bytes 81952 | tf_op jit(solution)/shard_map/ppermute | solution.py:30
  28.9 1.6 %collective-permute-start.4 = (bf16[16,640]{1,0:T(8,128)(2,1)S(1)}, bf16[16,640]{1,0:T(8,128)(2,1)S(1)}, u32[]{:S(2)}, u32[]{:S(2)}) collective-permute-start(bf16[16,640]{1,0:T(8,128)(2,1)S(1)} %convolution_convert_fusion.3), channel_id=1, source_target_pairs={{3,0},{0,1},{1,2},{2,3},{7,4},{4,5},{5,6},{6,7},{11,8},{8,9},{9,10... | collective-permute-start | bytes 61448 | tf_op jit(solution)/shard_map/ppermute | solution.py:30
  30.8 2.5 %collective-permute-start.5 = (bf16[16,640]{1,0:T(8,128)(2,1)S(1)}, bf16[16,640]{1,0:T(8,128)(2,1)S(1)}, u32[]{:S(2)}, u32[]{:S(2)}) collective-permute-start(bf16[16,640]{1,0:T(8,128)(2,1)S(1)} %convolution_convert_fusion.2), channel_id=1, source_target_pairs={{1,0},{2,1},{3,2},{0,3},{5,4},{6,5},{7,6},{4,7},{9,8},{10,9},{11,1... | collective-permute-start | bytes 61448 | tf_op jit(solution)/shard_map/ppermute | solution.py:30
  33.3 1.4 %collective-permute-done.4 = bf16[16,640]{1,0:T(8,128)(2,1)S(1)} collective-permute-done((bf16[16,640]{1,0:T(8,128)(2,1)S(1)}, bf16[16,640]{1,0:T(8,128)(2,1)S(1)}, u32[]{:S(2)}, u32[]{:S(2)}) %collective-permute-start.4) | collective-permute-done | bytes 20512 | tf_op jit(solution)/shard_map/ppermute | solution.py:30
  34.9 1.1 %fusion.2 = f32[640,1024]{1,0:T(8,128)S(1)} fusion(bf16[320,640]{1,0:T(8,128)(2,1)S(1)} %constant_dynamic-update-slice_fusion.2, s32[1024]{0:T(1024)S(1)} %bitcast.165), kind=kOutput, calls=%fused_computation.8 | convolution fusion | flops 419758080 | bytes 3035136 | tf_op jit(solution)/shard_map/tw,pt->wp/dot_general | solution.py:377
  36.0 1.2 %slice.212.rows_ref = bf16[512,1024]{1,0:T(8,128)(2,1)} slice(f32[640,1024]{1,0:T(8,128)S(1)} %fusion.2), slice={[0:512], [0:1024]} | slice | bytes 2097152 | tf_op jit(solution)/shard_map/slice | solution.py:378
  38.5 1.6 %broadcast_in_dim.57.energy_w_ref = f32[512,1024]{1,0:T(8,128)} broadcast(f32[512]{0:T(512)S(1)} %copy-done.13), dimensions={0} | broadcast | bytes 2099200 | tf_op jit(solution)/shard_map/broadcast_in_dim | solution.py:264
  40.0 9.7 %shard_map.175 = (f32[512,1024]{1,0:T(8,128)}, f32[512,128]{1,0:T(8,128)}, f32[128,1024]{1,0:T(8,128)}, f32[8,128]{1,0:T(8,128)}) custom-call(bf16[512,1024]{1,0:T(8,128)(2,1)} %slice.212.rows_ref, f32[512,128]{1,0:T(8,128)} %fusion.13.centre_ref, f32[128,1024]{1,0:T(8,128)} %concatenate.73.geo_ref, bf16[512,128]{1,0:T(8,128)(2,1)} %copy.58.basis_t_ref, ...), custom_call_target="tpu_custom_call" | custom-call | flops 1610612736 | bytes 8388608 | tf_op jit(solution)/shard_map/pallas_call | solution.py:226
  49.7 1.2 %slice_multiply_fusion.4 = (f32[1,1024]{1,0:T(1,128)S(1)}, f32[1,1024]{1,0:T(1,128)S(1)}, f32[1,1024]{1,0:T(1,128)S(1)}, f32[1,1024]{1,0:T(1,128)S(1)}, f32[1,10...) fusion(f32[128,1024]{1,0:T(8,128)} %get-tuple-element.10), kind=kLoop, calls=%fused_computation.191 | loop fusion | flops 5120 | bytes 73728 | tf_op jit(solution)/shard_map/transpose(jvp())/mul | solution.py:70
  50.9 1.0 %fusion.40 = (f32[1024]{0:T(1024)S(1)}, f32[1024]{0:T(1024)S(1)}) fusion(f32[128,1024]{1,0:T(8,128)} %get-tuple-element.10, f32[1024]{0:T(1024)S(1)} %get-tuple-element.68, f32[8]{0:T(128)S(1)} %copy-done.14, f32[1024]{0:T(1024)S(1)} %get-tuple-element.67), kind=kLoop, calls=%fused_computation.85 | loop fusion | flops 55296 | bytes 49184 | tf_op jit(solution)/shard_map/transpose(jvp())/reduce_sum | solution.py:58
  52.1 2.8 %fusion.3 = f32[320,640]{1,0:T(8,128)S(1)} fusion(f32[3,1024]{1,0:T(4,128)S(1)} %bitcast.177, f32[512,1024]{1,0:T(8,128)} %get-tuple-element.9, f32[640]{0:T(1024)S(1)} %pad.22.clone, s32[1024]{0:T(1024)S(1)} %bitcast.166), kind=kOutput, calls=%fused_computation.9 | convolution fusion | flops 424017920 | bytes 2935296 | tf_op jit(solution)/shard_map/wn,nr->wr/dot_general | solution.py:316
  54.9 1.1 %fusion.8 = f32[320,640]{1,0:T(8,128)S(1)} fusion(f32[320,640]{1,0:T(8,128)S(1)} %fusion.3, f32[3,1024]{1,0:T(4,128)S(1)} %bitcast.178, f32[512,1024]{1,0:T(8,128)S(1)} %copy-done.15, f32[640]{0:T(1024)S(1)} %pad.22.clone, f32[128,3]{1,0:T(8,128)S(1)} %bitcast.163, s32[1024]{0:T(1024)S(1)} %bitcast.167), kind=kOutput, calls=%fused_computation.13 | convolution fusion | flops 424427520 | bytes 3756032 | tf_op jit(solution)/shard_map/wn,nr->wr/dot_general | solution.py:318
  56.0 1.5 %collective-permute-start.7 = (f32[16,640]{1,0:T(8,128)S(1)}, f32[16,640]{1,0:T(8,128)S(1)}, u32[]{:S(2)}, u32[]{:S(2)}) collective-permute-start(f32[16,640]{1,0:T(8,128)S(1)} %get-tuple-element.32), channel_id=1, source_target_pairs={{3,0},{0,1},{1,2},{2,3},{7,4},{4,5},{5,6},{6,7},{11,8},{8,9},{9,10... | collective-permute-start | bytes 122888 | tf_op jit(solution)/shard_map/ppermute | solution.py:30
  57.6 2.5 %collective-permute-start.6 = (f32[16,640]{1,0:T(8,128)S(1)}, f32[16,640]{1,0:T(8,128)S(1)}, u32[]{:S(2)}, u32[]{:S(2)}) collective-permute-start(f32[16,640]{1,0:T(8,128)S(1)} %get-tuple-element.31), channel_id=1, source_target_pairs={{1,0},{2,1},{3,2},{0,3},{5,4},{6,5},{7,6},{4,7},{9,8},{10,9},{11,1... | collective-permute-start | bytes 122888 | tf_op jit(solution)/shard_map/ppermute | solution.py:30
  60.1 1.9 %collective-permute-done.7 = f32[16,640]{1,0:T(8,128)S(1)} collective-permute-done((f32[16,640]{1,0:T(8,128)S(1)}, f32[16,640]{1,0:T(8,128)S(1)}, u32[]{:S(2)}, u32[]{:S(2)}) %collective-permute-start.7) | collective-permute-done | bytes 40992 | tf_op jit(solution)/shard_map/ppermute | solution.py:30
  63.6 1.3 %collective-permute-start.8 = (f32[64,640]{1,0:T(8,128)S(1)}, f32[64,640]{1,0:T(8,128)S(1)}, u32[]{:S(2)}, u32[]{:S(2)}) collective-permute-start(f32[64,640]{1,0:T(8,128)S(1)} %get-tuple-element.34), channel_id=1, source_target_pairs={{4,0},{0,4},{5,1},{1,5},{6,2},{2,6},{7,3},{3,7},{12,8},{8,12},{13,... | collective-permute-start | bytes 491528 | tf_op jit(solution)/shard_map/ppermute | solution.py:30
  65.6 0.8 %collective-permute-start.9 = (f32[64,640]{1,0:T(8,128)S(1)}, f32[64,640]{1,0:T(8,128)S(1)}, u32[]{:S(2)}, u32[]{:S(2)}) collective-permute-start(f32[64,640]{1,0:T(8,128)S(1)} %get-tuple-element.33), channel_id=1, source_target_pairs={{4,0},{0,4},{5,1},{1,5},{6,2},{2,6},{7,3},{3,7},{12,8},{8,12},{13,... | collective-permute-start | bytes 491528 | tf_op jit(solution)/shard_map/ppermute | solution.py:30
  66.5 2.5 %collective-permute-done.8 = f32[64,640]{1,0:T(8,128)S(1)} collective-permute-done((f32[64,640]{1,0:T(8,128)S(1)}, f32[64,640]{1,0:T(8,128)S(1)}, u32[]{:S(2)}, u32[]{:S(2)}) %collective-permute-start.8) | collective-permute-done | bytes 163872 | tf_op jit(solution)/shard_map/ppermute | solution.py:30
  69.6 1.4 %collective-permute-done.9 = f32[64,640]{1,0:T(8,128)S(1)} collective-permute-done((f32[64,640]{1,0:T(8,128)S(1)}, f32[64,640]{1,0:T(8,128)S(1)}, u32[]{:S(2)}, u32[]{:S(2)}) %collective-permute-start.9) | collective-permute-done | bytes 163872 | tf_op jit(solution)/shard_map/ppermute | solution.py:30
  74.1 1.9 %collective-permute-done.11 = f32[16,640]{1,0:T(8,128)S(1)} collective-permute-done((f32[16,640]{1,0:T(8,128)S(1)}, f32[16,640]{1,0:T(8,128)S(1)}, u32[]{:S(2)}, u32[]{:S(2)}) %collective-permute-start.11) | collective-permute-done | bytes 40992 | tf_op jit(solution)/shard_map/ppermute | solution.py:30
  76.7 1.4 %convolution_add_fusion.6 = f32[128,512]{1,0:T(8,128)} fusion(f32[128,512]{1,0:T(8,128)S(1)} %fusion.134, bf16[512,512]{1,0:T(8,128)(2,1)S(1)} %copy-done, f32[128,640]{1,0:T(8,128)S(1)} %fusion.26), kind=kOutput, calls=%fused_computation.22 | convolution fusion | flops 402718720 | bytes 1310720 | tf_op jit(solution)/shard_map/dot_general | solution.py:425
  (127 shorter events, 18.7 us)
Async XLA Ops:
  0.6 6.3 %copy-start = (bf16[512,512]{1,0:T(8,128)(2,1)S(1)}, bf16[512,512]{1,0:T(8,128)(2,1)}, u32[]{:S(2)}) copy-start(bf16[512,512]{1,0:T(8,128)(2,1)} %param.25) | copy-start | bytes 1572868
  0.6 13.0 %copy-start.9 = (s32[1,192]{1,0:T(1,128)S(1)}, s32[1,192]{1,0:T(1,128)}, u32[]{:S(2)}) copy-start(s32[1,192]{1,0:T(1,128)} %param.21) | copy-start | bytes 2308
  0.7 12.6 %copy-start.1 = (s32[128]{0:T(128)S(1)}, s32[128]{0:T(128)}, u32[]{:S(2)}) copy-start(s32[128]{0:T(128)} %param.20) | copy-start | bytes 1540
  0.7 13.6 %copy-start.4 = (bf16[128,512]{1,0:T(8,128)(2,1)S(1)}, bf16[128,512]{1,0:T(8,128)(2,1)}, u32[]{:S(2)}) copy-start(bf16[128,512]{1,0:T(8,128)(2,1)} %param.18) | copy-start | bytes 393220
  0.7 10.4 %copy-start.8 = (f32[5,512]{1,0:T(8,128)S(1)}, f32[5,512]{1,0:T(8,128)}, u32[]{:S(2)}) copy-start(f32[5,512]{1,0:T(8,128)} %param.27) | copy-start | bytes 30724
  3.1 12.1 %copy-start.11 = (bf16[8,512]{1,0:T(8,128)(2,1)S(1)}, bf16[8,512]{1,0:T(8,128)(2,1)}, u32[]{:S(2)}) copy-start(bf16[8,512]{1,0:T(8,128)(2,1)} %param.28) | copy-start | bytes 24580
  3.3 12.6 %copy-start.10 = (f32[5,512]{1,0:T(8,128)S(1)}, f32[5,512]{1,0:T(8,128)}, u32[]{:S(2)}) copy-start(f32[5,512]{1,0:T(8,128)} %param.26) | copy-start | bytes 30724
  5.9 10.5 %copy-start.3 = (bf16[512,512]{1,0:T(8,128)(2,1)S(1)}, bf16[512,512]{1,0:T(8,128)(2,1)}, u32[]{:S(2)}) copy-start(bf16[512,512]{1,0:T(8,128)(2,1)} %param.24) | copy-start | bytes 1572868
  9.1 12.2 %collective-permute-start = (bf16[16,640]{1,0:T(8,128)(2,1)S(1)}, bf16[16,640]{1,0:T(8,128)(2,1)S(1)}, u32[]{:S(2)}, u32[]{:S(2)}) collective-permute-start(bf16[16,640]{1,0:T(8,128)(2,1)S(1)} %pad_maximum_fusion.2), channel_id=1, source_target_pairs={{24,0},{0,8},{8,16},{16,24},{25,1},{1,9},{9,17},{17,25},{26,2},{2,... | collective-permute-start | bytes 61448 | tf_op jit(solution)/shard_map/ppermute | solution.py:30
  9.8 7.7 %copy-start.12 = (s32[1024]{0:T(1024)S(1)}, s32[1024]{0:T(1024)}, u32[]{:S(2)}) copy-start(s32[1024]{0:T(1024)} %param.22) | copy-start | bytes 12292
  11.0 7.4 %copy-start.2 = (bf16[512,512]{1,0:T(8,128)(2,1)S(1)}, bf16[512,512]{1,0:T(8,128)(2,1)}, u32[]{:S(2)}) copy-start(bf16[512,512]{1,0:T(8,128)(2,1)} %update_ref.1) | copy-start | bytes 1572868
  11.3 10.1 %collective-permute-start.1 = (bf16[16,640]{1,0:T(8,128)(2,1)S(1)}, bf16[16,640]{1,0:T(8,128)(2,1)S(1)}, u32[]{:S(2)}, u32[]{:S(2)}) collective-permute-start(bf16[16,640]{1,0:T(8,128)(2,1)S(1)} %pad_maximum_fusion.3), channel_id=1, source_target_pairs={{8,0},{16,8},{24,16},{0,24},{9,1},{17,9},{25,17},{1,25},{10,2},{18... | collective-permute-start | bytes 61448 | tf_op jit(solution)/shard_map/ppermute | solution.py:30
  14.5 5.0 %copy-start.5 = (bf16[512,384]{1,0:T(8,128)(2,1)S(1)}, bf16[512,384]{1,0:T(8,128)(2,1)}, u32[]{:S(2)}) copy-start(bf16[512,384]{1,0:T(8,128)(2,1)} %split_ref.1) | copy-start | bytes 1179652
  15.9 4.5 %copy-start.6 = (bf16[192,512]{1,0:T(8,128)(2,1)S(1)}, bf16[192,512]{1,0:T(8,128)(2,1)}, u32[]{:S(2)}) copy-start(bf16[192,512]{1,0:T(8,128)(2,1)} %tensor_ref.1) | copy-start | bytes 589828
  21.6 5.3 %collective-permute-start.2 = (bf16[64,640]{1,0:T(8,128)(2,1)S(1)}, bf16[64,640]{1,0:T(8,128)(2,1)S(1)}, u32[]{:S(2)}, u32[]{:S(2)}) collective-permute-start(bf16[64,640]{1,0:T(8,128)(2,1)S(1)} %convolution_convert_fusion.1), channel_id=1, source_target_pairs={{4,0},{0,4},{5,1},{1,5},{6,2},{2,6},{7,3},{3,7},{12,8},{8,12},{13,... | collective-permute-start | bytes 245768 | tf_op jit(solution)/shard_map/ppermute | solution.py:30
  24.2 4.5 %collective-permute-start.3 = (bf16[64,640]{1,0:T(8,128)(2,1)S(1)}, bf16[64,640]{1,0:T(8,128)(2,1)S(1)}, u32[]{:S(2)}, u32[]{:S(2)}) collective-permute-start(bf16[64,640]{1,0:T(8,128)(2,1)S(1)} %convolution_convert_fusion), channel_id=1, source_target_pairs={{4,0},{0,4},{5,1},{1,5},{6,2},{2,6},{7,3},{3,7},{12,8},{8,12},{13,... | collective-permute-start | bytes 245768 | tf_op jit(solution)/shard_map/ppermute | solution.py:30
  28.9 5.7 %collective-permute-start.4 = (bf16[16,640]{1,0:T(8,128)(2,1)S(1)}, bf16[16,640]{1,0:T(8,128)(2,1)S(1)}, u32[]{:S(2)}, u32[]{:S(2)}) collective-permute-start(bf16[16,640]{1,0:T(8,128)(2,1)S(1)} %convolution_convert_fusion.3), channel_id=1, source_target_pairs={{3,0},{0,1},{1,2},{2,3},{7,4},{4,5},{5,6},{6,7},{11,8},{8,9},{9,10... | collective-permute-start | bytes 61448 | tf_op jit(solution)/shard_map/ppermute | solution.py:30
  30.8 4.1 %collective-permute-start.5 = (bf16[16,640]{1,0:T(8,128)(2,1)S(1)}, bf16[16,640]{1,0:T(8,128)(2,1)S(1)}, u32[]{:S(2)}, u32[]{:S(2)}) collective-permute-start(bf16[16,640]{1,0:T(8,128)(2,1)S(1)} %convolution_convert_fusion.2), channel_id=1, source_target_pairs={{1,0},{2,1},{3,2},{0,3},{5,4},{6,5},{7,6},{4,7},{9,8},{10,9},{11,1... | collective-permute-start | bytes 61448 | tf_op jit(solution)/shard_map/ppermute | solution.py:30
  34.9 2.4 %copy-start.14 = (f32[8]{0:T(128)S(1)}, f32[8]{0:T(128)}, u32[]{:S(2)}) copy-start(f32[8]{0:T(128)} %convert_multiply_fusion) | copy-start | bytes 100
  36.0 2.5 %copy-start.13 = (f32[512]{0:T(512)S(1)}, f32[512]{0:T(512)}, u32[]{:S(2)}) copy-start(f32[512]{0:T(512)} %param.32) | copy-start | bytes 6148
  52.1 2.8 %copy-start.15 = (f32[512,1024]{1,0:T(8,128)S(1)}, f32[512,1024]{1,0:T(8,128)}, u32[]{:S(2)}) copy-start(f32[512,1024]{1,0:T(8,128)} %get-tuple-element.9) | copy-start | bytes 6291460
  56.0 6.0 %collective-permute-start.7 = (f32[16,640]{1,0:T(8,128)S(1)}, f32[16,640]{1,0:T(8,128)S(1)}, u32[]{:S(2)}, u32[]{:S(2)}) collective-permute-start(f32[16,640]{1,0:T(8,128)S(1)} %get-tuple-element.32), channel_id=1, source_target_pairs={{3,0},{0,1},{1,2},{2,3},{7,4},{4,5},{5,6},{6,7},{11,8},{8,9},{9,10... | collective-permute-start | bytes 122888 | tf_op jit(solution)/shard_map/ppermute | solution.py:30
  57.6 5.2 %collective-permute-start.6 = (f32[16,640]{1,0:T(8,128)S(1)}, f32[16,640]{1,0:T(8,128)S(1)}, u32[]{:S(2)}, u32[]{:S(2)}) collective-permute-start(f32[16,640]{1,0:T(8,128)S(1)} %get-tuple-element.31), channel_id=1, source_target_pairs={{1,0},{2,1},{3,2},{0,3},{5,4},{6,5},{7,6},{4,7},{9,8},{10,9},{11,1... | collective-permute-start | bytes 122888 | tf_op jit(solution)/shard_map/ppermute | solution.py:30
  62.8 2.1 %copy-start.7 = (f32[512,128]{1,0:T(8,128)S(1)}, f32[512,128]{1,0:T(8,128)}, u32[]{:S(2)}) copy-start(f32[512,128]{1,0:T(8,128)} %get-tuple-element.11) | copy-start | bytes 786436
  63.6 5.4 %collective-permute-start.8 = (f32[64,640]{1,0:T(8,128)S(1)}, f32[64,640]{1,0:T(8,128)S(1)}, u32[]{:S(2)}, u32[]{:S(2)}) collective-permute-start(f32[64,640]{1,0:T(8,128)S(1)} %get-tuple-element.34), channel_id=1, source_target_pairs={{4,0},{0,4},{5,1},{1,5},{6,2},{2,6},{7,3},{3,7},{12,8},{8,12},{13,... | collective-permute-start | bytes 491528 | tf_op jit(solution)/shard_map/ppermute | solution.py:30
  65.6 6.2 %copy-start.16 = (f32[8,128]{1,0:T(8,128)S(1)}, f32[8,128]{1,0:T(8,128)}, u32[]{:S(2)}) copy-start(f32[8,128]{1,0:T(8,128)} %get-tuple-element.8) | copy-start | bytes 12292
  65.6 6.2 %copy-start.17 = (f32[5]{0:T(128)S(1)}, f32[5]{0:T(128)}, u32[]{:S(2)}) copy-start(f32[5]{0:T(128)} %param.33) | copy-start | bytes 64
  65.6 5.4 %collective-permute-start.9 = (f32[64,640]{1,0:T(8,128)S(1)}, f32[64,640]{1,0:T(8,128)S(1)}, u32[]{:S(2)}, u32[]{:S(2)}) collective-permute-start(f32[64,640]{1,0:T(8,128)S(1)} %get-tuple-element.33), channel_id=1, source_target_pairs={{4,0},{0,4},{5,1},{1,5},{6,2},{2,6},{7,3},{3,7},{12,8},{8,12},{13,... | collective-permute-start | bytes 491528 | tf_op jit(solution)/shard_map/ppermute | solution.py:30
  71.7 1.7 %collective-permute-start.10 = (f32[16,640]{1,0:T(8,128)S(1)}, f32[16,640]{1,0:T(8,128)S(1)}, u32[]{:S(2)}, u32[]{:S(2)}) collective-permute-start(f32[16,640]{1,0:T(8,128)S(1)} %get-tuple-element.45), channel_id=1, source_target_pairs={{8,0},{16,8},{24,16},{0,24},{9,1},{17,9},{25,17},{1,25},{10,2},{18... | collective-permute-start | bytes 122888 | tf_op jit(solution)/shard_map/ppermute | solution.py:30
  72.6 3.4 %collective-permute-start.11 = (f32[16,640]{1,0:T(8,128)S(1)}, f32[16,640]{1,0:T(8,128)S(1)}, u32[]{:S(2)}, u32[]{:S(2)}) collective-permute-start(f32[16,640]{1,0:T(8,128)S(1)} %get-tuple-element.44), channel_id=1, source_target_pairs={{24,0},{0,8},{8,16},{16,24},{25,1},{1,9},{9,17},{17,25},{26,2},{2,... | collective-permute-start | bytes 122888 | tf_op jit(solution)/shard_map/ppermute | solution.py:30

commit v13 on v12

--- a/solution.py
+++ b/solution.py
@@ -349,7 +349,9 @@
             pickers[segment] = onehot
             if section == 0:
                 chosen = jnp.dot(onehot, latent, preferred_element_type=jnp.float32)
-                kinds_of = jnp.take(species, picked, axis=0)
+                kinds_of = jnp.dot(
+                    onehot, species.astype(jnp.bfloat16)[:, None], preferred_element_type=jnp.float32
+                )[:, 0].astype(jnp.int32)
                 out = jnp.concatenate(
                     [
                         project(chosen.astype(jnp.bfloat16), kinds_of, neigh_proj, neigh_table),

time: 79.2 us -> 78.2 us (0.987)
  matrix products: 18.7 us -> 22 us
  local copies, waits for them, and re-layouts: 12.8 us -> 10.1 us
  other arithmetic: 5.69 us -> 4.07 us
    gather x2 -> x0, local copies, waits for them, and re-layouts: 2.64 us -> none  [shards(): kinds_of = jnp.take(species, picked, axis=0)]
    dot_general x0 -> x2, matrix products: none -> 1.71 us  [shards(): jnp.dot(onehot, species.astype(jnp.bfloat16)[:, None], preferred_element_...]
    select_n x2 -> x0, other arithmetic: 1.62 us -> none  [shards(): kinds_of = jnp.take(species, picked, axis=0)]
    dot_general x5, matrix products: 2.63 us -> 4.13 us  [lookup(): return jnp.dot(onehot, table, precision=lax.Precision.HIGHEST)]
    unnamed x44 -> x42, local copies, waits for them, and re-layouts: 3.59 us -> 3.56 us
  transfers between devices with their start and end apart: 12 -> 12, of which waited for: 9 -> 9; matrix products, arithmetic and copies ran while one was open for 16% -> 20% of each run, Pallas kernels for 0% -> 0%
where the time goes in v13:
time: 78.2 us; the launch traced here: 77.7 us
  matrix products  22 us (28%)
  starting transfers between devices  15.9 us (20%)
  waiting for transfers between devices  14 us (18%)
  local copies, waits for them, and re-layouts  10.1 us (13%)
  Pallas kernels  9.71 us (12%)
  other arithmetic  4.07 us (5%)
  between operations  1.89 us (2%)
    ppermute x12, starting transfers between devices, passed_along(): return lax.ppermute(block, axis, route)  15.9 us
    ppermute x12, waiting for transfers between devices, passed_along(): return lax.ppermute(block, axis, route)  14 us
    pallas_call x1, Pallas kernels, pair_terms(): pl.pallas_call(_pair_kernel, out_shape=(jax.ShapeDtypeStruct((width, pair...  9.71 us
    dot_general x5, matrix products, lookup(): return jnp.dot(onehot, table, precision=lax.Precision.HIGHEST)  4.13 us
    dot_general x4, matrix products, project(): jnp.dot(rows, weight, preferred_element_type=jnp.float32)  3.81 us
    unnamed x42, local copies, waits for them, and re-layouts  3.56 us
    dot_general x1, matrix products, spread_cols(): jnp.einsum('wn,nr->wr', high, onehot, preferred_element_type=jnp.float32)  2.82 us
    dot_general x6, matrix products, spread(): jnp.einsum('nr,nw->rw', onehot, high, preferred_element_type=jnp.float32)  2.1 us
  transfers between devices with their start and end apart: 12, of which 9 were waited for; matrix products, arithmetic and copies ran while one was open for 20% of the time, Pallas kernels for 0%

profile of v13, /device:TPU:0, one launch (start us, length us, event | category | flops | bytes accessed | tf_op | source)
XLA Modules:
  0.0 77.7 jit_solution(7692879381712983011)
XLA Ops:
  3.5 1.3 %fusion.16 = f32[16,512]{1,0:T(8,128)S(1)} fusion(bf16[512,512]{1,0:T(8,128)(2,1)S(1)} %copy-done, bf16[128,512]{1,0:T(8,128)(2,1)} %param.16, s32[16]{0:T(128)S(1)} %get-tuple-element.73), kind=kOutput, calls=%fused_computation.37 | convolution fusion | flops 10496000 | bytes 688192 | tf_op jit(solution)/shard_map/dot_general | solution.py:310
  4.8 0.9 %fusion.14 = bf16[16,512]{1,0:T(8,128)(2,1)S(1)} fusion(f32[16,512]{1,0:T(8,128)S(1)} %fusion.16, f32[5,512]{1,0:T(8,128)} %param.25, s32[16]{0:T(128)S(1)} %fusion.20), kind=kOutput, calls=%fused_computation.33 | convolution fusion | flops 507984 | bytes 59456 | tf_op jit(solution)/shard_map/dot_general | solution.py:306
  6.4 1.2 %fusion.17 = f32[16,512]{1,0:T(8,128)S(1)} fusion(bf16[512,512]{1,0:T(8,128)(2,1)S(1)} %copy-done, bf16[128,512]{1,0:T(8,128)(2,1)} %param.16, s32[16]{0:T(128)S(1)} %get-tuple-element.72), kind=kOutput, calls=%fused_computation.38 | convolution fusion | flops 10496000 | bytes 688192 | tf_op jit(solution)/shard_map/dot_general | solution.py:310
  8.5 1.0 %fusion.15 = bf16[16,512]{1,0:T(8,128)(2,1)S(1)} fusion(f32[16,512]{1,0:T(8,128)S(1)} %fusion.17, f32[5,512]{1,0:T(8,128)} %param.25, s32[16]{0:T(128)S(1)} %fusion.21), kind=kOutput, calls=%fused_computation.34 | convolution fusion | flops 507984 | bytes 59456 | tf_op jit(solution)/shard_map/dot_general | solution.py:306
  9.5 2.0 %collective-permute-start.1 = (bf16[16,640]{1,0:T(8,128)(2,1)S(1)}, bf16[16,640]{1,0:T(8,128)(2,1)S(1)}, u32[]{:S(2)}, u32[]{:S(2)}) collective-permute-start(bf16[16,640]{1,0:T(8,128)(2,1)S(1)} %pad_maximum_fusion.3), channel_id=1, source_target_pairs={{8,0},{16,8},{24,16},{0,24},{9,1},{17,9},{25,17},{1,25},{10,2},{18... | collective-permute-start | bytes 61448 | tf_op jit(solution)/shard_map/ppermute | solution.py:30
  11.5 1.0 %fusion.35 = f32[128,512]{1,0:T(8,128)S(1)} fusion(f32[5,512]{1,0:T(8,128)} %param.25, s32[128]{0:T(128)} %param.18), kind=kOutput, calls=%fused_computation.73 | convolution fusion | flops 3932800 | bytes 272896 | tf_op jit(solution)/shard_map/dot_general | solution.py:306
  15.4 1.0 %fusion.13.centre_ref = f32[512,128]{1,0:T(8,128)} fusion(f32[512,128]{1,0:T(8,128)S(1)} %convolution_bitcast_fusion, bf16[512,512]{1,0:T(8,128)(2,1)S(1)} %copy-done.2, bf16[128,512]{1,0:T(8,128)(2,1)S(1)} %copy-done.3), kind=kOutput, calls=%fused_computation.26 | convolution fusion | flops 67305472 | bytes 1179648 | tf_op jit(solution)/shard_map/dot_general | solution.py:310
  17.4 1.0 %copy.56 = bf16[512,512]{0,1:T(8,128)(2,1)} copy(bf16[512,512]{1,0:T(8,128)(2,1)S(1)} %copy-done.1) | data formatting | bytes 1048576 | tf_op args[12]
  18.4 0.9 %copy.55 = bf16[512,384]{0,1:T(8,128)(2,1)} copy(bf16[512,384]{1,0:T(8,128)(2,1)S(1)} %copy-done.4) | data formatting | bytes 786432 | tf_op args[11]
  20.5 2.4 %collective-permute-start.2 = (bf16[64,640]{1,0:T(8,128)(2,1)S(1)}, bf16[64,640]{1,0:T(8,128)(2,1)S(1)}, u32[]{:S(2)}, u32[]{:S(2)}) collective-permute-start(bf16[64,640]{1,0:T(8,128)(2,1)S(1)} %convolution_convert_fusion.1), channel_id=1, source_target_pairs={{4,0},{0,4},{5,1},{1,5},{6,2},{2,6},{7,3},{3,7},{12,8},{8,12},{13,... | collective-permute-start | bytes 245768 | tf_op jit(solution)/shard_map/ppermute | solution.py:30
  23.3 2.6 %collective-permute-done.2 = bf16[64,640]{1,0:T(8,128)(2,1)S(1)} collective-permute-done((bf16[64,640]{1,0:T(8,128)(2,1)S(1)}, bf16[64,640]{1,0:T(8,128)(2,1)S(1)}, u32[]{:S(2)}, u32[]{:S(2)}) %collective-permute-start.2) | collective-permute-done | bytes 81952 | tf_op jit(solution)/shard_map/ppermute | solution.py:30
  25.9 1.8 %collective-permute-done.3 = bf16[64,640]{1,0:T(8,128)(2,1)S(1)} collective-permute-done((bf16[64,640]{1,0:T(8,128)(2,1)S(1)}, bf16[64,640]{1,0:T(8,128)(2,1)S(1)}, u32[]{:S(2)}, u32[]{:S(2)}) %collective-permute-start.3) | collective-permute-done | bytes 81952 | tf_op jit(solution)/shard_map/ppermute | solution.py:30
  27.9 1.6 %collective-permute-start.4 = (bf16[16,640]{1,0:T(8,128)(2,1)S(1)}, bf16[16,640]{1,0:T(8,128)(2,1)S(1)}, u32[]{:S(2)}, u32[]{:S(2)}) collective-permute-start(bf16[16,640]{1,0:T(8,128)(2,1)S(1)} %convolution_convert_fusion.3), channel_id=1, source_target_pairs={{3,0},{0,1},{1,2},{2,3},{7,4},{4,5},{5,6},{6,7},{11,8},{8,9},{9,10... | collective-permute-start | bytes 61448 | tf_op jit(solution)/shard_map/ppermute | solution.py:30
  29.7 2.5 %collective-permute-start.5 = (bf16[16,640]{1,0:T(8,128)(2,1)S(1)}, bf16[16,640]{1,0:T(8,128)(2,1)S(1)}, u32[]{:S(2)}, u32[]{:S(2)}) collective-permute-start(bf16[16,640]{1,0:T(8,128)(2,1)S(1)} %convolution_convert_fusion.2), channel_id=1, source_target_pairs={{1,0},{2,1},{3,2},{0,3},{5,4},{6,5},{7,6},{4,7},{9,8},{10,9},{11,1... | collective-permute-start | bytes 61448 | tf_op jit(solution)/shard_map/ppermute | solution.py:30
  32.2 1.4 %collective-permute-done.4 = bf16[16,640]{1,0:T(8,128)(2,1)S(1)} collective-permute-done((bf16[16,640]{1,0:T(8,128)(2,1)S(1)}, bf16[16,640]{1,0:T(8,128)(2,1)S(1)}, u32[]{:S(2)}, u32[]{:S(2)}) %collective-permute-start.4) | collective-permute-done | bytes 20512 | tf_op jit(solution)/shard_map/ppermute | solution.py:30
  33.9 1.0 %fusion.2 = f32[640,1024]{1,0:T(8,128)S(1)} fusion(bf16[320,640]{1,0:T(8,128)(2,1)S(1)} %constant_dynamic-update-slice_fusion.2, s32[1024]{0:T(1024)S(1)} %bitcast.170), kind=kOutput, calls=%fused_computation.6 | convolution fusion | flops 419758080 | bytes 3035136 | tf_op jit(solution)/shard_map/tw,pt->wp/dot_general | solution.py:379
  34.9 1.2 %slice.200.rows_ref = bf16[512,1024]{1,0:T(8,128)(2,1)} slice(f32[640,1024]{1,0:T(8,128)S(1)} %fusion.2), slice={[0:512], [0:1024]} | slice | bytes 2097152 | tf_op jit(solution)/shard_map/slice | solution.py:380
  37.4 1.6 %broadcast_in_dim.53.energy_w_ref = f32[512,1024]{1,0:T(8,128)} broadcast(f32[512]{0:T(512)S(1)} %copy-done.11), dimensions={0} | broadcast | bytes 2099200 | tf_op jit(solution)/shard_map/broadcast_in_dim | solution.py:264
  39.0 9.7 %shard_map.175 = (f32[512,1024]{1,0:T(8,128)}, f32[512,128]{1,0:T(8,128)}, f32[128,1024]{1,0:T(8,128)}, f32[8,128]{1,0:T(8,128)}) custom-call(bf16[512,1024]{1,0:T(8,128)(2,1)} %slice.200.rows_ref, f32[512,128]{1,0:T(8,128)} %fusion.13.centre_ref, f32[128,1024]{1,0:T(8,128)} %concatenate.73.geo_ref, bf16[512,128]{1,0:T(8,128)(2,1)} %copy.58.basis_t_ref, ...), custom_call_target="tpu_custom_call" | custom-call | flops 1610612736 | bytes 8388608 | tf_op jit(solution)/shard_map/pallas_call | solution.py:226
  48.7 1.2 %slice_multiply_fusion.4 = (f32[1,1024]{1,0:T(1,128)S(1)}, f32[1,1024]{1,0:T(1,128)S(1)}, f32[1,1024]{1,0:T(1,128)S(1)}, f32[1,1024]{1,0:T(1,128)S(1)}, f32[1,10...) fusion(f32[128,1024]{1,0:T(8,128)} %get-tuple-element.9), kind=kLoop, calls=%fused_computation.191 | loop fusion | flops 5120 | bytes 73728 | tf_op jit(solution)/shard_map/transpose(jvp())/mul | solution.py:70
  49.9 1.0 %fusion.42 = (f32[1024]{0:T(1024)S(1)}, f32[1024]{0:T(1024)S(1)}) fusion(f32[128,1024]{1,0:T(8,128)} %get-tuple-element.9, f32[1024]{0:T(1024)S(1)} %get-tuple-element.67, f32[8]{0:T(128)S(1)} %copy-done.13, f32[1024]{0:T(1024)S(1)} %get-tuple-element.66), kind=kLoop, calls=%fused_computation.87 | loop fusion | flops 55296 | bytes 49184 | tf_op jit(solution)/shard_map/transpose(jvp())/reduce_sum | solution.py:58
  51.1 2.8 %fusion.3 = f32[320,640]{1,0:T(8,128)S(1)} fusion(f32[3,1024]{1,0:T(4,128)S(1)} %bitcast.182, f32[512,1024]{1,0:T(8,128)} %get-tuple-element.8, f32[640]{0:T(1024)S(1)} %pad.22.clone, s32[1024]{0:T(1024)S(1)} %bitcast.171), kind=kOutput, calls=%fused_computation.7 | convolution fusion | flops 424017920 | bytes 2935296 | tf_op jit(solution)/shard_map/wn,nr->wr/dot_general | solution.py:316
  53.9 1.1 %fusion.8 = f32[320,640]{1,0:T(8,128)S(1)} fusion(f32[320,640]{1,0:T(8,128)S(1)} %fusion.3, f32[3,1024]{1,0:T(4,128)S(1)} %bitcast.183, f32[512,1024]{1,0:T(8,128)S(1)} %copy-done.14, f32[640]{0:T(1024)S(1)} %pad.22.clone, f32[128,3]{1,0:T(8,128)S(1)} %bitcast.168, s32[1024]{0:T(1024)S(1)} %bitcast.172), kind=kOutput, calls=%fused_computation.11 | convolution fusion | flops 424427520 | bytes 3756032 | tf_op jit(solution)/shard_map/wn,nr->wr/dot_general | solution.py:318
  55.0 1.6 %collective-permute-start.7 = (f32[16,640]{1,0:T(8,128)S(1)}, f32[16,640]{1,0:T(8,128)S(1)}, u32[]{:S(2)}, u32[]{:S(2)}) collective-permute-start(f32[16,640]{1,0:T(8,128)S(1)} %get-tuple-element.31), channel_id=1, source_target_pairs={{3,0},{0,1},{1,2},{2,3},{7,4},{4,5},{5,6},{6,7},{11,8},{8,9},{9,10... | collective-permute-start | bytes 122888 | tf_op jit(solution)/shard_map/ppermute | solution.py:30
  56.6 2.5 %collective-permute-start.6 = (f32[16,640]{1,0:T(8,128)S(1)}, f32[16,640]{1,0:T(8,128)S(1)}, u32[]{:S(2)}, u32[]{:S(2)}) collective-permute-start(f32[16,640]{1,0:T(8,128)S(1)} %get-tuple-element.30), channel_id=1, source_target_pairs={{1,0},{2,1},{3,2},{0,3},{5,4},{6,5},{7,6},{4,7},{9,8},{10,9},{11,1... | collective-permute-start | bytes 122888 | tf_op jit(solution)/shard_map/ppermute | solution.py:30
  59.1 1.9 %collective-permute-done.7 = f32[16,640]{1,0:T(8,128)S(1)} collective-permute-done((f32[16,640]{1,0:T(8,128)S(1)}, f32[16,640]{1,0:T(8,128)S(1)}, u32[]{:S(2)}, u32[]{:S(2)}) %collective-permute-start.7) | collective-permute-done | bytes 40992 | tf_op jit(solution)/shard_map/ppermute | solution.py:30
  62.6 1.3 %collective-permute-start.8 = (f32[64,640]{1,0:T(8,128)S(1)}, f32[64,640]{1,0:T(8,128)S(1)}, u32[]{:S(2)}, u32[]{:S(2)}) collective-permute-start(f32[64,640]{1,0:T(8,128)S(1)} %get-tuple-element.33), channel_id=1, source_target_pairs={{4,0},{0,4},{5,1},{1,5},{6,2},{2,6},{7,3},{3,7},{12,8},{8,12},{13,... | collective-permute-start | bytes 491528 | tf_op jit(solution)/shard_map/ppermute | solution.py:30
  64.7 0.9 %collective-permute-start.9 = (f32[64,640]{1,0:T(8,128)S(1)}, f32[64,640]{1,0:T(8,128)S(1)}, u32[]{:S(2)}, u32[]{:S(2)}) collective-permute-start(f32[64,640]{1,0:T(8,128)S(1)} %get-tuple-element.32), channel_id=1, source_target_pairs={{4,0},{0,4},{5,1},{1,5},{6,2},{2,6},{7,3},{3,7},{12,8},{8,12},{13,... | collective-permute-start | bytes 491528 | tf_op jit(solution)/shard_map/ppermute | solution.py:30
  65.5 2.5 %collective-permute-done.8 = f32[64,640]{1,0:T(8,128)S(1)} collective-permute-done((f32[64,640]{1,0:T(8,128)S(1)}, f32[64,640]{1,0:T(8,128)S(1)}, u32[]{:S(2)}, u32[]{:S(2)}) %collective-permute-start.8) | collective-permute-done | bytes 163872 | tf_op jit(solution)/shard_map/ppermute | solution.py:30
  68.7 1.3 %collective-permute-done.9 = f32[64,640]{1,0:T(8,128)S(1)} collective-permute-done((f32[64,640]{1,0:T(8,128)S(1)}, f32[64,640]{1,0:T(8,128)S(1)}, u32[]{:S(2)}, u32[]{:S(2)}) %collective-permute-start.9) | collective-permute-done | bytes 163872 | tf_op jit(solution)/shard_map/ppermute | solution.py:30
  73.1 1.9 %collective-permute-done.11 = f32[16,640]{1,0:T(8,128)S(1)} collective-permute-done((f32[16,640]{1,0:T(8,128)S(1)}, f32[16,640]{1,0:T(8,128)S(1)}, u32[]{:S(2)}, u32[]{:S(2)}) %collective-permute-start.11) | collective-permute-done | bytes 40992 | tf_op jit(solution)/shard_map/ppermute | solution.py:30
  75.7 1.4 %convolution_add_fusion.6 = f32[128,512]{1,0:T(8,128)} fusion(f32[128,512]{1,0:T(8,128)S(1)} %fusion.138, bf16[512,512]{1,0:T(8,128)(2,1)S(1)} %copy-done, f32[128,640]{1,0:T(8,128)S(1)} %fusion.28), kind=kOutput, calls=%fused_computation.20 | convolution fusion | flops 402718720 | bytes 1310720 | tf_op jit(solution)/shard_map/dot_general | solution.py:427
  (122 shorter events, 18.3 us)
Async XLA Ops:
  0.6 2.8 %copy-start = (bf16[512,512]{1,0:T(8,128)(2,1)S(1)}, bf16[512,512]{1,0:T(8,128)(2,1)}, u32[]{:S(2)}) copy-start(bf16[512,512]{1,0:T(8,128)(2,1)} %param.23) | copy-start | bytes 1572868
  0.6 11.9 %copy-start.8 = (s32[1,192]{1,0:T(1,128)S(1)}, s32[1,192]{1,0:T(1,128)}, u32[]{:S(2)}) copy-start(s32[1,192]{1,0:T(1,128)} %param.19) | copy-start | bytes 2308
  0.7 14.2 %copy-start.12 = (s32[128]{0:T(128)S(1)}, s32[128]{0:T(128)}, u32[]{:S(2)}) copy-start(s32[128]{0:T(128)} %param.18) | copy-start | bytes 1540
  0.7 12.5 %copy-start.3 = (bf16[128,512]{1,0:T(8,128)(2,1)S(1)}, bf16[128,512]{1,0:T(8,128)(2,1)}, u32[]{:S(2)}) copy-start(bf16[128,512]{1,0:T(8,128)(2,1)} %param.16) | copy-start | bytes 393220
  0.7 13.5 %copy-start.9 = (bf16[8,512]{1,0:T(8,128)(2,1)S(1)}, bf16[8,512]{1,0:T(8,128)(2,1)}, u32[]{:S(2)}) copy-start(bf16[8,512]{1,0:T(8,128)(2,1)} %param.26) | copy-start | bytes 24580
  0.7 14.2 %copy-start.7 = (f32[5,512]{1,0:T(8,128)S(1)}, f32[5,512]{1,0:T(8,128)}, u32[]{:S(2)}) copy-start(f32[5,512]{1,0:T(8,128)} %param.24) | copy-start | bytes 30724
  3.5 11.9 %copy-start.2 = (bf16[512,512]{1,0:T(8,128)(2,1)S(1)}, bf16[512,512]{1,0:T(8,128)(2,1)}, u32[]{:S(2)}) copy-start(bf16[512,512]{1,0:T(8,128)(2,1)} %param.22) | copy-start | bytes 1572868
  5.7 14.6 %collective-permute-start = (bf16[16,640]{1,0:T(8,128)(2,1)S(1)}, bf16[16,640]{1,0:T(8,128)(2,1)S(1)}, u32[]{:S(2)}, u32[]{:S(2)}) collective-permute-start(bf16[16,640]{1,0:T(8,128)(2,1)S(1)} %pad_maximum_fusion.2), channel_id=1, source_target_pairs={{24,0},{0,8},{8,16},{16,24},{25,1},{1,9},{9,17},{17,25},{26,2},{2,... | collective-permute-start | bytes 61448 | tf_op jit(solution)/shard_map/ppermute | solution.py:30
  6.4 10.0 %copy-start.10 = (s32[1024]{0:T(1024)S(1)}, s32[1024]{0:T(1024)}, u32[]{:S(2)}) copy-start(s32[1024]{0:T(1024)} %param.20) | copy-start | bytes 12292
  8.5 8.9 %copy-start.1 = (bf16[512,512]{1,0:T(8,128)(2,1)S(1)}, bf16[512,512]{1,0:T(8,128)(2,1)}, u32[]{:S(2)}) copy-start(bf16[512,512]{1,0:T(8,128)(2,1)} %update_ref.1) | copy-start | bytes 1572868
  9.5 10.8 %collective-permute-start.1 = (bf16[16,640]{1,0:T(8,128)(2,1)S(1)}, bf16[16,640]{1,0:T(8,128)(2,1)S(1)}, u32[]{:S(2)}, u32[]{:S(2)}) collective-permute-start(bf16[16,640]{1,0:T(8,128)(2,1)S(1)} %pad_maximum_fusion.3), channel_id=1, source_target_pairs={{8,0},{16,8},{24,16},{0,24},{9,1},{17,9},{25,17},{1,25},{10,2},{18... | collective-permute-start | bytes 61448 | tf_op jit(solution)/shard_map/ppermute | solution.py:30
  13.4 5.0 %copy-start.4 = (bf16[512,384]{1,0:T(8,128)(2,1)S(1)}, bf16[512,384]{1,0:T(8,128)(2,1)}, u32[]{:S(2)}) copy-start(bf16[512,384]{1,0:T(8,128)(2,1)} %split_ref.1) | copy-start | bytes 1179652
  14.8 4.5 %copy-start.5 = (bf16[192,512]{1,0:T(8,128)(2,1)S(1)}, bf16[192,512]{1,0:T(8,128)(2,1)}, u32[]{:S(2)}) copy-start(bf16[192,512]{1,0:T(8,128)(2,1)} %tensor_ref.1) | copy-start | bytes 589828
  20.5 5.3 %collective-permute-start.2 = (bf16[64,640]{1,0:T(8,128)(2,1)S(1)}, bf16[64,640]{1,0:T(8,128)(2,1)S(1)}, u32[]{:S(2)}, u32[]{:S(2)}) collective-permute-start(bf16[64,640]{1,0:T(8,128)(2,1)S(1)} %convolution_convert_fusion.1), channel_id=1, source_target_pairs={{4,0},{0,4},{5,1},{1,5},{6,2},{2,6},{7,3},{3,7},{12,8},{8,12},{13,... | collective-permute-start | bytes 245768 | tf_op jit(solution)/shard_map/ppermute | solution.py:30
  23.2 4.5 %collective-permute-start.3 = (bf16[64,640]{1,0:T(8,128)(2,1)S(1)}, bf16[64,640]{1,0:T(8,128)(2,1)S(1)}, u32[]{:S(2)}, u32[]{:S(2)}) collective-permute-start(bf16[64,640]{1,0:T(8,128)(2,1)S(1)} %convolution_convert_fusion), channel_id=1, source_target_pairs={{4,0},{0,4},{5,1},{1,5},{6,2},{2,6},{7,3},{3,7},{12,8},{8,12},{13,... | collective-permute-start | bytes 245768 | tf_op jit(solution)/shard_map/ppermute | solution.py:30
  27.9 5.7 %collective-permute-start.4 = (bf16[16,640]{1,0:T(8,128)(2,1)S(1)}, bf16[16,640]{1,0:T(8,128)(2,1)S(1)}, u32[]{:S(2)}, u32[]{:S(2)}) collective-permute-start(bf16[16,640]{1,0:T(8,128)(2,1)S(1)} %convolution_convert_fusion.3), channel_id=1, source_target_pairs={{3,0},{0,1},{1,2},{2,3},{7,4},{4,5},{5,6},{6,7},{11,8},{8,9},{9,10... | collective-permute-start | bytes 61448 | tf_op jit(solution)/shard_map/ppermute | solution.py:30
  29.7 4.1 %collective-permute-start.5 = (bf16[16,640]{1,0:T(8,128)(2,1)S(1)}, bf16[16,640]{1,0:T(8,128)(2,1)S(1)}, u32[]{:S(2)}, u32[]{:S(2)}) collective-permute-start(bf16[16,640]{1,0:T(8,128)(2,1)S(1)} %convolution_convert_fusion.2), channel_id=1, source_target_pairs={{1,0},{2,1},{3,2},{0,3},{5,4},{6,5},{7,6},{4,7},{9,8},{10,9},{11,1... | collective-permute-start | bytes 61448 | tf_op jit(solution)/shard_map/ppermute | solution.py:30
  33.9 2.4 %copy-start.13 = (f32[8]{0:T(128)S(1)}, f32[8]{0:T(128)}, u32[]{:S(2)}) copy-start(f32[8]{0:T(128)} %convert_multiply_fusion) | copy-start | bytes 100
  34.9 2.5 %copy-start.11 = (f32[512]{0:T(512)S(1)}, f32[512]{0:T(512)}, u32[]{:S(2)}) copy-start(f32[512]{0:T(512)} %param.30) | copy-start | bytes 6148
  51.1 2.8 %copy-start.14 = (f32[512,1024]{1,0:T(8,128)S(1)}, f32[512,1024]{1,0:T(8,128)}, u32[]{:S(2)}) copy-start(f32[512,1024]{1,0:T(8,128)} %get-tuple-element.8) | copy-start | bytes 6291460
  55.0 6.0 %collective-permute-start.7 = (f32[16,640]{1,0:T(8,128)S(1)}, f32[16,640]{1,0:T(8,128)S(1)}, u32[]{:S(2)}, u32[]{:S(2)}) collective-permute-start(f32[16,640]{1,0:T(8,128)S(1)} %get-tuple-element.31), channel_id=1, source_target_pairs={{3,0},{0,1},{1,2},{2,3},{7,4},{4,5},{5,6},{6,7},{11,8},{8,9},{9,10... | collective-permute-start | bytes 122888 | tf_op jit(solution)/shard_map/ppermute | solution.py:30
  56.6 5.2 %collective-permute-start.6 = (f32[16,640]{1,0:T(8,128)S(1)}, f32[16,640]{1,0:T(8,128)S(1)}, u32[]{:S(2)}, u32[]{:S(2)}) collective-permute-start(f32[16,640]{1,0:T(8,128)S(1)} %get-tuple-element.30), channel_id=1, source_target_pairs={{1,0},{2,1},{3,2},{0,3},{5,4},{6,5},{7,6},{4,7},{9,8},{10,9},{11,1... | collective-permute-start | bytes 122888 | tf_op jit(solution)/shard_map/ppermute | solution.py:30
  61.8 2.1 %copy-start.6 = (f32[512,128]{1,0:T(8,128)S(1)}, f32[512,128]{1,0:T(8,128)}, u32[]{:S(2)}) copy-start(f32[512,128]{1,0:T(8,128)} %get-tuple-element.10) | copy-start | bytes 786436
  62.6 5.4 %collective-permute-start.8 = (f32[64,640]{1,0:T(8,128)S(1)}, f32[64,640]{1,0:T(8,128)S(1)}, u32[]{:S(2)}, u32[]{:S(2)}) collective-permute-start(f32[64,640]{1,0:T(8,128)S(1)} %get-tuple-element.33), channel_id=1, source_target_pairs={{4,0},{0,4},{5,1},{1,5},{6,2},{2,6},{7,3},{3,7},{12,8},{8,12},{13,... | collective-permute-start | bytes 491528 | tf_op jit(solution)/shard_map/ppermute | solution.py:30
  64.6 6.2 %copy-start.15 = (f32[8,128]{1,0:T(8,128)S(1)}, f32[8,128]{1,0:T(8,128)}, u32[]{:S(2)}) copy-start(f32[8,128]{1,0:T(8,128)} %get-tuple-element.7) | copy-start | bytes 12292
  64.7 6.2 %copy-start.16 = (f32[5]{0:T(128)S(1)}, f32[5]{0:T(128)}, u32[]{:S(2)}) copy-start(f32[5]{0:T(128)} %param.31) | copy-start | bytes 64
  64.7 5.4 %collective-permute-start.9 = (f32[64,640]{1,0:T(8,128)S(1)}, f32[64,640]{1,0:T(8,128)S(1)}, u32[]{:S(2)}, u32[]{:S(2)}) collective-permute-start(f32[64,640]{1,0:T(8,128)S(1)} %get-tuple-element.32), channel_id=1, source_target_pairs={{4,0},{0,4},{5,1},{1,5},{6,2},{2,6},{7,3},{3,7},{12,8},{8,12},{13,... | collective-permute-start | bytes 491528 | tf_op jit(solution)/shard_map/ppermute | solution.py:30
  70.8 1.7 %collective-permute-start.10 = (f32[16,640]{1,0:T(8,128)S(1)}, f32[16,640]{1,0:T(8,128)S(1)}, u32[]{:S(2)}, u32[]{:S(2)}) collective-permute-start(f32[16,640]{1,0:T(8,128)S(1)} %get-tuple-element.44), channel_id=1, source_target_pairs={{8,0},{16,8},{24,16},{0,24},{9,1},{17,9},{25,17},{1,25},{10,2},{18... | collective-permute-start | bytes 122888 | tf_op jit(solution)/shard_map/ppermute | solution.py:30
  71.6 3.4 %collective-permute-start.11 = (f32[16,640]{1,0:T(8,128)S(1)}, f32[16,640]{1,0:T(8,128)S(1)}, u32[]{:S(2)}, u32[]{:S(2)}) collective-permute-start(f32[16,640]{1,0:T(8,128)S(1)} %get-tuple-element.43), channel_id=1, source_target_pairs={{24,0},{0,8},{8,16},{16,24},{25,1},{1,9},{9,17},{17,25},{26,2},{2,... | collective-permute-start | bytes 122888 | tf_op jit(solution)/shard_map/ppermute | solution.py:30

commit v14 on v10

--- a/solution.py
+++ b/solution.py
@@ -311,18 +311,14 @@
         ).astype(jnp.bfloat16)
 
     def spread_cols(onehot, values):
-        high = values.astype(jnp.bfloat16)
-        low = (values - high.astype(jnp.float32)).astype(jnp.bfloat16)
         return jnp.einsum(
-            "wn,nr->wr", high, onehot, preferred_element_type=jnp.float32
-        ) + jnp.einsum("wn,nr->wr", low, onehot, preferred_element_type=jnp.float32)
+            "wn,nr->wr", values.astype(jnp.bfloat16), onehot, preferred_element_type=jnp.float32
+        )
 
     def spread(onehot, values):
-        high = values.astype(jnp.bfloat16)
-        low = (values - high.astype(jnp.float32)).astype(jnp.bfloat16)
         return jnp.einsum(
-            "nr,nw->rw", onehot, high, preferred_element_type=jnp.float32
-        ) + jnp.einsum("nr,nw->rw", onehot, low, preferred_element_type=jnp.float32)
+            "nr,nw->rw", onehot, values.astype(jnp.bfloat16), preferred_element_type=jnp.float32
+        )
 
     proj_c = project(latent, species, centre_proj, centre_table)
     proj_n = project(latent, species, neigh_proj, neigh_table)

time: 72.3 us -> 68.6 us (0.949)
  matrix products: 17.1 us -> 12.2 us
  other arithmetic: 3.43 us -> 5.4 us
  waiting for transfers between devices: 14.1 us -> 13.3 us
    dot_general x14 -> x7, matrix products: 8.03 us -> 3.15 us  [the longest x6 2.06 us: spread(): jnp.einsum('nr,nw->rw', onehot, values.astype(jnp.bfloat16), preferred_el...]
    another operation x0 -> x1, other arithmetic: none -> 1.75 us
    ppermute x12, waiting for transfers between devices: 14.1 us -> 13.3 us  [passed_along(): return lax.ppermute(block, axis, route)]
    unnamed x40 -> x38, local copies, waits for them, and re-layouts: 3.55 us -> 3.54 us
where the time goes in v14:
time: 68.6 us; the launch traced here: 68.1 us
  starting transfers between devices  15.7 us (23%)
  waiting for transfers between devices  13.3 us (19%)
  matrix products  12.2 us (18%)
  local copies, waits for them, and re-layouts  10.1 us (15%)
  Pallas kernels  9.67 us (14%)
  other arithmetic  5.4 us (8%)
  between operations  1.77 us (3%)
    ppermute x12, starting transfers between devices, passed_along(): return lax.ppermute(block, axis, route)  15.7 us
    ppermute x12, waiting for transfers between devices, passed_along(): return lax.ppermute(block, axis, route)  13.3 us
    pallas_call x1, Pallas kernels, pair_terms(): pl.pallas_call(_pair_kernel, out_shape=(jax.ShapeDtypeStruct((width, pair...  9.67 us
    unnamed x38, local copies, waits for them, and re-layouts  3.54 us
    dot_general x2, matrix products, project(): jnp.dot(rows, weight, preferred_element_type=jnp.float32)  2.44 us
    dot_general x3, matrix products, lookup(): return jnp.dot(onehot, table, precision=lax.Precision.HIGHEST)  2.23 us
    dot_general x6, matrix products, spread(): jnp.einsum('nr,nw->rw', onehot, values.astype(jnp.bfloat16), preferred_el...  2.06 us
    another operation x1, other arithmetic  1.75 us
  transfers between devices with their start and end apart: 12, of which 9 were waited for; matrix products, arithmetic and copies ran while one was open for 14% of the time, Pallas kernels for 0%

profile of v14, /device:TPU:0, one launch (start us, length us, event | category | flops | bytes accessed | tf_op | source)
XLA Modules:
  0.0 68.1 jit_solution(13712769074321914275)
XLA Ops:
  1.7 0.8 %slice_bitcast_fusion = (s32[16]{0:T(128)S(1)}, s32[16]{0:T(128)S(1)}, s32[16]{0:T(128)S(1)}, s32[16]{0:T(128)S(1)}) fusion(s32[1,192]{1,0:T(1,128)} %param.19), kind=kLoop, calls=%fused_computation.185 | loop fusion | bytes 512 | tf_op jit(solution)/shard_map/eq | solution.py:343
  2.5 1.0 %fusion.30 = f32[128,512]{1,0:T(8,128)S(1)} fusion(f32[5,512]{1,0:T(8,128)} %param.25, s32[128]{0:T(128)} %param.18), kind=kOutput, calls=%fused_computation.51 | convolution fusion | flops 3932800 | bytes 272896 | tf_op jit(solution)/shard_map/dot_general | solution.py:306
  3.5 1.4 %fusion.11 = bf16[128,512]{1,0:T(8,128)(2,1)S(1)} fusion(f32[128,512]{1,0:T(8,128)S(1)} %fusion.30, bf16[128,512]{1,0:T(8,128)(2,1)} %param.16, bf16[512,512]{1,0:T(8,128)(2,1)} %param.23), kind=kOutput, calls=%fused_computation.16 | convolution fusion | flops 67239936 | bytes 1048576 | tf_op jit(solution)/shard_map/dot_general | solution.py:310
  5.8 1.9 %collective-permute-start.1 = (bf16[16,640]{1,0:T(8,128)(2,1)S(1)}, bf16[16,640]{1,0:T(8,128)(2,1)S(1)}, u32[]{:S(2)}, u32[]{:S(2)}) collective-permute-start(bf16[16,640]{1,0:T(8,128)(2,1)S(1)} %convolution_convert_fusion.4), channel_id=1, source_target_pairs={{8,0},{16,8},{24,16},{0,24},{9,1},{17,9},{25,17},{1,25},{10,2},{18... | collective-permute-start | bytes 61448 | tf_op jit(solution)/shard_map/ppermute | solution.py:30
  9.8 1.0 %fusion.13.centre_ref = f32[512,128]{1,0:T(8,128)} fusion(f32[512,128]{1,0:T(8,128)S(1)} %convolution_bitcast_fusion, bf16[512,512]{1,0:T(8,128)(2,1)S(1)} %copy-done, bf16[128,512]{1,0:T(8,128)(2,1)S(1)} %copy-done.5), kind=kOutput, calls=%fused_computation.18 | convolution fusion | flops 67305472 | bytes 1179648 | tf_op jit(solution)/shard_map/dot_general | solution.py:310
  11.8 1.0 %copy.56 = bf16[512,512]{0,1:T(8,128)(2,1)} copy(bf16[512,512]{1,0:T(8,128)(2,1)S(1)} %copy-done.1) | data formatting | bytes 1048576 | tf_op args[12]
  12.8 0.9 %copy.55 = bf16[512,384]{0,1:T(8,128)(2,1)} copy(bf16[512,384]{1,0:T(8,128)(2,1)S(1)} %copy-done.3) | data formatting | bytes 786432 | tf_op args[11]
  13.8 0.8 %copy.57 = bf16[192,512]{0,1:T(8,128)(2,1)} copy(bf16[192,512]{1,0:T(8,128)(2,1)S(1)} %copy-done.4) | data formatting | bytes 393216 | tf_op args[13]
  15.0 2.4 %collective-permute-start.2 = (bf16[64,640]{1,0:T(8,128)(2,1)S(1)}, bf16[64,640]{1,0:T(8,128)(2,1)S(1)}, u32[]{:S(2)}, u32[]{:S(2)}) collective-permute-start(bf16[64,640]{1,0:T(8,128)(2,1)S(1)} %convolution_convert_fusion.1), channel_id=1, source_target_pairs={{4,0},{0,4},{5,1},{1,5},{6,2},{2,6},{7,3},{3,7},{12,8},{8,12},{13,... | collective-permute-start | bytes 245768 | tf_op jit(solution)/shard_map/ppermute | solution.py:30
  17.7 2.6 %collective-permute-done.2 = bf16[64,640]{1,0:T(8,128)(2,1)S(1)} collective-permute-done((bf16[64,640]{1,0:T(8,128)(2,1)S(1)}, bf16[64,640]{1,0:T(8,128)(2,1)S(1)}, u32[]{:S(2)}, u32[]{:S(2)}) %collective-permute-start.2) | collective-permute-done | bytes 81952 | tf_op jit(solution)/shard_map/ppermute | solution.py:30
  20.3 1.8 %collective-permute-done.3 = bf16[64,640]{1,0:T(8,128)(2,1)S(1)} collective-permute-done((bf16[64,640]{1,0:T(8,128)(2,1)S(1)}, bf16[64,640]{1,0:T(8,128)(2,1)S(1)}, u32[]{:S(2)}, u32[]{:S(2)}) %collective-permute-start.3) | collective-permute-done | bytes 81952 | tf_op jit(solution)/shard_map/ppermute | solution.py:30
  22.3 1.6 %collective-permute-start.4 = (bf16[16,640]{1,0:T(8,128)(2,1)S(1)}, bf16[16,640]{1,0:T(8,128)(2,1)S(1)}, u32[]{:S(2)}, u32[]{:S(2)}) collective-permute-start(bf16[16,640]{1,0:T(8,128)(2,1)S(1)} %convolution_convert_fusion.3), channel_id=1, source_target_pairs={{3,0},{0,1},{1,2},{2,3},{7,4},{4,5},{5,6},{6,7},{11,8},{8,9},{9,10... | collective-permute-start | bytes 61448 | tf_op jit(solution)/shard_map/ppermute | solution.py:30
  24.2 2.3 %collective-permute-start.5 = (bf16[16,640]{1,0:T(8,128)(2,1)S(1)}, bf16[16,640]{1,0:T(8,128)(2,1)S(1)}, u32[]{:S(2)}, u32[]{:S(2)}) collective-permute-start(bf16[16,640]{1,0:T(8,128)(2,1)S(1)} %convolution_convert_fusion.2), channel_id=1, source_target_pairs={{1,0},{2,1},{3,2},{0,3},{5,4},{6,5},{7,6},{4,7},{9,8},{10,9},{11,1... | collective-permute-start | bytes 61448 | tf_op jit(solution)/shard_map/ppermute | solution.py:30
  26.5 1.5 %collective-permute-done.4 = bf16[16,640]{1,0:T(8,128)(2,1)S(1)} collective-permute-done((bf16[16,640]{1,0:T(8,128)(2,1)S(1)}, bf16[16,640]{1,0:T(8,128)(2,1)S(1)}, u32[]{:S(2)}, u32[]{:S(2)}) %collective-permute-start.4) | collective-permute-done | bytes 20512 | tf_op jit(solution)/shard_map/ppermute | solution.py:30
  28.2 1.0 %fusion.1 = f32[640,1024]{1,0:T(8,128)S(1)} fusion(bf16[320,640]{1,0:T(8,128)(2,1)S(1)} %constant_dynamic-update-slice_fusion.3, s32[1024]{0:T(1024)S(1)} %bitcast.159), kind=kOutput, calls=%fused_computation.3 | convolution fusion | flops 419758080 | bytes 3035136 | tf_op jit(solution)/shard_map/tw,pt->wp/dot_general | solution.py:358
  29.3 1.2 %slice.197.rows_ref = bf16[512,1024]{1,0:T(8,128)(2,1)} slice(f32[640,1024]{1,0:T(8,128)S(1)} %fusion.1), slice={[0:512], [0:1024]} | slice | bytes 2097152 | tf_op jit(solution)/shard_map/slice | solution.py:359
  30.9 0.9 %concatenate.62.geo_ref = f32[128,1024]{1,0:T(8,128)} pad(f32[18,1024]{1,0:T(8,128)S(1)} %concatenate.61, f32[]{:T(128)} %constant.28.clone.1), padding=0_110x0_0 | pad | bytes 598020 | tf_op jit(solution)/shard_map/jvp()/concatenate | solution.py:80
  31.7 1.6 %broadcast_in_dim.99.energy_w_ref = f32[512,1024]{1,0:T(8,128)} broadcast(f32[512]{0:T(512)S(1)} %copy-done.11), dimensions={0} | broadcast | bytes 2099200 | tf_op jit(solution)/shard_map/broadcast_in_dim | solution.py:264
  33.3 9.7 %shard_map.175 = (f32[512,1024]{1,0:T(8,128)}, f32[512,128]{1,0:T(8,128)}, f32[128,1024]{1,0:T(8,128)}, f32[8,128]{1,0:T(8,128)}) custom-call(bf16[512,1024]{1,0:T(8,128)(2,1)} %slice.197.rows_ref, f32[512,128]{1,0:T(8,128)} %fusion.13.centre_ref, f32[128,1024]{1,0:T(8,128)} %concatenate.62.geo_ref, bf16[512,128]{1,0:T(8,128)(2,1)} %copy.58.basis_t_ref, ...), custom_call_target="tpu_custom_call" | custom-call | flops 1610612736 | bytes 8388608 | tf_op jit(solution)/shard_map/pallas_call | solution.py:226
  43.0 1.3 %slice_multiply_fusion.4 = (f32[1,1024]{1,0:T(1,128)S(1)}, f32[1,1024]{1,0:T(1,128)S(1)}, f32[1,1024]{1,0:T(1,128)S(1)}, f32[1,1024]{1,0:T(1,128)S(1)}, f32[1,10...) fusion(f32[128,1024]{1,0:T(8,128)} %get-tuple-element.9), kind=kLoop, calls=%fused_computation.149 | loop fusion | flops 5120 | bytes 73728 | tf_op jit(solution)/shard_map/transpose(jvp())/mul | solution.py:70
  44.2 1.0 %fusion.33 = (f32[1024]{0:T(1024)S(1)}, f32[1024]{0:T(1024)S(1)}) fusion(f32[128,1024]{1,0:T(8,128)} %get-tuple-element.9, f32[1024]{0:T(1024)S(1)} %get-tuple-element.67, f32[8]{0:T(128)S(1)} %convert_multiply_fusion, f32[1024]{0:T(1024)S(1)} %get-tuple-element.66), kind=kLoop, calls=%fused_computation.57 | loop fusion | flops 55296 | bytes 49184 | tf_op jit(solution)/shard_map/transpose(jvp())/reduce_sum | solution.py:58
  45.2 1.8 %convert.21 = bf16[512,1024]{1,0:T(8,128)(2,1)S(1)} convert(f32[512,1024]{1,0:T(8,128)} %get-tuple-element.8) | non-fusion elementwise | flops 524288 | bytes 3145728 | tf_op jit(solution)/shard_map/convert
  47.2 1.1 %fusion.7 = f32[320,640]{1,0:T(8,128)S(1)} fusion(bf16[3,1024]{1,0:T(4,128)(2,1)S(1)} %bitcast.180, bf16[512,1024]{1,0:T(8,128)(2,1)S(1)} %convert.21, f32[128,3]{1,0:T(8,128)S(1)} %bitcast.157, s32[1024]{0:T(1024)S(1)} %bitcast.160, bf16[640]{0:T(1024)(128)(2,1)S(1)} %pad.21.clone), kind=kOutput, calls=%fused_computation.9 | convolution fusion | flops 424222720 | bytes 1880832 | tf_op jit(solution)/shard_map/wn,nr->wr/dot_general | solution.py:314
  48.3 1.5 %collective-permute-start.7 = (bf16[16,640]{1,0:T(8,128)(2,1)S(1)}, bf16[16,640]{1,0:T(8,128)(2,1)S(1)}, u32[]{:S(2)}, u32[]{:S(2)}) collective-permute-start(bf16[16,640]{1,0:T(8,128)(2,1)S(1)} %get-tuple-element.31), channel_id=1, source_target_pairs={{3,0},{0,1},{1,2},{2,3},{7,4},{4,5},{5,6},{6,7},{11,8},{8,9},{9,10... | collective-permute-start | bytes 61448 | tf_op jit(solution)/shard_map/ppermute | solution.py:30
  49.8 2.7 %collective-permute-start.6 = (bf16[16,640]{1,0:T(8,128)(2,1)S(1)}, bf16[16,640]{1,0:T(8,128)(2,1)S(1)}, u32[]{:S(2)}, u32[]{:S(2)}) collective-permute-start(bf16[16,640]{1,0:T(8,128)(2,1)S(1)} %get-tuple-element.30), channel_id=1, source_target_pairs={{1,0},{2,1},{3,2},{0,3},{5,4},{6,5},{7,6},{4,7},{9,8},{10,9},{11,1... | collective-permute-start | bytes 61448 | tf_op jit(solution)/shard_map/ppermute | solution.py:30
  52.5 1.5 %collective-permute-done.7 = bf16[16,640]{1,0:T(8,128)(2,1)S(1)} collective-permute-done((bf16[16,640]{1,0:T(8,128)(2,1)S(1)}, bf16[16,640]{1,0:T(8,128)(2,1)S(1)}, u32[]{:S(2)}, u32[]{:S(2)}) %collective-permute-start.7) | collective-permute-done | bytes 20512 | tf_op jit(solution)/shard_map/ppermute | solution.py:30
  54.8 1.3 %collective-permute-start.8 = (bf16[64,640]{1,0:T(8,128)(2,1)S(1)}, bf16[64,640]{1,0:T(8,128)(2,1)S(1)}, u32[]{:S(2)}, u32[]{:S(2)}) collective-permute-start(bf16[64,640]{1,0:T(8,128)(2,1)S(1)} %get-tuple-element.33), channel_id=1, source_target_pairs={{4,0},{0,4},{5,1},{1,5},{6,2},{2,6},{7,3},{3,7},{12,8},{8,12},{13,... | collective-permute-start | bytes 245768 | tf_op jit(solution)/shard_map/ppermute | solution.py:30
  56.8 0.9 %collective-permute-start.9 = (bf16[64,640]{1,0:T(8,128)(2,1)S(1)}, bf16[64,640]{1,0:T(8,128)(2,1)S(1)}, u32[]{:S(2)}, u32[]{:S(2)}) collective-permute-start(bf16[64,640]{1,0:T(8,128)(2,1)S(1)} %get-tuple-element.32), channel_id=1, source_target_pairs={{4,0},{0,4},{5,1},{1,5},{6,2},{2,6},{7,3},{3,7},{12,8},{8,12},{13,... | collective-permute-start | bytes 245768 | tf_op jit(solution)/shard_map/ppermute | solution.py:30
  57.7 1.6 %collective-permute-done.8 = bf16[64,640]{1,0:T(8,128)(2,1)S(1)} collective-permute-done((bf16[64,640]{1,0:T(8,128)(2,1)S(1)}, bf16[64,640]{1,0:T(8,128)(2,1)S(1)}, u32[]{:S(2)}, u32[]{:S(2)}) %collective-permute-start.8) | collective-permute-done | bytes 81952 | tf_op jit(solution)/shard_map/ppermute | solution.py:30
  59.7 1.7 %collective-permute-done.9 = bf16[64,640]{1,0:T(8,128)(2,1)S(1)} collective-permute-done((bf16[64,640]{1,0:T(8,128)(2,1)S(1)}, bf16[64,640]{1,0:T(8,128)(2,1)S(1)}, u32[]{:S(2)}, u32[]{:S(2)}) %collective-permute-start.9) | collective-permute-done | bytes 81952 | tf_op jit(solution)/shard_map/ppermute | solution.py:30
  63.6 2.2 %collective-permute-done.11 = bf16[16,640]{1,0:T(8,128)(2,1)S(1)} collective-permute-done((bf16[16,640]{1,0:T(8,128)(2,1)S(1)}, bf16[16,640]{1,0:T(8,128)(2,1)S(1)}, u32[]{:S(2)}, u32[]{:S(2)}) %collective-permute-start.11) | collective-permute-done | bytes 20512 | tf_op jit(solution)/shard_map/ppermute | solution.py:30
  66.1 1.4 %convolution_add_fusion.1 = f32[128,512]{1,0:T(8,128)} fusion(f32[128,512]{1,0:T(8,128)S(1)} %fusion.105, bf16[512,512]{1,0:T(8,128)(2,1)S(1)} %copy-done.2, f32[128,640]{1,0:T(8,128)S(1)} %fusion.21), kind=kOutput, calls=%fused_computation.12 | convolution fusion | flops 402718720 | bytes 1310720 | tf_op jit(solution)/shard_map/dot_general | solution.py:406
  (104 shorter events, 11.1 us)
Async XLA Ops:
  0.6 9.2 %copy-start = (bf16[512,512]{1,0:T(8,128)(2,1)S(1)}, bf16[512,512]{1,0:T(8,128)(2,1)}, u32[]{:S(2)}) copy-start(bf16[512,512]{1,0:T(8,128)(2,1)} %param.22) | copy-start | bytes 1572868
  0.6 7.2 %copy-start.8 = (s32[1,192]{1,0:T(1,128)S(1)}, s32[1,192]{1,0:T(1,128)}, u32[]{:S(2)}) copy-start(s32[1,192]{1,0:T(1,128)} %param.19) | copy-start | bytes 2308
  0.7 8.7 %copy-start.12 = (s32[128]{0:T(128)S(1)}, s32[128]{0:T(128)}, u32[]{:S(2)}) copy-start(s32[128]{0:T(128)} %param.18) | copy-start | bytes 1540
  0.7 9.2 %copy-start.5 = (bf16[128,512]{1,0:T(8,128)(2,1)S(1)}, bf16[128,512]{1,0:T(8,128)(2,1)}, u32[]{:S(2)}) copy-start(bf16[128,512]{1,0:T(8,128)(2,1)} %param.16) | copy-start | bytes 393220
  0.7 8.0 %copy-start.9 = (bf16[8,512]{1,0:T(8,128)(2,1)S(1)}, bf16[8,512]{1,0:T(8,128)(2,1)}, u32[]{:S(2)}) copy-start(bf16[8,512]{1,0:T(8,128)(2,1)} %param.26) | copy-start | bytes 24580
  0.7 8.7 %copy-start.7 = (f32[5,512]{1,0:T(8,128)S(1)}, f32[5,512]{1,0:T(8,128)}, u32[]{:S(2)}) copy-start(f32[5,512]{1,0:T(8,128)} %param.24) | copy-start | bytes 30724
  3.5 7.4 %copy-start.10 = (s32[1024]{0:T(1024)S(1)}, s32[1024]{0:T(1024)}, u32[]{:S(2)}) copy-start(s32[1024]{0:T(1024)} %param.20) | copy-start | bytes 12292
  3.5 8.3 %copy-start.1 = (bf16[512,512]{1,0:T(8,128)(2,1)S(1)}, bf16[512,512]{1,0:T(8,128)(2,1)}, u32[]{:S(2)}) copy-start(bf16[512,512]{1,0:T(8,128)(2,1)} %update_ref.1) | copy-start | bytes 1572868
  5.1 7.7 %copy-start.3 = (bf16[512,384]{1,0:T(8,128)(2,1)S(1)}, bf16[512,384]{1,0:T(8,128)(2,1)}, u32[]{:S(2)}) copy-start(bf16[512,384]{1,0:T(8,128)(2,1)} %split_ref.1) | copy-start | bytes 1179652
  5.1 9.5 %collective-permute-start = (bf16[16,640]{1,0:T(8,128)(2,1)S(1)}, bf16[16,640]{1,0:T(8,128)(2,1)S(1)}, u32[]{:S(2)}, u32[]{:S(2)}) collective-permute-start(bf16[16,640]{1,0:T(8,128)(2,1)S(1)} %convolution_convert_fusion.5), channel_id=1, source_target_pairs={{24,0},{0,8},{8,16},{16,24},{25,1},{1,9},{9,17},{17,25},{26,2},{2,... | collective-permute-start | bytes 61448 | tf_op jit(solution)/shard_map/ppermute | solution.py:30
  5.8 8.9 %collective-permute-start.1 = (bf16[16,640]{1,0:T(8,128)(2,1)S(1)}, bf16[16,640]{1,0:T(8,128)(2,1)S(1)}, u32[]{:S(2)}, u32[]{:S(2)}) collective-permute-start(bf16[16,640]{1,0:T(8,128)(2,1)S(1)} %convolution_convert_fusion.4), channel_id=1, source_target_pairs={{8,0},{16,8},{24,16},{0,24},{9,1},{17,9},{25,17},{1,25},{10,2},{18... | collective-permute-start | bytes 61448 | tf_op jit(solution)/shard_map/ppermute | solution.py:30
  7.9 5.9 %copy-start.4 = (bf16[192,512]{1,0:T(8,128)(2,1)S(1)}, bf16[192,512]{1,0:T(8,128)(2,1)}, u32[]{:S(2)}) copy-start(bf16[192,512]{1,0:T(8,128)(2,1)} %tensor_ref.1) | copy-start | bytes 589828
  15.0 5.3 %collective-permute-start.2 = (bf16[64,640]{1,0:T(8,128)(2,1)S(1)}, bf16[64,640]{1,0:T(8,128)(2,1)S(1)}, u32[]{:S(2)}, u32[]{:S(2)}) collective-permute-start(bf16[64,640]{1,0:T(8,128)(2,1)S(1)} %convolution_convert_fusion.1), channel_id=1, source_target_pairs={{4,0},{0,4},{5,1},{1,5},{6,2},{2,6},{7,3},{3,7},{12,8},{8,12},{13,... | collective-permute-start | bytes 245768 | tf_op jit(solution)/shard_map/ppermute | solution.py:30
  17.6 4.5 %collective-permute-start.3 = (bf16[64,640]{1,0:T(8,128)(2,1)S(1)}, bf16[64,640]{1,0:T(8,128)(2,1)S(1)}, u32[]{:S(2)}, u32[]{:S(2)}) collective-permute-start(bf16[64,640]{1,0:T(8,128)(2,1)S(1)} %convolution_convert_fusion), channel_id=1, source_target_pairs={{4,0},{0,4},{5,1},{1,5},{6,2},{2,6},{7,3},{3,7},{12,8},{8,12},{13,... | collective-permute-start | bytes 245768 | tf_op jit(solution)/shard_map/ppermute | solution.py:30
  22.3 5.6 %collective-permute-start.4 = (bf16[16,640]{1,0:T(8,128)(2,1)S(1)}, bf16[16,640]{1,0:T(8,128)(2,1)S(1)}, u32[]{:S(2)}, u32[]{:S(2)}) collective-permute-start(bf16[16,640]{1,0:T(8,128)(2,1)S(1)} %convolution_convert_fusion.3), channel_id=1, source_target_pairs={{3,0},{0,1},{1,2},{2,3},{7,4},{4,5},{5,6},{6,7},{11,8},{8,9},{9,10... | collective-permute-start | bytes 61448 | tf_op jit(solution)/shard_map/ppermute | solution.py:30
  24.2 4.0 %collective-permute-start.5 = (bf16[16,640]{1,0:T(8,128)(2,1)S(1)}, bf16[16,640]{1,0:T(8,128)(2,1)S(1)}, u32[]{:S(2)}, u32[]{:S(2)}) collective-permute-start(bf16[16,640]{1,0:T(8,128)(2,1)S(1)} %convolution_convert_fusion.2), channel_id=1, source_target_pairs={{1,0},{2,1},{3,2},{0,3},{5,4},{6,5},{7,6},{4,7},{9,8},{10,9},{11,1... | collective-permute-start | bytes 61448 | tf_op jit(solution)/shard_map/ppermute | solution.py:30
  29.3 2.5 %copy-start.11 = (f32[512]{0:T(512)S(1)}, f32[512]{0:T(512)}, u32[]{:S(2)}) copy-start(f32[512]{0:T(512)} %param.30) | copy-start | bytes 6148
  48.3 7.8 %copy-start.6 = (f32[512,128]{1,0:T(8,128)S(1)}, f32[512,128]{1,0:T(8,128)}, u32[]{:S(2)}) copy-start(f32[512,128]{1,0:T(8,128)} %get-tuple-element.10) | copy-start | bytes 786436
  48.3 5.7 %collective-permute-start.7 = (bf16[16,640]{1,0:T(8,128)(2,1)S(1)}, bf16[16,640]{1,0:T(8,128)(2,1)S(1)}, u32[]{:S(2)}, u32[]{:S(2)}) collective-permute-start(bf16[16,640]{1,0:T(8,128)(2,1)S(1)} %get-tuple-element.31), channel_id=1, source_target_pairs={{3,0},{0,1},{1,2},{2,3},{7,4},{4,5},{5,6},{6,7},{11,8},{8,9},{9,10... | collective-permute-start | bytes 61448 | tf_op jit(solution)/shard_map/ppermute | solution.py:30
  49.8 4.6 %collective-permute-start.6 = (bf16[16,640]{1,0:T(8,128)(2,1)S(1)}, bf16[16,640]{1,0:T(8,128)(2,1)S(1)}, u32[]{:S(2)}, u32[]{:S(2)}) collective-permute-start(bf16[16,640]{1,0:T(8,128)(2,1)S(1)} %get-tuple-element.30), channel_id=1, source_target_pairs={{1,0},{2,1},{3,2},{0,3},{5,4},{6,5},{7,6},{4,7},{9,8},{10,9},{11,1... | collective-permute-start | bytes 61448 | tf_op jit(solution)/shard_map/ppermute | solution.py:30
  54.8 7.0 %copy-start.13 = (f32[8,128]{1,0:T(8,128)S(1)}, f32[8,128]{1,0:T(8,128)}, u32[]{:S(2)}) copy-start(f32[8,128]{1,0:T(8,128)} %get-tuple-element.7) | copy-start | bytes 12292
  54.8 7.0 %copy-start.14 = (f32[5]{0:T(128)S(1)}, f32[5]{0:T(128)}, u32[]{:S(2)}) copy-start(f32[5]{0:T(128)} %param.31) | copy-start | bytes 64
  54.8 4.5 %collective-permute-start.8 = (bf16[64,640]{1,0:T(8,128)(2,1)S(1)}, bf16[64,640]{1,0:T(8,128)(2,1)S(1)}, u32[]{:S(2)}, u32[]{:S(2)}) collective-permute-start(bf16[64,640]{1,0:T(8,128)(2,1)S(1)} %get-tuple-element.33), channel_id=1, source_target_pairs={{4,0},{0,4},{5,1},{1,5},{6,2},{2,6},{7,3},{3,7},{12,8},{8,12},{13,... | collective-permute-start | bytes 245768 | tf_op jit(solution)/shard_map/ppermute | solution.py:30
  56.1 10.0 %copy-start.2 = (bf16[512,512]{1,0:T(8,128)(2,1)S(1)}, bf16[512,512]{1,0:T(8,128)(2,1)}, u32[]{:S(2)}) copy-start(bf16[512,512]{1,0:T(8,128)(2,1)} %param.23) | copy-start | bytes 1572868
  56.8 4.5 %collective-permute-start.9 = (bf16[64,640]{1,0:T(8,128)(2,1)S(1)}, bf16[64,640]{1,0:T(8,128)(2,1)S(1)}, u32[]{:S(2)}, u32[]{:S(2)}) collective-permute-start(bf16[64,640]{1,0:T(8,128)(2,1)S(1)} %get-tuple-element.32), channel_id=1, source_target_pairs={{4,0},{0,4},{5,1},{1,5},{6,2},{2,6},{7,3},{3,7},{12,8},{8,12},{13,... | collective-permute-start | bytes 245768 | tf_op jit(solution)/shard_map/ppermute | solution.py:30
  61.7 1.5 %collective-permute-start.10 = (bf16[16,640]{1,0:T(8,128)(2,1)S(1)}, bf16[16,640]{1,0:T(8,128)(2,1)S(1)}, u32[]{:S(2)}, u32[]{:S(2)}) collective-permute-start(bf16[16,640]{1,0:T(8,128)(2,1)S(1)} %get-tuple-element.44), channel_id=1, source_target_pairs={{8,0},{16,8},{24,16},{0,24},{9,1},{17,9},{25,17},{1,25},{10,2},{18... | collective-permute-start | bytes 61448 | tf_op jit(solution)/shard_map/ppermute | solution.py:30
  62.6 3.2 %collective-permute-start.11 = (bf16[16,640]{1,0:T(8,128)(2,1)S(1)}, bf16[16,640]{1,0:T(8,128)(2,1)S(1)}, u32[]{:S(2)}, u32[]{:S(2)}) collective-permute-start(bf16[16,640]{1,0:T(8,128)(2,1)S(1)} %get-tuple-element.43), channel_id=1, source_target_pairs={{24,0},{0,8},{8,16},{16,24},{25,1},{1,9},{9,17},{17,25},{26,2},{2,... | collective-permute-start | bytes 61448 | tf_op jit(solution)/shard_map/ppermute | solution.py:30

commit v15 on v14

--- a/solution.py
+++ b/solution.py
@@ -400,12 +400,15 @@
             + spread(pickers[segs[0]], back_first)
             + spread(pickers[segs[1]], back_second)
         )
-    back_neigh = neigh_proj.astype(jnp.float32).T
-    back_centre = centre_proj.astype(jnp.float32).T
-    latent_grad = jnp.dot(grad_centre.T, back_centre, precision=lax.Precision.HIGHEST)
-    latent_grad = latent_grad + jnp.dot(
-        sums[:, :width], back_neigh, precision=lax.Precision.HIGHEST
-    )
+    def times_transposed(values, weight):
+        high = values.astype(jnp.bfloat16)
+        low = (values - high.astype(jnp.float32)).astype(jnp.bfloat16)
+        return jnp.einsum(
+            "ah,ih->ai", high, weight, preferred_element_type=jnp.float32
+        ) + jnp.einsum("ah,ih->ai", low, weight, preferred_element_type=jnp.float32)
+
+    latent_grad = times_transposed(grad_centre.T, centre_proj)
+    latent_grad = latent_grad + times_transposed(sums[:, :width], neigh_proj)
     forces = -sums[:, width : width + 3].T
     energies = live * (lookup(species, species_shift[:, None])[:, 0] + atom_energy)
     return (energies, forces, latent_grad)

time: 68.6 us -> 69.5 us (1.013)
  matrix products: 12.2 us -> 13.1 us
    dot_general x6, matrix products: 1.27 us -> 2.5 us  [shards(): jnp.dot(onehot, table, preferred_element_type=jnp.float32)]
    dot_general x2 -> x4, matrix products: 2.07 us -> 1.93 us  [the longest x2 1.33 us: times_transposed(): jnp.einsum('ah,ih->ai', low, weight, preferred_element_type=jnp.float32)]
where the time goes in v15:
time: 69.5 us; the launch traced here: 69 us
  starting transfers between devices  15.5 us (22%)
  waiting for transfers between devices  13.5 us (19%)
  matrix products  13.1 us (19%)
  local copies, waits for them, and re-layouts  10.1 us (15%)
  Pallas kernels  9.68 us (14%)
  other arithmetic  5.39 us (8%)
  between operations  1.79 us (3%)
    ppermute x12, starting transfers between devices, passed_along(): return lax.ppermute(block, axis, route)  15.5 us
    ppermute x12, waiting for transfers between devices, passed_along(): return lax.ppermute(block, axis, route)  13.5 us
    pallas_call x1, Pallas kernels, pair_terms(): pl.pallas_call(_pair_kernel, out_shape=(jax.ShapeDtypeStruct((width, pair...  9.68 us
    unnamed x38, local copies, waits for them, and re-layouts  3.54 us
    dot_general x6, matrix products, shards(): jnp.dot(onehot, table, preferred_element_type=jnp.float32)  2.5 us
    dot_general x3, matrix products, lookup(): return jnp.dot(onehot, table, precision=lax.Precision.HIGHEST)  2.24 us
    dot_general x2, matrix products, project(): jnp.dot(rows, weight, preferred_element_type=jnp.float32)  2.24 us
    dot_general x6, matrix products, spread(): jnp.einsum('nr,nw->rw', onehot, values.astype(jnp.bfloat16), preferred_el...  2.06 us
  transfers between devices with their start and end apart: 12, of which 9 were waited for; matrix products, arithmetic and copies ran while one was open for 14% of the time, Pallas kernels for 0%

profile of v15, /device:TPU:0, one launch (start us, length us, event | category | flops | bytes accessed | tf_op | source)
XLA Modules:
  0.0 69.0 jit_solution(3188303554057793833)
XLA Ops:
  2.5 1.0 %fusion.33 = f32[128,512]{1,0:T(8,128)S(1)} fusion(f32[5,512]{1,0:T(8,128)} %param.25, s32[128]{0:T(128)} %param.18), kind=kOutput, calls=%fused_computation.58 | convolution fusion | flops 3932800 | bytes 272896 | tf_op jit(solution)/shard_map/dot_general | solution.py:306
  3.6 1.2 %fusion.12 = bf16[128,512]{1,0:T(8,128)(2,1)S(1)} fusion(f32[128,512]{1,0:T(8,128)S(1)} %fusion.33, bf16[128,512]{1,0:T(8,128)(2,1)} %param.16, bf16[512,512]{1,0:T(8,128)(2,1)S(1)} %copy-done), kind=kOutput, calls=%fused_computation.18 | convolution fusion | flops 67239936 | bytes 1048576 | tf_op jit(solution)/shard_map/dot_general | solution.py:310
  6.0 0.8 %convolution_convert_fusion.4 = bf16[16,640]{1,0:T(8,128)(2,1)} fusion(s32[16]{0:T(128)S(1)} %get-tuple-element.72, bf16[128,122]{1,0:T(8,128)(2,1)S(1)} %broadcast_in_dim.43, bf16[128,6]{1,0:T(8,128)(2,1)S(1)} %bitcast.173, bf16[128,512]{1,0:T(8,128)(2,1)S(1)} %fusion.12), kind=kOutput, calls=%fused_computation.25 | convolution fusion | flops 3125248 | bytes 184384 | tf_op jit(solution)/shard_map/dot_general | solution.py:346
  6.9 1.9 %collective-permute-start.1 = (bf16[16,640]{1,0:T(8,128)(2,1)}, bf16[16,640]{1,0:T(8,128)(2,1)S(1)}, u32[]{:S(2)}, u32[]{:S(2)}) collective-permute-start(bf16[16,640]{1,0:T(8,128)(2,1)} %convolution_convert_fusion.4), channel_id=1, source_target_pairs={{8,0},{16,8},{24,16},{0,24},{9,1},{17,9},{25,17},{1,25},{10,2},{18... | collective-permute-start | bytes 61448 | tf_op jit(solution)/shard_map/ppermute | solution.py:30
  10.9 1.0 %fusion.14.centre_ref = f32[512,128]{1,0:T(8,128)} fusion(f32[512,128]{1,0:T(8,128)S(1)} %convolution_bitcast_fusion, bf16[512,512]{1,0:T(8,128)(2,1)S(1)} %copy-done.1, bf16[128,512]{1,0:T(8,128)(2,1)S(1)} %copy-done.6), kind=kOutput, calls=%fused_computation.20 | convolution fusion | flops 67305472 | bytes 1179648 | tf_op jit(solution)/shard_map/dot_general | solution.py:310
  12.8 1.0 %copy.56 = bf16[512,512]{0,1:T(8,128)(2,1)} copy(bf16[512,512]{1,0:T(8,128)(2,1)S(1)} %copy-done.2) | data formatting | bytes 1048576 | tf_op args[12]
  13.9 0.9 %copy.55 = bf16[512,384]{0,1:T(8,128)(2,1)} copy(bf16[512,384]{1,0:T(8,128)(2,1)S(1)} %copy-done.3) | data formatting | bytes 786432 | tf_op args[11]
  14.8 0.8 %copy.57 = bf16[192,512]{0,1:T(8,128)(2,1)} copy(bf16[192,512]{1,0:T(8,128)(2,1)S(1)} %copy-done.5) | data formatting | bytes 393216 | tf_op args[13]
  16.0 2.4 %collective-permute-start.2 = (bf16[64,640]{1,0:T(8,128)(2,1)S(1)}, bf16[64,640]{1,0:T(8,128)(2,1)S(1)}, u32[]{:S(2)}, u32[]{:S(2)}) collective-permute-start(bf16[64,640]{1,0:T(8,128)(2,1)S(1)} %convolution_convert_fusion.1), channel_id=1, source_target_pairs={{4,0},{0,4},{5,1},{1,5},{6,2},{2,6},{7,3},{3,7},{12,8},{8,12},{13,... | collective-permute-start | bytes 245768 | tf_op jit(solution)/shard_map/ppermute | solution.py:30
  18.7 2.6 %collective-permute-done.2 = bf16[64,640]{1,0:T(8,128)(2,1)S(1)} collective-permute-done((bf16[64,640]{1,0:T(8,128)(2,1)S(1)}, bf16[64,640]{1,0:T(8,128)(2,1)S(1)}, u32[]{:S(2)}, u32[]{:S(2)}) %collective-permute-start.2) | collective-permute-done | bytes 81952 | tf_op jit(solution)/shard_map/ppermute | solution.py:30
  21.3 1.8 %collective-permute-done.3 = bf16[64,640]{1,0:T(8,128)(2,1)S(1)} collective-permute-done((bf16[64,640]{1,0:T(8,128)(2,1)S(1)}, bf16[64,640]{1,0:T(8,128)(2,1)S(1)}, u32[]{:S(2)}, u32[]{:S(2)}) %collective-permute-start.3) | collective-permute-done | bytes 81952 | tf_op jit(solution)/shard_map/ppermute | solution.py:30
  23.4 1.6 %collective-permute-start.4 = (bf16[16,640]{1,0:T(8,128)(2,1)S(1)}, bf16[16,640]{1,0:T(8,128)(2,1)S(1)}, u32[]{:S(2)}, u32[]{:S(2)}) collective-permute-start(bf16[16,640]{1,0:T(8,128)(2,1)S(1)} %convolution_convert_fusion.3), channel_id=1, source_target_pairs={{3,0},{0,1},{1,2},{2,3},{7,4},{4,5},{5,6},{6,7},{11,8},{8,9},{9,10... | collective-permute-start | bytes 61448 | tf_op jit(solution)/shard_map/ppermute | solution.py:30
  25.2 2.3 %collective-permute-start.5 = (bf16[16,640]{1,0:T(8,128)(2,1)S(1)}, bf16[16,640]{1,0:T(8,128)(2,1)S(1)}, u32[]{:S(2)}, u32[]{:S(2)}) collective-permute-start(bf16[16,640]{1,0:T(8,128)(2,1)S(1)} %convolution_convert_fusion.2), channel_id=1, source_target_pairs={{1,0},{2,1},{3,2},{0,3},{5,4},{6,5},{7,6},{4,7},{9,8},{10,9},{11,1... | collective-permute-start | bytes 61448 | tf_op jit(solution)/shard_map/ppermute | solution.py:30
  27.5 1.5 %collective-permute-done.4 = bf16[16,640]{1,0:T(8,128)(2,1)S(1)} collective-permute-done((bf16[16,640]{1,0:T(8,128)(2,1)S(1)}, bf16[16,640]{1,0:T(8,128)(2,1)S(1)}, u32[]{:S(2)}, u32[]{:S(2)}) %collective-permute-start.4) | collective-permute-done | bytes 20512 | tf_op jit(solution)/shard_map/ppermute | solution.py:30
  29.2 1.0 %fusion.1 = f32[640,1024]{1,0:T(8,128)S(1)} fusion(bf16[320,640]{1,0:T(8,128)(2,1)S(1)} %constant_dynamic-update-slice_fusion.3, s32[1024]{0:T(1024)S(1)} %bitcast.179), kind=kOutput, calls=%fused_computation.3 | convolution fusion | flops 419758080 | bytes 3035136 | tf_op jit(solution)/shard_map/tw,pt->wp/dot_general | solution.py:358
  30.3 1.2 %slice.202.rows_ref = bf16[512,1024]{1,0:T(8,128)(2,1)} slice(f32[640,1024]{1,0:T(8,128)S(1)} %fusion.1), slice={[0:512], [0:1024]} | slice | bytes 2097152 | tf_op jit(solution)/shard_map/slice | solution.py:359
  31.9 0.8 %concatenate.62.geo_ref = f32[128,1024]{1,0:T(8,128)} pad(f32[18,1024]{1,0:T(8,128)S(1)} %concatenate.61, f32[]{:T(128)} %constant.28.clone.1), padding=0_110x0_0 | pad | bytes 598020 | tf_op jit(solution)/shard_map/jvp()/concatenate | solution.py:80
  32.7 1.6 %broadcast_in_dim.99.energy_w_ref = f32[512,1024]{1,0:T(8,128)} broadcast(f32[512]{0:T(512)S(1)} %copy-done.11), dimensions={0} | broadcast | bytes 2099200 | tf_op jit(solution)/shard_map/broadcast_in_dim | solution.py:264
  34.3 9.7 %shard_map.175 = (f32[512,1024]{1,0:T(8,128)}, f32[512,128]{1,0:T(8,128)}, f32[128,1024]{1,0:T(8,128)}, f32[8,128]{1,0:T(8,128)}) custom-call(bf16[512,1024]{1,0:T(8,128)(2,1)} %slice.202.rows_ref, f32[512,128]{1,0:T(8,128)} %fusion.14.centre_ref, f32[128,1024]{1,0:T(8,128)} %concatenate.62.geo_ref, bf16[512,128]{1,0:T(8,128)(2,1)} %copy.58.basis_t_ref, ...), custom_call_target="tpu_custom_call" | custom-call | flops 1610612736 | bytes 8388608 | tf_op jit(solution)/shard_map/pallas_call | solution.py:226
  44.0 1.3 %slice_multiply_fusion.4 = (f32[1,1024]{1,0:T(1,128)S(1)}, f32[1,1024]{1,0:T(1,128)S(1)}, f32[1,1024]{1,0:T(1,128)S(1)}, f32[1,1024]{1,0:T(1,128)S(1)}, f32[1,10...) fusion(f32[128,1024]{1,0:T(8,128)} %get-tuple-element.9), kind=kLoop, calls=%fused_computation.157 | loop fusion | flops 5120 | bytes 73728 | tf_op jit(solution)/shard_map/transpose(jvp())/mul | solution.py:70
  45.3 1.0 %fusion.37 = (f32[1024]{0:T(1024)S(1)}, f32[1024]{0:T(1024)S(1)}) fusion(f32[128,1024]{1,0:T(8,128)} %get-tuple-element.9, f32[1024]{0:T(1024)S(1)} %get-tuple-element.67, f32[8]{0:T(128)S(1)} %convert_multiply_fusion, f32[1024]{0:T(1024)S(1)} %get-tuple-element.66), kind=kLoop, calls=%fused_computation.65 | loop fusion | flops 55296 | bytes 49184 | tf_op jit(solution)/shard_map/transpose(jvp())/reduce_sum | solution.py:58
  46.2 1.8 %convert.21 = bf16[512,1024]{1,0:T(8,128)(2,1)S(1)} convert(f32[512,1024]{1,0:T(8,128)} %get-tuple-element.8) | non-fusion elementwise | flops 524288 | bytes 3145728 | tf_op jit(solution)/shard_map/convert
  48.2 1.1 %fusion.7 = f32[320,640]{1,0:T(8,128)S(1)} fusion(bf16[3,1024]{1,0:T(4,128)(2,1)S(1)} %bitcast.200, bf16[512,1024]{1,0:T(8,128)(2,1)S(1)} %convert.21, f32[128,3]{1,0:T(8,128)S(1)} %bitcast.177, s32[1024]{0:T(1024)S(1)} %bitcast.180, bf16[640]{0:T(1024)(128)(2,1)S(1)} %pad.21.clone), kind=kOutput, calls=%fused_computation.9 | convolution fusion | flops 424222720 | bytes 1880832 | tf_op jit(solution)/shard_map/wn,nr->wr/dot_general | solution.py:314
  49.3 1.4 %collective-permute-start.7 = (bf16[16,640]{1,0:T(8,128)(2,1)S(1)}, bf16[16,640]{1,0:T(8,128)(2,1)S(1)}, u32[]{:S(2)}, u32[]{:S(2)}) collective-permute-start(bf16[16,640]{1,0:T(8,128)(2,1)S(1)} %get-tuple-element.31), channel_id=1, source_target_pairs={{3,0},{0,1},{1,2},{2,3},{7,4},{4,5},{5,6},{6,7},{11,8},{8,9},{9,10... | collective-permute-start | bytes 61448 | tf_op jit(solution)/shard_map/ppermute | solution.py:30
  50.8 2.5 %collective-permute-start.6 = (bf16[16,640]{1,0:T(8,128)(2,1)S(1)}, bf16[16,640]{1,0:T(8,128)(2,1)S(1)}, u32[]{:S(2)}, u32[]{:S(2)}) collective-permute-start(bf16[16,640]{1,0:T(8,128)(2,1)S(1)} %get-tuple-element.30), channel_id=1, source_target_pairs={{1,0},{2,1},{3,2},{0,3},{5,4},{6,5},{7,6},{4,7},{9,8},{10,9},{11,1... | collective-permute-start | bytes 61448 | tf_op jit(solution)/shard_map/ppermute | solution.py:30
  53.3 1.7 %collective-permute-done.7 = bf16[16,640]{1,0:T(8,128)(2,1)S(1)} collective-permute-done((bf16[16,640]{1,0:T(8,128)(2,1)S(1)}, bf16[16,640]{1,0:T(8,128)(2,1)S(1)}, u32[]{:S(2)}, u32[]{:S(2)}) %collective-permute-start.7) | collective-permute-done | bytes 20512 | tf_op jit(solution)/shard_map/ppermute | solution.py:30
  55.9 1.3 %collective-permute-start.8 = (bf16[64,640]{1,0:T(8,128)(2,1)S(1)}, bf16[64,640]{1,0:T(8,128)(2,1)S(1)}, u32[]{:S(2)}, u32[]{:S(2)}) collective-permute-start(bf16[64,640]{1,0:T(8,128)(2,1)S(1)} %get-tuple-element.33), channel_id=1, source_target_pairs={{4,0},{0,4},{5,1},{1,5},{6,2},{2,6},{7,3},{3,7},{12,8},{8,12},{13,... | collective-permute-start | bytes 245768 | tf_op jit(solution)/shard_map/ppermute | solution.py:30
  57.4 0.9 %collective-permute-start.9 = (bf16[64,640]{1,0:T(8,128)(2,1)S(1)}, bf16[64,640]{1,0:T(8,128)(2,1)S(1)}, u32[]{:S(2)}, u32[]{:S(2)}) collective-permute-start(bf16[64,640]{1,0:T(8,128)(2,1)S(1)} %get-tuple-element.32), channel_id=1, source_target_pairs={{4,0},{0,4},{5,1},{1,5},{6,2},{2,6},{7,3},{3,7},{12,8},{8,12},{13,... | collective-permute-start | bytes 245768 | tf_op jit(solution)/shard_map/ppermute | solution.py:30
  58.3 2.0 %collective-permute-done.8 = bf16[64,640]{1,0:T(8,128)(2,1)S(1)} collective-permute-done((bf16[64,640]{1,0:T(8,128)(2,1)S(1)}, bf16[64,640]{1,0:T(8,128)(2,1)S(1)}, u32[]{:S(2)}, u32[]{:S(2)}) %collective-permute-start.8) | collective-permute-done | bytes 81952 | tf_op jit(solution)/shard_map/ppermute | solution.py:30
  60.7 1.3 %collective-permute-done.9 = bf16[64,640]{1,0:T(8,128)(2,1)S(1)} collective-permute-done((bf16[64,640]{1,0:T(8,128)(2,1)S(1)}, bf16[64,640]{1,0:T(8,128)(2,1)S(1)}, u32[]{:S(2)}, u32[]{:S(2)}) %collective-permute-start.9) | collective-permute-done | bytes 81952 | tf_op jit(solution)/shard_map/ppermute | solution.py:30
  64.2 2.2 %collective-permute-done.11 = bf16[16,640]{1,0:T(8,128)(2,1)S(1)} collective-permute-done((bf16[16,640]{1,0:T(8,128)(2,1)S(1)}, bf16[16,640]{1,0:T(8,128)(2,1)S(1)}, u32[]{:S(2)}, u32[]{:S(2)}) %collective-permute-start.11) | collective-permute-done | bytes 20512 | tf_op jit(solution)/shard_map/ppermute | solution.py:30
  68.0 1.0 %fusion.11 = f32[128,512]{1,0:T(8,128)} fusion(f32[128,512]{1,0:T(8,128)S(1)} %convolution_add_fusion.1, f32[128,512]{1,0:T(8,128)S(1)} %fusion.110, bf16[512,512]{1,0:T(8,128)(2,1)S(1)} %copy-done.1, f32[512,128]{1,0:T(8,128)S(1)} %copy-done.4), kind=kOutput, calls=%fused_computation.16 | convolution fusion | flops 67502080 | bytes 1572864 | tf_op jit(solution)/shard_map/ah,ih->ai/dot_general | solution.py:408
  (106 shorter events, 12.5 us)
Async XLA Ops:
  0.6 2.9 %copy-start = (bf16[512,512]{1,0:T(8,128)(2,1)S(1)}, bf16[512,512]{1,0:T(8,128)(2,1)}, u32[]{:S(2)}) copy-start(bf16[512,512]{1,0:T(8,128)(2,1)} %param.23) | copy-start | bytes 1572868
  0.6 8.3 %copy-start.8 = (s32[1,192]{1,0:T(1,128)S(1)}, s32[1,192]{1,0:T(1,128)}, u32[]{:S(2)}) copy-start(s32[1,192]{1,0:T(1,128)} %param.19) | copy-start | bytes 2308
  0.7 9.7 %copy-start.12 = (s32[128]{0:T(128)S(1)}, s32[128]{0:T(128)}, u32[]{:S(2)}) copy-start(s32[128]{0:T(128)} %param.18) | copy-start | bytes 1540
  0.7 10.2 %copy-start.6 = (bf16[128,512]{1,0:T(8,128)(2,1)S(1)}, bf16[128,512]{1,0:T(8,128)(2,1)}, u32[]{:S(2)}) copy-start(bf16[128,512]{1,0:T(8,128)(2,1)} %param.16) | copy-start | bytes 393220
  0.7 9.0 %copy-start.9 = (bf16[8,512]{1,0:T(8,128)(2,1)S(1)}, bf16[8,512]{1,0:T(8,128)(2,1)}, u32[]{:S(2)}) copy-start(bf16[8,512]{1,0:T(8,128)(2,1)} %param.26) | copy-start | bytes 24580
  0.7 9.7 %copy-start.7 = (f32[5,512]{1,0:T(8,128)S(1)}, f32[5,512]{1,0:T(8,128)}, u32[]{:S(2)}) copy-start(f32[5,512]{1,0:T(8,128)} %param.24) | copy-start | bytes 30724
  0.7 10.1 %copy-start.1 = (bf16[512,512]{1,0:T(8,128)(2,1)S(1)}, bf16[512,512]{1,0:T(8,128)(2,1)}, u32[]{:S(2)}) copy-start(bf16[512,512]{1,0:T(8,128)(2,1)} %param.22) | copy-start | bytes 1572868
  3.5 8.4 %copy-start.10 = (s32[1024]{0:T(1024)S(1)}, s32[1024]{0:T(1024)}, u32[]{:S(2)}) copy-start(s32[1024]{0:T(1024)} %param.20) | copy-start | bytes 12292
  3.5 9.3 %copy-start.2 = (bf16[512,512]{1,0:T(8,128)(2,1)S(1)}, bf16[512,512]{1,0:T(8,128)(2,1)}, u32[]{:S(2)}) copy-start(bf16[512,512]{1,0:T(8,128)(2,1)} %update_ref.1) | copy-start | bytes 1572868
  5.6 8.3 %copy-start.3 = (bf16[512,384]{1,0:T(8,128)(2,1)S(1)}, bf16[512,384]{1,0:T(8,128)(2,1)}, u32[]{:S(2)}) copy-start(bf16[512,384]{1,0:T(8,128)(2,1)} %split_ref.1) | copy-start | bytes 1179652
  5.6 10.1 %collective-permute-start = (bf16[16,640]{1,0:T(8,128)(2,1)}, bf16[16,640]{1,0:T(8,128)(2,1)S(1)}, u32[]{:S(2)}, u32[]{:S(2)}) collective-permute-start(bf16[16,640]{1,0:T(8,128)(2,1)} %convolution_convert_fusion.5), channel_id=1, source_target_pairs={{24,0},{0,8},{8,16},{16,24},{25,1},{1,9},{9,17},{17,25},{26,2},{2,... | collective-permute-start | bytes 61448 | tf_op jit(solution)/shard_map/ppermute | solution.py:30
  6.9 8.9 %collective-permute-start.1 = (bf16[16,640]{1,0:T(8,128)(2,1)}, bf16[16,640]{1,0:T(8,128)(2,1)S(1)}, u32[]{:S(2)}, u32[]{:S(2)}) collective-permute-start(bf16[16,640]{1,0:T(8,128)(2,1)} %convolution_convert_fusion.4), channel_id=1, source_target_pairs={{8,0},{16,8},{24,16},{0,24},{9,1},{17,9},{25,17},{1,25},{10,2},{18... | collective-permute-start | bytes 61448 | tf_op jit(solution)/shard_map/ppermute | solution.py:30
  8.9 5.9 %copy-start.5 = (bf16[192,512]{1,0:T(8,128)(2,1)S(1)}, bf16[192,512]{1,0:T(8,128)(2,1)}, u32[]{:S(2)}) copy-start(bf16[192,512]{1,0:T(8,128)(2,1)} %tensor_ref.1) | copy-start | bytes 589828
  16.0 5.3 %collective-permute-start.2 = (bf16[64,640]{1,0:T(8,128)(2,1)S(1)}, bf16[64,640]{1,0:T(8,128)(2,1)S(1)}, u32[]{:S(2)}, u32[]{:S(2)}) collective-permute-start(bf16[64,640]{1,0:T(8,128)(2,1)S(1)} %convolution_convert_fusion.1), channel_id=1, source_target_pairs={{4,0},{0,4},{5,1},{1,5},{6,2},{2,6},{7,3},{3,7},{12,8},{8,12},{13,... | collective-permute-start | bytes 245768 | tf_op jit(solution)/shard_map/ppermute | solution.py:30
  18.6 4.5 %collective-permute-start.3 = (bf16[64,640]{1,0:T(8,128)(2,1)S(1)}, bf16[64,640]{1,0:T(8,128)(2,1)S(1)}, u32[]{:S(2)}, u32[]{:S(2)}) collective-permute-start(bf16[64,640]{1,0:T(8,128)(2,1)S(1)} %convolution_convert_fusion), channel_id=1, source_target_pairs={{4,0},{0,4},{5,1},{1,5},{6,2},{2,6},{7,3},{3,7},{12,8},{8,12},{13,... | collective-permute-start | bytes 245768 | tf_op jit(solution)/shard_map/ppermute | solution.py:30
  23.4 5.6 %collective-permute-start.4 = (bf16[16,640]{1,0:T(8,128)(2,1)S(1)}, bf16[16,640]{1,0:T(8,128)(2,1)S(1)}, u32[]{:S(2)}, u32[]{:S(2)}) collective-permute-start(bf16[16,640]{1,0:T(8,128)(2,1)S(1)} %convolution_convert_fusion.3), channel_id=1, source_target_pairs={{3,0},{0,1},{1,2},{2,3},{7,4},{4,5},{5,6},{6,7},{11,8},{8,9},{9,10... | collective-permute-start | bytes 61448 | tf_op jit(solution)/shard_map/ppermute | solution.py:30
  25.2 4.0 %collective-permute-start.5 = (bf16[16,640]{1,0:T(8,128)(2,1)S(1)}, bf16[16,640]{1,0:T(8,128)(2,1)S(1)}, u32[]{:S(2)}, u32[]{:S(2)}) collective-permute-start(bf16[16,640]{1,0:T(8,128)(2,1)S(1)} %convolution_convert_fusion.2), channel_id=1, source_target_pairs={{1,0},{2,1},{3,2},{0,3},{5,4},{6,5},{7,6},{4,7},{9,8},{10,9},{11,1... | collective-permute-start | bytes 61448 | tf_op jit(solution)/shard_map/ppermute | solution.py:30
  30.3 2.5 %copy-start.11 = (f32[512]{0:T(512)S(1)}, f32[512]{0:T(512)}, u32[]{:S(2)}) copy-start(f32[512]{0:T(512)} %param.30) | copy-start | bytes 6148
  49.3 7.8 %copy-start.4 = (f32[512,128]{1,0:T(8,128)S(1)}, f32[512,128]{1,0:T(8,128)}, u32[]{:S(2)}) copy-start(f32[512,128]{1,0:T(8,128)} %get-tuple-element.10) | copy-start | bytes 786436
  49.3 5.7 %collective-permute-start.7 = (bf16[16,640]{1,0:T(8,128)(2,1)S(1)}, bf16[16,640]{1,0:T(8,128)(2,1)S(1)}, u32[]{:S(2)}, u32[]{:S(2)}) collective-permute-start(bf16[16,640]{1,0:T(8,128)(2,1)S(1)} %get-tuple-element.31), channel_id=1, source_target_pairs={{3,0},{0,1},{1,2},{2,3},{7,4},{4,5},{5,6},{6,7},{11,8},{8,9},{9,10... | collective-permute-start | bytes 61448 | tf_op jit(solution)/shard_map/ppermute | solution.py:30
  50.8 4.6 %collective-permute-start.6 = (bf16[16,640]{1,0:T(8,128)(2,1)S(1)}, bf16[16,640]{1,0:T(8,128)(2,1)S(1)}, u32[]{:S(2)}, u32[]{:S(2)}) collective-permute-start(bf16[16,640]{1,0:T(8,128)(2,1)S(1)} %get-tuple-element.30), channel_id=1, source_target_pairs={{1,0},{2,1},{3,2},{0,3},{5,4},{6,5},{7,6},{4,7},{9,8},{10,9},{11,1... | collective-permute-start | bytes 61448 | tf_op jit(solution)/shard_map/ppermute | solution.py:30
  55.8 6.6 %copy-start.13 = (f32[8,128]{1,0:T(8,128)S(1)}, f32[8,128]{1,0:T(8,128)}, u32[]{:S(2)}) copy-start(f32[8,128]{1,0:T(8,128)} %get-tuple-element.7) | copy-start | bytes 12292
  55.8 6.6 %copy-start.14 = (f32[5]{0:T(128)S(1)}, f32[5]{0:T(128)}, u32[]{:S(2)}) copy-start(f32[5]{0:T(128)} %param.31) | copy-start | bytes 64
  55.9 4.5 %collective-permute-start.8 = (bf16[64,640]{1,0:T(8,128)(2,1)S(1)}, bf16[64,640]{1,0:T(8,128)(2,1)S(1)}, u32[]{:S(2)}, u32[]{:S(2)}) collective-permute-start(bf16[64,640]{1,0:T(8,128)(2,1)S(1)} %get-tuple-element.33), channel_id=1, source_target_pairs={{4,0},{0,4},{5,1},{1,5},{6,2},{2,6},{7,3},{3,7},{12,8},{8,12},{13,... | collective-permute-start | bytes 245768 | tf_op jit(solution)/shard_map/ppermute | solution.py:30
  57.4 4.5 %collective-permute-start.9 = (bf16[64,640]{1,0:T(8,128)(2,1)S(1)}, bf16[64,640]{1,0:T(8,128)(2,1)S(1)}, u32[]{:S(2)}, u32[]{:S(2)}) collective-permute-start(bf16[64,640]{1,0:T(8,128)(2,1)S(1)} %get-tuple-element.32), channel_id=1, source_target_pairs={{4,0},{0,4},{5,1},{1,5},{6,2},{2,6},{7,3},{3,7},{12,8},{8,12},{13,... | collective-permute-start | bytes 245768 | tf_op jit(solution)/shard_map/ppermute | solution.py:30
  62.3 1.5 %collective-permute-start.10 = (bf16[16,640]{1,0:T(8,128)(2,1)S(1)}, bf16[16,640]{1,0:T(8,128)(2,1)S(1)}, u32[]{:S(2)}, u32[]{:S(2)}) collective-permute-start(bf16[16,640]{1,0:T(8,128)(2,1)S(1)} %get-tuple-element.44), channel_id=1, source_target_pairs={{8,0},{16,8},{24,16},{0,24},{9,1},{17,9},{25,17},{1,25},{10,2},{18... | collective-permute-start | bytes 61448 | tf_op jit(solution)/shard_map/ppermute | solution.py:30
  63.2 3.2 %collective-permute-start.11 = (bf16[16,640]{1,0:T(8,128)(2,1)S(1)}, bf16[16,640]{1,0:T(8,128)(2,1)S(1)}, u32[]{:S(2)}, u32[]{:S(2)}) collective-permute-start(bf16[16,640]{1,0:T(8,128)(2,1)S(1)} %get-tuple-element.43), channel_id=1, source_target_pairs={{24,0},{0,8},{8,16},{16,24},{25,1},{1,9},{9,17},{17,25},{26,2},{2,... | collective-permute-start | bytes 61448 | tf_op jit(solution)/shard_map/ppermute | solution.py:30

commit v16 on v14

--- a/solution.py
+++ b/solution.py
@@ -377,15 +377,12 @@
     )
     (grad_delta,) = geo_pull(grad_geo)
     pairs = grad_neigh.shape[1]
-    grads = jnp.concatenate(
-        [
-            grad_neigh,
-            grad_delta.reshape(3, pairs),
-            jnp.zeros((extra - 3, pairs), jnp.float32),
-        ],
-        axis=0,
-    )
-    sums = spread_cols(select, grads).T
+    pos_grads = jnp.concatenate(
+        [grad_delta.reshape(3, pairs), jnp.zeros((extra - 3, pairs), jnp.float32)], axis=0
+    )
+    sums = jnp.concatenate(
+        [spread_cols(select, grad_neigh), spread_cols(select, pos_grads)], axis=0
+    ).T
     own_pos = grad_delta.sum(axis=1)
     sums = sums - jnp.pad(own_pos.T, ((0, total_rows - atoms), (width, extra - 3)))
     for section in (2, 1, 0):

time: 68.6 us -> 68.9 us (level)
  matrix products: 12.2 us -> 14.3 us
  other arithmetic: 5.4 us -> 3.71 us
    dot_general x1 -> x2, matrix products: 1.09 us -> 3.22 us  [spread_cols(): jnp.einsum('wn,nr->wr', values.astype(jnp.bfloat16), onehot, preferred_el...]
    another operation x1 -> x0, other arithmetic: 1.75 us -> none
where the time goes in v16:
time: 68.9 us; the launch traced here: 68.5 us
  starting transfers between devices  15.7 us (23%)
  matrix products  14.3 us (21%)
  waiting for transfers between devices  13.3 us (19%)
  local copies, waits for them, and re-layouts  10 us (15%)
  Pallas kernels  9.67 us (14%)
  other arithmetic  3.71 us (5%)
  between operations  1.77 us (3%)
    ppermute x12, starting transfers between devices, passed_along(): return lax.ppermute(block, axis, route)  15.7 us
    ppermute x12, waiting for transfers between devices, passed_along(): return lax.ppermute(block, axis, route)  13.3 us
    pallas_call x1, Pallas kernels, pair_terms(): pl.pallas_call(_pair_kernel, out_shape=(jax.ShapeDtypeStruct((width, pair...  9.67 us
    unnamed x38, local copies, waits for them, and re-layouts  3.54 us
    dot_general x2, matrix products, spread_cols(): jnp.einsum('wn,nr->wr', values.astype(jnp.bfloat16), onehot, preferred_el...  3.22 us
    dot_general x2, matrix products, project(): jnp.dot(rows, weight, preferred_element_type=jnp.float32)  2.44 us
    dot_general x3, matrix products, lookup(): return jnp.dot(onehot, table, precision=lax.Precision.HIGHEST)  2.23 us
    dot_general x6, matrix products, spread(): jnp.einsum('nr,nw->rw', onehot, values.astype(jnp.bfloat16), preferred_el...  2.05 us
  transfers between devices with their start and end apart: 12, of which 9 were waited for; matrix products, arithmetic and copies ran while one was open for 14% of the time, Pallas kernels for 0%

profile of v16, /device:TPU:0, one launch (start us, length us, event | category | flops | bytes accessed | tf_op | source)
XLA Modules:
  0.0 68.5 jit_solution(8614842942878598960)
XLA Ops:
  0.7 0.8 %fusion.99 = (f32[3,128]{1,0:T(4,128)S(1)}, bf16[3,128]{1,0:T(4,128)(2,1)S(1)}, bf16[3,128]{1,0:T(4,128)(2,1)S(1)}) fusion(s32[3,128]{1,0:T(4,128)} %param.17), kind=kLoop, calls=%fused_computation.199 | loop fusion | flops 7680 | bytes 4608 | tf_op jit(solution)/shard_map/convert_element_type | solution.py:361
  1.7 0.8 %slice_bitcast_fusion = (s32[16]{0:T(128)S(1)}, s32[16]{0:T(128)S(1)}, s32[16]{0:T(128)S(1)}, s32[16]{0:T(128)S(1)}) fusion(s32[1,192]{1,0:T(1,128)} %param.19), kind=kLoop, calls=%fused_computation.184 | loop fusion | bytes 512 | tf_op jit(solution)/shard_map/eq | solution.py:343
  2.5 1.0 %fusion.25 = f32[128,512]{1,0:T(8,128)S(1)} fusion(f32[5,512]{1,0:T(8,128)} %param.25, s32[128]{0:T(128)} %param.18), kind=kOutput, calls=%fused_computation.50 | convolution fusion | flops 3932800 | bytes 272896 | tf_op jit(solution)/shard_map/dot_general | solution.py:306
  3.5 1.4 %fusion.4 = bf16[128,512]{1,0:T(8,128)(2,1)S(1)} fusion(f32[128,512]{1,0:T(8,128)S(1)} %fusion.25, bf16[128,512]{1,0:T(8,128)(2,1)} %param.16, bf16[512,512]{1,0:T(8,128)(2,1)} %param.23), kind=kOutput, calls=%fused_computation.11 | convolution fusion | flops 67239936 | bytes 1048576 | tf_op jit(solution)/shard_map/dot_general | solution.py:310
  5.8 1.9 %collective-permute-start.1 = (bf16[16,640]{1,0:T(8,128)(2,1)S(1)}, bf16[16,640]{1,0:T(8,128)(2,1)S(1)}, u32[]{:S(2)}, u32[]{:S(2)}) collective-permute-start(bf16[16,640]{1,0:T(8,128)(2,1)S(1)} %convolution_convert_fusion.4), channel_id=1, source_target_pairs={{8,0},{16,8},{24,16},{0,24},{9,1},{17,9},{25,17},{1,25},{10,2},{18... | collective-permute-start | bytes 61448 | tf_op jit(solution)/shard_map/ppermute | solution.py:30
  9.8 1.0 %fusion.6.centre_ref = f32[512,128]{1,0:T(8,128)} fusion(f32[512,128]{1,0:T(8,128)S(1)} %convolution_bitcast_fusion, bf16[512,512]{1,0:T(8,128)(2,1)S(1)} %copy-done, bf16[128,512]{1,0:T(8,128)(2,1)S(1)} %copy-done.5), kind=kOutput, calls=%fused_computation.13 | convolution fusion | flops 67305472 | bytes 1179648 | tf_op jit(solution)/shard_map/dot_general | solution.py:310
  11.8 1.0 %copy.56 = bf16[512,512]{0,1:T(8,128)(2,1)} copy(bf16[512,512]{1,0:T(8,128)(2,1)S(1)} %copy-done.1) | data formatting | bytes 1048576 | tf_op args[12]
  12.8 0.9 %copy.55 = bf16[512,384]{0,1:T(8,128)(2,1)} copy(bf16[512,384]{1,0:T(8,128)(2,1)S(1)} %copy-done.3) | data formatting | bytes 786432 | tf_op args[11]
  13.8 0.8 %copy.57 = bf16[192,512]{0,1:T(8,128)(2,1)} copy(bf16[192,512]{1,0:T(8,128)(2,1)S(1)} %copy-done.4) | data formatting | bytes 393216 | tf_op args[13]
  14.9 2.4 %collective-permute-start.2 = (bf16[64,640]{1,0:T(8,128)(2,1)S(1)}, bf16[64,640]{1,0:T(8,128)(2,1)S(1)}, u32[]{:S(2)}, u32[]{:S(2)}) collective-permute-start(bf16[64,640]{1,0:T(8,128)(2,1)S(1)} %convolution_convert_fusion.1), channel_id=1, source_target_pairs={{4,0},{0,4},{5,1},{1,5},{6,2},{2,6},{7,3},{3,7},{12,8},{8,12},{13,... | collective-permute-start | bytes 245768 | tf_op jit(solution)/shard_map/ppermute | solution.py:30
  17.6 2.6 %collective-permute-done.2 = bf16[64,640]{1,0:T(8,128)(2,1)S(1)} collective-permute-done((bf16[64,640]{1,0:T(8,128)(2,1)S(1)}, bf16[64,640]{1,0:T(8,128)(2,1)S(1)}, u32[]{:S(2)}, u32[]{:S(2)}) %collective-permute-start.2) | collective-permute-done | bytes 81952 | tf_op jit(solution)/shard_map/ppermute | solution.py:30
  20.2 1.8 %collective-permute-done.3 = bf16[64,640]{1,0:T(8,128)(2,1)S(1)} collective-permute-done((bf16[64,640]{1,0:T(8,128)(2,1)S(1)}, bf16[64,640]{1,0:T(8,128)(2,1)S(1)}, u32[]{:S(2)}, u32[]{:S(2)}) %collective-permute-start.3) | collective-permute-done | bytes 81952 | tf_op jit(solution)/shard_map/ppermute | solution.py:30
  22.3 1.6 %collective-permute-start.4 = (bf16[16,640]{1,0:T(8,128)(2,1)S(1)}, bf16[16,640]{1,0:T(8,128)(2,1)S(1)}, u32[]{:S(2)}, u32[]{:S(2)}) collective-permute-start(bf16[16,640]{1,0:T(8,128)(2,1)S(1)} %convolution_convert_fusion.3), channel_id=1, source_target_pairs={{3,0},{0,1},{1,2},{2,3},{7,4},{4,5},{5,6},{6,7},{11,8},{8,9},{9,10... | collective-permute-start | bytes 61448 | tf_op jit(solution)/shard_map/ppermute | solution.py:30
  24.1 2.3 %collective-permute-start.5 = (bf16[16,640]{1,0:T(8,128)(2,1)S(1)}, bf16[16,640]{1,0:T(8,128)(2,1)S(1)}, u32[]{:S(2)}, u32[]{:S(2)}) collective-permute-start(bf16[16,640]{1,0:T(8,128)(2,1)S(1)} %convolution_convert_fusion.2), channel_id=1, source_target_pairs={{1,0},{2,1},{3,2},{0,3},{5,4},{6,5},{7,6},{4,7},{9,8},{10,9},{11,1... | collective-permute-start | bytes 61448 | tf_op jit(solution)/shard_map/ppermute | solution.py:30
  26.4 1.5 %collective-permute-done.4 = bf16[16,640]{1,0:T(8,128)(2,1)S(1)} collective-permute-done((bf16[16,640]{1,0:T(8,128)(2,1)S(1)}, bf16[16,640]{1,0:T(8,128)(2,1)S(1)}, u32[]{:S(2)}, u32[]{:S(2)}) %collective-permute-start.4) | collective-permute-done | bytes 20512 | tf_op jit(solution)/shard_map/ppermute | solution.py:30
  28.1 1.0 %fusion.2 = f32[640,1024]{1,0:T(8,128)S(1)} fusion(bf16[320,640]{1,0:T(8,128)(2,1)S(1)} %constant_dynamic-update-slice_fusion.3, s32[1024]{0:T(1024)S(1)} %bitcast.162), kind=kOutput, calls=%fused_computation.4 | convolution fusion | flops 419758080 | bytes 3035136 | tf_op jit(solution)/shard_map/tw,pt->wp/dot_general | solution.py:358
  29.2 1.2 %slice.197.rows_ref = bf16[512,1024]{1,0:T(8,128)(2,1)} slice(f32[640,1024]{1,0:T(8,128)S(1)} %fusion.2), slice={[0:512], [0:1024]} | slice | bytes 2097152 | tf_op jit(solution)/shard_map/slice | solution.py:359
  30.8 0.9 %concatenate.64.geo_ref = f32[128,1024]{1,0:T(8,128)} pad(f32[18,1024]{1,0:T(8,128)S(1)} %concatenate.63, f32[]{:T(128)} %constant.28.clone.1), padding=0_110x0_0 | pad | bytes 598020 | tf_op jit(solution)/shard_map/jvp()/concatenate | solution.py:80
  31.6 1.6 %broadcast_in_dim.52.energy_w_ref = f32[512,1024]{1,0:T(8,128)} broadcast(f32[512]{0:T(512)S(1)} %copy-done.11), dimensions={0} | broadcast | bytes 2099200 | tf_op jit(solution)/shard_map/broadcast_in_dim | solution.py:264
  33.2 9.7 %shard_map.175 = (f32[512,1024]{1,0:T(8,128)}, f32[512,128]{1,0:T(8,128)}, f32[128,1024]{1,0:T(8,128)}, f32[8,128]{1,0:T(8,128)}) custom-call(bf16[512,1024]{1,0:T(8,128)(2,1)} %slice.197.rows_ref, f32[512,128]{1,0:T(8,128)} %fusion.6.centre_ref, f32[128,1024]{1,0:T(8,128)} %concatenate.64.geo_ref, bf16[512,128]{1,0:T(8,128)(2,1)} %copy.58.basis_t_ref, ...), custom_call_target="tpu_custom_call" | custom-call | flops 1610612736 | bytes 8388608 | tf_op jit(solution)/shard_map/pallas_call | solution.py:226
  42.9 1.3 %slice_multiply_fusion.4 = (f32[1,1024]{1,0:T(1,128)S(1)}, f32[1,1024]{1,0:T(1,128)S(1)}, f32[1,1024]{1,0:T(1,128)S(1)}, f32[1,1024]{1,0:T(1,128)S(1)}, f32[1,10...) fusion(f32[128,1024]{1,0:T(8,128)} %get-tuple-element.9), kind=kLoop, calls=%fused_computation.148 | loop fusion | flops 5120 | bytes 73728 | tf_op jit(solution)/shard_map/transpose(jvp())/mul | solution.py:70
  44.1 1.0 %fusion.28 = (f32[1024]{0:T(1024)S(1)}, f32[1024]{0:T(1024)S(1)}) fusion(f32[128,1024]{1,0:T(8,128)} %get-tuple-element.9, f32[1024]{0:T(1024)S(1)} %get-tuple-element.67, f32[8]{0:T(128)S(1)} %convert_multiply_fusion, f32[1024]{0:T(1024)S(1)} %get-tuple-element.66), kind=kLoop, calls=%fused_computation.56 | loop fusion | flops 55296 | bytes 49184 | tf_op jit(solution)/shard_map/transpose(jvp())/reduce_sum | solution.py:58
  45.1 2.5 %fusion.1 = f32[512,320]{0,1:T(8,128)S(1)} fusion(f32[512,1024]{1,0:T(8,128)} %get-tuple-element.8, s32[1024]{0:T(1024)S(1)} %bitcast.163), kind=kOutput, calls=%fused_computation.3 | convolution fusion | flops 336396288 | bytes 2756608 | tf_op jit(solution)/shard_map/wn,nr->wr/dot_general | solution.py:314
  48.7 1.5 %collective-permute-start.7 = (bf16[16,640]{1,0:T(8,128)(2,1)S(1)}, bf16[16,640]{1,0:T(8,128)(2,1)S(1)}, u32[]{:S(2)}, u32[]{:S(2)}) collective-permute-start(bf16[16,640]{1,0:T(8,128)(2,1)S(1)} %get-tuple-element.31), channel_id=1, source_target_pairs={{3,0},{0,1},{1,2},{2,3},{7,4},{4,5},{5,6},{6,7},{11,8},{8,9},{9,10... | collective-permute-start | bytes 61448 | tf_op jit(solution)/shard_map/ppermute | solution.py:30
  50.1 2.7 %collective-permute-start.6 = (bf16[16,640]{1,0:T(8,128)(2,1)S(1)}, bf16[16,640]{1,0:T(8,128)(2,1)S(1)}, u32[]{:S(2)}, u32[]{:S(2)}) collective-permute-start(bf16[16,640]{1,0:T(8,128)(2,1)S(1)} %get-tuple-element.30), channel_id=1, source_target_pairs={{1,0},{2,1},{3,2},{0,3},{5,4},{6,5},{7,6},{4,7},{9,8},{10,9},{11,1... | collective-permute-start | bytes 61448 | tf_op jit(solution)/shard_map/ppermute | solution.py:30
  52.8 1.5 %collective-permute-done.7 = bf16[16,640]{1,0:T(8,128)(2,1)S(1)} collective-permute-done((bf16[16,640]{1,0:T(8,128)(2,1)S(1)}, bf16[16,640]{1,0:T(8,128)(2,1)S(1)}, u32[]{:S(2)}, u32[]{:S(2)}) %collective-permute-start.7) | collective-permute-done | bytes 20512 | tf_op jit(solution)/shard_map/ppermute | solution.py:30
  55.2 1.3 %collective-permute-start.8 = (bf16[64,640]{1,0:T(8,128)(2,1)S(1)}, bf16[64,640]{1,0:T(8,128)(2,1)S(1)}, u32[]{:S(2)}, u32[]{:S(2)}) collective-permute-start(bf16[64,640]{1,0:T(8,128)(2,1)S(1)} %get-tuple-element.33), channel_id=1, source_target_pairs={{4,0},{0,4},{5,1},{1,5},{6,2},{2,6},{7,3},{3,7},{12,8},{8,12},{13,... | collective-permute-start | bytes 245768 | tf_op jit(solution)/shard_map/ppermute | solution.py:30
  57.2 0.9 %collective-permute-start.9 = (bf16[64,640]{1,0:T(8,128)(2,1)S(1)}, bf16[64,640]{1,0:T(8,128)(2,1)S(1)}, u32[]{:S(2)}, u32[]{:S(2)}) collective-permute-start(bf16[64,640]{1,0:T(8,128)(2,1)S(1)} %get-tuple-element.32), channel_id=1, source_target_pairs={{4,0},{0,4},{5,1},{1,5},{6,2},{2,6},{7,3},{3,7},{12,8},{8,12},{13,... | collective-permute-start | bytes 245768 | tf_op jit(solution)/shard_map/ppermute | solution.py:30
  58.0 1.6 %collective-permute-done.8 = bf16[64,640]{1,0:T(8,128)(2,1)S(1)} collective-permute-done((bf16[64,640]{1,0:T(8,128)(2,1)S(1)}, bf16[64,640]{1,0:T(8,128)(2,1)S(1)}, u32[]{:S(2)}, u32[]{:S(2)}) %collective-permute-start.8) | collective-permute-done | bytes 81952 | tf_op jit(solution)/shard_map/ppermute | solution.py:30
  60.0 1.7 %collective-permute-done.9 = bf16[64,640]{1,0:T(8,128)(2,1)S(1)} collective-permute-done((bf16[64,640]{1,0:T(8,128)(2,1)S(1)}, bf16[64,640]{1,0:T(8,128)(2,1)S(1)}, u32[]{:S(2)}, u32[]{:S(2)}) %collective-permute-start.9) | collective-permute-done | bytes 81952 | tf_op jit(solution)/shard_map/ppermute | solution.py:30
  63.9 2.2 %collective-permute-done.11 = bf16[16,640]{1,0:T(8,128)(2,1)S(1)} collective-permute-done((bf16[16,640]{1,0:T(8,128)(2,1)S(1)}, bf16[16,640]{1,0:T(8,128)(2,1)S(1)}, u32[]{:S(2)}, u32[]{:S(2)}) %collective-permute-start.11) | collective-permute-done | bytes 20512 | tf_op jit(solution)/shard_map/ppermute | solution.py:30
  66.5 1.4 %convolution_add_fusion.1 = f32[128,512]{1,0:T(8,128)} fusion(f32[128,512]{1,0:T(8,128)S(1)} %fusion.100, bf16[512,512]{1,0:T(8,128)(2,1)S(1)} %copy-done.2, f32[128,640]{1,0:T(8,128)S(1)} %fusion.15), kind=kOutput, calls=%fused_computation.7 | convolution fusion | flops 402718720 | bytes 1310720 | tf_op jit(solution)/shard_map/dot_general | solution.py:403
  (103 shorter events, 11.0 us)
Async XLA Ops:
  0.6 9.2 %copy-start = (bf16[512,512]{1,0:T(8,128)(2,1)S(1)}, bf16[512,512]{1,0:T(8,128)(2,1)}, u32[]{:S(2)}) copy-start(bf16[512,512]{1,0:T(8,128)(2,1)} %param.22) | copy-start | bytes 1572868
  0.6 7.2 %copy-start.8 = (s32[1,192]{1,0:T(1,128)S(1)}, s32[1,192]{1,0:T(1,128)}, u32[]{:S(2)}) copy-start(s32[1,192]{1,0:T(1,128)} %param.19) | copy-start | bytes 2308
  0.7 8.7 %copy-start.12 = (s32[128]{0:T(128)S(1)}, s32[128]{0:T(128)}, u32[]{:S(2)}) copy-start(s32[128]{0:T(128)} %param.18) | copy-start | bytes 1540
  0.7 9.2 %copy-start.5 = (bf16[128,512]{1,0:T(8,128)(2,1)S(1)}, bf16[128,512]{1,0:T(8,128)(2,1)}, u32[]{:S(2)}) copy-start(bf16[128,512]{1,0:T(8,128)(2,1)} %param.16) | copy-start | bytes 393220
  0.7 8.0 %copy-start.9 = (bf16[8,512]{1,0:T(8,128)(2,1)S(1)}, bf16[8,512]{1,0:T(8,128)(2,1)}, u32[]{:S(2)}) copy-start(bf16[8,512]{1,0:T(8,128)(2,1)} %param.26) | copy-start | bytes 24580
  0.7 8.7 %copy-start.7 = (f32[5,512]{1,0:T(8,128)S(1)}, f32[5,512]{1,0:T(8,128)}, u32[]{:S(2)}) copy-start(f32[5,512]{1,0:T(8,128)} %param.24) | copy-start | bytes 30724
  3.5 7.4 %copy-start.10 = (s32[1024]{0:T(1024)S(1)}, s32[1024]{0:T(1024)}, u32[]{:S(2)}) copy-start(s32[1024]{0:T(1024)} %param.20) | copy-start | bytes 12292
  3.5 8.3 %copy-start.1 = (bf16[512,512]{1,0:T(8,128)(2,1)S(1)}, bf16[512,512]{1,0:T(8,128)(2,1)}, u32[]{:S(2)}) copy-start(bf16[512,512]{1,0:T(8,128)(2,1)} %update_ref.1) | copy-start | bytes 1572868
  5.1 7.7 %copy-start.3 = (bf16[512,384]{1,0:T(8,128)(2,1)S(1)}, bf16[512,384]{1,0:T(8,128)(2,1)}, u32[]{:S(2)}) copy-start(bf16[512,384]{1,0:T(8,128)(2,1)} %split_ref.1) | copy-start | bytes 1179652
  5.1 9.5 %collective-permute-start = (bf16[16,640]{1,0:T(8,128)(2,1)S(1)}, bf16[16,640]{1,0:T(8,128)(2,1)S(1)}, u32[]{:S(2)}, u32[]{:S(2)}) collective-permute-start(bf16[16,640]{1,0:T(8,128)(2,1)S(1)} %convolution_convert_fusion.5), channel_id=1, source_target_pairs={{24,0},{0,8},{8,16},{16,24},{25,1},{1,9},{9,17},{17,25},{26,2},{2,... | collective-permute-start | bytes 61448 | tf_op jit(solution)/shard_map/ppermute | solution.py:30
  5.8 8.8 %collective-permute-start.1 = (bf16[16,640]{1,0:T(8,128)(2,1)S(1)}, bf16[16,640]{1,0:T(8,128)(2,1)S(1)}, u32[]{:S(2)}, u32[]{:S(2)}) collective-permute-start(bf16[16,640]{1,0:T(8,128)(2,1)S(1)} %convolution_convert_fusion.4), channel_id=1, source_target_pairs={{8,0},{16,8},{24,16},{0,24},{9,1},{17,9},{25,17},{1,25},{10,2},{18... | collective-permute-start | bytes 61448 | tf_op jit(solution)/shard_map/ppermute | solution.py:30
  7.9 5.9 %copy-start.4 = (bf16[192,512]{1,0:T(8,128)(2,1)S(1)}, bf16[192,512]{1,0:T(8,128)(2,1)}, u32[]{:S(2)}) copy-start(bf16[192,512]{1,0:T(8,128)(2,1)} %tensor_ref.1) | copy-start | bytes 589828
  14.9 5.3 %collective-permute-start.2 = (bf16[64,640]{1,0:T(8,128)(2,1)S(1)}, bf16[64,640]{1,0:T(8,128)(2,1)S(1)}, u32[]{:S(2)}, u32[]{:S(2)}) collective-permute-start(bf16[64,640]{1,0:T(8,128)(2,1)S(1)} %convolution_convert_fusion.1), channel_id=1, source_target_pairs={{4,0},{0,4},{5,1},{1,5},{6,2},{2,6},{7,3},{3,7},{12,8},{8,12},{13,... | collective-permute-start | bytes 245768 | tf_op jit(solution)/shard_map/ppermute | solution.py:30
  17.5 4.5 %collective-permute-start.3 = (bf16[64,640]{1,0:T(8,128)(2,1)S(1)}, bf16[64,640]{1,0:T(8,128)(2,1)S(1)}, u32[]{:S(2)}, u32[]{:S(2)}) collective-permute-start(bf16[64,640]{1,0:T(8,128)(2,1)S(1)} %convolution_convert_fusion), channel_id=1, source_target_pairs={{4,0},{0,4},{5,1},{1,5},{6,2},{2,6},{7,3},{3,7},{12,8},{8,12},{13,... | collective-permute-start | bytes 245768 | tf_op jit(solution)/shard_map/ppermute | solution.py:30
  22.3 5.6 %collective-permute-start.4 = (bf16[16,640]{1,0:T(8,128)(2,1)S(1)}, bf16[16,640]{1,0:T(8,128)(2,1)S(1)}, u32[]{:S(2)}, u32[]{:S(2)}) collective-permute-start(bf16[16,640]{1,0:T(8,128)(2,1)S(1)} %convolution_convert_fusion.3), channel_id=1, source_target_pairs={{3,0},{0,1},{1,2},{2,3},{7,4},{4,5},{5,6},{6,7},{11,8},{8,9},{9,10... | collective-permute-start | bytes 61448 | tf_op jit(solution)/shard_map/ppermute | solution.py:30
  24.1 4.0 %collective-permute-start.5 = (bf16[16,640]{1,0:T(8,128)(2,1)S(1)}, bf16[16,640]{1,0:T(8,128)(2,1)S(1)}, u32[]{:S(2)}, u32[]{:S(2)}) collective-permute-start(bf16[16,640]{1,0:T(8,128)(2,1)S(1)} %convolution_convert_fusion.2), channel_id=1, source_target_pairs={{1,0},{2,1},{3,2},{0,3},{5,4},{6,5},{7,6},{4,7},{9,8},{10,9},{11,1... | collective-permute-start | bytes 61448 | tf_op jit(solution)/shard_map/ppermute | solution.py:30
  29.2 2.5 %copy-start.11 = (f32[512]{0:T(512)S(1)}, f32[512]{0:T(512)}, u32[]{:S(2)}) copy-start(f32[512]{0:T(512)} %param.30) | copy-start | bytes 6148
  48.6 7.8 %copy-start.6 = (f32[512,128]{1,0:T(8,128)S(1)}, f32[512,128]{1,0:T(8,128)}, u32[]{:S(2)}) copy-start(f32[512,128]{1,0:T(8,128)} %get-tuple-element.10) | copy-start | bytes 786436
  48.7 5.7 %collective-permute-start.7 = (bf16[16,640]{1,0:T(8,128)(2,1)S(1)}, bf16[16,640]{1,0:T(8,128)(2,1)S(1)}, u32[]{:S(2)}, u32[]{:S(2)}) collective-permute-start(bf16[16,640]{1,0:T(8,128)(2,1)S(1)} %get-tuple-element.31), channel_id=1, source_target_pairs={{3,0},{0,1},{1,2},{2,3},{7,4},{4,5},{5,6},{6,7},{11,8},{8,9},{9,10... | collective-permute-start | bytes 61448 | tf_op jit(solution)/shard_map/ppermute | solution.py:30
  50.1 4.6 %collective-permute-start.6 = (bf16[16,640]{1,0:T(8,128)(2,1)S(1)}, bf16[16,640]{1,0:T(8,128)(2,1)S(1)}, u32[]{:S(2)}, u32[]{:S(2)}) collective-permute-start(bf16[16,640]{1,0:T(8,128)(2,1)S(1)} %get-tuple-element.30), channel_id=1, source_target_pairs={{1,0},{2,1},{3,2},{0,3},{5,4},{6,5},{7,6},{4,7},{9,8},{10,9},{11,1... | collective-permute-start | bytes 61448 | tf_op jit(solution)/shard_map/ppermute | solution.py:30
  55.1 7.0 %copy-start.13 = (f32[8,128]{1,0:T(8,128)S(1)}, f32[8,128]{1,0:T(8,128)}, u32[]{:S(2)}) copy-start(f32[8,128]{1,0:T(8,128)} %get-tuple-element.7) | copy-start | bytes 12292
  55.1 7.0 %copy-start.14 = (f32[5]{0:T(128)S(1)}, f32[5]{0:T(128)}, u32[]{:S(2)}) copy-start(f32[5]{0:T(128)} %param.31) | copy-start | bytes 64
  55.2 4.5 %collective-permute-start.8 = (bf16[64,640]{1,0:T(8,128)(2,1)S(1)}, bf16[64,640]{1,0:T(8,128)(2,1)S(1)}, u32[]{:S(2)}, u32[]{:S(2)}) collective-permute-start(bf16[64,640]{1,0:T(8,128)(2,1)S(1)} %get-tuple-element.33), channel_id=1, source_target_pairs={{4,0},{0,4},{5,1},{1,5},{6,2},{2,6},{7,3},{3,7},{12,8},{8,12},{13,... | collective-permute-start | bytes 245768 | tf_op jit(solution)/shard_map/ppermute | solution.py:30
  56.5 10.0 %copy-start.2 = (bf16[512,512]{1,0:T(8,128)(2,1)S(1)}, bf16[512,512]{1,0:T(8,128)(2,1)}, u32[]{:S(2)}) copy-start(bf16[512,512]{1,0:T(8,128)(2,1)} %param.23) | copy-start | bytes 1572868
  57.2 4.5 %collective-permute-start.9 = (bf16[64,640]{1,0:T(8,128)(2,1)S(1)}, bf16[64,640]{1,0:T(8,128)(2,1)S(1)}, u32[]{:S(2)}, u32[]{:S(2)}) collective-permute-start(bf16[64,640]{1,0:T(8,128)(2,1)S(1)} %get-tuple-element.32), channel_id=1, source_target_pairs={{4,0},{0,4},{5,1},{1,5},{6,2},{2,6},{7,3},{3,7},{12,8},{8,12},{13,... | collective-permute-start | bytes 245768 | tf_op jit(solution)/shard_map/ppermute | solution.py:30
  62.0 1.5 %collective-permute-start.10 = (bf16[16,640]{1,0:T(8,128)(2,1)S(1)}, bf16[16,640]{1,0:T(8,128)(2,1)S(1)}, u32[]{:S(2)}, u32[]{:S(2)}) collective-permute-start(bf16[16,640]{1,0:T(8,128)(2,1)S(1)} %get-tuple-element.44), channel_id=1, source_target_pairs={{8,0},{16,8},{24,16},{0,24},{9,1},{17,9},{25,17},{1,25},{10,2},{18... | collective-permute-start | bytes 61448 | tf_op jit(solution)/shard_map/ppermute | solution.py:30
  62.9 3.2 %collective-permute-start.11 = (bf16[16,640]{1,0:T(8,128)(2,1)S(1)}, bf16[16,640]{1,0:T(8,128)(2,1)S(1)}, u32[]{:S(2)}, u32[]{:S(2)}) collective-permute-start(bf16[16,640]{1,0:T(8,128)(2,1)S(1)} %get-tuple-element.43), channel_id=1, source_target_pairs={{24,0},{0,8},{8,16},{16,24},{25,1},{1,9},{9,17},{17,25},{26,2},{2,... | collective-permute-start | bytes 61448 | tf_op jit(solution)/shard_map/ppermute | solution.py:30

commit v17 on v14

--- a/solution.py
+++ b/solution.py
@@ -157,9 +157,9 @@
         z = _mm(update_t_ref[...], hidden.astype(bf16)) + _mm(tensor_t_ref[...], scalars)
         gate = _sigmoid(z)
         update = z * gate
-        readout = jnp.sum((hidden + update) * energy_w_ref[...], axis=0, keepdims=True)
+        readout = jnp.sum((hidden + update) * twice(energy_w_ref[...]), axis=0, keepdims=True)
         energy = energy + envelope * readout
-        dz = (envelope * energy_w_ref[...]) * (gate * (1.0 + z * (1.0 - gate)))
+        dz = (envelope * twice(energy_w_ref[...])) * (gate * (1.0 + z * (1.0 - gate)))
         dz_low = dz.astype(bf16)
         dscalars = _mm(tensor_ref[...], dz_low).astype(bf16).astype(f32)
         dlow_s[:, at] = _mm(update_ref[...], dz_low)
@@ -200,7 +200,7 @@
             dweights.append(dweight)
         dmixed = jnp.concatenate([damp_s[:, at]] + dweights, axis=0).astype(bf16)
         dlow = dlow_s[:, at] + _mm(split_ref[...], dmixed)
-        dhidden = envelope * energy_w_ref[...] + dlow
+        dhidden = envelope * twice(energy_w_ref[...]) + dlow
         pre = pre_s[:, at]
         sig = _sigmoid(pre)
         act = pre * sig
@@ -261,7 +261,7 @@
         tensor_proj.T,
         tensor_proj,
         basis_pad,
-        jnp.broadcast_to(energy_proj.astype(f32)[:, None], (width, SLOTS * atoms)),
+        jnp.broadcast_to(energy_proj.astype(f32)[:, None], (width, atoms)),
     )
     grad_rows_t, grad_centre_t, grad_geo, energy = outs
     return grad_rows_t, grad_centre_t, grad_geo, energy[0]

time: 68.6 us -> 67.1 us (0.978)
  local copies, waits for them, and re-layouts: 10.1 us -> 9.35 us
    broadcast_in_dim x1, local copies, waits for them, and re-layouts: 1.56 us -> 0.83 us  [pair_terms(): jnp.broadcast_to(energy_proj.astype(f32)[:, None], (width, atoms))]
where the time goes in v17:
time: 67.1 us; the launch traced here: 66.6 us
  starting transfers between devices  15.7 us (23%)
  waiting for transfers between devices  13.3 us (20%)
  matrix products  12.2 us (18%)
  local copies, waits for them, and re-layouts  9.35 us (14%)
  Pallas kernels  9.02 us (13%)
  other arithmetic  5.34 us (8%)
  between operations  1.77 us (3%)
    ppermute x12, starting transfers between devices, passed_along(): return lax.ppermute(block, axis, route)  15.7 us
    ppermute x12, waiting for transfers between devices, passed_along(): return lax.ppermute(block, axis, route)  13.3 us
    pallas_call x1, Pallas kernels, pair_terms(): pl.pallas_call(_pair_kernel, out_shape=(jax.ShapeDtypeStruct((width, pair...  9.02 us
    unnamed x38, local copies, waits for them, and re-layouts  3.57 us
    dot_general x2, matrix products, project(): jnp.dot(rows, weight, preferred_element_type=jnp.float32)  2.44 us
    dot_general x3, matrix products, lookup(): return jnp.dot(onehot, table, precision=lax.Precision.HIGHEST)  2.23 us
    dot_general x6, matrix products, spread(): jnp.einsum('nr,nw->rw', onehot, values.astype(jnp.bfloat16), preferred_el...  2.06 us
    another operation x1, other arithmetic  1.75 us
  transfers between devices with their start and end apart: 12, of which 9 were waited for; matrix products, arithmetic and copies ran while one was open for 14% of the time, Pallas kernels for 0%

profile of v17, /device:TPU:0, one launch (start us, length us, event | category | flops | bytes accessed | tf_op | source)
XLA Modules:
  0.0 66.6 jit_solution(4419077783460955624)
XLA Ops:
  1.7 0.8 %slice_bitcast_fusion = (s32[16]{0:T(128)S(1)}, s32[16]{0:T(128)S(1)}, s32[16]{0:T(128)S(1)}, s32[16]{0:T(128)S(1)}) fusion(s32[1,192]{1,0:T(1,128)} %param.19), kind=kLoop, calls=%fused_computation.185 | loop fusion | bytes 512 | tf_op jit(solution)/shard_map/eq | solution.py:343
  2.5 1.0 %fusion.30 = f32[128,512]{1,0:T(8,128)S(1)} fusion(f32[5,512]{1,0:T(8,128)} %param.25, s32[128]{0:T(128)} %param.18), kind=kOutput, calls=%fused_computation.51 | convolution fusion | flops 3932800 | bytes 272896 | tf_op jit(solution)/shard_map/dot_general | solution.py:306
  3.5 1.4 %fusion.11 = bf16[128,512]{1,0:T(8,128)(2,1)S(1)} fusion(f32[128,512]{1,0:T(8,128)S(1)} %fusion.30, bf16[128,512]{1,0:T(8,128)(2,1)} %param.16, bf16[512,512]{1,0:T(8,128)(2,1)} %param.23), kind=kOutput, calls=%fused_computation.16 | convolution fusion | flops 67239936 | bytes 1048576 | tf_op jit(solution)/shard_map/dot_general | solution.py:310
  5.8 1.9 %collective-permute-start.1 = (bf16[16,640]{1,0:T(8,128)(2,1)S(1)}, bf16[16,640]{1,0:T(8,128)(2,1)S(1)}, u32[]{:S(2)}, u32[]{:S(2)}) collective-permute-start(bf16[16,640]{1,0:T(8,128)(2,1)S(1)} %convolution_convert_fusion.4), channel_id=1, source_target_pairs={{8,0},{16,8},{24,16},{0,24},{9,1},{17,9},{25,17},{1,25},{10,2},{18... | collective-permute-start | bytes 61448 | tf_op jit(solution)/shard_map/ppermute | solution.py:30
  9.8 1.0 %fusion.13.centre_ref = f32[512,128]{1,0:T(8,128)} fusion(f32[512,128]{1,0:T(8,128)S(1)} %convolution_bitcast_fusion, bf16[512,512]{1,0:T(8,128)(2,1)S(1)} %copy-done, bf16[128,512]{1,0:T(8,128)(2,1)S(1)} %copy-done.3), kind=kOutput, calls=%fused_computation.18 | convolution fusion | flops 67305472 | bytes 1179648 | tf_op jit(solution)/shard_map/dot_general | solution.py:310
  11.8 1.0 %copy.56 = bf16[512,512]{0,1:T(8,128)(2,1)} copy(bf16[512,512]{1,0:T(8,128)(2,1)S(1)} %copy-done.2) | data formatting | bytes 1048576 | tf_op args[12]
  12.8 1.0 %copy.55 = bf16[512,384]{0,1:T(8,128)(2,1)} copy(bf16[512,384]{1,0:T(8,128)(2,1)S(1)} %copy-done.4) | data formatting | bytes 786432 | tf_op args[11]
  13.8 0.8 %copy.57 = bf16[192,512]{0,1:T(8,128)(2,1)} copy(bf16[192,512]{1,0:T(8,128)(2,1)S(1)} %copy-done.6) | data formatting | bytes 393216 | tf_op args[13]
  15.0 2.4 %collective-permute-start.2 = (bf16[64,640]{1,0:T(8,128)(2,1)S(1)}, bf16[64,640]{1,0:T(8,128)(2,1)S(1)}, u32[]{:S(2)}, u32[]{:S(2)}) collective-permute-start(bf16[64,640]{1,0:T(8,128)(2,1)S(1)} %convolution_convert_fusion.1), channel_id=1, source_target_pairs={{4,0},{0,4},{5,1},{1,5},{6,2},{2,6},{7,3},{3,7},{12,8},{8,12},{13,... | collective-permute-start | bytes 245768 | tf_op jit(solution)/shard_map/ppermute | solution.py:30
  17.7 2.6 %collective-permute-done.2 = bf16[64,640]{1,0:T(8,128)(2,1)S(1)} collective-permute-done((bf16[64,640]{1,0:T(8,128)(2,1)S(1)}, bf16[64,640]{1,0:T(8,128)(2,1)S(1)}, u32[]{:S(2)}, u32[]{:S(2)}) %collective-permute-start.2) | collective-permute-done | bytes 81952 | tf_op jit(solution)/shard_map/ppermute | solution.py:30
  20.3 1.8 %collective-permute-done.3 = bf16[64,640]{1,0:T(8,128)(2,1)S(1)} collective-permute-done((bf16[64,640]{1,0:T(8,128)(2,1)S(1)}, bf16[64,640]{1,0:T(8,128)(2,1)S(1)}, u32[]{:S(2)}, u32[]{:S(2)}) %collective-permute-start.3) | collective-permute-done | bytes 81952 | tf_op jit(solution)/shard_map/ppermute | solution.py:30
  22.3 1.6 %collective-permute-start.4 = (bf16[16,640]{1,0:T(8,128)(2,1)S(1)}, bf16[16,640]{1,0:T(8,128)(2,1)S(1)}, u32[]{:S(2)}, u32[]{:S(2)}) collective-permute-start(bf16[16,640]{1,0:T(8,128)(2,1)S(1)} %convolution_convert_fusion.3), channel_id=1, source_target_pairs={{3,0},{0,1},{1,2},{2,3},{7,4},{4,5},{5,6},{6,7},{11,8},{8,9},{9,10... | collective-permute-start | bytes 61448 | tf_op jit(solution)/shard_map/ppermute | solution.py:30
  24.2 2.3 %collective-permute-start.5 = (bf16[16,640]{1,0:T(8,128)(2,1)S(1)}, bf16[16,640]{1,0:T(8,128)(2,1)S(1)}, u32[]{:S(2)}, u32[]{:S(2)}) collective-permute-start(bf16[16,640]{1,0:T(8,128)(2,1)S(1)} %convolution_convert_fusion.2), channel_id=1, source_target_pairs={{1,0},{2,1},{3,2},{0,3},{5,4},{6,5},{7,6},{4,7},{9,8},{10,9},{11,1... | collective-permute-start | bytes 61448 | tf_op jit(solution)/shard_map/ppermute | solution.py:30
  26.5 1.5 %collective-permute-done.4 = bf16[16,640]{1,0:T(8,128)(2,1)S(1)} collective-permute-done((bf16[16,640]{1,0:T(8,128)(2,1)S(1)}, bf16[16,640]{1,0:T(8,128)(2,1)S(1)}, u32[]{:S(2)}, u32[]{:S(2)}) %collective-permute-start.4) | collective-permute-done | bytes 20512 | tf_op jit(solution)/shard_map/ppermute | solution.py:30
  28.2 1.0 %fusion.1 = f32[640,1024]{1,0:T(8,128)S(1)} fusion(bf16[320,640]{1,0:T(8,128)(2,1)S(1)} %constant_dynamic-update-slice_fusion.3, s32[1024]{0:T(1024)S(1)} %bitcast.159), kind=kOutput, calls=%fused_computation.3 | convolution fusion | flops 419758080 | bytes 3035136 | tf_op jit(solution)/shard_map/tw,pt->wp/dot_general | solution.py:358
  29.3 1.1 %slice.197.rows_ref = bf16[512,1024]{1,0:T(8,128)(2,1)} slice(f32[640,1024]{1,0:T(8,128)S(1)} %fusion.1), slice={[0:512], [0:1024]} | slice | bytes 2097152 | tf_op jit(solution)/shard_map/slice | solution.py:359
  30.8 0.9 %concatenate.62.geo_ref = f32[128,1024]{1,0:T(8,128)} pad(f32[18,1024]{1,0:T(8,128)S(1)} %concatenate.61, f32[]{:T(128)} %constant.28.clone.1), padding=0_110x0_0 | pad | bytes 598020 | tf_op jit(solution)/shard_map/jvp()/concatenate | solution.py:80
  31.7 0.8 %broadcast_in_dim.99.energy_w_ref = f32[512,128]{1,0:T(8,128)} broadcast(f32[512]{0:T(512)S(1)} %copy-done.11), dimensions={0} | broadcast | bytes 264192 | tf_op jit(solution)/shard_map/broadcast_in_dim | solution.py:264
  32.5 9.0 %shard_map.175 = (f32[512,1024]{1,0:T(8,128)}, f32[512,128]{1,0:T(8,128)}, f32[128,1024]{1,0:T(8,128)}, f32[8,128]{1,0:T(8,128)}) custom-call(bf16[512,1024]{1,0:T(8,128)(2,1)} %slice.197.rows_ref, f32[512,128]{1,0:T(8,128)} %fusion.13.centre_ref, f32[128,1024]{1,0:T(8,128)} %concatenate.62.geo_ref, bf16[512,128]{1,0:T(8,128)(2,1)} %copy.58.basis_t_ref, ...), custom_call_target="tpu_custom_call" | custom-call | flops 1610612736 | bytes 8388608 | tf_op jit(solution)/shard_map/pallas_call | solution.py:226
  41.5 1.2 %slice_multiply_fusion.4 = (f32[1,1024]{1,0:T(1,128)S(1)}, f32[1,1024]{1,0:T(1,128)S(1)}, f32[1,1024]{1,0:T(1,128)S(1)}, f32[1,1024]{1,0:T(1,128)S(1)}, f32[1,10...) fusion(f32[128,1024]{1,0:T(8,128)} %get-tuple-element.9), kind=kLoop, calls=%fused_computation.149 | loop fusion | flops 5120 | bytes 73728 | tf_op jit(solution)/shard_map/transpose(jvp())/mul | solution.py:70
  42.8 1.0 %fusion.33 = (f32[1024]{0:T(1024)S(1)}, f32[1024]{0:T(1024)S(1)}) fusion(f32[128,1024]{1,0:T(8,128)} %get-tuple-element.9, f32[1024]{0:T(1024)S(1)} %get-tuple-element.67, f32[8]{0:T(128)S(1)} %convert_multiply_fusion, f32[1024]{0:T(1024)S(1)} %get-tuple-element.66), kind=kLoop, calls=%fused_computation.57 | loop fusion | flops 55296 | bytes 49184 | tf_op jit(solution)/shard_map/transpose(jvp())/reduce_sum | solution.py:58
  43.7 1.8 %convert.21 = bf16[512,1024]{1,0:T(8,128)(2,1)S(1)} convert(f32[512,1024]{1,0:T(8,128)} %get-tuple-element.8) | non-fusion elementwise | flops 524288 | bytes 3145728 | tf_op jit(solution)/shard_map/convert
  45.7 1.1 %fusion.7 = f32[320,640]{1,0:T(8,128)S(1)} fusion(bf16[3,1024]{1,0:T(4,128)(2,1)S(1)} %bitcast.180, bf16[512,1024]{1,0:T(8,128)(2,1)S(1)} %convert.21, f32[128,3]{1,0:T(8,128)S(1)} %bitcast.157, s32[1024]{0:T(1024)S(1)} %bitcast.160, bf16[640]{0:T(1024)(128)(2,1)S(1)} %pad.21.clone), kind=kOutput, calls=%fused_computation.9 | convolution fusion | flops 424222720 | bytes 1880832 | tf_op jit(solution)/shard_map/wn,nr->wr/dot_general | solution.py:314
  46.8 1.5 %collective-permute-start.7 = (bf16[16,640]{1,0:T(8,128)(2,1)S(1)}, bf16[16,640]{1,0:T(8,128)(2,1)S(1)}, u32[]{:S(2)}, u32[]{:S(2)}) collective-permute-start(bf16[16,640]{1,0:T(8,128)(2,1)S(1)} %get-tuple-element.31), channel_id=1, source_target_pairs={{3,0},{0,1},{1,2},{2,3},{7,4},{4,5},{5,6},{6,7},{11,8},{8,9},{9,10... | collective-permute-start | bytes 61448 | tf_op jit(solution)/shard_map/ppermute | solution.py:30
  48.3 2.7 %collective-permute-start.6 = (bf16[16,640]{1,0:T(8,128)(2,1)S(1)}, bf16[16,640]{1,0:T(8,128)(2,1)S(1)}, u32[]{:S(2)}, u32[]{:S(2)}) collective-permute-start(bf16[16,640]{1,0:T(8,128)(2,1)S(1)} %get-tuple-element.30), channel_id=1, source_target_pairs={{1,0},{2,1},{3,2},{0,3},{5,4},{6,5},{7,6},{4,7},{9,8},{10,9},{11,1... | collective-permute-start | bytes 61448 | tf_op jit(solution)/shard_map/ppermute | solution.py:30
  51.0 1.5 %collective-permute-done.7 = bf16[16,640]{1,0:T(8,128)(2,1)S(1)} collective-permute-done((bf16[16,640]{1,0:T(8,128)(2,1)S(1)}, bf16[16,640]{1,0:T(8,128)(2,1)S(1)}, u32[]{:S(2)}, u32[]{:S(2)}) %collective-permute-start.7) | collective-permute-done | bytes 20512 | tf_op jit(solution)/shard_map/ppermute | solution.py:30
  53.3 1.3 %collective-permute-start.8 = (bf16[64,640]{1,0:T(8,128)(2,1)S(1)}, bf16[64,640]{1,0:T(8,128)(2,1)S(1)}, u32[]{:S(2)}, u32[]{:S(2)}) collective-permute-start(bf16[64,640]{1,0:T(8,128)(2,1)S(1)} %get-tuple-element.33), channel_id=1, source_target_pairs={{4,0},{0,4},{5,1},{1,5},{6,2},{2,6},{7,3},{3,7},{12,8},{8,12},{13,... | collective-permute-start | bytes 245768 | tf_op jit(solution)/shard_map/ppermute | solution.py:30
  55.4 0.9 %collective-permute-start.9 = (bf16[64,640]{1,0:T(8,128)(2,1)S(1)}, bf16[64,640]{1,0:T(8,128)(2,1)S(1)}, u32[]{:S(2)}, u32[]{:S(2)}) collective-permute-start(bf16[64,640]{1,0:T(8,128)(2,1)S(1)} %get-tuple-element.32), channel_id=1, source_target_pairs={{4,0},{0,4},{5,1},{1,5},{6,2},{2,6},{7,3},{3,7},{12,8},{8,12},{13,... | collective-permute-start | bytes 245768 | tf_op jit(solution)/shard_map/ppermute | solution.py:30
  56.2 1.6 %collective-permute-done.8 = bf16[64,640]{1,0:T(8,128)(2,1)S(1)} collective-permute-done((bf16[64,640]{1,0:T(8,128)(2,1)S(1)}, bf16[64,640]{1,0:T(8,128)(2,1)S(1)}, u32[]{:S(2)}, u32[]{:S(2)}) %collective-permute-start.8) | collective-permute-done | bytes 81952 | tf_op jit(solution)/shard_map/ppermute | solution.py:30
  58.2 1.7 %collective-permute-done.9 = bf16[64,640]{1,0:T(8,128)(2,1)S(1)} collective-permute-done((bf16[64,640]{1,0:T(8,128)(2,1)S(1)}, bf16[64,640]{1,0:T(8,128)(2,1)S(1)}, u32[]{:S(2)}, u32[]{:S(2)}) %collective-permute-start.9) | collective-permute-done | bytes 81952 | tf_op jit(solution)/shard_map/ppermute | solution.py:30
  62.1 2.2 %collective-permute-done.11 = bf16[16,640]{1,0:T(8,128)(2,1)S(1)} collective-permute-done((bf16[16,640]{1,0:T(8,128)(2,1)S(1)}, bf16[16,640]{1,0:T(8,128)(2,1)S(1)}, u32[]{:S(2)}, u32[]{:S(2)}) %collective-permute-start.11) | collective-permute-done | bytes 20512 | tf_op jit(solution)/shard_map/ppermute | solution.py:30
  64.6 1.4 %convolution_add_fusion.1 = f32[128,512]{1,0:T(8,128)} fusion(f32[128,512]{1,0:T(8,128)S(1)} %fusion.105, bf16[512,512]{1,0:T(8,128)(2,1)S(1)} %copy-done.1, f32[128,640]{1,0:T(8,128)S(1)} %fusion.21), kind=kOutput, calls=%fused_computation.12 | convolution fusion | flops 402718720 | bytes 1310720 | tf_op jit(solution)/shard_map/dot_general | solution.py:406
  (104 shorter events, 11.0 us)
Async XLA Ops:
  0.6 9.2 %copy-start = (bf16[512,512]{1,0:T(8,128)(2,1)S(1)}, bf16[512,512]{1,0:T(8,128)(2,1)}, u32[]{:S(2)}) copy-start(bf16[512,512]{1,0:T(8,128)(2,1)} %param.22) | copy-start | bytes 1572868
  0.6 7.2 %copy-start.8 = (s32[1,192]{1,0:T(1,128)S(1)}, s32[1,192]{1,0:T(1,128)}, u32[]{:S(2)}) copy-start(s32[1,192]{1,0:T(1,128)} %param.19) | copy-start | bytes 2308
  0.7 8.7 %copy-start.12 = (s32[128]{0:T(128)S(1)}, s32[128]{0:T(128)}, u32[]{:S(2)}) copy-start(s32[128]{0:T(128)} %param.18) | copy-start | bytes 1540
  0.7 9.1 %copy-start.3 = (bf16[128,512]{1,0:T(8,128)(2,1)S(1)}, bf16[128,512]{1,0:T(8,128)(2,1)}, u32[]{:S(2)}) copy-start(bf16[128,512]{1,0:T(8,128)(2,1)} %param.16) | copy-start | bytes 393220
  0.7 8.0 %copy-start.9 = (bf16[8,512]{1,0:T(8,128)(2,1)S(1)}, bf16[8,512]{1,0:T(8,128)(2,1)}, u32[]{:S(2)}) copy-start(bf16[8,512]{1,0:T(8,128)(2,1)} %param.26) | copy-start | bytes 24580
  0.7 8.7 %copy-start.7 = (f32[5,512]{1,0:T(8,128)S(1)}, f32[5,512]{1,0:T(8,128)}, u32[]{:S(2)}) copy-start(f32[5,512]{1,0:T(8,128)} %param.24) | copy-start | bytes 30724
  3.5 7.4 %copy-start.10 = (s32[1024]{0:T(1024)S(1)}, s32[1024]{0:T(1024)}, u32[]{:S(2)}) copy-start(s32[1024]{0:T(1024)} %param.20) | copy-start | bytes 12292
  3.5 8.3 %copy-start.2 = (bf16[512,512]{1,0:T(8,128)(2,1)S(1)}, bf16[512,512]{1,0:T(8,128)(2,1)}, u32[]{:S(2)}) copy-start(bf16[512,512]{1,0:T(8,128)(2,1)} %update_ref.1) | copy-start | bytes 1572868
  5.1 7.6 %copy-start.4 = (bf16[512,384]{1,0:T(8,128)(2,1)S(1)}, bf16[512,384]{1,0:T(8,128)(2,1)}, u32[]{:S(2)}) copy-start(bf16[512,384]{1,0:T(8,128)(2,1)} %split_ref.1) | copy-start | bytes 1179652
  5.1 9.5 %collective-permute-start = (bf16[16,640]{1,0:T(8,128)(2,1)S(1)}, bf16[16,640]{1,0:T(8,128)(2,1)S(1)}, u32[]{:S(2)}, u32[]{:S(2)}) collective-permute-start(bf16[16,640]{1,0:T(8,128)(2,1)S(1)} %convolution_convert_fusion.5), channel_id=1, source_target_pairs={{24,0},{0,8},{8,16},{16,24},{25,1},{1,9},{9,17},{17,25},{26,2},{2,... | collective-permute-start | bytes 61448 | tf_op jit(solution)/shard_map/ppermute | solution.py:30
  5.8 8.9 %collective-permute-start.1 = (bf16[16,640]{1,0:T(8,128)(2,1)S(1)}, bf16[16,640]{1,0:T(8,128)(2,1)S(1)}, u32[]{:S(2)}, u32[]{:S(2)}) collective-permute-start(bf16[16,640]{1,0:T(8,128)(2,1)S(1)} %convolution_convert_fusion.4), channel_id=1, source_target_pairs={{8,0},{16,8},{24,16},{0,24},{9,1},{17,9},{25,17},{1,25},{10,2},{18... | collective-permute-start | bytes 61448 | tf_op jit(solution)/shard_map/ppermute | solution.py:30
  7.9 5.9 %copy-start.6 = (bf16[192,512]{1,0:T(8,128)(2,1)S(1)}, bf16[192,512]{1,0:T(8,128)(2,1)}, u32[]{:S(2)}) copy-start(bf16[192,512]{1,0:T(8,128)(2,1)} %tensor_ref.1) | copy-start | bytes 589828
  15.0 5.3 %collective-permute-start.2 = (bf16[64,640]{1,0:T(8,128)(2,1)S(1)}, bf16[64,640]{1,0:T(8,128)(2,1)S(1)}, u32[]{:S(2)}, u32[]{:S(2)}) collective-permute-start(bf16[64,640]{1,0:T(8,128)(2,1)S(1)} %convolution_convert_fusion.1), channel_id=1, source_target_pairs={{4,0},{0,4},{5,1},{1,5},{6,2},{2,6},{7,3},{3,7},{12,8},{8,12},{13,... | collective-permute-start | bytes 245768 | tf_op jit(solution)/shard_map/ppermute | solution.py:30
  17.6 4.5 %collective-permute-start.3 = (bf16[64,640]{1,0:T(8,128)(2,1)S(1)}, bf16[64,640]{1,0:T(8,128)(2,1)S(1)}, u32[]{:S(2)}, u32[]{:S(2)}) collective-permute-start(bf16[64,640]{1,0:T(8,128)(2,1)S(1)} %convolution_convert_fusion), channel_id=1, source_target_pairs={{4,0},{0,4},{5,1},{1,5},{6,2},{2,6},{7,3},{3,7},{12,8},{8,12},{13,... | collective-permute-start | bytes 245768 | tf_op jit(solution)/shard_map/ppermute | solution.py:30
  22.3 5.6 %collective-permute-start.4 = (bf16[16,640]{1,0:T(8,128)(2,1)S(1)}, bf16[16,640]{1,0:T(8,128)(2,1)S(1)}, u32[]{:S(2)}, u32[]{:S(2)}) collective-permute-start(bf16[16,640]{1,0:T(8,128)(2,1)S(1)} %convolution_convert_fusion.3), channel_id=1, source_target_pairs={{3,0},{0,1},{1,2},{2,3},{7,4},{4,5},{5,6},{6,7},{11,8},{8,9},{9,10... | collective-permute-start | bytes 61448 | tf_op jit(solution)/shard_map/ppermute | solution.py:30
  24.2 4.0 %collective-permute-start.5 = (bf16[16,640]{1,0:T(8,128)(2,1)S(1)}, bf16[16,640]{1,0:T(8,128)(2,1)S(1)}, u32[]{:S(2)}, u32[]{:S(2)}) collective-permute-start(bf16[16,640]{1,0:T(8,128)(2,1)S(1)} %convolution_convert_fusion.2), channel_id=1, source_target_pairs={{1,0},{2,1},{3,2},{0,3},{5,4},{6,5},{7,6},{4,7},{9,8},{10,9},{11,1... | collective-permute-start | bytes 61448 | tf_op jit(solution)/shard_map/ppermute | solution.py:30
  29.3 2.4 %copy-start.11 = (f32[512]{0:T(512)S(1)}, f32[512]{0:T(512)}, u32[]{:S(2)}) copy-start(f32[512]{0:T(512)} %param.30) | copy-start | bytes 6148
  46.8 7.8 %copy-start.5 = (f32[512,128]{1,0:T(8,128)S(1)}, f32[512,128]{1,0:T(8,128)}, u32[]{:S(2)}) copy-start(f32[512,128]{1,0:T(8,128)} %get-tuple-element.10) | copy-start | bytes 786436
  46.8 5.7 %collective-permute-start.7 = (bf16[16,640]{1,0:T(8,128)(2,1)S(1)}, bf16[16,640]{1,0:T(8,128)(2,1)S(1)}, u32[]{:S(2)}, u32[]{:S(2)}) collective-permute-start(bf16[16,640]{1,0:T(8,128)(2,1)S(1)} %get-tuple-element.31), channel_id=1, source_target_pairs={{3,0},{0,1},{1,2},{2,3},{7,4},{4,5},{5,6},{6,7},{11,8},{8,9},{9,10... | collective-permute-start | bytes 61448 | tf_op jit(solution)/shard_map/ppermute | solution.py:30
  48.3 4.6 %collective-permute-start.6 = (bf16[16,640]{1,0:T(8,128)(2,1)S(1)}, bf16[16,640]{1,0:T(8,128)(2,1)S(1)}, u32[]{:S(2)}, u32[]{:S(2)}) collective-permute-start(bf16[16,640]{1,0:T(8,128)(2,1)S(1)} %get-tuple-element.30), channel_id=1, source_target_pairs={{1,0},{2,1},{3,2},{0,3},{5,4},{6,5},{7,6},{4,7},{9,8},{10,9},{11,1... | collective-permute-start | bytes 61448 | tf_op jit(solution)/shard_map/ppermute | solution.py:30
  53.3 7.0 %copy-start.13 = (f32[5]{0:T(128)S(1)}, f32[5]{0:T(128)}, u32[]{:S(2)}) copy-start(f32[5]{0:T(128)} %param.31) | copy-start | bytes 64
  53.3 7.0 %copy-start.14 = (f32[8,128]{1,0:T(8,128)S(1)}, f32[8,128]{1,0:T(8,128)}, u32[]{:S(2)}) copy-start(f32[8,128]{1,0:T(8,128)} %get-tuple-element.7) | copy-start | bytes 12292
  53.3 4.5 %collective-permute-start.8 = (bf16[64,640]{1,0:T(8,128)(2,1)S(1)}, bf16[64,640]{1,0:T(8,128)(2,1)S(1)}, u32[]{:S(2)}, u32[]{:S(2)}) collective-permute-start(bf16[64,640]{1,0:T(8,128)(2,1)S(1)} %get-tuple-element.33), channel_id=1, source_target_pairs={{4,0},{0,4},{5,1},{1,5},{6,2},{2,6},{7,3},{3,7},{12,8},{8,12},{13,... | collective-permute-start | bytes 245768 | tf_op jit(solution)/shard_map/ppermute | solution.py:30
  54.6 10.0 %copy-start.1 = (bf16[512,512]{1,0:T(8,128)(2,1)S(1)}, bf16[512,512]{1,0:T(8,128)(2,1)}, u32[]{:S(2)}) copy-start(bf16[512,512]{1,0:T(8,128)(2,1)} %param.23) | copy-start | bytes 1572868
  55.4 4.5 %collective-permute-start.9 = (bf16[64,640]{1,0:T(8,128)(2,1)S(1)}, bf16[64,640]{1,0:T(8,128)(2,1)S(1)}, u32[]{:S(2)}, u32[]{:S(2)}) collective-permute-start(bf16[64,640]{1,0:T(8,128)(2,1)S(1)} %get-tuple-element.32), channel_id=1, source_target_pairs={{4,0},{0,4},{5,1},{1,5},{6,2},{2,6},{7,3},{3,7},{12,8},{8,12},{13,... | collective-permute-start | bytes 245768 | tf_op jit(solution)/shard_map/ppermute | solution.py:30
  60.2 1.5 %collective-permute-start.10 = (bf16[16,640]{1,0:T(8,128)(2,1)S(1)}, bf16[16,640]{1,0:T(8,128)(2,1)S(1)}, u32[]{:S(2)}, u32[]{:S(2)}) collective-permute-start(bf16[16,640]{1,0:T(8,128)(2,1)S(1)} %get-tuple-element.44), channel_id=1, source_target_pairs={{8,0},{16,8},{24,16},{0,24},{9,1},{17,9},{25,17},{1,25},{10,2},{18... | collective-permute-start | bytes 61448 | tf_op jit(solution)/shard_map/ppermute | solution.py:30
  61.1 3.2 %collective-permute-start.11 = (bf16[16,640]{1,0:T(8,128)(2,1)S(1)}, bf16[16,640]{1,0:T(8,128)(2,1)S(1)}, u32[]{:S(2)}, u32[]{:S(2)}) collective-permute-start(bf16[16,640]{1,0:T(8,128)(2,1)S(1)} %get-tuple-element.43), channel_id=1, source_target_pairs={{24,0},{0,8},{8,16},{16,24},{25,1},{1,9},{9,17},{17,25},{26,2},{2,... | collective-permute-start | bytes 61448 | tf_op jit(solution)/shard_map/ppermute | solution.py:30

commit v18 on v17

--- a/solution.py
+++ b/solution.py
@@ -355,9 +355,13 @@
     select = (neighbour[:, None] == jnp.arange(total_rows, dtype=jnp.int32)[None, :]).astype(
         jnp.bfloat16
     )
-    gathered = jnp.einsum("tw,pt->wp", table, select, preferred_element_type=jnp.float32)
-    neigh_cols = gathered[:width].astype(jnp.bfloat16)
-    coords_n = gathered[width : width + 3] * 16.0 + gathered[width + 3 : width + 6]
+    neigh_cols = jnp.einsum(
+        "tw,pt->wp", table[:, :width], select, preferred_element_type=jnp.float32
+    ).astype(jnp.bfloat16)
+    gathered = jnp.einsum(
+        "tw,pt->wp", table[:, width:], select, preferred_element_type=jnp.float32
+    )
+    coords_n = gathered[0:3] * 16.0 + gathered[3:6]
     delta = (coords_n.reshape(3, K, atoms) - positions.astype(jnp.float32)[:, None, :]) * (
         1.0 / 64.0
     )

time: 67.1 us -> 67.3 us (level)
  matrix products: 12.2 us -> 13.6 us
  local copies, waits for them, and re-layouts: 9.35 us -> 8.2 us
    dot_general x1 -> x2, matrix products: 1.04 us -> 2.48 us  [the longest x1 1.92 us: shards(): jnp.einsum('tw,pt->wp', table[:, :width], select, preferred_element_type=...]
    slice x1 -> x0, local copies, waits for them, and re-layouts: 1.15 us -> none  [shards(): neigh_cols = gathered[:width].astype(jnp.bfloat16)]
where the time goes in v18:
time: 67.3 us; the launch traced here: 66.9 us
  starting transfers between devices  15.7 us (23%)
  matrix products  13.6 us (20%)
  waiting for transfers between devices  13.3 us (20%)
  Pallas kernels  9.03 us (13%)
  local copies, waits for them, and re-layouts  8.2 us (12%)
  other arithmetic  5.31 us (8%)
  between operations  1.77 us (3%)
    ppermute x12, starting transfers between devices, passed_along(): return lax.ppermute(block, axis, route)  15.7 us
    ppermute x12, waiting for transfers between devices, passed_along(): return lax.ppermute(block, axis, route)  13.3 us
    pallas_call x1, Pallas kernels, pair_terms(): pl.pallas_call(_pair_kernel, out_shape=(jax.ShapeDtypeStruct((width, pair...  9.03 us
    unnamed x38, local copies, waits for them, and re-layouts  3.57 us
    dot_general x2, matrix products, project(): jnp.dot(rows, weight, preferred_element_type=jnp.float32)  2.42 us
    dot_general x3, matrix products, lookup(): return jnp.dot(onehot, table, precision=lax.Precision.HIGHEST)  2.23 us
    dot_general x6, matrix products, spread(): jnp.einsum('nr,nw->rw', onehot, values.astype(jnp.bfloat16), preferred_el...  2.05 us
    dot_general x1, matrix products, shards(): jnp.einsum('tw,pt->wp', table[:, :width], select, preferred_element_type=...  1.92 us
  transfers between devices with their start and end apart: 12, of which 9 were waited for; matrix products, arithmetic and copies ran while one was open for 14% of the time, Pallas kernels for 0%

profile of v18, /device:TPU:0, one launch (start us, length us, event | category | flops | bytes accessed | tf_op | source)
XLA Modules:
  0.0 66.9 jit_solution(7730592659589811278)
XLA Ops:
  1.6 0.8 %slice_bitcast_fusion = (s32[16]{0:T(128)S(1)}, s32[16]{0:T(128)S(1)}, s32[16]{0:T(128)S(1)}, s32[16]{0:T(128)S(1)}) fusion(s32[1,192]{1,0:T(1,128)} %param.19), kind=kLoop, calls=%fused_computation.189 | loop fusion | bytes 512 | tf_op jit(solution)/shard_map/eq | solution.py:343
  2.4 1.0 %fusion.35 = f32[128,512]{1,0:T(8,128)S(1)} fusion(f32[5,512]{1,0:T(8,128)} %param.25, s32[128]{0:T(128)} %param.18), kind=kOutput, calls=%fused_computation.55 | convolution fusion | flops 3932800 | bytes 272896 | tf_op jit(solution)/shard_map/dot_general | solution.py:306
  3.5 1.4 %fusion.13 = bf16[128,512]{1,0:T(8,128)(2,1)S(1)} fusion(f32[128,512]{1,0:T(8,128)S(1)} %fusion.35, bf16[128,512]{1,0:T(8,128)(2,1)} %param.16, bf16[512,512]{1,0:T(8,128)(2,1)} %param.23), kind=kOutput, calls=%fused_computation.17 | convolution fusion | flops 67239936 | bytes 1048576 | tf_op jit(solution)/shard_map/dot_general | solution.py:310
  5.8 1.9 %collective-permute-start.1 = (bf16[16,640]{1,0:T(8,128)(2,1)S(1)}, bf16[16,640]{1,0:T(8,128)(2,1)S(1)}, u32[]{:S(2)}, u32[]{:S(2)}) collective-permute-start(bf16[16,640]{1,0:T(8,128)(2,1)S(1)} %convolution_convert_fusion.4), channel_id=1, source_target_pairs={{8,0},{16,8},{24,16},{0,24},{9,1},{17,9},{25,17},{1,25},{10,2},{18... | collective-permute-start | bytes 61448 | tf_op jit(solution)/shard_map/ppermute | solution.py:30
  9.8 1.1 %fusion.15.centre_ref = f32[512,128]{1,0:T(8,128)} fusion(f32[512,128]{1,0:T(8,128)S(1)} %convolution_bitcast_fusion, bf16[512,512]{1,0:T(8,128)(2,1)S(1)} %copy-done, bf16[128,512]{1,0:T(8,128)(2,1)S(1)} %copy-done.3), kind=kOutput, calls=%fused_computation.19 | convolution fusion | flops 67305472 | bytes 1179648 | tf_op jit(solution)/shard_map/dot_general | solution.py:310
  11.0 0.8 %copy.58.basis_t_ref = bf16[512,128]{1,0:T(8,128)(2,1)} copy(bf16[512,128]{0,1:T(8,128)(2,1)S(1)} %get-tuple-element.63) | data formatting | bytes 262144 | tf_op jit(solution)/shard_map/transpose | solution.py:256
  11.7 1.0 %copy.56 = bf16[512,512]{0,1:T(8,128)(2,1)} copy(bf16[512,512]{1,0:T(8,128)(2,1)S(1)} %copy-done.2) | data formatting | bytes 1048576 | tf_op args[12]
  12.7 1.0 %copy.55 = bf16[512,384]{0,1:T(8,128)(2,1)} copy(bf16[512,384]{1,0:T(8,128)(2,1)S(1)} %copy-done.4) | data formatting | bytes 786432 | tf_op args[11]
  13.7 0.8 %copy.57 = bf16[192,512]{0,1:T(8,128)(2,1)} copy(bf16[192,512]{1,0:T(8,128)(2,1)S(1)} %copy-done.6) | data formatting | bytes 393216 | tf_op args[13]
  14.9 2.4 %collective-permute-start.2 = (bf16[64,640]{1,0:T(8,128)(2,1)S(1)}, bf16[64,640]{1,0:T(8,128)(2,1)S(1)}, u32[]{:S(2)}, u32[]{:S(2)}) collective-permute-start(bf16[64,640]{1,0:T(8,128)(2,1)S(1)} %convolution_convert_fusion.1), channel_id=1, source_target_pairs={{4,0},{0,4},{5,1},{1,5},{6,2},{2,6},{7,3},{3,7},{12,8},{8,12},{13,... | collective-permute-start | bytes 245768 | tf_op jit(solution)/shard_map/ppermute | solution.py:30
  17.6 2.6 %collective-permute-done.2 = bf16[64,640]{1,0:T(8,128)(2,1)S(1)} collective-permute-done((bf16[64,640]{1,0:T(8,128)(2,1)S(1)}, bf16[64,640]{1,0:T(8,128)(2,1)S(1)}, u32[]{:S(2)}, u32[]{:S(2)}) %collective-permute-start.2) | collective-permute-done | bytes 81952 | tf_op jit(solution)/shard_map/ppermute | solution.py:30
  20.3 1.8 %collective-permute-done.3 = bf16[64,640]{1,0:T(8,128)(2,1)S(1)} collective-permute-done((bf16[64,640]{1,0:T(8,128)(2,1)S(1)}, bf16[64,640]{1,0:T(8,128)(2,1)S(1)}, u32[]{:S(2)}, u32[]{:S(2)}) %collective-permute-start.3) | collective-permute-done | bytes 81952 | tf_op jit(solution)/shard_map/ppermute | solution.py:30
  22.3 1.6 %collective-permute-start.4 = (bf16[16,640]{1,0:T(8,128)(2,1)S(1)}, bf16[16,640]{1,0:T(8,128)(2,1)S(1)}, u32[]{:S(2)}, u32[]{:S(2)}) collective-permute-start(bf16[16,640]{1,0:T(8,128)(2,1)S(1)} %convolution_convert_fusion.3), channel_id=1, source_target_pairs={{3,0},{0,1},{1,2},{2,3},{7,4},{4,5},{5,6},{6,7},{11,8},{8,9},{9,10... | collective-permute-start | bytes 61448 | tf_op jit(solution)/shard_map/ppermute | solution.py:30
  24.1 2.3 %collective-permute-start.5 = (bf16[16,640]{1,0:T(8,128)(2,1)S(1)}, bf16[16,640]{1,0:T(8,128)(2,1)S(1)}, u32[]{:S(2)}, u32[]{:S(2)}) collective-permute-start(bf16[16,640]{1,0:T(8,128)(2,1)S(1)} %convolution_convert_fusion.2), channel_id=1, source_target_pairs={{1,0},{2,1},{3,2},{0,3},{5,4},{6,5},{7,6},{4,7},{9,8},{10,9},{11,1... | collective-permute-start | bytes 61448 | tf_op jit(solution)/shard_map/ppermute | solution.py:30
  26.4 1.5 %collective-permute-done.4 = bf16[16,640]{1,0:T(8,128)(2,1)S(1)} collective-permute-done((bf16[16,640]{1,0:T(8,128)(2,1)S(1)}, bf16[16,640]{1,0:T(8,128)(2,1)S(1)}, u32[]{:S(2)}, u32[]{:S(2)}) %collective-permute-start.4) | collective-permute-done | bytes 20512 | tf_op jit(solution)/shard_map/ppermute | solution.py:30
  28.7 1.9 %fusion.3.rows_ref = bf16[512,1024]{1,0:T(8,128)(2,1)} fusion(s32[1024]{0:T(1024)S(1)} %bitcast.179, bf16[320,640]{1,0:T(8,128)(2,1)S(1)} %constant_dynamic-update-slice_fusion.3), kind=kOutput, calls=%fused_computation.4 | convolution fusion | flops 336396288 | bytes 1380352 | tf_op jit(solution)/shard_map/tw,pt->wp/dot_general | solution.py:358
  31.1 0.9 %concatenate.62.geo_ref = f32[128,1024]{1,0:T(8,128)} pad(f32[18,1024]{1,0:T(8,128)S(1)} %concatenate.61, f32[]{:T(128)} %constant.28.clone.1), padding=0_110x0_0 | pad | bytes 598020 | tf_op jit(solution)/shard_map/jvp()/concatenate | solution.py:80
  31.9 0.8 %broadcast_in_dim.99.energy_w_ref = f32[512,128]{1,0:T(8,128)} broadcast(f32[512]{0:T(512)S(1)} %copy-done.11), dimensions={0} | broadcast | bytes 264192 | tf_op jit(solution)/shard_map/broadcast_in_dim | solution.py:264
  32.8 9.0 %shard_map.175 = (f32[512,1024]{1,0:T(8,128)}, f32[512,128]{1,0:T(8,128)}, f32[128,1024]{1,0:T(8,128)}, f32[8,128]{1,0:T(8,128)}) custom-call(bf16[512,1024]{1,0:T(8,128)(2,1)} %fusion.3.rows_ref, f32[512,128]{1,0:T(8,128)} %fusion.15.centre_ref, f32[128,1024]{1,0:T(8,128)} %concatenate.62.geo_ref, bf16[512,128]{1,0:T(8,128)(2,1)} %copy.58.basis_t_ref, ...), custom_call_target="tpu_custom_call" | custom-call | flops 1610612736 | bytes 8388608 | tf_op jit(solution)/shard_map/pallas_call | solution.py:226
  41.8 1.2 %slice_multiply_fusion.4 = (f32[1,1024]{1,0:T(1,128)S(1)}, f32[1,1024]{1,0:T(1,128)S(1)}, f32[1,1024]{1,0:T(1,128)S(1)}, f32[1,1024]{1,0:T(1,128)S(1)}, f32[1,10...) fusion(f32[128,1024]{1,0:T(8,128)} %get-tuple-element.9), kind=kLoop, calls=%fused_computation.153 | loop fusion | flops 5120 | bytes 73728 | tf_op jit(solution)/shard_map/transpose(jvp())/mul | solution.py:70
  43.0 1.0 %fusion.38 = (f32[1024]{0:T(1024)S(1)}, f32[1024]{0:T(1024)S(1)}) fusion(f32[128,1024]{1,0:T(8,128)} %get-tuple-element.9, f32[1024]{0:T(1024)S(1)} %get-tuple-element.67, f32[8]{0:T(128)S(1)} %convert_multiply_fusion, f32[1024]{0:T(1024)S(1)} %get-tuple-element.66), kind=kLoop, calls=%fused_computation.61 | loop fusion | flops 55296 | bytes 49184 | tf_op jit(solution)/shard_map/transpose(jvp())/reduce_sum | solution.py:58
  44.0 1.8 %convert.17 = bf16[512,1024]{1,0:T(8,128)(2,1)S(1)} convert(f32[512,1024]{1,0:T(8,128)} %get-tuple-element.8) | non-fusion elementwise | flops 524288 | bytes 3145728 | tf_op jit(solution)/shard_map/convert
  46.0 1.1 %fusion.9 = f32[320,640]{1,0:T(8,128)S(1)} fusion(bf16[3,1024]{1,0:T(4,128)(2,1)S(1)} %bitcast.177, bf16[512,1024]{1,0:T(8,128)(2,1)S(1)} %convert.17, f32[128,3]{1,0:T(8,128)S(1)} %bitcast.156, s32[1024]{0:T(1024)S(1)} %bitcast.180, bf16[640]{0:T(1024)(128)(2,1)S(1)} %pad.21.clone), kind=kOutput, calls=%fused_computation.10 | convolution fusion | flops 424222720 | bytes 1880832 | tf_op jit(solution)/shard_map/wn,nr->wr/dot_general | solution.py:314
  47.1 1.5 %collective-permute-start.7 = (bf16[16,640]{1,0:T(8,128)(2,1)S(1)}, bf16[16,640]{1,0:T(8,128)(2,1)S(1)}, u32[]{:S(2)}, u32[]{:S(2)}) collective-permute-start(bf16[16,640]{1,0:T(8,128)(2,1)S(1)} %get-tuple-element.29), channel_id=1, source_target_pairs={{3,0},{0,1},{1,2},{2,3},{7,4},{4,5},{5,6},{6,7},{11,8},{8,9},{9,10... | collective-permute-start | bytes 61448 | tf_op jit(solution)/shard_map/ppermute | solution.py:30
  48.5 2.7 %collective-permute-start.6 = (bf16[16,640]{1,0:T(8,128)(2,1)S(1)}, bf16[16,640]{1,0:T(8,128)(2,1)S(1)}, u32[]{:S(2)}, u32[]{:S(2)}) collective-permute-start(bf16[16,640]{1,0:T(8,128)(2,1)S(1)} %get-tuple-element.28), channel_id=1, source_target_pairs={{1,0},{2,1},{3,2},{0,3},{5,4},{6,5},{7,6},{4,7},{9,8},{10,9},{11,1... | collective-permute-start | bytes 61448 | tf_op jit(solution)/shard_map/ppermute | solution.py:30
  51.2 1.5 %collective-permute-done.7 = bf16[16,640]{1,0:T(8,128)(2,1)S(1)} collective-permute-done((bf16[16,640]{1,0:T(8,128)(2,1)S(1)}, bf16[16,640]{1,0:T(8,128)(2,1)S(1)}, u32[]{:S(2)}, u32[]{:S(2)}) %collective-permute-start.7) | collective-permute-done | bytes 20512 | tf_op jit(solution)/shard_map/ppermute | solution.py:30
  53.6 1.3 %collective-permute-start.8 = (bf16[64,640]{1,0:T(8,128)(2,1)S(1)}, bf16[64,640]{1,0:T(8,128)(2,1)S(1)}, u32[]{:S(2)}, u32[]{:S(2)}) collective-permute-start(bf16[64,640]{1,0:T(8,128)(2,1)S(1)} %get-tuple-element.31), channel_id=1, source_target_pairs={{4,0},{0,4},{5,1},{1,5},{6,2},{2,6},{7,3},{3,7},{12,8},{8,12},{13,... | collective-permute-start | bytes 245768 | tf_op jit(solution)/shard_map/ppermute | solution.py:30
  55.6 0.9 %collective-permute-start.9 = (bf16[64,640]{1,0:T(8,128)(2,1)S(1)}, bf16[64,640]{1,0:T(8,128)(2,1)S(1)}, u32[]{:S(2)}, u32[]{:S(2)}) collective-permute-start(bf16[64,640]{1,0:T(8,128)(2,1)S(1)} %get-tuple-element.30), channel_id=1, source_target_pairs={{4,0},{0,4},{5,1},{1,5},{6,2},{2,6},{7,3},{3,7},{12,8},{8,12},{13,... | collective-permute-start | bytes 245768 | tf_op jit(solution)/shard_map/ppermute | solution.py:30
  56.5 1.6 %collective-permute-done.8 = bf16[64,640]{1,0:T(8,128)(2,1)S(1)} collective-permute-done((bf16[64,640]{1,0:T(8,128)(2,1)S(1)}, bf16[64,640]{1,0:T(8,128)(2,1)S(1)}, u32[]{:S(2)}, u32[]{:S(2)}) %collective-permute-start.8) | collective-permute-done | bytes 81952 | tf_op jit(solution)/shard_map/ppermute | solution.py:30
  58.4 1.7 %collective-permute-done.9 = bf16[64,640]{1,0:T(8,128)(2,1)S(1)} collective-permute-done((bf16[64,640]{1,0:T(8,128)(2,1)S(1)}, bf16[64,640]{1,0:T(8,128)(2,1)S(1)}, u32[]{:S(2)}, u32[]{:S(2)}) %collective-permute-start.9) | collective-permute-done | bytes 81952 | tf_op jit(solution)/shard_map/ppermute | solution.py:30
  62.3 2.2 %collective-permute-done.11 = bf16[16,640]{1,0:T(8,128)(2,1)S(1)} collective-permute-done((bf16[16,640]{1,0:T(8,128)(2,1)S(1)}, bf16[16,640]{1,0:T(8,128)(2,1)S(1)}, u32[]{:S(2)}, u32[]{:S(2)}) %collective-permute-start.11) | collective-permute-done | bytes 20512 | tf_op jit(solution)/shard_map/ppermute | solution.py:30
  64.9 1.4 %convolution_add_fusion.1 = f32[128,512]{1,0:T(8,128)} fusion(f32[128,512]{1,0:T(8,128)S(1)} %fusion.110, bf16[512,512]{1,0:T(8,128)(2,1)S(1)} %copy-done.1, f32[128,640]{1,0:T(8,128)S(1)} %fusion.24), kind=kOutput, calls=%fused_computation.13 | convolution fusion | flops 402718720 | bytes 1310720 | tf_op jit(solution)/shard_map/dot_general | solution.py:410
  (104 shorter events, 10.8 us)
Async XLA Ops:
  0.6 9.1 %copy-start = (bf16[512,512]{1,0:T(8,128)(2,1)S(1)}, bf16[512,512]{1,0:T(8,128)(2,1)}, u32[]{:S(2)}) copy-start(bf16[512,512]{1,0:T(8,128)(2,1)} %param.22) | copy-start | bytes 1572868
  0.6 7.2 %copy-start.8 = (s32[1,192]{1,0:T(1,128)S(1)}, s32[1,192]{1,0:T(1,128)}, u32[]{:S(2)}) copy-start(s32[1,192]{1,0:T(1,128)} %param.19) | copy-start | bytes 2308
  0.7 8.6 %copy-start.12 = (s32[128]{0:T(128)S(1)}, s32[128]{0:T(128)}, u32[]{:S(2)}) copy-start(s32[128]{0:T(128)} %param.18) | copy-start | bytes 1540
  0.7 7.9 %copy-start.9 = (bf16[8,512]{1,0:T(8,128)(2,1)S(1)}, bf16[8,512]{1,0:T(8,128)(2,1)}, u32[]{:S(2)}) copy-start(bf16[8,512]{1,0:T(8,128)(2,1)} %param.26) | copy-start | bytes 24580
  0.7 8.6 %copy-start.7 = (f32[5,512]{1,0:T(8,128)S(1)}, f32[5,512]{1,0:T(8,128)}, u32[]{:S(2)}) copy-start(f32[5,512]{1,0:T(8,128)} %param.24) | copy-start | bytes 30724
  3.5 6.3 %copy-start.3 = (bf16[128,512]{1,0:T(8,128)(2,1)S(1)}, bf16[128,512]{1,0:T(8,128)(2,1)}, u32[]{:S(2)}) copy-start(bf16[128,512]{1,0:T(8,128)(2,1)} %param.16) | copy-start | bytes 393220
  4.9 6.0 %copy-start.10 = (s32[1024]{0:T(1024)S(1)}, s32[1024]{0:T(1024)}, u32[]{:S(2)}) copy-start(s32[1024]{0:T(1024)} %param.20) | copy-start | bytes 12292
  5.1 6.7 %copy-start.2 = (bf16[512,512]{1,0:T(8,128)(2,1)S(1)}, bf16[512,512]{1,0:T(8,128)(2,1)}, u32[]{:S(2)}) copy-start(bf16[512,512]{1,0:T(8,128)(2,1)} %update_ref.1) | copy-start | bytes 1572868
  5.1 9.6 %collective-permute-start = (bf16[16,640]{1,0:T(8,128)(2,1)S(1)}, bf16[16,640]{1,0:T(8,128)(2,1)S(1)}, u32[]{:S(2)}, u32[]{:S(2)}) collective-permute-start(bf16[16,640]{1,0:T(8,128)(2,1)S(1)} %convolution_convert_fusion.5), channel_id=1, source_target_pairs={{24,0},{0,8},{8,16},{16,24},{25,1},{1,9},{9,17},{17,25},{26,2},{2,... | collective-permute-start | bytes 61448 | tf_op jit(solution)/shard_map/ppermute | solution.py:30
  5.8 8.9 %collective-permute-start.1 = (bf16[16,640]{1,0:T(8,128)(2,1)S(1)}, bf16[16,640]{1,0:T(8,128)(2,1)S(1)}, u32[]{:S(2)}, u32[]{:S(2)}) collective-permute-start(bf16[16,640]{1,0:T(8,128)(2,1)S(1)} %convolution_convert_fusion.4), channel_id=1, source_target_pairs={{8,0},{16,8},{24,16},{0,24},{9,1},{17,9},{25,17},{1,25},{10,2},{18... | collective-permute-start | bytes 61448 | tf_op jit(solution)/shard_map/ppermute | solution.py:30
  8.6 4.1 %copy-start.4 = (bf16[512,384]{1,0:T(8,128)(2,1)S(1)}, bf16[512,384]{1,0:T(8,128)(2,1)}, u32[]{:S(2)}) copy-start(bf16[512,384]{1,0:T(8,128)(2,1)} %split_ref.1) | copy-start | bytes 1179652
  9.8 4.0 %copy-start.6 = (bf16[192,512]{1,0:T(8,128)(2,1)S(1)}, bf16[192,512]{1,0:T(8,128)(2,1)}, u32[]{:S(2)}) copy-start(bf16[192,512]{1,0:T(8,128)(2,1)} %tensor_ref.1) | copy-start | bytes 589828
  14.9 5.3 %collective-permute-start.2 = (bf16[64,640]{1,0:T(8,128)(2,1)S(1)}, bf16[64,640]{1,0:T(8,128)(2,1)S(1)}, u32[]{:S(2)}, u32[]{:S(2)}) collective-permute-start(bf16[64,640]{1,0:T(8,128)(2,1)S(1)} %convolution_convert_fusion.1), channel_id=1, source_target_pairs={{4,0},{0,4},{5,1},{1,5},{6,2},{2,6},{7,3},{3,7},{12,8},{8,12},{13,... | collective-permute-start | bytes 245768 | tf_op jit(solution)/shard_map/ppermute | solution.py:30
  17.5 4.5 %collective-permute-start.3 = (bf16[64,640]{1,0:T(8,128)(2,1)S(1)}, bf16[64,640]{1,0:T(8,128)(2,1)S(1)}, u32[]{:S(2)}, u32[]{:S(2)}) collective-permute-start(bf16[64,640]{1,0:T(8,128)(2,1)S(1)} %convolution_convert_fusion), channel_id=1, source_target_pairs={{4,0},{0,4},{5,1},{1,5},{6,2},{2,6},{7,3},{3,7},{12,8},{8,12},{13,... | collective-permute-start | bytes 245768 | tf_op jit(solution)/shard_map/ppermute | solution.py:30
  22.3 5.6 %collective-permute-start.4 = (bf16[16,640]{1,0:T(8,128)(2,1)S(1)}, bf16[16,640]{1,0:T(8,128)(2,1)S(1)}, u32[]{:S(2)}, u32[]{:S(2)}) collective-permute-start(bf16[16,640]{1,0:T(8,128)(2,1)S(1)} %convolution_convert_fusion.3), channel_id=1, source_target_pairs={{3,0},{0,1},{1,2},{2,3},{7,4},{4,5},{5,6},{6,7},{11,8},{8,9},{9,10... | collective-permute-start | bytes 61448 | tf_op jit(solution)/shard_map/ppermute | solution.py:30
  24.1 4.0 %collective-permute-start.5 = (bf16[16,640]{1,0:T(8,128)(2,1)S(1)}, bf16[16,640]{1,0:T(8,128)(2,1)S(1)}, u32[]{:S(2)}, u32[]{:S(2)}) collective-permute-start(bf16[16,640]{1,0:T(8,128)(2,1)S(1)} %convolution_convert_fusion.2), channel_id=1, source_target_pairs={{1,0},{2,1},{3,2},{0,3},{5,4},{6,5},{7,6},{4,7},{9,8},{10,9},{11,1... | collective-permute-start | bytes 61448 | tf_op jit(solution)/shard_map/ppermute | solution.py:30
  28.7 3.2 %copy-start.11 = (f32[512]{0:T(512)S(1)}, f32[512]{0:T(512)}, u32[]{:S(2)}) copy-start(f32[512]{0:T(512)} %param.30) | copy-start | bytes 6148
  47.1 5.7 %collective-permute-start.7 = (bf16[16,640]{1,0:T(8,128)(2,1)S(1)}, bf16[16,640]{1,0:T(8,128)(2,1)S(1)}, u32[]{:S(2)}, u32[]{:S(2)}) collective-permute-start(bf16[16,640]{1,0:T(8,128)(2,1)S(1)} %get-tuple-element.29), channel_id=1, source_target_pairs={{3,0},{0,1},{1,2},{2,3},{7,4},{4,5},{5,6},{6,7},{11,8},{8,9},{9,10... | collective-permute-start | bytes 61448 | tf_op jit(solution)/shard_map/ppermute | solution.py:30
  48.5 6.3 %copy-start.5 = (f32[512,128]{1,0:T(8,128)S(1)}, f32[512,128]{1,0:T(8,128)}, u32[]{:S(2)}) copy-start(f32[512,128]{1,0:T(8,128)} %get-tuple-element.10) | copy-start | bytes 786436
  48.5 4.6 %collective-permute-start.6 = (bf16[16,640]{1,0:T(8,128)(2,1)S(1)}, bf16[16,640]{1,0:T(8,128)(2,1)S(1)}, u32[]{:S(2)}, u32[]{:S(2)}) collective-permute-start(bf16[16,640]{1,0:T(8,128)(2,1)S(1)} %get-tuple-element.28), channel_id=1, source_target_pairs={{1,0},{2,1},{3,2},{0,3},{5,4},{6,5},{7,6},{4,7},{9,8},{10,9},{11,1... | collective-permute-start | bytes 61448 | tf_op jit(solution)/shard_map/ppermute | solution.py:30
  53.5 7.0 %copy-start.13 = (f32[5]{0:T(128)S(1)}, f32[5]{0:T(128)}, u32[]{:S(2)}) copy-start(f32[5]{0:T(128)} %param.31) | copy-start | bytes 64
  53.5 7.0 %copy-start.14 = (f32[8,128]{1,0:T(8,128)S(1)}, f32[8,128]{1,0:T(8,128)}, u32[]{:S(2)}) copy-start(f32[8,128]{1,0:T(8,128)} %get-tuple-element.7) | copy-start | bytes 12292
  53.6 4.5 %collective-permute-start.8 = (bf16[64,640]{1,0:T(8,128)(2,1)S(1)}, bf16[64,640]{1,0:T(8,128)(2,1)S(1)}, u32[]{:S(2)}, u32[]{:S(2)}) collective-permute-start(bf16[64,640]{1,0:T(8,128)(2,1)S(1)} %get-tuple-element.31), channel_id=1, source_target_pairs={{4,0},{0,4},{5,1},{1,5},{6,2},{2,6},{7,3},{3,7},{12,8},{8,12},{13,... | collective-permute-start | bytes 245768 | tf_op jit(solution)/shard_map/ppermute | solution.py:30
  55.6 4.5 %collective-permute-start.9 = (bf16[64,640]{1,0:T(8,128)(2,1)S(1)}, bf16[64,640]{1,0:T(8,128)(2,1)S(1)}, u32[]{:S(2)}, u32[]{:S(2)}) collective-permute-start(bf16[64,640]{1,0:T(8,128)(2,1)S(1)} %get-tuple-element.30), channel_id=1, source_target_pairs={{4,0},{0,4},{5,1},{1,5},{6,2},{2,6},{7,3},{3,7},{12,8},{8,12},{13,... | collective-permute-start | bytes 245768 | tf_op jit(solution)/shard_map/ppermute | solution.py:30
  58.4 6.5 %copy-start.1 = (bf16[512,512]{1,0:T(8,128)(2,1)S(1)}, bf16[512,512]{1,0:T(8,128)(2,1)}, u32[]{:S(2)}) copy-start(bf16[512,512]{1,0:T(8,128)(2,1)} %param.23) | copy-start | bytes 1572868
  60.5 1.5 %collective-permute-start.10 = (bf16[16,640]{1,0:T(8,128)(2,1)S(1)}, bf16[16,640]{1,0:T(8,128)(2,1)S(1)}, u32[]{:S(2)}, u32[]{:S(2)}) collective-permute-start(bf16[16,640]{1,0:T(8,128)(2,1)S(1)} %get-tuple-element.44), channel_id=1, source_target_pairs={{8,0},{16,8},{24,16},{0,24},{9,1},{17,9},{25,17},{1,25},{10,2},{18... | collective-permute-start | bytes 61448 | tf_op jit(solution)/shard_map/ppermute | solution.py:30
  61.3 3.2 %collective-permute-start.11 = (bf16[16,640]{1,0:T(8,128)(2,1)S(1)}, bf16[16,640]{1,0:T(8,128)(2,1)S(1)}, u32[]{:S(2)}, u32[]{:S(2)}) collective-permute-start(bf16[16,640]{1,0:T(8,128)(2,1)S(1)} %get-tuple-element.43), channel_id=1, source_target_pairs={{24,0},{0,8},{8,16},{16,24},{25,1},{1,9},{9,17},{17,25},{26,2},{2,... | collective-permute-start | bytes 61448 | tf_op jit(solution)/shard_map/ppermute | solution.py:30

commit v19 on v17

--- a/solution.py
+++ b/solution.py
@@ -207,7 +207,7 @@
         dgeo = dgeo + jnp.where(sub == 8, jnp.sum(dhidden * act, axis=0, keepdims=True), 0.0)
         dpre = dhidden * envelope * (sig * (1.0 + pre * (1.0 - sig)))
         grad_rows_ref[:, at] = dpre
-        dgeo = dgeo + split_mm(basis_ref[...], dpre)
+        dgeo = dgeo + _mm(basis_ref[...], dpre.astype(bf16))
         grad_geo_ref[:, at] = dgeo
         return centre_grad + fold(dpre)
 

time: 67.1 us -> 67.1 us (level)
  no operation moved by 1% of the time
where the time goes in v19:
time: 67.1 us; the launch traced here: 66.6 us
  starting transfers between devices  15.7 us (23%)
  waiting for transfers between devices  13.3 us (20%)
  matrix products  12.2 us (18%)
  local copies, waits for them, and re-layouts  9.35 us (14%)
  Pallas kernels  9.02 us (13%)
  other arithmetic  5.34 us (8%)
  between operations  1.77 us (3%)
    ppermute x12, starting transfers between devices, passed_along(): return lax.ppermute(block, axis, route)  15.7 us
    ppermute x12, waiting for transfers between devices, passed_along(): return lax.ppermute(block, axis, route)  13.3 us
    pallas_call x1, Pallas kernels, pair_terms(): pl.pallas_call(_pair_kernel, out_shape=(jax.ShapeDtypeStruct((width, pair...  9.02 us
    unnamed x38, local copies, waits for them, and re-layouts  3.57 us
    dot_general x2, matrix products, project(): jnp.dot(rows, weight, preferred_element_type=jnp.float32)  2.44 us
    dot_general x3, matrix products, lookup(): return jnp.dot(onehot, table, precision=lax.Precision.HIGHEST)  2.23 us
    dot_general x6, matrix products, spread(): jnp.einsum('nr,nw->rw', onehot, values.astype(jnp.bfloat16), preferred_el...  2.05 us
    another operation x1, other arithmetic  1.75 us
  transfers between devices with their start and end apart: 12, of which 9 were waited for; matrix products, arithmetic and copies ran while one was open for 14% of the time, Pallas kernels for 0%

profile of v19, /device:TPU:0, one launch (start us, length us, event | category | flops | bytes accessed | tf_op | source)
XLA Modules:
  0.0 66.6 jit_solution(349354476788488422)
XLA Ops:
  1.7 0.8 %slice_bitcast_fusion = (s32[16]{0:T(128)S(1)}, s32[16]{0:T(128)S(1)}, s32[16]{0:T(128)S(1)}, s32[16]{0:T(128)S(1)}) fusion(s32[1,192]{1,0:T(1,128)} %param.19), kind=kLoop, calls=%fused_computation.185 | loop fusion | bytes 512 | tf_op jit(solution)/shard_map/eq | solution.py:343
  2.5 1.0 %fusion.30 = f32[128,512]{1,0:T(8,128)S(1)} fusion(f32[5,512]{1,0:T(8,128)} %param.25, s32[128]{0:T(128)} %param.18), kind=kOutput, calls=%fused_computation.51 | convolution fusion | flops 3932800 | bytes 272896 | tf_op jit(solution)/shard_map/dot_general | solution.py:306
  3.5 1.4 %fusion.11 = bf16[128,512]{1,0:T(8,128)(2,1)S(1)} fusion(f32[128,512]{1,0:T(8,128)S(1)} %fusion.30, bf16[128,512]{1,0:T(8,128)(2,1)} %param.16, bf16[512,512]{1,0:T(8,128)(2,1)} %param.23), kind=kOutput, calls=%fused_computation.16 | convolution fusion | flops 67239936 | bytes 1048576 | tf_op jit(solution)/shard_map/dot_general | solution.py:310
  5.8 1.9 %collective-permute-start.1 = (bf16[16,640]{1,0:T(8,128)(2,1)S(1)}, bf16[16,640]{1,0:T(8,128)(2,1)S(1)}, u32[]{:S(2)}, u32[]{:S(2)}) collective-permute-start(bf16[16,640]{1,0:T(8,128)(2,1)S(1)} %convolution_convert_fusion.4), channel_id=1, source_target_pairs={{8,0},{16,8},{24,16},{0,24},{9,1},{17,9},{25,17},{1,25},{10,2},{18... | collective-permute-start | bytes 61448 | tf_op jit(solution)/shard_map/ppermute | solution.py:30
  9.8 1.0 %fusion.13.centre_ref = f32[512,128]{1,0:T(8,128)} fusion(f32[512,128]{1,0:T(8,128)S(1)} %convolution_bitcast_fusion, bf16[512,512]{1,0:T(8,128)(2,1)S(1)} %copy-done, bf16[128,512]{1,0:T(8,128)(2,1)S(1)} %copy-done.3), kind=kOutput, calls=%fused_computation.18 | convolution fusion | flops 67305472 | bytes 1179648 | tf_op jit(solution)/shard_map/dot_general | solution.py:310
  11.8 1.0 %copy.56 = bf16[512,512]{0,1:T(8,128)(2,1)} copy(bf16[512,512]{1,0:T(8,128)(2,1)S(1)} %copy-done.2) | data formatting | bytes 1048576 | tf_op args[12]
  12.8 1.0 %copy.55 = bf16[512,384]{0,1:T(8,128)(2,1)} copy(bf16[512,384]{1,0:T(8,128)(2,1)S(1)} %copy-done.4) | data formatting | bytes 786432 | tf_op args[11]
  13.8 0.8 %copy.57 = bf16[192,512]{0,1:T(8,128)(2,1)} copy(bf16[192,512]{1,0:T(8,128)(2,1)S(1)} %copy-done.6) | data formatting | bytes 393216 | tf_op args[13]
  15.0 2.4 %collective-permute-start.2 = (bf16[64,640]{1,0:T(8,128)(2,1)S(1)}, bf16[64,640]{1,0:T(8,128)(2,1)S(1)}, u32[]{:S(2)}, u32[]{:S(2)}) collective-permute-start(bf16[64,640]{1,0:T(8,128)(2,1)S(1)} %convolution_convert_fusion.1), channel_id=1, source_target_pairs={{4,0},{0,4},{5,1},{1,5},{6,2},{2,6},{7,3},{3,7},{12,8},{8,12},{13,... | collective-permute-start | bytes 245768 | tf_op jit(solution)/shard_map/ppermute | solution.py:30
  17.7 2.6 %collective-permute-done.2 = bf16[64,640]{1,0:T(8,128)(2,1)S(1)} collective-permute-done((bf16[64,640]{1,0:T(8,128)(2,1)S(1)}, bf16[64,640]{1,0:T(8,128)(2,1)S(1)}, u32[]{:S(2)}, u32[]{:S(2)}) %collective-permute-start.2) | collective-permute-done | bytes 81952 | tf_op jit(solution)/shard_map/ppermute | solution.py:30
  20.3 1.8 %collective-permute-done.3 = bf16[64,640]{1,0:T(8,128)(2,1)S(1)} collective-permute-done((bf16[64,640]{1,0:T(8,128)(2,1)S(1)}, bf16[64,640]{1,0:T(8,128)(2,1)S(1)}, u32[]{:S(2)}, u32[]{:S(2)}) %collective-permute-start.3) | collective-permute-done | bytes 81952 | tf_op jit(solution)/shard_map/ppermute | solution.py:30
  22.3 1.6 %collective-permute-start.4 = (bf16[16,640]{1,0:T(8,128)(2,1)S(1)}, bf16[16,640]{1,0:T(8,128)(2,1)S(1)}, u32[]{:S(2)}, u32[]{:S(2)}) collective-permute-start(bf16[16,640]{1,0:T(8,128)(2,1)S(1)} %convolution_convert_fusion.3), channel_id=1, source_target_pairs={{3,0},{0,1},{1,2},{2,3},{7,4},{4,5},{5,6},{6,7},{11,8},{8,9},{9,10... | collective-permute-start | bytes 61448 | tf_op jit(solution)/shard_map/ppermute | solution.py:30
  24.2 2.3 %collective-permute-start.5 = (bf16[16,640]{1,0:T(8,128)(2,1)S(1)}, bf16[16,640]{1,0:T(8,128)(2,1)S(1)}, u32[]{:S(2)}, u32[]{:S(2)}) collective-permute-start(bf16[16,640]{1,0:T(8,128)(2,1)S(1)} %convolution_convert_fusion.2), channel_id=1, source_target_pairs={{1,0},{2,1},{3,2},{0,3},{5,4},{6,5},{7,6},{4,7},{9,8},{10,9},{11,1... | collective-permute-start | bytes 61448 | tf_op jit(solution)/shard_map/ppermute | solution.py:30
  26.5 1.5 %collective-permute-done.4 = bf16[16,640]{1,0:T(8,128)(2,1)S(1)} collective-permute-done((bf16[16,640]{1,0:T(8,128)(2,1)S(1)}, bf16[16,640]{1,0:T(8,128)(2,1)S(1)}, u32[]{:S(2)}, u32[]{:S(2)}) %collective-permute-start.4) | collective-permute-done | bytes 20512 | tf_op jit(solution)/shard_map/ppermute | solution.py:30
  28.2 1.0 %fusion.1 = f32[640,1024]{1,0:T(8,128)S(1)} fusion(bf16[320,640]{1,0:T(8,128)(2,1)S(1)} %constant_dynamic-update-slice_fusion.3, s32[1024]{0:T(1024)S(1)} %bitcast.159), kind=kOutput, calls=%fused_computation.3 | convolution fusion | flops 419758080 | bytes 3035136 | tf_op jit(solution)/shard_map/tw,pt->wp/dot_general | solution.py:358
  29.3 1.1 %slice.197.rows_ref = bf16[512,1024]{1,0:T(8,128)(2,1)} slice(f32[640,1024]{1,0:T(8,128)S(1)} %fusion.1), slice={[0:512], [0:1024]} | slice | bytes 2097152 | tf_op jit(solution)/shard_map/slice | solution.py:359
  30.8 0.9 %concatenate.62.geo_ref = f32[128,1024]{1,0:T(8,128)} pad(f32[18,1024]{1,0:T(8,128)S(1)} %concatenate.61, f32[]{:T(128)} %constant.28.clone.1), padding=0_110x0_0 | pad | bytes 598020 | tf_op jit(solution)/shard_map/jvp()/concatenate | solution.py:80
  31.7 0.8 %broadcast_in_dim.99.energy_w_ref = f32[512,128]{1,0:T(8,128)} broadcast(f32[512]{0:T(512)S(1)} %copy-done.11), dimensions={0} | broadcast | bytes 264192 | tf_op jit(solution)/shard_map/broadcast_in_dim | solution.py:264
  32.5 9.0 %shard_map.175 = (f32[512,1024]{1,0:T(8,128)}, f32[512,128]{1,0:T(8,128)}, f32[128,1024]{1,0:T(8,128)}, f32[8,128]{1,0:T(8,128)}) custom-call(bf16[512,1024]{1,0:T(8,128)(2,1)} %slice.197.rows_ref, f32[512,128]{1,0:T(8,128)} %fusion.13.centre_ref, f32[128,1024]{1,0:T(8,128)} %concatenate.62.geo_ref, bf16[512,128]{1,0:T(8,128)(2,1)} %copy.58.basis_t_ref, ...), custom_call_target="tpu_custom_call" | custom-call | flops 1610612736 | bytes 8388608 | tf_op jit(solution)/shard_map/pallas_call | solution.py:226
  41.5 1.2 %slice_multiply_fusion.4 = (f32[1,1024]{1,0:T(1,128)S(1)}, f32[1,1024]{1,0:T(1,128)S(1)}, f32[1,1024]{1,0:T(1,128)S(1)}, f32[1,1024]{1,0:T(1,128)S(1)}, f32[1,10...) fusion(f32[128,1024]{1,0:T(8,128)} %get-tuple-element.9), kind=kLoop, calls=%fused_computation.149 | loop fusion | flops 5120 | bytes 73728 | tf_op jit(solution)/shard_map/transpose(jvp())/mul | solution.py:70
  42.8 1.0 %fusion.33 = (f32[1024]{0:T(1024)S(1)}, f32[1024]{0:T(1024)S(1)}) fusion(f32[128,1024]{1,0:T(8,128)} %get-tuple-element.9, f32[1024]{0:T(1024)S(1)} %get-tuple-element.67, f32[8]{0:T(128)S(1)} %convert_multiply_fusion, f32[1024]{0:T(1024)S(1)} %get-tuple-element.66), kind=kLoop, calls=%fused_computation.57 | loop fusion | flops 55296 | bytes 49184 | tf_op jit(solution)/shard_map/transpose(jvp())/reduce_sum | solution.py:58
  43.7 1.8 %convert.21 = bf16[512,1024]{1,0:T(8,128)(2,1)S(1)} convert(f32[512,1024]{1,0:T(8,128)} %get-tuple-element.8) | non-fusion elementwise | flops 524288 | bytes 3145728 | tf_op jit(solution)/shard_map/convert
  45.7 1.1 %fusion.7 = f32[320,640]{1,0:T(8,128)S(1)} fusion(bf16[3,1024]{1,0:T(4,128)(2,1)S(1)} %bitcast.180, bf16[512,1024]{1,0:T(8,128)(2,1)S(1)} %convert.21, f32[128,3]{1,0:T(8,128)S(1)} %bitcast.157, s32[1024]{0:T(1024)S(1)} %bitcast.160, bf16[640]{0:T(1024)(128)(2,1)S(1)} %pad.21.clone), kind=kOutput, calls=%fused_computation.9 | convolution fusion | flops 424222720 | bytes 1880832 | tf_op jit(solution)/shard_map/wn,nr->wr/dot_general | solution.py:314
  46.8 1.5 %collective-permute-start.7 = (bf16[16,640]{1,0:T(8,128)(2,1)S(1)}, bf16[16,640]{1,0:T(8,128)(2,1)S(1)}, u32[]{:S(2)}, u32[]{:S(2)}) collective-permute-start(bf16[16,640]{1,0:T(8,128)(2,1)S(1)} %get-tuple-element.31), channel_id=1, source_target_pairs={{3,0},{0,1},{1,2},{2,3},{7,4},{4,5},{5,6},{6,7},{11,8},{8,9},{9,10... | collective-permute-start | bytes 61448 | tf_op jit(solution)/shard_map/ppermute | solution.py:30
  48.3 2.7 %collective-permute-start.6 = (bf16[16,640]{1,0:T(8,128)(2,1)S(1)}, bf16[16,640]{1,0:T(8,128)(2,1)S(1)}, u32[]{:S(2)}, u32[]{:S(2)}) collective-permute-start(bf16[16,640]{1,0:T(8,128)(2,1)S(1)} %get-tuple-element.30), channel_id=1, source_target_pairs={{1,0},{2,1},{3,2},{0,3},{5,4},{6,5},{7,6},{4,7},{9,8},{10,9},{11,1... | collective-permute-start | bytes 61448 | tf_op jit(solution)/shard_map/ppermute | solution.py:30
  51.0 1.5 %collective-permute-done.7 = bf16[16,640]{1,0:T(8,128)(2,1)S(1)} collective-permute-done((bf16[16,640]{1,0:T(8,128)(2,1)S(1)}, bf16[16,640]{1,0:T(8,128)(2,1)S(1)}, u32[]{:S(2)}, u32[]{:S(2)}) %collective-permute-start.7) | collective-permute-done | bytes 20512 | tf_op jit(solution)/shard_map/ppermute | solution.py:30
  53.4 1.3 %collective-permute-start.8 = (bf16[64,640]{1,0:T(8,128)(2,1)S(1)}, bf16[64,640]{1,0:T(8,128)(2,1)S(1)}, u32[]{:S(2)}, u32[]{:S(2)}) collective-permute-start(bf16[64,640]{1,0:T(8,128)(2,1)S(1)} %get-tuple-element.33), channel_id=1, source_target_pairs={{4,0},{0,4},{5,1},{1,5},{6,2},{2,6},{7,3},{3,7},{12,8},{8,12},{13,... | collective-permute-start | bytes 245768 | tf_op jit(solution)/shard_map/ppermute | solution.py:30
  55.3 0.9 %collective-permute-start.9 = (bf16[64,640]{1,0:T(8,128)(2,1)S(1)}, bf16[64,640]{1,0:T(8,128)(2,1)S(1)}, u32[]{:S(2)}, u32[]{:S(2)}) collective-permute-start(bf16[64,640]{1,0:T(8,128)(2,1)S(1)} %get-tuple-element.32), channel_id=1, source_target_pairs={{4,0},{0,4},{5,1},{1,5},{6,2},{2,6},{7,3},{3,7},{12,8},{8,12},{13,... | collective-permute-start | bytes 245768 | tf_op jit(solution)/shard_map/ppermute | solution.py:30
  56.2 1.6 %collective-permute-done.8 = bf16[64,640]{1,0:T(8,128)(2,1)S(1)} collective-permute-done((bf16[64,640]{1,0:T(8,128)(2,1)S(1)}, bf16[64,640]{1,0:T(8,128)(2,1)S(1)}, u32[]{:S(2)}, u32[]{:S(2)}) %collective-permute-start.8) | collective-permute-done | bytes 81952 | tf_op jit(solution)/shard_map/ppermute | solution.py:30
  58.2 1.7 %collective-permute-done.9 = bf16[64,640]{1,0:T(8,128)(2,1)S(1)} collective-permute-done((bf16[64,640]{1,0:T(8,128)(2,1)S(1)}, bf16[64,640]{1,0:T(8,128)(2,1)S(1)}, u32[]{:S(2)}, u32[]{:S(2)}) %collective-permute-start.9) | collective-permute-done | bytes 81952 | tf_op jit(solution)/shard_map/ppermute | solution.py:30
  62.1 2.2 %collective-permute-done.11 = bf16[16,640]{1,0:T(8,128)(2,1)S(1)} collective-permute-done((bf16[16,640]{1,0:T(8,128)(2,1)S(1)}, bf16[16,640]{1,0:T(8,128)(2,1)S(1)}, u32[]{:S(2)}, u32[]{:S(2)}) %collective-permute-start.11) | collective-permute-done | bytes 20512 | tf_op jit(solution)/shard_map/ppermute | solution.py:30
  64.6 1.4 %convolution_add_fusion.1 = f32[128,512]{1,0:T(8,128)} fusion(f32[128,512]{1,0:T(8,128)S(1)} %fusion.105, bf16[512,512]{1,0:T(8,128)(2,1)S(1)} %copy-done.1, f32[128,640]{1,0:T(8,128)S(1)} %fusion.21), kind=kOutput, calls=%fused_computation.12 | convolution fusion | flops 402718720 | bytes 1310720 | tf_op jit(solution)/shard_map/dot_general | solution.py:406
  (104 shorter events, 11.0 us)
Async XLA Ops:
  0.6 9.2 %copy-start = (bf16[512,512]{1,0:T(8,128)(2,1)S(1)}, bf16[512,512]{1,0:T(8,128)(2,1)}, u32[]{:S(2)}) copy-start(bf16[512,512]{1,0:T(8,128)(2,1)} %param.22) | copy-start | bytes 1572868
  0.6 7.2 %copy-start.8 = (s32[1,192]{1,0:T(1,128)S(1)}, s32[1,192]{1,0:T(1,128)}, u32[]{:S(2)}) copy-start(s32[1,192]{1,0:T(1,128)} %param.19) | copy-start | bytes 2308
  0.7 8.7 %copy-start.12 = (s32[128]{0:T(128)S(1)}, s32[128]{0:T(128)}, u32[]{:S(2)}) copy-start(s32[128]{0:T(128)} %param.18) | copy-start | bytes 1540
  0.7 9.1 %copy-start.3 = (bf16[128,512]{1,0:T(8,128)(2,1)S(1)}, bf16[128,512]{1,0:T(8,128)(2,1)}, u32[]{:S(2)}) copy-start(bf16[128,512]{1,0:T(8,128)(2,1)} %param.16) | copy-start | bytes 393220
  0.7 8.0 %copy-start.9 = (bf16[8,512]{1,0:T(8,128)(2,1)S(1)}, bf16[8,512]{1,0:T(8,128)(2,1)}, u32[]{:S(2)}) copy-start(bf16[8,512]{1,0:T(8,128)(2,1)} %param.26) | copy-start | bytes 24580
  0.7 8.7 %copy-start.7 = (f32[5,512]{1,0:T(8,128)S(1)}, f32[5,512]{1,0:T(8,128)}, u32[]{:S(2)}) copy-start(f32[5,512]{1,0:T(8,128)} %param.24) | copy-start | bytes 30724
  3.5 7.4 %copy-start.10 = (s32[1024]{0:T(1024)S(1)}, s32[1024]{0:T(1024)}, u32[]{:S(2)}) copy-start(s32[1024]{0:T(1024)} %param.20) | copy-start | bytes 12292
  3.5 8.3 %copy-start.2 = (bf16[512,512]{1,0:T(8,128)(2,1)S(1)}, bf16[512,512]{1,0:T(8,128)(2,1)}, u32[]{:S(2)}) copy-start(bf16[512,512]{1,0:T(8,128)(2,1)} %update_ref.1) | copy-start | bytes 1572868
  5.1 7.6 %copy-start.4 = (bf16[512,384]{1,0:T(8,128)(2,1)S(1)}, bf16[512,384]{1,0:T(8,128)(2,1)}, u32[]{:S(2)}) copy-start(bf16[512,384]{1,0:T(8,128)(2,1)} %split_ref.1) | copy-start | bytes 1179652
  5.1 9.5 %collective-permute-start = (bf16[16,640]{1,0:T(8,128)(2,1)S(1)}, bf16[16,640]{1,0:T(8,128)(2,1)S(1)}, u32[]{:S(2)}, u32[]{:S(2)}) collective-permute-start(bf16[16,640]{1,0:T(8,128)(2,1)S(1)} %convolution_convert_fusion.5), channel_id=1, source_target_pairs={{24,0},{0,8},{8,16},{16,24},{25,1},{1,9},{9,17},{17,25},{26,2},{2,... | collective-permute-start | bytes 61448 | tf_op jit(solution)/shard_map/ppermute | solution.py:30
  5.8 8.9 %collective-permute-start.1 = (bf16[16,640]{1,0:T(8,128)(2,1)S(1)}, bf16[16,640]{1,0:T(8,128)(2,1)S(1)}, u32[]{:S(2)}, u32[]{:S(2)}) collective-permute-start(bf16[16,640]{1,0:T(8,128)(2,1)S(1)} %convolution_convert_fusion.4), channel_id=1, source_target_pairs={{8,0},{16,8},{24,16},{0,24},{9,1},{17,9},{25,17},{1,25},{10,2},{18... | collective-permute-start | bytes 61448 | tf_op jit(solution)/shard_map/ppermute | solution.py:30
  7.9 5.9 %copy-start.6 = (bf16[192,512]{1,0:T(8,128)(2,1)S(1)}, bf16[192,512]{1,0:T(8,128)(2,1)}, u32[]{:S(2)}) copy-start(bf16[192,512]{1,0:T(8,128)(2,1)} %tensor_ref.1) | copy-start | bytes 589828
  15.0 5.3 %collective-permute-start.2 = (bf16[64,640]{1,0:T(8,128)(2,1)S(1)}, bf16[64,640]{1,0:T(8,128)(2,1)S(1)}, u32[]{:S(2)}, u32[]{:S(2)}) collective-permute-start(bf16[64,640]{1,0:T(8,128)(2,1)S(1)} %convolution_convert_fusion.1), channel_id=1, source_target_pairs={{4,0},{0,4},{5,1},{1,5},{6,2},{2,6},{7,3},{3,7},{12,8},{8,12},{13,... | collective-permute-start | bytes 245768 | tf_op jit(solution)/shard_map/ppermute | solution.py:30
  17.6 4.5 %collective-permute-start.3 = (bf16[64,640]{1,0:T(8,128)(2,1)S(1)}, bf16[64,640]{1,0:T(8,128)(2,1)S(1)}, u32[]{:S(2)}, u32[]{:S(2)}) collective-permute-start(bf16[64,640]{1,0:T(8,128)(2,1)S(1)} %convolution_convert_fusion), channel_id=1, source_target_pairs={{4,0},{0,4},{5,1},{1,5},{6,2},{2,6},{7,3},{3,7},{12,8},{8,12},{13,... | collective-permute-start | bytes 245768 | tf_op jit(solution)/shard_map/ppermute | solution.py:30
  22.3 5.6 %collective-permute-start.4 = (bf16[16,640]{1,0:T(8,128)(2,1)S(1)}, bf16[16,640]{1,0:T(8,128)(2,1)S(1)}, u32[]{:S(2)}, u32[]{:S(2)}) collective-permute-start(bf16[16,640]{1,0:T(8,128)(2,1)S(1)} %convolution_convert_fusion.3), channel_id=1, source_target_pairs={{3,0},{0,1},{1,2},{2,3},{7,4},{4,5},{5,6},{6,7},{11,8},{8,9},{9,10... | collective-permute-start | bytes 61448 | tf_op jit(solution)/shard_map/ppermute | solution.py:30
  24.2 4.0 %collective-permute-start.5 = (bf16[16,640]{1,0:T(8,128)(2,1)S(1)}, bf16[16,640]{1,0:T(8,128)(2,1)S(1)}, u32[]{:S(2)}, u32[]{:S(2)}) collective-permute-start(bf16[16,640]{1,0:T(8,128)(2,1)S(1)} %convolution_convert_fusion.2), channel_id=1, source_target_pairs={{1,0},{2,1},{3,2},{0,3},{5,4},{6,5},{7,6},{4,7},{9,8},{10,9},{11,1... | collective-permute-start | bytes 61448 | tf_op jit(solution)/shard_map/ppermute | solution.py:30
  29.3 2.4 %copy-start.11 = (f32[512]{0:T(512)S(1)}, f32[512]{0:T(512)}, u32[]{:S(2)}) copy-start(f32[512]{0:T(512)} %param.30) | copy-start | bytes 6148
  46.8 7.8 %copy-start.5 = (f32[512,128]{1,0:T(8,128)S(1)}, f32[512,128]{1,0:T(8,128)}, u32[]{:S(2)}) copy-start(f32[512,128]{1,0:T(8,128)} %get-tuple-element.10) | copy-start | bytes 786436
  46.8 5.7 %collective-permute-start.7 = (bf16[16,640]{1,0:T(8,128)(2,1)S(1)}, bf16[16,640]{1,0:T(8,128)(2,1)S(1)}, u32[]{:S(2)}, u32[]{:S(2)}) collective-permute-start(bf16[16,640]{1,0:T(8,128)(2,1)S(1)} %get-tuple-element.31), channel_id=1, source_target_pairs={{3,0},{0,1},{1,2},{2,3},{7,4},{4,5},{5,6},{6,7},{11,8},{8,9},{9,10... | collective-permute-start | bytes 61448 | tf_op jit(solution)/shard_map/ppermute | solution.py:30
  48.3 4.6 %collective-permute-start.6 = (bf16[16,640]{1,0:T(8,128)(2,1)S(1)}, bf16[16,640]{1,0:T(8,128)(2,1)S(1)}, u32[]{:S(2)}, u32[]{:S(2)}) collective-permute-start(bf16[16,640]{1,0:T(8,128)(2,1)S(1)} %get-tuple-element.30), channel_id=1, source_target_pairs={{1,0},{2,1},{3,2},{0,3},{5,4},{6,5},{7,6},{4,7},{9,8},{10,9},{11,1... | collective-permute-start | bytes 61448 | tf_op jit(solution)/shard_map/ppermute | solution.py:30
  53.3 7.0 %copy-start.13 = (f32[5]{0:T(128)S(1)}, f32[5]{0:T(128)}, u32[]{:S(2)}) copy-start(f32[5]{0:T(128)} %param.31) | copy-start | bytes 64
  53.3 7.0 %copy-start.14 = (f32[8,128]{1,0:T(8,128)S(1)}, f32[8,128]{1,0:T(8,128)}, u32[]{:S(2)}) copy-start(f32[8,128]{1,0:T(8,128)} %get-tuple-element.7) | copy-start | bytes 12292
  53.4 4.5 %collective-permute-start.8 = (bf16[64,640]{1,0:T(8,128)(2,1)S(1)}, bf16[64,640]{1,0:T(8,128)(2,1)S(1)}, u32[]{:S(2)}, u32[]{:S(2)}) collective-permute-start(bf16[64,640]{1,0:T(8,128)(2,1)S(1)} %get-tuple-element.33), channel_id=1, source_target_pairs={{4,0},{0,4},{5,1},{1,5},{6,2},{2,6},{7,3},{3,7},{12,8},{8,12},{13,... | collective-permute-start | bytes 245768 | tf_op jit(solution)/shard_map/ppermute | solution.py:30
  54.6 10.0 %copy-start.1 = (bf16[512,512]{1,0:T(8,128)(2,1)S(1)}, bf16[512,512]{1,0:T(8,128)(2,1)}, u32[]{:S(2)}) copy-start(bf16[512,512]{1,0:T(8,128)(2,1)} %param.23) | copy-start | bytes 1572868
  55.3 4.5 %collective-permute-start.9 = (bf16[64,640]{1,0:T(8,128)(2,1)S(1)}, bf16[64,640]{1,0:T(8,128)(2,1)S(1)}, u32[]{:S(2)}, u32[]{:S(2)}) collective-permute-start(bf16[64,640]{1,0:T(8,128)(2,1)S(1)} %get-tuple-element.32), channel_id=1, source_target_pairs={{4,0},{0,4},{5,1},{1,5},{6,2},{2,6},{7,3},{3,7},{12,8},{8,12},{13,... | collective-permute-start | bytes 245768 | tf_op jit(solution)/shard_map/ppermute | solution.py:30
  60.2 1.5 %collective-permute-start.10 = (bf16[16,640]{1,0:T(8,128)(2,1)S(1)}, bf16[16,640]{1,0:T(8,128)(2,1)S(1)}, u32[]{:S(2)}, u32[]{:S(2)}) collective-permute-start(bf16[16,640]{1,0:T(8,128)(2,1)S(1)} %get-tuple-element.44), channel_id=1, source_target_pairs={{8,0},{16,8},{24,16},{0,24},{9,1},{17,9},{25,17},{1,25},{10,2},{18... | collective-permute-start | bytes 61448 | tf_op jit(solution)/shard_map/ppermute | solution.py:30
  61.1 3.2 %collective-permute-start.11 = (bf16[16,640]{1,0:T(8,128)(2,1)S(1)}, bf16[16,640]{1,0:T(8,128)(2,1)S(1)}, u32[]{:S(2)}, u32[]{:S(2)}) collective-permute-start(bf16[16,640]{1,0:T(8,128)(2,1)S(1)} %get-tuple-element.43), channel_id=1, source_target_pairs={{24,0},{0,8},{8,16},{16,24},{25,1},{1,9},{9,17},{17,25},{26,2},{2,... | collective-permute-start | bytes 61448 | tf_op jit(solution)/shard_map/ppermute | solution.py:30

commit v20 on v16

--- a/solution.py
+++ b/solution.py
@@ -157,9 +157,9 @@
         z = _mm(update_t_ref[...], hidden.astype(bf16)) + _mm(tensor_t_ref[...], scalars)
         gate = _sigmoid(z)
         update = z * gate
-        readout = jnp.sum((hidden + update) * energy_w_ref[...], axis=0, keepdims=True)
+        readout = jnp.sum((hidden + update) * twice(energy_w_ref[...]), axis=0, keepdims=True)
         energy = energy + envelope * readout
-        dz = (envelope * energy_w_ref[...]) * (gate * (1.0 + z * (1.0 - gate)))
+        dz = (envelope * twice(energy_w_ref[...])) * (gate * (1.0 + z * (1.0 - gate)))
         dz_low = dz.astype(bf16)
         dscalars = _mm(tensor_ref[...], dz_low).astype(bf16).astype(f32)
         dlow_s[:, at] = _mm(update_ref[...], dz_low)
@@ -200,7 +200,7 @@
             dweights.append(dweight)
         dmixed = jnp.concatenate([damp_s[:, at]] + dweights, axis=0).astype(bf16)
         dlow = dlow_s[:, at] + _mm(split_ref[...], dmixed)
-        dhidden = envelope * energy_w_ref[...] + dlow
+        dhidden = envelope * twice(energy_w_ref[...]) + dlow
         pre = pre_s[:, at]
         sig = _sigmoid(pre)
         act = pre * sig
@@ -261,7 +261,7 @@
         tensor_proj.T,
         tensor_proj,
         basis_pad,
-        jnp.broadcast_to(energy_proj.astype(f32)[:, None], (width, SLOTS * atoms)),
+        jnp.broadcast_to(energy_proj.astype(f32)[:, None], (width, atoms)),
     )
     grad_rows_t, grad_centre_t, grad_geo, energy = outs
     return grad_rows_t, grad_centre_t, grad_geo, energy[0]

time: 68.9 us -> 67.4 us (0.978)
  local copies, waits for them, and re-layouts: 10 us -> 9.26 us
    broadcast_in_dim x1, local copies, waits for them, and re-layouts: 1.56 us -> 0.83 us  [pair_terms(): jnp.broadcast_to(energy_proj.astype(f32)[:, None], (width, atoms))]
where the time goes in v20:
time: 67.4 us; the launch traced here: 67 us
  starting transfers between devices  15.7 us (23%)
  matrix products  14.3 us (21%)
  waiting for transfers between devices  13.3 us (20%)
  local copies, waits for them, and re-layouts  9.26 us (14%)
  Pallas kernels  9.02 us (13%)
  other arithmetic  3.65 us (5%)
  between operations  1.77 us (3%)
    ppermute x12, starting transfers between devices, passed_along(): return lax.ppermute(block, axis, route)  15.7 us
    ppermute x12, waiting for transfers between devices, passed_along(): return lax.ppermute(block, axis, route)  13.3 us
    pallas_call x1, Pallas kernels, pair_terms(): pl.pallas_call(_pair_kernel, out_shape=(jax.ShapeDtypeStruct((width, pair...  9.02 us
    unnamed x38, local copies, waits for them, and re-layouts  3.57 us
    dot_general x2, matrix products, spread_cols(): jnp.einsum('wn,nr->wr', values.astype(jnp.bfloat16), onehot, preferred_el...  3.22 us
    dot_general x2, matrix products, project(): jnp.dot(rows, weight, preferred_element_type=jnp.float32)  2.44 us
    dot_general x3, matrix products, lookup(): return jnp.dot(onehot, table, precision=lax.Precision.HIGHEST)  2.23 us
    dot_general x6, matrix products, spread(): jnp.einsum('nr,nw->rw', onehot, values.astype(jnp.bfloat16), preferred_el...  2.06 us
  transfers between devices with their start and end apart: 12, of which 9 were waited for; matrix products, arithmetic and copies ran while one was open for 14% of the time, Pallas kernels for 0%

profile of v20, /device:TPU:0, one launch (start us, length us, event | category | flops | bytes accessed | tf_op | source)
XLA Modules:
  0.0 67.0 jit_solution(9944415055695581769)
XLA Ops:
  0.7 0.8 %fusion.99 = (f32[3,128]{1,0:T(4,128)S(1)}, bf16[3,128]{1,0:T(4,128)(2,1)S(1)}, bf16[3,128]{1,0:T(4,128)(2,1)S(1)}) fusion(s32[3,128]{1,0:T(4,128)} %param.17), kind=kLoop, calls=%fused_computation.199 | loop fusion | flops 7680 | bytes 4608 | tf_op jit(solution)/shard_map/convert_element_type | solution.py:361
  1.7 0.8 %slice_bitcast_fusion = (s32[16]{0:T(128)S(1)}, s32[16]{0:T(128)S(1)}, s32[16]{0:T(128)S(1)}, s32[16]{0:T(128)S(1)}) fusion(s32[1,192]{1,0:T(1,128)} %param.19), kind=kLoop, calls=%fused_computation.184 | loop fusion | bytes 512 | tf_op jit(solution)/shard_map/eq | solution.py:343
  2.5 1.0 %fusion.25 = f32[128,512]{1,0:T(8,128)S(1)} fusion(f32[5,512]{1,0:T(8,128)} %param.25, s32[128]{0:T(128)} %param.18), kind=kOutput, calls=%fused_computation.50 | convolution fusion | flops 3932800 | bytes 272896 | tf_op jit(solution)/shard_map/dot_general | solution.py:306
  3.5 1.4 %fusion.4 = bf16[128,512]{1,0:T(8,128)(2,1)S(1)} fusion(f32[128,512]{1,0:T(8,128)S(1)} %fusion.25, bf16[128,512]{1,0:T(8,128)(2,1)} %param.16, bf16[512,512]{1,0:T(8,128)(2,1)} %param.23), kind=kOutput, calls=%fused_computation.11 | convolution fusion | flops 67239936 | bytes 1048576 | tf_op jit(solution)/shard_map/dot_general | solution.py:310
  5.8 1.9 %collective-permute-start.1 = (bf16[16,640]{1,0:T(8,128)(2,1)S(1)}, bf16[16,640]{1,0:T(8,128)(2,1)S(1)}, u32[]{:S(2)}, u32[]{:S(2)}) collective-permute-start(bf16[16,640]{1,0:T(8,128)(2,1)S(1)} %convolution_convert_fusion.4), channel_id=1, source_target_pairs={{8,0},{16,8},{24,16},{0,24},{9,1},{17,9},{25,17},{1,25},{10,2},{18... | collective-permute-start | bytes 61448 | tf_op jit(solution)/shard_map/ppermute | solution.py:30
  9.8 1.0 %fusion.6.centre_ref = f32[512,128]{1,0:T(8,128)} fusion(f32[512,128]{1,0:T(8,128)S(1)} %convolution_bitcast_fusion, bf16[512,512]{1,0:T(8,128)(2,1)S(1)} %copy-done, bf16[128,512]{1,0:T(8,128)(2,1)S(1)} %copy-done.3), kind=kOutput, calls=%fused_computation.13 | convolution fusion | flops 67305472 | bytes 1179648 | tf_op jit(solution)/shard_map/dot_general | solution.py:310
  11.8 1.0 %copy.56 = bf16[512,512]{0,1:T(8,128)(2,1)} copy(bf16[512,512]{1,0:T(8,128)(2,1)S(1)} %copy-done.2) | data formatting | bytes 1048576 | tf_op args[12]
  12.8 1.0 %copy.55 = bf16[512,384]{0,1:T(8,128)(2,1)} copy(bf16[512,384]{1,0:T(8,128)(2,1)S(1)} %copy-done.4) | data formatting | bytes 786432 | tf_op args[11]
  13.8 0.8 %copy.57 = bf16[192,512]{0,1:T(8,128)(2,1)} copy(bf16[192,512]{1,0:T(8,128)(2,1)S(1)} %copy-done.6) | data formatting | bytes 393216 | tf_op args[13]
  14.9 2.4 %collective-permute-start.2 = (bf16[64,640]{1,0:T(8,128)(2,1)S(1)}, bf16[64,640]{1,0:T(8,128)(2,1)S(1)}, u32[]{:S(2)}, u32[]{:S(2)}) collective-permute-start(bf16[64,640]{1,0:T(8,128)(2,1)S(1)} %convolution_convert_fusion.1), channel_id=1, source_target_pairs={{4,0},{0,4},{5,1},{1,5},{6,2},{2,6},{7,3},{3,7},{12,8},{8,12},{13,... | collective-permute-start | bytes 245768 | tf_op jit(solution)/shard_map/ppermute | solution.py:30
  17.6 2.6 %collective-permute-done.2 = bf16[64,640]{1,0:T(8,128)(2,1)S(1)} collective-permute-done((bf16[64,640]{1,0:T(8,128)(2,1)S(1)}, bf16[64,640]{1,0:T(8,128)(2,1)S(1)}, u32[]{:S(2)}, u32[]{:S(2)}) %collective-permute-start.2) | collective-permute-done | bytes 81952 | tf_op jit(solution)/shard_map/ppermute | solution.py:30
  20.2 1.8 %collective-permute-done.3 = bf16[64,640]{1,0:T(8,128)(2,1)S(1)} collective-permute-done((bf16[64,640]{1,0:T(8,128)(2,1)S(1)}, bf16[64,640]{1,0:T(8,128)(2,1)S(1)}, u32[]{:S(2)}, u32[]{:S(2)}) %collective-permute-start.3) | collective-permute-done | bytes 81952 | tf_op jit(solution)/shard_map/ppermute | solution.py:30
  22.3 1.6 %collective-permute-start.4 = (bf16[16,640]{1,0:T(8,128)(2,1)S(1)}, bf16[16,640]{1,0:T(8,128)(2,1)S(1)}, u32[]{:S(2)}, u32[]{:S(2)}) collective-permute-start(bf16[16,640]{1,0:T(8,128)(2,1)S(1)} %convolution_convert_fusion.3), channel_id=1, source_target_pairs={{3,0},{0,1},{1,2},{2,3},{7,4},{4,5},{5,6},{6,7},{11,8},{8,9},{9,10... | collective-permute-start | bytes 61448 | tf_op jit(solution)/shard_map/ppermute | solution.py:30
  24.1 2.3 %collective-permute-start.5 = (bf16[16,640]{1,0:T(8,128)(2,1)S(1)}, bf16[16,640]{1,0:T(8,128)(2,1)S(1)}, u32[]{:S(2)}, u32[]{:S(2)}) collective-permute-start(bf16[16,640]{1,0:T(8,128)(2,1)S(1)} %convolution_convert_fusion.2), channel_id=1, source_target_pairs={{1,0},{2,1},{3,2},{0,3},{5,4},{6,5},{7,6},{4,7},{9,8},{10,9},{11,1... | collective-permute-start | bytes 61448 | tf_op jit(solution)/shard_map/ppermute | solution.py:30
  26.4 1.5 %collective-permute-done.4 = bf16[16,640]{1,0:T(8,128)(2,1)S(1)} collective-permute-done((bf16[16,640]{1,0:T(8,128)(2,1)S(1)}, bf16[16,640]{1,0:T(8,128)(2,1)S(1)}, u32[]{:S(2)}, u32[]{:S(2)}) %collective-permute-start.4) | collective-permute-done | bytes 20512 | tf_op jit(solution)/shard_map/ppermute | solution.py:30
  28.1 1.0 %fusion.2 = f32[640,1024]{1,0:T(8,128)S(1)} fusion(bf16[320,640]{1,0:T(8,128)(2,1)S(1)} %constant_dynamic-update-slice_fusion.3, s32[1024]{0:T(1024)S(1)} %bitcast.162), kind=kOutput, calls=%fused_computation.4 | convolution fusion | flops 419758080 | bytes 3035136 | tf_op jit(solution)/shard_map/tw,pt->wp/dot_general | solution.py:358
  29.2 1.1 %slice.197.rows_ref = bf16[512,1024]{1,0:T(8,128)(2,1)} slice(f32[640,1024]{1,0:T(8,128)S(1)} %fusion.2), slice={[0:512], [0:1024]} | slice | bytes 2097152 | tf_op jit(solution)/shard_map/slice | solution.py:359
  30.8 0.9 %concatenate.64.geo_ref = f32[128,1024]{1,0:T(8,128)} pad(f32[18,1024]{1,0:T(8,128)S(1)} %concatenate.63, f32[]{:T(128)} %constant.28.clone.1), padding=0_110x0_0 | pad | bytes 598020 | tf_op jit(solution)/shard_map/jvp()/concatenate | solution.py:80
  31.6 0.8 %broadcast_in_dim.52.energy_w_ref = f32[512,128]{1,0:T(8,128)} broadcast(f32[512]{0:T(512)S(1)} %copy-done.11), dimensions={0} | broadcast | bytes 264192 | tf_op jit(solution)/shard_map/broadcast_in_dim | solution.py:264
  32.4 9.0 %shard_map.175 = (f32[512,1024]{1,0:T(8,128)}, f32[512,128]{1,0:T(8,128)}, f32[128,1024]{1,0:T(8,128)}, f32[8,128]{1,0:T(8,128)}) custom-call(bf16[512,1024]{1,0:T(8,128)(2,1)} %slice.197.rows_ref, f32[512,128]{1,0:T(8,128)} %fusion.6.centre_ref, f32[128,1024]{1,0:T(8,128)} %concatenate.64.geo_ref, bf16[512,128]{1,0:T(8,128)(2,1)} %copy.58.basis_t_ref, ...), custom_call_target="tpu_custom_call" | custom-call | flops 1610612736 | bytes 8388608 | tf_op jit(solution)/shard_map/pallas_call | solution.py:226
  41.5 1.2 %slice_multiply_fusion.4 = (f32[1,1024]{1,0:T(1,128)S(1)}, f32[1,1024]{1,0:T(1,128)S(1)}, f32[1,1024]{1,0:T(1,128)S(1)}, f32[1,1024]{1,0:T(1,128)S(1)}, f32[1,10...) fusion(f32[128,1024]{1,0:T(8,128)} %get-tuple-element.9), kind=kLoop, calls=%fused_computation.148 | loop fusion | flops 5120 | bytes 73728 | tf_op jit(solution)/shard_map/transpose(jvp())/mul | solution.py:70
  42.7 1.0 %fusion.28 = (f32[1024]{0:T(1024)S(1)}, f32[1024]{0:T(1024)S(1)}) fusion(f32[128,1024]{1,0:T(8,128)} %get-tuple-element.9, f32[1024]{0:T(1024)S(1)} %get-tuple-element.67, f32[8]{0:T(128)S(1)} %convert_multiply_fusion, f32[1024]{0:T(1024)S(1)} %get-tuple-element.66), kind=kLoop, calls=%fused_computation.56 | loop fusion | flops 55296 | bytes 49184 | tf_op jit(solution)/shard_map/transpose(jvp())/reduce_sum | solution.py:58
  43.6 2.5 %fusion.1 = f32[512,320]{0,1:T(8,128)S(1)} fusion(f32[512,1024]{1,0:T(8,128)} %get-tuple-element.8, s32[1024]{0:T(1024)S(1)} %bitcast.163), kind=kOutput, calls=%fused_computation.3 | convolution fusion | flops 336396288 | bytes 2756608 | tf_op jit(solution)/shard_map/wn,nr->wr/dot_general | solution.py:314
  47.2 1.5 %collective-permute-start.7 = (bf16[16,640]{1,0:T(8,128)(2,1)S(1)}, bf16[16,640]{1,0:T(8,128)(2,1)S(1)}, u32[]{:S(2)}, u32[]{:S(2)}) collective-permute-start(bf16[16,640]{1,0:T(8,128)(2,1)S(1)} %get-tuple-element.31), channel_id=1, source_target_pairs={{3,0},{0,1},{1,2},{2,3},{7,4},{4,5},{5,6},{6,7},{11,8},{8,9},{9,10... | collective-permute-start | bytes 61448 | tf_op jit(solution)/shard_map/ppermute | solution.py:30
  48.7 2.7 %collective-permute-start.6 = (bf16[16,640]{1,0:T(8,128)(2,1)S(1)}, bf16[16,640]{1,0:T(8,128)(2,1)S(1)}, u32[]{:S(2)}, u32[]{:S(2)}) collective-permute-start(bf16[16,640]{1,0:T(8,128)(2,1)S(1)} %get-tuple-element.30), channel_id=1, source_target_pairs={{1,0},{2,1},{3,2},{0,3},{5,4},{6,5},{7,6},{4,7},{9,8},{10,9},{11,1... | collective-permute-start | bytes 61448 | tf_op jit(solution)/shard_map/ppermute | solution.py:30
  51.4 1.5 %collective-permute-done.7 = bf16[16,640]{1,0:T(8,128)(2,1)S(1)} collective-permute-done((bf16[16,640]{1,0:T(8,128)(2,1)S(1)}, bf16[16,640]{1,0:T(8,128)(2,1)S(1)}, u32[]{:S(2)}, u32[]{:S(2)}) %collective-permute-start.7) | collective-permute-done | bytes 20512 | tf_op jit(solution)/shard_map/ppermute | solution.py:30
  53.7 1.3 %collective-permute-start.8 = (bf16[64,640]{1,0:T(8,128)(2,1)S(1)}, bf16[64,640]{1,0:T(8,128)(2,1)S(1)}, u32[]{:S(2)}, u32[]{:S(2)}) collective-permute-start(bf16[64,640]{1,0:T(8,128)(2,1)S(1)} %get-tuple-element.33), channel_id=1, source_target_pairs={{4,0},{0,4},{5,1},{1,5},{6,2},{2,6},{7,3},{3,7},{12,8},{8,12},{13,... | collective-permute-start | bytes 245768 | tf_op jit(solution)/shard_map/ppermute | solution.py:30
  55.7 0.9 %collective-permute-start.9 = (bf16[64,640]{1,0:T(8,128)(2,1)S(1)}, bf16[64,640]{1,0:T(8,128)(2,1)S(1)}, u32[]{:S(2)}, u32[]{:S(2)}) collective-permute-start(bf16[64,640]{1,0:T(8,128)(2,1)S(1)} %get-tuple-element.32), channel_id=1, source_target_pairs={{4,0},{0,4},{5,1},{1,5},{6,2},{2,6},{7,3},{3,7},{12,8},{8,12},{13,... | collective-permute-start | bytes 245768 | tf_op jit(solution)/shard_map/ppermute | solution.py:30
  56.6 1.6 %collective-permute-done.8 = bf16[64,640]{1,0:T(8,128)(2,1)S(1)} collective-permute-done((bf16[64,640]{1,0:T(8,128)(2,1)S(1)}, bf16[64,640]{1,0:T(8,128)(2,1)S(1)}, u32[]{:S(2)}, u32[]{:S(2)}) %collective-permute-start.8) | collective-permute-done | bytes 81952 | tf_op jit(solution)/shard_map/ppermute | solution.py:30
  58.6 1.6 %collective-permute-done.9 = bf16[64,640]{1,0:T(8,128)(2,1)S(1)} collective-permute-done((bf16[64,640]{1,0:T(8,128)(2,1)S(1)}, bf16[64,640]{1,0:T(8,128)(2,1)S(1)}, u32[]{:S(2)}, u32[]{:S(2)}) %collective-permute-start.9) | collective-permute-done | bytes 81952 | tf_op jit(solution)/shard_map/ppermute | solution.py:30
  62.4 2.2 %collective-permute-done.11 = bf16[16,640]{1,0:T(8,128)(2,1)S(1)} collective-permute-done((bf16[16,640]{1,0:T(8,128)(2,1)S(1)}, bf16[16,640]{1,0:T(8,128)(2,1)S(1)}, u32[]{:S(2)}, u32[]{:S(2)}) %collective-permute-start.11) | collective-permute-done | bytes 20512 | tf_op jit(solution)/shard_map/ppermute | solution.py:30
  65.0 1.4 %convolution_add_fusion.1 = f32[128,512]{1,0:T(8,128)} fusion(f32[128,512]{1,0:T(8,128)S(1)} %fusion.100, bf16[512,512]{1,0:T(8,128)(2,1)S(1)} %copy-done.1, f32[128,640]{1,0:T(8,128)S(1)} %fusion.15), kind=kOutput, calls=%fused_computation.7 | convolution fusion | flops 402718720 | bytes 1310720 | tf_op jit(solution)/shard_map/dot_general | solution.py:403
  (103 shorter events, 10.9 us)
Async XLA Ops:
  0.6 9.2 %copy-start = (bf16[512,512]{1,0:T(8,128)(2,1)S(1)}, bf16[512,512]{1,0:T(8,128)(2,1)}, u32[]{:S(2)}) copy-start(bf16[512,512]{1,0:T(8,128)(2,1)} %param.22) | copy-start | bytes 1572868
  0.6 7.2 %copy-start.8 = (s32[1,192]{1,0:T(1,128)S(1)}, s32[1,192]{1,0:T(1,128)}, u32[]{:S(2)}) copy-start(s32[1,192]{1,0:T(1,128)} %param.19) | copy-start | bytes 2308
  0.7 8.7 %copy-start.12 = (s32[128]{0:T(128)S(1)}, s32[128]{0:T(128)}, u32[]{:S(2)}) copy-start(s32[128]{0:T(128)} %param.18) | copy-start | bytes 1540
  0.7 9.1 %copy-start.3 = (bf16[128,512]{1,0:T(8,128)(2,1)S(1)}, bf16[128,512]{1,0:T(8,128)(2,1)}, u32[]{:S(2)}) copy-start(bf16[128,512]{1,0:T(8,128)(2,1)} %param.16) | copy-start | bytes 393220
  0.7 8.0 %copy-start.9 = (bf16[8,512]{1,0:T(8,128)(2,1)S(1)}, bf16[8,512]{1,0:T(8,128)(2,1)}, u32[]{:S(2)}) copy-start(bf16[8,512]{1,0:T(8,128)(2,1)} %param.26) | copy-start | bytes 24580
  0.7 8.7 %copy-start.7 = (f32[5,512]{1,0:T(8,128)S(1)}, f32[5,512]{1,0:T(8,128)}, u32[]{:S(2)}) copy-start(f32[5,512]{1,0:T(8,128)} %param.24) | copy-start | bytes 30724
  3.5 7.4 %copy-start.10 = (s32[1024]{0:T(1024)S(1)}, s32[1024]{0:T(1024)}, u32[]{:S(2)}) copy-start(s32[1024]{0:T(1024)} %param.20) | copy-start | bytes 12292
  3.5 8.3 %copy-start.2 = (bf16[512,512]{1,0:T(8,128)(2,1)S(1)}, bf16[512,512]{1,0:T(8,128)(2,1)}, u32[]{:S(2)}) copy-start(bf16[512,512]{1,0:T(8,128)(2,1)} %update_ref.1) | copy-start | bytes 1572868
  5.1 7.6 %copy-start.4 = (bf16[512,384]{1,0:T(8,128)(2,1)S(1)}, bf16[512,384]{1,0:T(8,128)(2,1)}, u32[]{:S(2)}) copy-start(bf16[512,384]{1,0:T(8,128)(2,1)} %split_ref.1) | copy-start | bytes 1179652
  5.1 9.5 %collective-permute-start = (bf16[16,640]{1,0:T(8,128)(2,1)S(1)}, bf16[16,640]{1,0:T(8,128)(2,1)S(1)}, u32[]{:S(2)}, u32[]{:S(2)}) collective-permute-start(bf16[16,640]{1,0:T(8,128)(2,1)S(1)} %convolution_convert_fusion.5), channel_id=1, source_target_pairs={{24,0},{0,8},{8,16},{16,24},{25,1},{1,9},{9,17},{17,25},{26,2},{2,... | collective-permute-start | bytes 61448 | tf_op jit(solution)/shard_map/ppermute | solution.py:30
  5.8 8.8 %collective-permute-start.1 = (bf16[16,640]{1,0:T(8,128)(2,1)S(1)}, bf16[16,640]{1,0:T(8,128)(2,1)S(1)}, u32[]{:S(2)}, u32[]{:S(2)}) collective-permute-start(bf16[16,640]{1,0:T(8,128)(2,1)S(1)} %convolution_convert_fusion.4), channel_id=1, source_target_pairs={{8,0},{16,8},{24,16},{0,24},{9,1},{17,9},{25,17},{1,25},{10,2},{18... | collective-permute-start | bytes 61448 | tf_op jit(solution)/shard_map/ppermute | solution.py:30
  7.9 5.9 %copy-start.6 = (bf16[192,512]{1,0:T(8,128)(2,1)S(1)}, bf16[192,512]{1,0:T(8,128)(2,1)}, u32[]{:S(2)}) copy-start(bf16[192,512]{1,0:T(8,128)(2,1)} %tensor_ref.1) | copy-start | bytes 589828
  14.9 5.3 %collective-permute-start.2 = (bf16[64,640]{1,0:T(8,128)(2,1)S(1)}, bf16[64,640]{1,0:T(8,128)(2,1)S(1)}, u32[]{:S(2)}, u32[]{:S(2)}) collective-permute-start(bf16[64,640]{1,0:T(8,128)(2,1)S(1)} %convolution_convert_fusion.1), channel_id=1, source_target_pairs={{4,0},{0,4},{5,1},{1,5},{6,2},{2,6},{7,3},{3,7},{12,8},{8,12},{13,... | collective-permute-start | bytes 245768 | tf_op jit(solution)/shard_map/ppermute | solution.py:30
  17.5 4.5 %collective-permute-start.3 = (bf16[64,640]{1,0:T(8,128)(2,1)S(1)}, bf16[64,640]{1,0:T(8,128)(2,1)S(1)}, u32[]{:S(2)}, u32[]{:S(2)}) collective-permute-start(bf16[64,640]{1,0:T(8,128)(2,1)S(1)} %convolution_convert_fusion), channel_id=1, source_target_pairs={{4,0},{0,4},{5,1},{1,5},{6,2},{2,6},{7,3},{3,7},{12,8},{8,12},{13,... | collective-permute-start | bytes 245768 | tf_op jit(solution)/shard_map/ppermute | solution.py:30
  22.3 5.6 %collective-permute-start.4 = (bf16[16,640]{1,0:T(8,128)(2,1)S(1)}, bf16[16,640]{1,0:T(8,128)(2,1)S(1)}, u32[]{:S(2)}, u32[]{:S(2)}) collective-permute-start(bf16[16,640]{1,0:T(8,128)(2,1)S(1)} %convolution_convert_fusion.3), channel_id=1, source_target_pairs={{3,0},{0,1},{1,2},{2,3},{7,4},{4,5},{5,6},{6,7},{11,8},{8,9},{9,10... | collective-permute-start | bytes 61448 | tf_op jit(solution)/shard_map/ppermute | solution.py:30
  24.1 4.0 %collective-permute-start.5 = (bf16[16,640]{1,0:T(8,128)(2,1)S(1)}, bf16[16,640]{1,0:T(8,128)(2,1)S(1)}, u32[]{:S(2)}, u32[]{:S(2)}) collective-permute-start(bf16[16,640]{1,0:T(8,128)(2,1)S(1)} %convolution_convert_fusion.2), channel_id=1, source_target_pairs={{1,0},{2,1},{3,2},{0,3},{5,4},{6,5},{7,6},{4,7},{9,8},{10,9},{11,1... | collective-permute-start | bytes 61448 | tf_op jit(solution)/shard_map/ppermute | solution.py:30
  29.2 2.4 %copy-start.11 = (f32[512]{0:T(512)S(1)}, f32[512]{0:T(512)}, u32[]{:S(2)}) copy-start(f32[512]{0:T(512)} %param.30) | copy-start | bytes 6148
  47.2 7.8 %copy-start.5 = (f32[512,128]{1,0:T(8,128)S(1)}, f32[512,128]{1,0:T(8,128)}, u32[]{:S(2)}) copy-start(f32[512,128]{1,0:T(8,128)} %get-tuple-element.10) | copy-start | bytes 786436
  47.2 5.7 %collective-permute-start.7 = (bf16[16,640]{1,0:T(8,128)(2,1)S(1)}, bf16[16,640]{1,0:T(8,128)(2,1)S(1)}, u32[]{:S(2)}, u32[]{:S(2)}) collective-permute-start(bf16[16,640]{1,0:T(8,128)(2,1)S(1)} %get-tuple-element.31), channel_id=1, source_target_pairs={{3,0},{0,1},{1,2},{2,3},{7,4},{4,5},{5,6},{6,7},{11,8},{8,9},{9,10... | collective-permute-start | bytes 61448 | tf_op jit(solution)/shard_map/ppermute | solution.py:30
  48.7 4.6 %collective-permute-start.6 = (bf16[16,640]{1,0:T(8,128)(2,1)S(1)}, bf16[16,640]{1,0:T(8,128)(2,1)S(1)}, u32[]{:S(2)}, u32[]{:S(2)}) collective-permute-start(bf16[16,640]{1,0:T(8,128)(2,1)S(1)} %get-tuple-element.30), channel_id=1, source_target_pairs={{1,0},{2,1},{3,2},{0,3},{5,4},{6,5},{7,6},{4,7},{9,8},{10,9},{11,1... | collective-permute-start | bytes 61448 | tf_op jit(solution)/shard_map/ppermute | solution.py:30
  53.7 7.0 %copy-start.13 = (f32[5]{0:T(128)S(1)}, f32[5]{0:T(128)}, u32[]{:S(2)}) copy-start(f32[5]{0:T(128)} %param.31) | copy-start | bytes 64
  53.7 7.0 %copy-start.14 = (f32[8,128]{1,0:T(8,128)S(1)}, f32[8,128]{1,0:T(8,128)}, u32[]{:S(2)}) copy-start(f32[8,128]{1,0:T(8,128)} %get-tuple-element.7) | copy-start | bytes 12292
  53.7 4.5 %collective-permute-start.8 = (bf16[64,640]{1,0:T(8,128)(2,1)S(1)}, bf16[64,640]{1,0:T(8,128)(2,1)S(1)}, u32[]{:S(2)}, u32[]{:S(2)}) collective-permute-start(bf16[64,640]{1,0:T(8,128)(2,1)S(1)} %get-tuple-element.33), channel_id=1, source_target_pairs={{4,0},{0,4},{5,1},{1,5},{6,2},{2,6},{7,3},{3,7},{12,8},{8,12},{13,... | collective-permute-start | bytes 245768 | tf_op jit(solution)/shard_map/ppermute | solution.py:30
  55.0 10.0 %copy-start.1 = (bf16[512,512]{1,0:T(8,128)(2,1)S(1)}, bf16[512,512]{1,0:T(8,128)(2,1)}, u32[]{:S(2)}) copy-start(bf16[512,512]{1,0:T(8,128)(2,1)} %param.23) | copy-start | bytes 1572868
  55.7 4.5 %collective-permute-start.9 = (bf16[64,640]{1,0:T(8,128)(2,1)S(1)}, bf16[64,640]{1,0:T(8,128)(2,1)S(1)}, u32[]{:S(2)}, u32[]{:S(2)}) collective-permute-start(bf16[64,640]{1,0:T(8,128)(2,1)S(1)} %get-tuple-element.32), channel_id=1, source_target_pairs={{4,0},{0,4},{5,1},{1,5},{6,2},{2,6},{7,3},{3,7},{12,8},{8,12},{13,... | collective-permute-start | bytes 245768 | tf_op jit(solution)/shard_map/ppermute | solution.py:30
  60.6 1.5 %collective-permute-start.10 = (bf16[16,640]{1,0:T(8,128)(2,1)S(1)}, bf16[16,640]{1,0:T(8,128)(2,1)S(1)}, u32[]{:S(2)}, u32[]{:S(2)}) collective-permute-start(bf16[16,640]{1,0:T(8,128)(2,1)S(1)} %get-tuple-element.44), channel_id=1, source_target_pairs={{8,0},{16,8},{24,16},{0,24},{9,1},{17,9},{25,17},{1,25},{10,2},{18... | collective-permute-start | bytes 61448 | tf_op jit(solution)/shard_map/ppermute | solution.py:30
  61.4 3.2 %collective-permute-start.11 = (bf16[16,640]{1,0:T(8,128)(2,1)S(1)}, bf16[16,640]{1,0:T(8,128)(2,1)S(1)}, u32[]{:S(2)}, u32[]{:S(2)}) collective-permute-start(bf16[16,640]{1,0:T(8,128)(2,1)S(1)} %get-tuple-element.43), channel_id=1, source_target_pairs={{24,0},{0,8},{8,16},{16,24},{25,1},{1,9},{9,17},{17,25},{26,2},{2,... | collective-permute-start | bytes 61448 | tf_op jit(solution)/shard_map/ppermute | solution.py:30
